TPU v7x, 256 devices: a whole 4x4x8 slice. The times are simulated.
256 devices in a mesh: dp: 8 (over y_lo, x), space: 32 (over y_hi, z, core).
Axes of the slice: x: 4, y: 4 (y_hi: 2, y_lo: 2; y = y_hi * 2 + y_lo), z: 8, core: 2. Of those that a mesh axis runs over, the one named last changes fastest.
Arguments:
- images: bfloat16 [8, 256, 64, 1536], P('dp', 'space'), may hold values from -8 to 8
- dw_kernel: bfloat16 [7, 7, 1536], replicated, may hold values from -0.875 to 0.875
- dw_bias: float32 [1536], replicated, may hold values from -3 to 3
- ln_gain: float32 [1536], replicated, may hold values from 0.1 to 1.9
- ln_shift: float32 [1536], replicated, may hold values from -2 to 2
- proj: bfloat16 [1536, 1024], replicated, may hold values from -0.15625 to 0.15625
- text: float32 [8, 1024], P('dp'), may hold values from -6 to 6
- logit_scale: float32 [1], replicated, may hold values from 10 to 100
Outputs:
- loss: float32 [], replicated
- grad_images: bfloat16 [8, 256, 64, 1536], P('dp', 'space')
- kernel_grad: float32 [7, 7, 1536], replicated
- text_grad: float32 [8, 1024], P('dp')
All inputs are finite; a program needn't handle non-finite values.
Results may differ from a plain program's by a relative error of at most 0.0013.
Values may be sent and summed in bfloat16 or wider, within the bound.
No kernel may reach another device: no remote copies, remote signals or barrier semaphores. Data moves between devices by JAX's collectives and lax.ppermute only.
A program may use at most 128 MiB of HBM per device.

v0:
```python
import jax
import jax.numpy as jnp
from jax import lax
from jax.sharding import PartitionSpec as P


def with_halo(block, sides, width):
    for axis, dim in sides:
        count = lax.axis_size(axis)
        forward = [(i, i + 1) for i in range(count - 1)]
        backward = [(target, source) for source, target in forward]
        low = lax.ppermute(
            lax.slice_in_dim(block, block.shape[dim] - width, None, axis=dim), axis, forward
        )
        high = lax.ppermute(lax.slice_in_dim(block, 0, width, axis=dim), axis, backward)
        block = jnp.concatenate([low, block, high], axis=dim)
    return block


def butterfly_sum(values, axes):
    for axis in axes:
        count = lax.axis_size(axis)
        if count & (count - 1):
            values = lax.psum(values, axis)
            continue
        step = 1
        while step < count:
            pairs = [(i, i ^ step) for i in range(count)]
            values = values + lax.ppermute(values, axis, pairs)
            step *= 2
    return values


def normalize(values):
    centre_value = jnp.mean(values, axis=-1, keepdims=True)
    centred = values - centre_value
    spread = jnp.mean(centred * centred, axis=-1, keepdims=True)
    inv_dev = lax.rsqrt(spread + 1e-06)
    return (centred * inv_dev, inv_dev)


def depthwise(extended, kernel, reach_cols, **options):
    channels = kernel.shape[-1]
    return lax.conv_general_dilated(
        extended,
        kernel.reshape(kernel.shape[0], kernel.shape[1], 1, channels),
        (1, 1),
        ((0, 0), (reach_cols, reach_cols)),
        dimension_numbers=("NHWC", "HWIO", "NHWC"),
        feature_group_count=channels,
        **options,
    )


def logsum(scores, axis):
    highest = jnp.max(scores, axis=axis, keepdims=True)
    return jnp.squeeze(highest, axis) + jnp.log(jnp.sum(jnp.exp(scores - highest), axis=axis))


def shards(images, dw_kernel, dw_bias, ln_gain, ln_shift, proj, text, logit_scale):
    batch_dev, row_count, col_count, channels = images.shape
    height = row_count * lax.axis_size("space")
    pixel_count = height * col_count
    batch_count = batch_dev * lax.axis_size("dp")
    reach_rows = dw_kernel.shape[0] // 2
    kernel_float = dw_kernel.astype(jnp.float32)
    extended = with_halo(images, (("space", 1),), reach_rows)
    padded_all = jnp.pad(
        extended.astype(jnp.float32), ((0, 0), (0, 0), (reach_rows, reach_rows), (0, 0))
    )
    conv_out = (
        depthwise(extended, dw_kernel, reach_rows, preferred_element_type=jnp.float32) + dw_bias
    )
    normed, inv_dev = normalize(conv_out)
    pool_part = jnp.sum(normed * ln_gain + ln_shift, axis=(1, 2))
    pool_sum = butterfly_sum(pool_part, ("space",))
    first_row = lax.axis_index("dp") * batch_dev
    packed = jnp.concatenate([pool_sum, text], axis=1)
    table = lax.dynamic_update_slice(
        jnp.zeros((batch_count, packed.shape[1]), jnp.float32), packed, (first_row, 0)
    )
    table = butterfly_sum(table, ("dp",))
    pooled = table[:, :channels] / pixel_count
    all_text = table[:, channels:]
    proj_float = proj.astype(jnp.float32)
    embedded = jnp.dot(pooled, proj_float, precision=lax.Precision.HIGHEST)
    emb_norm = jnp.sqrt(jnp.sum(embedded * embedded, axis=-1, keepdims=True))
    unit_img = embedded / emb_norm
    text_norm = jnp.sqrt(jnp.sum(all_text * all_text, axis=-1, keepdims=True))
    unit_txt = all_text / text_norm
    factor = logit_scale[0]
    scores = factor * jnp.dot(unit_img, unit_txt.T, precision=lax.Precision.HIGHEST)
    row_logsum = logsum(scores, 1)
    col_logsum = logsum(scores, 0)
    identity = jnp.eye(batch_count, dtype=jnp.float32)
    diagonal = jnp.sum(scores * identity, axis=1)
    loss = (jnp.sum(row_logsum - diagonal) + jnp.sum(col_logsum - diagonal)) / (2 * batch_count)
    score_grad = (
        0.5
        * (
            jnp.exp(scores - row_logsum[:, None])
            + jnp.exp(scores - col_logsum[None, :])
        )
        - identity
    )
    unit_img_grad = factor * jnp.dot(score_grad, unit_txt, precision=lax.Precision.HIGHEST)
    unit_txt_grad = factor * jnp.dot(score_grad.T, unit_img, precision=lax.Precision.HIGHEST)
    text_grad_all = (
        unit_txt_grad - unit_txt * jnp.sum(unit_txt * unit_txt_grad, axis=-1, keepdims=True)
    ) / text_norm
    emb_grad_all = (
        unit_img_grad - unit_img * jnp.sum(unit_img * unit_img_grad, axis=-1, keepdims=True)
    ) / emb_norm
    text_grad = lax.dynamic_slice_in_dim(text_grad_all, first_row, batch_dev, axis=0)
    emb_grad = lax.dynamic_slice_in_dim(emb_grad_all, first_row, batch_dev, axis=0)
    weighted = jnp.dot(emb_grad, proj_float.T, precision=lax.Precision.HIGHEST) * ln_gain
    weight_rows = weighted[:, None, None, :]
    weight_mean = jnp.mean(weighted, axis=-1)[:, None, None, None]
    spread_term = jnp.mean(weight_rows * normed, axis=-1, keepdims=True)
    grad_own = inv_dev * (weight_rows - weight_mean - normed * spread_term)
    grad_wide = with_halo(grad_own, (("space", 1),), reach_rows)
    input_grad = depthwise(
        grad_wide, kernel_float[::-1, ::-1], reach_rows, precision=lax.Precision.HIGHEST
    )
    kernel_part = jnp.stack(
        [
            jnp.stack(
                [
                    jnp.sum(
                        grad_own * padded_all[:, a : a + row_count, d : d + col_count, :],
                        axis=(0, 1, 2),
                    )
                    for d in range(kernel_float.shape[1])
                ]
            )
            for a in range(kernel_float.shape[0])
        ]
    )
    kernel_grad = butterfly_sum(kernel_part, ("space", "dp")) / pixel_count
    return (loss, input_grad.astype(jnp.bfloat16), kernel_grad, text_grad)


def solution(mesh):
    placed = (P("dp", "space", None, None), P(), P(), P(), P(), P(), P("dp", None), P())
    return jax.shard_map(
        shards,
        mesh=mesh,
        in_specs=placed,
        out_specs=(P(), P("dp", "space", None, None), P(), P("dp", None)),
        check_vma=False,
    )
```

profile of v0, /device:TPU:28, one launch (start us, length us, event | category | flops | bytes accessed | tf_op | source)
XLA Modules:
  0.0 384.8 jit_solution(1527274902223453817)
XLA Ops:
  0.7 1.5 fusion.59
  2.1 2.1 collective-permute-start
  4.2 7.9 %collective-permute-start.1 = (bf16[1,3,64,1536]{3,2,1,0:T(8,128)(2,1)S(1)}, bf16[1,3,64,1536]{3,2,1,0:T(8,128)(2,1)S(1)}, u32[]{:S(2)}, u32[]{:S(2)}) collective-permute-start(bf16[1,3,64,1536]{3,2,1,0:T(8,128)(2,1)S(1)} %get-tuple-element.78), channel_id=1, source_target_pairs={{1,0},{2,1},{3,2},{4,3},{5,4},{6,5},{7,6},{8,7},{9,8},{10,9},{11,1... | collective-permute-start | bytes 1769480 | tf_op jit(solution)/shard_map/ppermute | solution.py:15
  12.1 0.9 copy.28
  13.0 4.7 %collective-permute-done = bf16[1,3,64,1536]{3,2,1,0:T(8,128)(2,1)S(1)} collective-permute-done((bf16[1,3,64,1536]{3,2,1,0:T(8,128)(2,1)S(1)}, bf16[1,3,64,1536]{3,2,1,0:T(8,128)(2,1)S(1)}, u32[]{:S(2)}, u32[]{:S(2)}) %collective-permute-start) | collective-permute-done | bytes 589856 | tf_op jit(solution)/shard_map/ppermute | solution.py:12
  18.2 1.2 collective-permute-done.1
  20.0 4.1 %fusion.28 = (f32[1,14,64,1536]{3,1,2,0:T(8,128)}, bf16[14,1,64,1536]{3,0,2,1:T(8,128)(2,1)S(1)}) fusion(bf16[1,3,64,1536]{3,1,2,0:T(4,128)(2,1)S(1)} %copy.29, bf16[1,8,64,1536]{3,1,2,0:T(8,128)(2,1)S(1)} %copy.28, bf16[1,3,64,1536]{3,1,2,0:T(4,128)(2,1)S(1)} %copy.27), kind=kLoop, calls=%fused_computation.84 | loop fusion | flops 9633792 | bytes 11010048 | tf_op jit(solution)/shard_map/convert_element_type | solution.py:69
  24.4 1.7 copy.31
  27.1 14.5 %select_add_fusion = f32[8,8,9,1536]{3,1,2,0:T(8,128)S(1)} fusion(bf16[14,1,7,6,1536]{4,2,3,0,1:T(8,128)(2,1)S(1)} %slice.231, bf16[14,1,8,9,1536]{4,2,3,0,1:T(8,128)(2,1)S(1)} %copy.31, f32[1536]{0:T(1024)S(1)} %copy-done.15, pred[8,9]{0,1:T(8,128)(4,1)S(1)} %copy-done.16, bf16[7,7,1,1536]{3,1,0,2:T(8,128)(2,1)S(1)} %bitcast.72), kind=kOutput, calls=%fused_computation.17 | convolution fusion | flops 103956480 | bytes 8598600 | tf_op jit(solution)/shard_map/conv_general_dilated | solution.py:44
  41.6 2.1 copy.33
  44.4 1.1 copy-done.2
  46.2 1.2 collective-permute-done.2
  47.5 3.6 collective-permute-done.3
  51.1 3.3 collective-permute-start.4
  54.4 1.6 collective-permute-done.4
  56.1 3.9 %collective-permute-start.5 = (f32[1,1536]{1,0:T(1,128)S(1)}, f32[1,1536]{1,0:T(1,128)S(1)}, u32[]{:S(2)}, u32[]{:S(2)}) collective-permute-start(f32[1,1536]{1,0:T(1,128)S(1)} %add.111), channel_id=1, source_target_pairs={{0,8},{1,9},{2,10},{3,11},{4,12},{5,13},{6,14},{7,15},{8,0},{9,1},... | collective-permute-start | bytes 18440 | tf_op jit(solution)/shard_map/ppermute | solution.py:29
  60.0 3.7 collective-permute-done.5
  63.7 1.3 collective-permute-start.6
  65.0 3.9 %collective-permute-done.6 = f32[1,1536]{1,0:T(1,128)S(1)} collective-permute-done((f32[1,1536]{1,0:T(1,128)S(1)}, f32[1,1536]{1,0:T(1,128)S(1)}, u32[]{:S(2)}, u32[]{:S(2)}) %collective-permute-start.6) | collective-permute-done | bytes 6176 | tf_op jit(solution)/shard_map/ppermute | solution.py:29
  69.2 1.3 collective-permute-start.7
  70.5 3.8 collective-permute-done.7
  74.8 5.8 %collective-permute-done.8 = f32[8,2560]{1,0:T(8,128)S(1)} collective-permute-done((f32[8,2560]{1,0:T(8,128)S(1)}, f32[8,2560]{1,0:T(8,128)S(1)}, u32[]{:S(2)}, u32[]{:S(2)}) %collective-permute-start.8) | collective-permute-done | bytes 81952 | tf_op jit(solution)/shard_map/ppermute | solution.py:29
  80.7 0.8 collective-permute-start.9
  82.1 3.0 collective-permute-done.9
  85.3 1.4 multiply_reduce_fusion.47
  89.7 3.8 convolution_reduce_fusion
  95.4 55.3 %multiply_reduce_fusion = (f32[1536]{0:T(1024)S(1)}, f32[1536]{0:T(1024)S(1)}, f32[1536]{0:T(1024)S(1)}, f32[1536]{0:T(1024)S(1)}, f32[1536]{0:T(1024)S(1)}, /*i...) fusion(f32[1,14,64,1536]{3,1,2,0:T(8,128)} %get-tuple-element.7, ...), kind=kLoop, calls=%fused_computation.34 | loop fusion | flops 32216064 | bytes 22142976 | tf_op jit(solution)/shard_map/reduce_sum | solution.py:129
  150.7 42.4 %multiply_reduce_fusion.15 = (f32[1536]{0:T(1024)S(1)}, f32[1536]{0:T(1024)S(1)}, f32[1536]{0:T(1024)S(1)}, f32[1536]{0:T(1024)S(1)}, f32[1536]{0:T(1024)S(1)}, ...) fusion(f32[1,8,64,1536]{3,1,2,0:T(8,128)S(1)} %get-tuple-elemen, ...), kind=kLoop, calls=%fused_computation.49 | loop fusion | flops 28283904 | bytes 15839232 | tf_op jit(solution)/shard_map/reduce_sum | solution.py:129
  193.1 23.5 %multiply_reduce_fusion.31 = (f32[1536]{0:T(1024)S(1)}, f32[1536]{0:T(1024)S(1)}, f32[1536]{0:T(1024)S(1)}, f32[1536]{0:T(1024)S(1)}, f32[1536]{0:T(1024)S(1)}, ...) fusion(f32[1,8,64,1536]{3,1,2,0:T(8,128)S(1)} %get-tuple-elemen, ...), kind=kLoop, calls=%fused_computation.65 | loop fusion | flops 20427264 | bytes 15808512 | tf_op jit(solution)/shard_map/reduce_sum | solution.py:129
  243.2 1.5 stack.208
  244.7 0.8 bitcast_dynamic-update-slice_fusion.5
  245.5 1.5 stack.217
  247.7 1.5 stack.226
  250.0 1.5 stack.235
  251.5 0.8 bitcast_dynamic-update-slice_fusion.2
  252.3 1.5 stack.244
  254.5 1.5 stack.253
  256.0 0.8 bitcast_dynamic-update-slice_fusion
  256.8 1.6 collective-permute-done.12
  258.5 2.4 collective-permute-start.13
  261.4 1.4 copy.34
  262.8 1.9 collective-permute-start.10
  264.7 1.4 copy.35
  266.1 7.2 %collective-permute-start.11 = (f32[1,3,64,1536]{3,2,1,0:T(8,128)}, f32[1,3,64,1536]{3,2,1,0:T(8,128)}, u32[]{:S(2)}, u32[]{:S(2)}) collective-permute-start(f32[1,3,64,1536]{3,2,1,0:T(8,128)} %copy.35), channel_id=1, source_target_pairs={{1,0},{2,1},{3,2},{4,3},{5,4},{6,5},{7,6},{8,7},{9,8},{10,9},{11,1... | collective-permute-start | bytes 3538952 | tf_op jit(solution)/shard_map/ppermute | solution.py:15
  273.5 30.1 %collective-permute-done.14 = f32[7,7,1536]{2,1,0:T(8,128)S(1)} collective-permute-done((f32[7,7,1536]{2,1,0:T(8,128)S(1)}, f32[7,7,1536]{2,1,0:T(8,128)S(1)}, u32[]{:S(2)}, u32[]{:S(2)}) %collective-permute-start.14) | collective-permute-done | bytes 301088 | tf_op jit(solution)/shard_map/ppermute | solution.py:29
  303.7 3.1 collective-permute-start.15
  306.8 6.1 %rev.3 = f32[7,7,1536]{2,1,0:T(8,128)} reverse(bf16[7,7,1536]{2,1,0:T(8,128)(2,1)} %param.9), dimensions={0,1} | reverse | bytes 451584 | tf_op jit(solution)/shard_map/rev | solution.py:123
  312.8 1.3 dynamic-slice.4
  314.1 4.2 %collective-permute-done.15 = f32[7,7,1536]{2,1,0:T(8,128)} collective-permute-done((f32[7,7,1536]{2,1,0:T(8,128)S(1)}, f32[7,7,1536]{2,1,0:T(8,128)}, u32[]{:S(2)}, u32[]{:S(2)}) %collective-permute-start.15) | collective-permute-done | bytes 301088 | tf_op jit(solution)/shard_map/ppermute | solution.py:29
  318.3 1.1 add.125
  319.5 1.8 collective-permute-start.16
  321.2 1.6 multiply_reduce_fusion.44
  324.7 2.7 fusion.34
  327.5 2.1 copy.36
  329.6 2.1 copy.37
  331.7 1.0 add.126
  332.7 1.4 collective-permute-start.17
  334.1 1.2 maximum_bitcast_fusion
  335.3 16.9 %copy.44 = f32[14,1,64,1536]{3,1,2,0:T(1,128)S(1)} copy(f32[14,1,64,1536]{3,0,2,1:T(8,128)S(1)} %maximum_bitcast_fusion) | data formatting | bytes 11010048
  352.2 4.3 %pad.7.clone = f32[14,1,72,1536]{3,1,2,0:T(1,128)S(1)} pad(f32[14,1,64,1536]{3,1,2,0:T(1,128)S(1)} %copy.44, f32[]{:T(128)} %constant.30.clone.1), padding=0_0x0_0x3_5x0_0 | pad | bytes 11698180 | tf_op jit(solution)/shard_map/concatenate | solution.py:16
  357.6 1.6 collective-permute-start.18
  359.2 15.6 %select_convert_fusion = bf16[8,8,9,1536]{3,1,2,0:T(8,128)(2,1)S(1)} fusion(f32[14,1,7,6,1536]{4,2,3,0,1:T(8,128)S(1)} %slice.237, f32[14,1,8,9,1536]{4,2,3,0,1:T(8,128)S(1)} %copy.40, pred[8,9]{0,1:T(8,128)(4,1)S(1)} %copy-done.17, f32[7,7,1,1536]{3,1,0,2:T(8,128)S(1)} %bitcast.71), kind=kOutput, calls=%fused_computation.16 | convolution fusion | flops 529735680 | bytes 11876424 | tf_op jit(solution)/shard_map/conv_general_dilated | solution.py:44
  375.5 1.6 copy.43
  377.1 5.5 %collective-permute-done.19 = f32[7,7,1536]{2,1,0:T(8,128)S(1)} collective-permute-done((f32[7,7,1536]{2,1,0:T(8,128)S(1)}, f32[7,7,1536]{2,1,0:T(8,128)S(1)}, u32[]{:S(2)}, u32[]{:S(2)}) %collective-permute-start.19) | collective-permute-done | bytes 301088 | tf_op jit(solution)/shard_map/ppermute | solution.py:29
  (149 shorter events, 41.7 us)
Async XLA Ops:
  0.6 84.7 %copy-start = (bf16[1536,1024]{1,0:T(8,128)(2,1)S(1)}, bf16[1536,1024]{1,0:T(8,128)(2,1)}, u32[]{:S(2)}) copy-start(bf16[1536,1024]{1,0:T(8,128)(2,1)} %param.13) | copy-start | bytes 9437188
  0.6 11.4 %copy-start.4 = (bf16[1,8,64,1536]{3,2,1,0:T(8,128)(2,1)S(1)}, bf16[1,8,64,1536]{3,2,1,0:T(8,128)(2,1)}, u32[]{:S(2)}) copy-start(bf16[1,8,64,1536]{3,2,1,0:T(8,128)(2,1)} %param.8) | copy-start | bytes 4718596
  2.1 15.6 %collective-permute-start = (bf16[1,3,64,1536]{3,2,1,0:T(8,128)(2,1)S(1)}, bf16[1,3,64,1536]{3,2,1,0:T(8,128)(2,1)S(1)}, u32[]{:S(2)}, u32[]{:S(2)}) collective-permute-start(bf16[1,3,64,1536]{3,2,1,0:T(8,128)(2,1)S(1)} %get-tuple-element.77), channel_id=1, source_target_pairs={{0,1},{1,2},{2,3},{3,4},{4,5},{5,6},{6,7},{7,8},{8,9},{9,10},{10,1... | collective-permute-start | bytes 1769480 | tf_op jit(solution)/shard_map/ppermute | solution.py:12
  4.2 15.3 %collective-permute-start.1 = (bf16[1,3,64,1536]{3,2,1,0:T(8,128)(2,1)S(1)}, bf16[1,3,64,1536]{3,2,1,0:T(8,128)(2,1)S(1)}, u32[]{:S(2)}, u32[]{:S(2)}) collective-permute-start(bf16[1,3,64,1536]{3,2,1,0:T(8,128)(2,1)S(1)} %get-tuple-element.78), channel_id=1, source_target_pairs={{1,0},{2,1},{3,2},{4,3},{5,4},{6,5},{7,6},{8,7},{9,8},{10,9},{11,1... | collective-permute-start | bytes 1769480 | tf_op jit(solution)/shard_map/ppermute | solution.py:15
  26.2 0.9 copy-start.7
  26.2 0.9 copy-start.15
  26.2 0.9 copy-start.16
  43.7 1.8 copy-start.2
  43.7 1.8 copy-start.9
  43.7 1.8 copy-start.11
  43.9 25.0 %copy-start.10 = (f32[1,1024]{1,0:T(1,128)S(1)}, f32[1,1024]{1,0:T(1,128)}, u32[]{:S(2)}) copy-start(f32[1,1024]{1,0:T(1,128)} %param.14) | copy-start | bytes 12292
  46.1 1.3 collective-permute-start.2
  47.4 3.7 collective-permute-start.3
  51.1 4.9 %collective-permute-start.4 = (f32[1,1536]{1,0:T(1,128)S(1)}, f32[1,1536]{1,0:T(1,128)S(1)}, u32[]{:S(2)}, u32[]{:S(2)}) collective-permute-start(f32[1,1536]{1,0:T(1,128)S(1)} %add.110), channel_id=1, source_target_pairs={{0,4},{1,5},{2,6},{3,7},{4,0},{5,1},{6,2},{7,3},{8,12},{9,13},{10,... | collective-permute-start | bytes 18440 | tf_op jit(solution)/shard_map/ppermute | solution.py:29
  56.1 7.6 %collective-permute-start.5 = (f32[1,1536]{1,0:T(1,128)S(1)}, f32[1,1536]{1,0:T(1,128)S(1)}, u32[]{:S(2)}, u32[]{:S(2)}) collective-permute-start(f32[1,1536]{1,0:T(1,128)S(1)} %add.111), channel_id=1, source_target_pairs={{0,8},{1,9},{2,10},{3,11},{4,12},{5,13},{6,14},{7,15},{8,0},{9,1},... | collective-permute-start | bytes 18440 | tf_op jit(solution)/shard_map/ppermute | solution.py:29
  63.7 5.2 %collective-permute-start.6 = (f32[1,1536]{1,0:T(1,128)S(1)}, f32[1,1536]{1,0:T(1,128)S(1)}, u32[]{:S(2)}, u32[]{:S(2)}) collective-permute-start(f32[1,1536]{1,0:T(1,128)S(1)} %add.112), channel_id=1, source_target_pairs={{0,16},{1,17},{2,18},{3,19},{4,20},{5,21},{6,22},{7,23},{8,24},{9,... | collective-permute-start | bytes 18440 | tf_op jit(solution)/shard_map/ppermute | solution.py:29
  69.2 5.1 %collective-permute-start.7 = (f32[8,2560]{1,0:T(8,128)S(1)}, f32[8,2560]{1,0:T(8,128)S(1)}, u32[]{:S(2)}, u32[]{:S(2)}) collective-permute-start(f32[8,2560]{1,0:T(8,128)S(1)} %dynamic_update_slice.5), channel_id=1, source_target_pairs={{0,32},{32,0},{64,96},{96,64},{128,160},{160,128},{192,224},{224,1... | collective-permute-start | bytes 245768 | tf_op jit(solution)/shard_map/ppermute | solution.py:29
  74.6 6.0 %collective-permute-start.8 = (f32[8,2560]{1,0:T(8,128)S(1)}, f32[8,2560]{1,0:T(8,128)S(1)}, u32[]{:S(2)}, u32[]{:S(2)}) collective-permute-start(f32[8,2560]{1,0:T(8,128)S(1)} %add.115), channel_id=1, source_target_pairs={{0,64},{32,96},{64,0},{96,32},{128,192},{160,224},{192,128},{224,1... | collective-permute-start | bytes 245768 | tf_op jit(solution)/shard_map/ppermute | solution.py:29
  80.7 4.5 %collective-permute-start.9 = (f32[8,2560]{1,0:T(8,128)S(1)}, f32[8,2560]{1,0:T(8,128)S(1)}, u32[]{:S(2)}, u32[]{:S(2)}) collective-permute-start(f32[8,2560]{1,0:T(8,128)S(1)} %add.116), channel_id=1, source_target_pairs={{0,128},{32,160},{64,192},{96,224},{128,0},{160,32},{192,64},{224,... | collective-permute-start | bytes 245768 | tf_op jit(solution)/shard_map/ppermute | solution.py:29
  85.3 8.8 %copy-start.3 = (f32[8,8,9,1536]{3,0,2,1:T(8,128)S(1)}, f32[8,8,9,1536]{3,0,2,1:T(8,128)}, u32[]{:S(2)}) copy-start(f32[8,8,9,1536]{3,0,2,1:T(8,128)} %copy-done.2) | copy-start | bytes 10616836
  86.8 1.2 copy-start.14
  87.8 0.9 copy-start.8
  88.6 1.0 copy-start.12
  88.6 1.0 copy-start.13
  256.8 1.7 collective-permute-start.12
  258.5 14.8 %collective-permute-start.13 = (f32[7,7,1536]{2,1,0:T(8,128)S(1)}, f32[7,7,1536]{2,1,0:T(8,128)S(1)}, u32[]{:S(2)}, u32[]{:S(2)}) collective-permute-start(f32[7,7,1536]{2,1,0:T(8,128)S(1)} %add.122), channel_id=1, source_target_pairs={{0,2},{1,3},{2,0},{3,1},{4,6},{5,7},{6,4},{7,5},{8,10},{9,11},{10,... | collective-permute-start | bytes 903176 | tf_op jit(solution)/shard_map/ppermute | solution.py:29
  262.8 64.7 %collective-permute-start.10 = (f32[1,3,64,1536]{3,2,1,0:T(8,128)}, f32[1,3,64,1536]{3,2,1,0:T(8,128)}, u32[]{:S(2)}, u32[]{:S(2)}) collective-permute-start(f32[1,3,64,1536]{3,2,1,0:T(8,128)} %copy.34), channel_id=1, source_target_pairs={{0,1},{1,2},{2,3},{3,4},{4,5},{5,6},{6,7},{7,8},{8,9},{9,10},{10,1... | collective-permute-start | bytes 3538952 | tf_op jit(solution)/shard_map/ppermute | solution.py:12
  266.1 63.5 %collective-permute-start.11 = (f32[1,3,64,1536]{3,2,1,0:T(8,128)}, f32[1,3,64,1536]{3,2,1,0:T(8,128)}, u32[]{:S(2)}, u32[]{:S(2)}) collective-permute-start(f32[1,3,64,1536]{3,2,1,0:T(8,128)} %copy.35), channel_id=1, source_target_pairs={{1,0},{2,1},{3,2},{4,3},{5,4},{6,5},{7,6},{8,7},{9,8},{10,9},{11,1... | collective-permute-start | bytes 3538952 | tf_op jit(solution)/shard_map/ppermute | solution.py:15
  273.4 30.2 %collective-permute-start.14 = (f32[7,7,1536]{2,1,0:T(8,128)S(1)}, f32[7,7,1536]{2,1,0:T(8,128)S(1)}, u32[]{:S(2)}, u32[]{:S(2)}) collective-permute-start(f32[7,7,1536]{2,1,0:T(8,128)S(1)} %add.123), channel_id=1, source_target_pairs={{0,4},{1,5},{2,6},{3,7},{4,0},{5,1},{6,2},{7,3},{8,12},{9,13},{10,... | collective-permute-start | bytes 903176 | tf_op jit(solution)/shard_map/ppermute | solution.py:29
  303.7 10.5 %copy-start.5 = (f32[7,7,1536]{2,1,0:T(8,128)}, f32[7,7,1536]{2,1,0:T(8,128)S(1)}, u32[]{:S(2)}) copy-start(f32[7,7,1536]{2,1,0:T(8,128)S(1)} %add.124) | copy-start | bytes 903172
  303.7 14.7 %collective-permute-start.15 = (f32[7,7,1536]{2,1,0:T(8,128)S(1)}, f32[7,7,1536]{2,1,0:T(8,128)}, u32[]{:S(2)}, u32[]{:S(2)}) collective-permute-start(f32[7,7,1536]{2,1,0:T(8,128)S(1)} %add.124), channel_id=1, source_target_pairs={{0,8},{1,9},{2,10},{3,11},{4,12},{5,13},{6,14},{7,15},{8,0},{9,1},... | collective-permute-start | bytes 903176 | tf_op jit(solution)/shard_map/ppermute | solution.py:29
  319.5 12.2 %collective-permute-start.16 = (f32[7,7,1536]{2,1,0:T(8,128)S(1)}, f32[7,7,1536]{2,1,0:T(8,128)}, u32[]{:S(2)}, u32[]{:S(2)}) collective-permute-start(f32[7,7,1536]{2,1,0:T(8,128)S(1)} %add.125), channel_id=1, source_target_pairs={{0,16},{1,17},{2,18},{3,19},{4,20},{5,21},{6,22},{7,23},{8,24},{9,... | collective-permute-start | bytes 903176 | tf_op jit(solution)/shard_map/ppermute | solution.py:29
  332.7 24.8 %collective-permute-start.17 = (f32[7,7,1536]{2,1,0:T(8,128)S(1)}, f32[7,7,1536]{2,1,0:T(8,128)S(1)}, u32[]{:S(2)}, u32[]{:S(2)}) collective-permute-start(f32[7,7,1536]{2,1,0:T(8,128)S(1)} %add.126), channel_id=1, source_target_pairs={{0,32},{32,0},{64,96},{96,64},{128,160},{160,128},{192,224},{224,1... | collective-permute-start | bytes 903176 | tf_op jit(solution)/shard_map/ppermute | solution.py:29
  357.0 2.1 copy-start.6
  357.0 2.1 copy-start.17
  357.6 17.7 %collective-permute-start.18 = (f32[7,7,1536]{2,1,0:T(8,128)S(1)}, f32[7,7,1536]{2,1,0:T(8,128)S(1)}, u32[]{:S(2)}, u32[]{:S(2)}) collective-permute-start(f32[7,7,1536]{2,1,0:T(8,128)S(1)} %add.127), channel_id=1, source_target_pairs={{0,64},{32,96},{64,0},{96,32},{128,192},{160,224},{192,128},{224,1... | collective-permute-start | bytes 903176 | tf_op jit(solution)/shard_map/ppermute | solution.py:29
  375.3 7.3 %collective-permute-start.19 = (f32[7,7,1536]{2,1,0:T(8,128)S(1)}, f32[7,7,1536]{2,1,0:T(8,128)S(1)}, u32[]{:S(2)}, u32[]{:S(2)}) collective-permute-start(f32[7,7,1536]{2,1,0:T(8,128)S(1)} %add.128), channel_id=1, source_target_pairs={{0,128},{32,160},{64,192},{96,224},{128,0},{160,32},{192,64},{224,... | collective-permute-start | bytes 903176 | tf_op jit(solution)/shard_map/ppermute | solution.py:29
  375.4 8.0 %copy-start.1 = (bf16[1536,1024]{1,0:T(8,128)(2,1)S(1)}, bf16[1536,1024]{1,0:T(8,128)(2,1)}, u32[]{:S(2)}) copy-start(bf16[1536,1024]{1,0:T(8,128)(2,1)} %param.13) | copy-start | bytes 9437188
where the time goes:
time: 391 us; the launch traced here: 385 us
  other arithmetic  136 us (35%)
  local copies, waits for them, and re-layouts  91.4 us (23%)
  waiting for transfers between devices  74.1 us (19%)
  starting transfers between devices  40.5 us (10%)
  matrix products  37.7 us (10%)
  between operations  5.12 us (1%)
    reduce_sum x3, other arithmetic, shards(): jnp.sum(grad_own * padded_all[:, a:a + row_count, d:d + col_count, :], ax...  121 us
    ppermute x16, waiting for transfers between devices, butterfly_sum(): values = values + lax.ppermute(values, axis, pairs)  68.1 us
    another operation x56, local copies, waits for them, and re-layouts, shards(): jnp.stack([jnp.sum(grad_own * padded_all[:, a:a + row_count, d:d + col_co...  34.6 us
    conv_general_dilated x2, matrix products, depthwise(): lax.conv_general_dilated(extended, kernel.reshape(kernel.shape[0], kernel...  30.1 us
    unnamed x45, local copies, waits for them, and re-layouts  25.8 us
    ppermute x16, starting transfers between devices, butterfly_sum(): values = values + lax.ppermute(values, axis, pairs)  21.4 us
    ppermute x2, starting transfers between devices, with_halo(): lax.ppermute(lax.slice_in_dim(block, 0, width, axis=dim), axis, backward)  15.1 us
  transfers between devices with their start and end apart: 20, of which 14 were waited for; matrix products, arithmetic and copies ran while one was open for 17% of the time, Pallas kernels for 0%

commit v1 on v0

--- a/solution.py
+++ b/solution.py
@@ -1,6 +1,7 @@
 import jax
 import jax.numpy as jnp
 from jax import lax
+from jax.experimental import pallas as pl
 from jax.sharding import PartitionSpec as P
 
 
@@ -51,6 +52,31 @@
         **options,
     )
 
+
+def kernel_terms(grad_rows, padded, reach, lanes=128):
+    row_count, col_count, channels = grad_rows.shape
+    side = 2 * reach + 1
+    groups = col_count // 8
+
+    def body(g_ref, x_ref, o_ref):
+        for a in range(side):
+            for d in range(side):
+                acc = jnp.zeros((8, lanes), jnp.float32)
+                for h in range(row_count):
+                    prod = g_ref[h] * x_ref[h + a, pl.ds(d, col_count), :]
+                    acc = acc + prod.reshape(groups, 8, lanes).sum(axis=0)
+                o_ref[a, pl.ds(d, 1), :] = acc.sum(axis=0, keepdims=True)
+
+    return pl.pallas_call(
+        body,
+        grid=(channels // lanes,),
+        in_specs=[
+            pl.BlockSpec((row_count, col_count, lanes), lambda i: (0, 0, i)),
+            pl.BlockSpec(padded.shape[:2] + (lanes,), lambda i: (0, 0, i)),
+        ],
+        out_specs=pl.BlockSpec((side, side, lanes), lambda i: (0, 0, i)),
+        out_shape=jax.ShapeDtypeStruct((side, side, channels), jnp.float32),
+    )(grad_rows, padded)
 
 def logsum(scores, axis):
     highest = jnp.max(scores, axis=axis, keepdims=True)
@@ -122,20 +148,9 @@
     input_grad = depthwise(
         grad_wide, kernel_float[::-1, ::-1], reach_rows, precision=lax.Precision.HIGHEST
     )
-    kernel_part = jnp.stack(
-        [
-            jnp.stack(
-                [
-                    jnp.sum(
-                        grad_own * padded_all[:, a : a + row_count, d : d + col_count, :],
-                        axis=(0, 1, 2),
-                    )
-                    for d in range(kernel_float.shape[1])
-                ]
-            )
-            for a in range(kernel_float.shape[0])
-        ]
-    )
+    kernel_part = kernel_terms(grad_own[0], padded_all[0], reach_rows)
+    for image in range(1, batch_dev):
+        kernel_part = kernel_part + kernel_terms(grad_own[image], padded_all[image], reach_rows)
     kernel_grad = butterfly_sum(kernel_part, ("space", "dp")) / pixel_count
     return (loss, input_grad.astype(jnp.bfloat16), kernel_grad, text_grad)
 

time: 391 us -> 242 us (0.62); the launches traced: 385 us -> 241 us
  other arithmetic: 136 us -> 22.2 us
  local copies, waits for them, and re-layouts: 91.4 us -> 33.6 us
  Pallas kernels: 0 us -> 14.7 us
  starting transfers between devices: 40.5 us -> 48 us
  matrix products: 37.7 us -> 44.7 us
    reduce_sum x3 -> x0, other arithmetic: 121 us -> none  [shards(): jnp.sum(grad_own * padded_all[:, a:a + row_count, d:d + col_count, :], ax...]
    another operation x57 -> x0, local copies, waits for them, and re-layouts: 35.4 us -> none  [the longest x56 34.6 us: shards(): jnp.stack([jnp.sum(grad_own * padded_all[:, a:a + row_count, d:d + col_co...]
    unnamed x45 -> x47, local copies, waits for them, and re-layouts: 25.8 us -> 2.67 us
    pallas_call x0 -> x1, Pallas kernels: none -> 14.7 us  [kernel_terms(): pl.pallas_call(body, grid=(channels // lanes,), in_specs=[pl.BlockSpec((r...]
    conv_general_dilated x4 -> x3, local copies, waits for them, and re-layouts: 3.16 us -> 14 us  [depthwise(): lax.conv_general_dilated(extended, kernel.reshape(kernel.shape[0], kernel...]
    squeeze x0 -> x2, other arithmetic: none -> 7.8 us  [shards(): kernel_part = kernel_terms(grad_own[0], padded_all[0], reach_rows)]
    ppermute x16, starting transfers between devices: 21.4 us -> 28.9 us  [butterfly_sum(): values = values + lax.ppermute(values, axis, pairs)]
    conv_general_dilated x2, matrix products: 30.1 us -> 37 us  [depthwise(): lax.conv_general_dilated(extended, kernel.reshape(kernel.shape[0], kernel...]
  transfers between devices with their start and end apart: 20 -> 20, of which waited for: 14 -> 13; matrix products, arithmetic and copies ran while one was open for 17% -> 25% of each run, Pallas kernels for 0% -> 0%
where the time goes in v1:
time: 242 us; the launch traced here: 241 us
  waiting for transfers between devices  72.3 us (30%)
  starting transfers between devices  48 us (20%)
  matrix products  44.7 us (18%)
  local copies, waits for them, and re-layouts  33.6 us (14%)
  other arithmetic  22.2 us (9%)
  Pallas kernels  14.7 us (6%)
  between operations  4.94 us (2%)
    ppermute x16, waiting for transfers between devices, butterfly_sum(): values = values + lax.ppermute(values, axis, pairs)  65.1 us
    conv_general_dilated x2, matrix products, depthwise(): lax.conv_general_dilated(extended, kernel.reshape(kernel.shape[0], kernel...  37 us
    ppermute x16, starting transfers between devices, butterfly_sum(): values = values + lax.ppermute(values, axis, pairs)  28.9 us
    ppermute x2, starting transfers between devices, with_halo(): lax.ppermute(lax.slice_in_dim(block, 0, width, axis=dim), axis, backward)  15.1 us
    pallas_call x1, Pallas kernels, kernel_terms(): pl.pallas_call(body, grid=(channels // lanes,), in_specs=[pl.BlockSpec((r...  14.7 us
    conv_general_dilated x3, local copies, waits for them, and re-layouts, depthwise(): lax.conv_general_dilated(extended, kernel.reshape(kernel.shape[0], kernel...  14 us
    squeeze x2, other arithmetic, shards(): kernel_part = kernel_terms(grad_own[0], padded_all[0], reach_rows)  7.8 us
    rev x1, local copies, waits for them, and re-layouts, shards(): kernel_float[::-1, ::-1]  6.09 us
  transfers between devices with their start and end apart: 20, of which 13 were waited for; matrix products, arithmetic and copies ran while one was open for 25% of the time, Pallas kernels for 0%

profile of v1, /device:TPU:28, one launch (start us, length us, event | category | flops | bytes accessed | tf_op | source)
XLA Modules:
  0.0 240.5 jit_solution(8952013321625101139)
XLA Ops:
  0.7 1.5 fusion.38
  2.2 2.1 collective-permute-start
  4.2 7.9 %collective-permute-start.1 = (bf16[1,3,64,1536]{3,2,1,0:T(8,128)(2,1)S(1)}, bf16[1,3,64,1536]{3,2,1,0:T(8,128)(2,1)S(1)}, u32[]{:S(2)}, u32[]{:S(2)}) collective-permute-start(bf16[1,3,64,1536]{3,2,1,0:T(8,128)(2,1)S(1)} %get-tuple-element.21), channel_id=1, source_target_pairs={{1,0},{2,1},{3,2},{4,3},{5,4},{6,5},{7,6},{8,7},{9,8},{10,9},{11,1... | collective-permute-start | bytes 1769480 | tf_op jit(solution)/shard_map/ppermute | solution.py:16
  12.1 5.6 %collective-permute-done = bf16[1,3,64,1536]{3,2,1,0:T(8,128)(2,1)S(1)} collective-permute-done((bf16[1,3,64,1536]{3,2,1,0:T(8,128)(2,1)S(1)}, bf16[1,3,64,1536]{3,2,1,0:T(8,128)(2,1)S(1)}, u32[]{:S(2)}, u32[]{:S(2)}) %collective-permute-start) | collective-permute-done | bytes 589856 | tf_op jit(solution)/shard_map/ppermute | solution.py:13
  17.9 1.6 collective-permute-done.1
  19.6 21.5 %fusion.5 = f32[1,8,64,1536]{3,0,2,1:T(1,128)S(1)} fusion(bf16[1,14,64,1536]{3,2,1,0:T(8,128)(2,1)S(1)} %constant_dynamic-update-slice_fusion, bf16[7,7,1,1536]{3,1,0,2:T(8,128)(2,1)S(1)} %bitcast.37), kind=kOutput, calls=%fused_computation.7 | convolution fusion | flops 75005952 | bytes 6048768 | tf_op jit(solution)/shard_map/conv_general_dilated | solution.py:45
  41.4 0.5 multiply_reduce_fusion.1
  41.9 0.8 copy-done.2
  42.7 0.7 add_reduce_fusion
  43.5 1.2 collective-permute-done.2
  44.8 3.6 %collective-permute-done.3 = f32[1,1536]{1,0:T(1,128)S(1)} collective-permute-done((f32[1,1536]{1,0:T(1,128)S(1)}, f32[1,1536]{1,0:T(1,128)S(1)}, u32[]{:S(2)}, u32[]{:S(2)}) %collective-permute-start.3) | collective-permute-done | bytes 6176 | tf_op jit(solution)/shard_map/ppermute | solution.py:30
  48.4 3.3 %collective-permute-start.4 = (f32[1,1536]{1,0:T(1,128)S(1)}, f32[1,1536]{1,0:T(1,128)S(1)}, u32[]{:S(2)}, u32[]{:S(2)}) collective-permute-start(f32[1,1536]{1,0:T(1,128)S(1)} %add.110), channel_id=1, source_target_pairs={{0,4},{1,5},{2,6},{3,7},{4,0},{5,1},{6,2},{7,3},{8,12},{9,13},{10,... | collective-permute-start | bytes 18440 | tf_op jit(solution)/shard_map/ppermute | solution.py:30
  51.7 1.6 collective-permute-done.4
  53.4 3.9 %collective-permute-start.5 = (f32[1,1536]{1,0:T(1,128)S(1)}, f32[1,1536]{1,0:T(1,128)S(1)}, u32[]{:S(2)}, u32[]{:S(2)}) collective-permute-start(f32[1,1536]{1,0:T(1,128)S(1)} %add.111), channel_id=1, source_target_pairs={{0,8},{1,9},{2,10},{3,11},{4,12},{5,13},{6,14},{7,15},{8,0},{9,1},... | collective-permute-start | bytes 18440 | tf_op jit(solution)/shard_map/ppermute | solution.py:30
  57.3 3.7 %collective-permute-done.5 = f32[1,1536]{1,0:T(1,128)S(1)} collective-permute-done((f32[1,1536]{1,0:T(1,128)S(1)}, f32[1,1536]{1,0:T(1,128)S(1)}, u32[]{:S(2)}, u32[]{:S(2)}) %collective-permute-start.5) | collective-permute-done | bytes 6176 | tf_op jit(solution)/shard_map/ppermute | solution.py:30
  61.0 1.3 collective-permute-start.6
  62.3 3.9 %collective-permute-done.6 = f32[1,1536]{1,0:T(1,128)S(1)} collective-permute-done((f32[1,1536]{1,0:T(1,128)S(1)}, f32[1,1536]{1,0:T(1,128)S(1)}, u32[]{:S(2)}, u32[]{:S(2)}) %collective-permute-start.6) | collective-permute-done | bytes 6176 | tf_op jit(solution)/shard_map/ppermute | solution.py:30
  66.6 1.3 collective-permute-start.7
  67.8 3.8 %collective-permute-done.7 = f32[8,2560]{1,0:T(8,128)S(1)} collective-permute-done((f32[8,2560]{1,0:T(8,128)S(1)}, f32[8,2560]{1,0:T(8,128)S(1)}, u32[]{:S(2)}, u32[]{:S(2)}) %collective-permute-start.7) | collective-permute-done | bytes 81952 | tf_op jit(solution)/shard_map/ppermute | solution.py:30
  72.8 5.2 %collective-permute-done.8 = f32[8,2560]{1,0:T(8,128)S(1)} collective-permute-done((f32[8,2560]{1,0:T(8,128)S(1)}, f32[8,2560]{1,0:T(8,128)S(1)}, u32[]{:S(2)}, u32[]{:S(2)}) %collective-permute-start.8) | collective-permute-done | bytes 81952 | tf_op jit(solution)/shard_map/ppermute | solution.py:30
  78.0 1.0 collective-permute-start.9
  79.0 5.3 %bitcast_convert_fusion.x_ref = f32[14,70,1536]{2,1,0:T(8,128)} fusion(bf16[1,14,64,1536]{3,2,1,0:T(8,128)(2,1)} %copy-done.8), kind=kLoop, calls=%fused_computation.17 | loop fusion | flops 1505280 | bytes 8773632 | tf_op jit(solution)/shard_map/squeeze | solution.py:151
  84.4 1.4 multiply_reduce_fusion.5
  85.9 0.6 dynamic-slice.2
  86.6 0.3 fusion.35
  87.0 0.7 subtract_reduce_fusion
  87.7 0.4 multiply_reduce_fusion.3
  88.2 0.6 dynamic-slice.1
  88.8 3.8 %convolution_reduce_fusion = f32[1536]{0:T(1024)S(1)} fusion(bf16[1536,1024]{1,0:T(8,128)(2,1)S(1)} %copy-done, f32[8,1024]{1,0:T(8,128)S(1)} %get-tuple-element.27, s32[]{:T(128)S(6)} %select_n.2, f32[8,1024]{1,0:T(8,128)S(1)} %get-tuple-element.31, f32[1]{0:T(128)} %dynamic-slice.2, f32[1]{0:T(128)} %dynamic-slice.1), kind=kOutput, calls=%fused_computation.23 | convolution fusion | flops 18877440 | bytes 3160076 | tf_op jit(solution)/shard_map/dot_general | solution.py:142
  92.6 0.6 fusion.36
  93.2 0.7 multiply_reduce_fusion
  94.6 2.5 %fusion.45.g_ref = f32[8,64,1536]{2,1,0:T(8,128)} fusion(f32[8,64]{1,0:T(8,128)S(1)} %broadcast_multiply_fusion, f32[8,64]{1,0:T(8,128)S(1)} %broadcast_multiply_fusion.1, f32[1536]{0:T(1024)S(1)} %copy-done.12, f32[1,8,64,1536]{3,0,2,1:T(1,128)S(1)} %copy-done.4, f32[1536]{0:T(1024)S(1)} %broadcast_subtract_fusion, f32[8,64]{1,0:T(8,128)S(1)} %add_rsqrt_fusion), kind=kLoop, calls=%fused_computation.81 | loop fusion | flops 4718592 | bytes 6309888 | tf_op jit(solution)/shard_map/squeeze | solution.py:151
  97.1 14.7 %shard_map.111 = f32[7,7,1536]{2,1,0:T(8,128)} custom-call(f32[8,64,1536]{2,1,0:T(8,128)} %fusion.45.g_ref, f32[14,70,1536]{2,1,0:T(8,128)} %bitcast_convert_fusion.x_ref), custom_call_target="tpu_custom_call" | custom-call | tf_op jit(solution)/shard_map/pallas_call | solution.py:70
  111.8 0.9 subtract_multiply_fusion
  112.7 1.0 collective-permute-done.12
  113.7 2.0 collective-permute-start.13
  115.7 1.6 fusion.37
  117.3 1.9 collective-permute-start.10
  119.2 7.3 %collective-permute-start.11 = (f32[1,3,64,1536]{3,2,1,0:T(8,128)}, f32[1,3,64,1536]{3,2,1,0:T(8,128)}, u32[]{:S(2)}, u32[]{:S(2)}) collective-permute-start(f32[1,3,64,1536]{3,2,1,0:T(8,128)} %get-tuple-element.20), channel_id=1, source_target_pairs={{1,0},{2,1},{3,2},{4,3},{5,4},{6,5},{7,6},{8,7},{9,8},{10,9},{11,1... | collective-permute-start | bytes 3538952 | tf_op jit(solution)/shard_map/ppermute | solution.py:16
  126.6 0.4 collective-permute-start.14
  126.9 31.4 %collective-permute-done.14 = f32[7,7,1536]{2,1,0:T(8,128)S(1)} collective-permute-done((f32[7,7,1536]{2,1,0:T(8,128)S(1)}, f32[7,7,1536]{2,1,0:T(8,128)S(1)}, u32[]{:S(2)}, u32[]{:S(2)}) %collective-permute-start.14) | collective-permute-done | bytes 301088 | tf_op jit(solution)/shard_map/ppermute | solution.py:30
  158.4 1.1 collective-permute-start.15
  159.4 6.1 %rev.3 = f32[7,7,1536]{2,1,0:T(8,128)} reverse(bf16[7,7,1536]{2,1,0:T(8,128)(2,1)} %param.9), dimensions={0,1} | reverse | bytes 451584 | tf_op jit(solution)/shard_map/rev | solution.py:149
  165.5 1.3 dynamic-slice.4
  166.8 4.2 %collective-permute-done.15 = f32[7,7,1536]{2,1,0:T(8,128)} collective-permute-done((f32[7,7,1536]{2,1,0:T(8,128)S(1)}, f32[7,7,1536]{2,1,0:T(8,128)}, u32[]{:S(2)}, u32[]{:S(2)}) %collective-permute-start.15) | collective-permute-done | bytes 301088 | tf_op jit(solution)/shard_map/ppermute | solution.py:30
  171.0 1.1 add.125
  172.2 3.7 %collective-permute-start.16 = (f32[7,7,1536]{2,1,0:T(8,128)S(1)}, f32[7,7,1536]{2,1,0:T(8,128)}, u32[]{:S(2)}, u32[]{:S(2)}) collective-permute-start(f32[7,7,1536]{2,1,0:T(8,128)S(1)} %add.125), channel_id=1, source_target_pairs={{0,16},{1,17},{2,18},{3,19},{4,20},{5,21},{6,22},{7,23},{8,24},{9,... | collective-permute-start | bytes 903176 | tf_op jit(solution)/shard_map/ppermute | solution.py:30
  175.8 1.7 multiply_reduce_fusion.2
  177.5 0.6 dynamic-slice.3
  179.4 2.6 %fusion.16 = f32[1,1024]{1,0:T(1,128)} fusion(f32[8,1024]{1,0:T(8,128)} %get-tuple-element.29, s32[]{:T(128)S(6)} %select_n.2, f32[8,1024]{1,0:T(8,128)S(1)} %get-tuple-element.30, f32[1]{0:T(128)} %dynamic-slice.4, f32[1]{0:T(128)} %dynamic-slice.3), kind=kLoop, calls=%fused_computation.43 | loop fusion | flops 3072 | bytes 12300 | tf_op jit(solution)/shard_map/div | solution.py:134
  182.0 1.8 add.126
  183.8 0.9 collective-permute-start.17
  184.7 2.2 maximum_bitcast_fusion
  186.9 3.4 %pad.6 = f32[14,1,72,1536]{3,2,0,1:T(8,128)} pad(f32[14,1,64,1536]{3,2,0,1:T(8,128)S(1)} %maximum_bitcast_fusion, f32[]{:T(128)} %constant.31.clone.1), padding=0_0x0_0x3_5x0_0 | pad | bytes 11698180 | tf_op jit(solution)/shard_map/concatenate | solution.py:17
  190.3 10.3 %reshape.148 = f32[14,1,8,9,1536]{4,1,3,2,0:T(1,128)} reshape(f32[14,1,72,1536]{3,2,0,1:T(8,128)} %pad.6) | data formatting | bytes 12386304 | tf_op jit(solution)/shard_map/conv_general_dilated | solution.py:45
  200.6 3.2 %copy.22 = f32[14,1,8,9,1536]{4,2,3,0,1:T(8,128)S(1)} copy(f32[14,1,8,9,1536]{4,1,3,2,0:T(1,128)} %reshape.148) | data formatting | bytes 12386304 | tf_op jit(solution)/shard_map/conv_general_dilated | solution.py:45
  203.9 0.5 slice.30
  204.4 1.0 add.127
  205.4 9.7 %collective-permute-start.18 = (f32[7,7,1536]{2,1,0:T(8,128)S(1)}, f32[7,7,1536]{2,1,0:T(8,128)S(1)}, u32[]{:S(2)}, u32[]{:S(2)}) collective-permute-start(f32[7,7,1536]{2,1,0:T(8,128)S(1)} %add.127), channel_id=1, source_target_pairs={{0,64},{32,96},{64,0},{96,32},{128,192},{160,224},{192,128},{224,1... | collective-permute-start | bytes 903176 | tf_op jit(solution)/shard_map/ppermute | solution.py:30
  215.1 15.6 %select_convert_fusion = bf16[8,8,9,1536]{3,1,2,0:T(8,128)(2,1)S(1)} fusion(f32[14,1,7,6,1536]{4,2,3,0,1:T(8,128)S(1)} %slice.30, f32[14,1,8,9,1536]{4,2,3,0,1:T(8,128)S(1)} %copy.22, pred[8,9]{0,1:T(8,128)(4,1)S(1)} %copy-done.21, f32[7,7,1,1536]{3,1,0,2:T(8,128)S(1)} %bitcast.36), kind=kOutput, calls=%fused_computation.11 | convolution fusion | flops 529735680 | bytes 11876424 | tf_op jit(solution)/shard_map/conv_general_dilated | solution.py:45
  230.7 0.5 copy.24
  231.5 1.6 copy.25
  233.1 5.5 %collective-permute-done.19 = f32[7,7,1536]{2,1,0:T(8,128)S(1)} collective-permute-done((f32[7,7,1536]{2,1,0:T(8,128)S(1)}, f32[7,7,1536]{2,1,0:T(8,128)S(1)}, u32[]{:S(2)}, u32[]{:S(2)}) %collective-permute-start.19) | collective-permute-done | bytes 301088 | tf_op jit(solution)/shard_map/ppermute | solution.py:30
  238.6 0.8 add_multiply_fusion
  (86 shorter events, 2.4 us)
Async XLA Ops:
  0.6 83.8 %copy-start = (bf16[1536,1024]{1,0:T(8,128)(2,1)S(1)}, bf16[1536,1024]{1,0:T(8,128)(2,1)}, u32[]{:S(2)}) copy-start(bf16[1536,1024]{1,0:T(8,128)(2,1)} %param.13) | copy-start | bytes 9437188
  0.6 17.1 %copy-start.7 = (bf16[1,8,64,1536]{3,2,1,0:T(8,128)(2,1)S(1)}, bf16[1,8,64,1536]{3,2,1,0:T(8,128)(2,1)}, u32[]{:S(2)}) copy-start(bf16[1,8,64,1536]{3,2,1,0:T(8,128)(2,1)} %param.8) | copy-start | bytes 4718596
  2.1 17.4 %copy-start.13 = (bf16[7,7,1536]{2,1,0:T(8,128)(2,1)S(1)}, bf16[7,7,1536]{2,1,0:T(8,128)(2,1)}, u32[]{:S(2)}) copy-start(bf16[7,7,1536]{2,1,0:T(8,128)(2,1)} %param.9) | copy-start | bytes 451588
  2.2 15.6 %collective-permute-start = (bf16[1,3,64,1536]{3,2,1,0:T(8,128)(2,1)S(1)}, bf16[1,3,64,1536]{3,2,1,0:T(8,128)(2,1)S(1)}, u32[]{:S(2)}, u32[]{:S(2)}) collective-permute-start(bf16[1,3,64,1536]{3,2,1,0:T(8,128)(2,1)S(1)} %get-tuple-element.22), channel_id=1, source_target_pairs={{0,1},{1,2},{2,3},{3,4},{4,5},{5,6},{6,7},{7,8},{8,9},{9,10},{10,1... | collective-permute-start | bytes 1769480 | tf_op jit(solution)/shard_map/ppermute | solution.py:13
  4.2 15.3 %collective-permute-start.1 = (bf16[1,3,64,1536]{3,2,1,0:T(8,128)(2,1)S(1)}, bf16[1,3,64,1536]{3,2,1,0:T(8,128)(2,1)S(1)}, u32[]{:S(2)}, u32[]{:S(2)}) collective-permute-start(bf16[1,3,64,1536]{3,2,1,0:T(8,128)(2,1)S(1)} %get-tuple-element.21), channel_id=1, source_target_pairs={{1,0},{2,1},{3,2},{4,3},{5,4},{6,5},{7,6},{8,7},{9,8},{10,9},{11,1... | collective-permute-start | bytes 1769480 | tf_op jit(solution)/shard_map/ppermute | solution.py:16
  19.5 21.5 %copy-start.8 = (bf16[1,14,64,1536]{3,2,1,0:T(8,128)(2,1)}, bf16[1,14,64,1536]{3,2,1,0:T(8,128)(2,1)S(1)}, u32[]{:S(2)}) copy-start(bf16[1,14,64,1536]{3,2,1,0:T(8,128)(2,1)S(1)} %constant_dynamic-update-slice_fusion) | copy-start | bytes 8257540
  19.5 21.5 %copy-start.12 = (f32[1536]{0:T(1024)S(1)}, f32[1536]{0:T(1024)}, u32[]{:S(2)}) copy-start(f32[1536]{0:T(1024)} %param.10) | copy-start | bytes 18436
  41.0 1.7 copy-start.2
  41.1 1.7 copy-start.15
  41.1 1.7 copy-start.17
  41.4 24.9 %copy-start.16 = (f32[1,1024]{1,0:T(1,128)S(1)}, f32[1,1024]{1,0:T(1,128)}, u32[]{:S(2)}) copy-start(f32[1,1024]{1,0:T(1,128)} %param.14) | copy-start | bytes 12292
  43.4 1.3 collective-permute-start.2
  44.7 3.7 %collective-permute-start.3 = (f32[1,1536]{1,0:T(1,128)S(1)}, f32[1,1536]{1,0:T(1,128)S(1)}, u32[]{:S(2)}, u32[]{:S(2)}) collective-permute-start(f32[1,1536]{1,0:T(1,128)S(1)} %reshape_add_fusion), channel_id=1, source_target_pairs={{0,2},{1,3},{2,0},{3,1},{4,6},{5,7},{6,4},{7,5},{8,10},{9,11},{10,... | collective-permute-start | bytes 18440 | tf_op jit(solution)/shard_map/ppermute | solution.py:30
  48.4 4.9 %collective-permute-start.4 = (f32[1,1536]{1,0:T(1,128)S(1)}, f32[1,1536]{1,0:T(1,128)S(1)}, u32[]{:S(2)}, u32[]{:S(2)}) collective-permute-start(f32[1,1536]{1,0:T(1,128)S(1)} %add.110), channel_id=1, source_target_pairs={{0,4},{1,5},{2,6},{3,7},{4,0},{5,1},{6,2},{7,3},{8,12},{9,13},{10,... | collective-permute-start | bytes 18440 | tf_op jit(solution)/shard_map/ppermute | solution.py:30
  53.4 7.6 %collective-permute-start.5 = (f32[1,1536]{1,0:T(1,128)S(1)}, f32[1,1536]{1,0:T(1,128)S(1)}, u32[]{:S(2)}, u32[]{:S(2)}) collective-permute-start(f32[1,1536]{1,0:T(1,128)S(1)} %add.111), channel_id=1, source_target_pairs={{0,8},{1,9},{2,10},{3,11},{4,12},{5,13},{6,14},{7,15},{8,0},{9,1},... | collective-permute-start | bytes 18440 | tf_op jit(solution)/shard_map/ppermute | solution.py:30
  61.0 5.2 %collective-permute-start.6 = (f32[1,1536]{1,0:T(1,128)S(1)}, f32[1,1536]{1,0:T(1,128)S(1)}, u32[]{:S(2)}, u32[]{:S(2)}) collective-permute-start(f32[1,1536]{1,0:T(1,128)S(1)} %add.112), channel_id=1, source_target_pairs={{0,16},{1,17},{2,18},{3,19},{4,20},{5,21},{6,22},{7,23},{8,24},{9,... | collective-permute-start | bytes 18440 | tf_op jit(solution)/shard_map/ppermute | solution.py:30
  66.6 5.1 %collective-permute-start.7 = (f32[8,2560]{1,0:T(8,128)S(1)}, f32[8,2560]{1,0:T(8,128)S(1)}, u32[]{:S(2)}, u32[]{:S(2)}) collective-permute-start(f32[8,2560]{1,0:T(8,128)S(1)} %dynamic_update_slice.5), channel_id=1, source_target_pairs={{0,32},{32,0},{64,96},{96,64},{128,160},{160,128},{192,224},{224,1... | collective-permute-start | bytes 245768 | tf_op jit(solution)/shard_map/ppermute | solution.py:30
  71.9 6.0 %collective-permute-start.8 = (f32[8,2560]{1,0:T(8,128)S(1)}, f32[8,2560]{1,0:T(8,128)S(1)}, u32[]{:S(2)}, u32[]{:S(2)}) collective-permute-start(f32[8,2560]{1,0:T(8,128)S(1)} %add.115), channel_id=1, source_target_pairs={{0,64},{32,96},{64,0},{96,32},{128,192},{160,224},{192,128},{224,1... | collective-permute-start | bytes 245768 | tf_op jit(solution)/shard_map/ppermute | solution.py:30
  78.0 6.3 %collective-permute-start.9 = (f32[8,2560]{1,0:T(8,128)S(1)}, f32[8,2560]{1,0:T(8,128)S(1)}, u32[]{:S(2)}, u32[]{:S(2)}) collective-permute-start(f32[8,2560]{1,0:T(8,128)S(1)} %add.116), channel_id=1, source_target_pairs={{0,128},{32,160},{64,192},{96,224},{128,0},{160,32},{192,64},{224,... | collective-permute-start | bytes 245768 | tf_op jit(solution)/shard_map/ppermute | solution.py:30
  84.4 8.8 %copy-start.3 = (f32[1,8,64,1536]{3,0,2,1:T(1,128)S(1)}, f32[1,8,64,1536]{3,0,2,1:T(1,128)}, u32[]{:S(2)}) copy-start(f32[1,8,64,1536]{3,0,2,1:T(1,128)} %copy-done.2) | copy-start | bytes 9437188
  85.9 1.9 copy-start.20
  86.9 7.0 %copy-start.14 = (f32[8,8]{0,1:T(8,128)}, f32[8,8]{0,1:T(8,128)S(1)}, u32[]{:S(2)}) copy-start(f32[8,8]{0,1:T(8,128)S(1)} %get-tuple-element.25) | copy-start | bytes 772
  87.7 1.0 copy-start.18
  87.7 1.0 copy-start.19
  92.6 2.0 copy-start.4
  111.8 1.9 copy-start.9
  111.8 1.9 collective-permute-start.12
  112.7 13.9 %copy-start.5 = (f32[1,8,64,1536]{3,2,1,0:T(8,128)}, f32[1,8,64,1536]{3,2,1,0:T(8,128)S(1)}, u32[]{:S(2)}) copy-start(f32[1,8,64,1536]{3,2,1,0:T(8,128)S(1)} %subtract_multiply_fusion) | copy-start | bytes 9437188
  113.7 12.8 %collective-permute-start.13 = (f32[7,7,1536]{2,1,0:T(8,128)S(1)}, f32[7,7,1536]{2,1,0:T(8,128)S(1)}, u32[]{:S(2)}, u32[]{:S(2)}) collective-permute-start(f32[7,7,1536]{2,1,0:T(8,128)S(1)} %add.122), channel_id=1, source_target_pairs={{0,2},{1,3},{2,0},{3,1},{4,6},{5,7},{6,4},{7,5},{8,10},{9,11},{10,... | collective-permute-start | bytes 903176 | tf_op jit(solution)/shard_map/ppermute | solution.py:30
  117.3 67.4 %collective-permute-start.10 = (f32[1,3,64,1536]{3,2,1,0:T(8,128)}, f32[1,3,64,1536]{3,2,1,0:T(8,128)}, u32[]{:S(2)}, u32[]{:S(2)}) collective-permute-start(f32[1,3,64,1536]{3,2,1,0:T(8,128)} %get-tuple-element.19), channel_id=1, source_target_pairs={{0,1},{1,2},{2,3},{3,4},{4,5},{5,6},{6,7},{7,8},{8,9},{9,10},{10,1... | collective-permute-start | bytes 3538952 | tf_op jit(solution)/shard_map/ppermute | solution.py:13
  119.2 65.5 %collective-permute-start.11 = (f32[1,3,64,1536]{3,2,1,0:T(8,128)}, f32[1,3,64,1536]{3,2,1,0:T(8,128)}, u32[]{:S(2)}, u32[]{:S(2)}) collective-permute-start(f32[1,3,64,1536]{3,2,1,0:T(8,128)} %get-tuple-element.20), channel_id=1, source_target_pairs={{1,0},{2,1},{3,2},{4,3},{5,4},{6,5},{7,6},{8,7},{9,8},{10,9},{11,1... | collective-permute-start | bytes 3538952 | tf_op jit(solution)/shard_map/ppermute | solution.py:16
  126.6 31.8 %collective-permute-start.14 = (f32[7,7,1536]{2,1,0:T(8,128)S(1)}, f32[7,7,1536]{2,1,0:T(8,128)S(1)}, u32[]{:S(2)}, u32[]{:S(2)}) collective-permute-start(f32[7,7,1536]{2,1,0:T(8,128)S(1)} %add.123), channel_id=1, source_target_pairs={{0,4},{1,5},{2,6},{3,7},{4,0},{5,1},{6,2},{7,3},{8,12},{9,13},{10,... | collective-permute-start | bytes 903176 | tf_op jit(solution)/shard_map/ppermute | solution.py:30
  126.9 57.7 %copy-start.6 = (f32[1,8,64,1536]{3,2,1,0:T(8,128)S(1)}, f32[1,8,64,1536]{3,2,1,0:T(8,128)}, u32[]{:S(2)}) copy-start(f32[1,8,64,1536]{3,2,1,0:T(8,128)} %copy-done.5) | copy-start | bytes 9437188
  158.4 8.5 %copy-start.10 = (f32[7,7,1536]{2,1,0:T(8,128)}, f32[7,7,1536]{2,1,0:T(8,128)S(1)}, u32[]{:S(2)}) copy-start(f32[7,7,1536]{2,1,0:T(8,128)S(1)} %add.124) | copy-start | bytes 903172
  158.4 12.7 %collective-permute-start.15 = (f32[7,7,1536]{2,1,0:T(8,128)S(1)}, f32[7,7,1536]{2,1,0:T(8,128)}, u32[]{:S(2)}, u32[]{:S(2)}) collective-permute-start(f32[7,7,1536]{2,1,0:T(8,128)S(1)} %add.124), channel_id=1, source_target_pairs={{0,8},{1,9},{2,10},{3,11},{4,12},{5,13},{6,14},{7,15},{8,0},{9,1},... | collective-permute-start | bytes 903176 | tf_op jit(solution)/shard_map/ppermute | solution.py:30
  172.2 9.9 %collective-permute-start.16 = (f32[7,7,1536]{2,1,0:T(8,128)S(1)}, f32[7,7,1536]{2,1,0:T(8,128)}, u32[]{:S(2)}, u32[]{:S(2)}) collective-permute-start(f32[7,7,1536]{2,1,0:T(8,128)S(1)} %add.125), channel_id=1, source_target_pairs={{0,16},{1,17},{2,18},{3,19},{4,20},{5,21},{6,22},{7,23},{8,24},{9,... | collective-permute-start | bytes 903176 | tf_op jit(solution)/shard_map/ppermute | solution.py:30
  183.8 20.6 %collective-permute-start.17 = (f32[7,7,1536]{2,1,0:T(8,128)}, f32[7,7,1536]{2,1,0:T(8,128)S(1)}, u32[]{:S(2)}, u32[]{:S(2)}) collective-permute-start(f32[7,7,1536]{2,1,0:T(8,128)} %add.126), channel_id=1, source_target_pairs={{0,32},{32,0},{64,96},{96,64},{128,160},{160,128},{192,224},{224,1... | collective-permute-start | bytes 903176 | tf_op jit(solution)/shard_map/ppermute | solution.py:30
  203.9 11.2 %copy-start.11 = (f32[7,7,1536]{2,1,0:T(8,128)S(1)}, f32[7,7,1536]{2,1,0:T(8,128)}, u32[]{:S(2)}) copy-start(f32[7,7,1536]{2,1,0:T(8,128)} %rev.3) | copy-start | bytes 903172
  203.9 11.2 %copy-start.21 = (pred[8,9]{0,1:T(8,128)(4,1)S(1)}, pred[8,9]{0,1:T(8,128)(4,1)}, u32[]{:S(2)}) copy-start(pred[8,9]{0,1:T(8,128)(4,1)} %constant.51) | copy-start | bytes 220
  205.4 25.8 %collective-permute-start.18 = (f32[7,7,1536]{2,1,0:T(8,128)S(1)}, f32[7,7,1536]{2,1,0:T(8,128)S(1)}, u32[]{:S(2)}, u32[]{:S(2)}) collective-permute-start(f32[7,7,1536]{2,1,0:T(8,128)S(1)} %add.127), channel_id=1, source_target_pairs={{0,64},{32,96},{64,0},{96,32},{128,192},{160,224},{192,128},{224,1... | collective-permute-start | bytes 903176 | tf_op jit(solution)/shard_map/ppermute | solution.py:30
  231.3 7.3 %collective-permute-start.19 = (f32[7,7,1536]{2,1,0:T(8,128)S(1)}, f32[7,7,1536]{2,1,0:T(8,128)S(1)}, u32[]{:S(2)}, u32[]{:S(2)}) collective-permute-start(f32[7,7,1536]{2,1,0:T(8,128)S(1)} %add.128), channel_id=1, source_target_pairs={{0,128},{32,160},{64,192},{96,224},{128,0},{160,32},{192,64},{224,... | collective-permute-start | bytes 903176 | tf_op jit(solution)/shard_map/ppermute | solution.py:30
  231.4 8.0 %copy-start.1 = (bf16[1536,1024]{1,0:T(8,128)(2,1)S(1)}, bf16[1536,1024]{1,0:T(8,128)(2,1)}, u32[]{:S(2)}) copy-start(bf16[1536,1024]{1,0:T(8,128)(2,1)} %param.13) | copy-start | bytes 9437188

commit v2 on v1

--- a/solution.py
+++ b/solution.py
@@ -30,6 +30,39 @@
             values = values + lax.ppermute(values, axis, pairs)
             step *= 2
     return values
+
+
+def halving_sum(values, axes):
+    steps = []
+    for axis in axes:
+        count = lax.axis_size(axis)
+        if count & (count - 1):
+            return butterfly_sum(values, axes)
+        step = 1
+        while step < count:
+            steps.append((axis, count, step))
+            step *= 2
+    parts = 1 << len(steps)
+    flat = values.reshape(-1)
+    size = flat.shape[0]
+    padded_size = -(-size // parts) * parts
+    chunk = jnp.pad(flat, (0, padded_size - size))
+    for axis, count, step in steps:
+        pairs = [(i, i ^ step) for i in range(count)]
+        upper = (lax.axis_index(axis) // step) % 2 == 1
+        half = chunk.shape[0] // 2
+        low, high = chunk[:half], chunk[half:]
+        keep = jnp.where(upper, high, low)
+        give = jnp.where(upper, low, high)
+        chunk = keep + lax.ppermute(give, axis, pairs)
+    for axis, count, step in reversed(steps):
+        pairs = [(i, i ^ step) for i in range(count)]
+        upper = (lax.axis_index(axis) // step) % 2 == 1
+        other = lax.ppermute(chunk, axis, pairs)
+        chunk = jnp.where(
+            upper, jnp.concatenate([other, chunk]), jnp.concatenate([chunk, other])
+        )
+    return chunk[:size].reshape(values.shape)
 
 
 def normalize(values):
@@ -151,7 +184,7 @@
     kernel_part = kernel_terms(grad_own[0], padded_all[0], reach_rows)
     for image in range(1, batch_dev):
         kernel_part = kernel_part + kernel_terms(grad_own[image], padded_all[image], reach_rows)
-    kernel_grad = butterfly_sum(kernel_part, ("space", "dp")) / pixel_count
+    kernel_grad = halving_sum(kernel_part, ("space", "dp")) / pixel_count
     return (loss, input_grad.astype(jnp.bfloat16), kernel_grad, text_grad)
 
 

time: 242 us -> 260 us (1.074)
  waiting for transfers between devices: 72.3 us -> 83.8 us
  starting transfers between devices: 48 us -> 52.6 us
    ppermute x0 -> x16, waiting for transfers between devices: none -> 44.3 us  [the longest x8 24.8 us: halving_sum(): chunk = keep + lax.ppermute(give, axis, pairs)]
    ppermute x16 -> x8, waiting for transfers between devices: 65.1 us -> 23 us  [butterfly_sum(): values = values + lax.ppermute(values, axis, pairs)]
    ppermute x0 -> x16, starting transfers between devices: none -> 22 us  [the longest x8 11.9 us: halving_sum(): chunk = keep + lax.ppermute(give, axis, pairs)]
    ppermute x16 -> x8, starting transfers between devices: 28.9 us -> 11.2 us  [butterfly_sum(): values = values + lax.ppermute(values, axis, pairs)]
    ppermute x2, waiting for transfers between devices: 5.63 us -> 13.4 us  [with_halo(): lax.ppermute(lax.slice_in_dim(block, block.shape[dim] - width, None, axis...]
    add x14 -> x7, other arithmetic: 4.16 us -> 0.06 us  [butterfly_sum(): values = values + lax.ppermute(values, axis, pairs)]
  transfers between devices with their start and end apart: 20 -> 28, of which waited for: 13 -> 25; matrix products, arithmetic and copies ran while one was open for 25% -> 7% of each run, Pallas kernels for 0% -> 0%
where the time goes in v2:
time: 260 us; the launch traced here: 256 us
  waiting for transfers between devices  83.8 us (32%)
  starting transfers between devices  52.6 us (20%)
  matrix products  43.4 us (17%)
  local copies, waits for them, and re-layouts  35.1 us (14%)
  other arithmetic  21.7 us (8%)
  Pallas kernels  14.7 us (6%)
  between operations  4.96 us (2%)
    conv_general_dilated x2, matrix products, depthwise(): lax.conv_general_dilated(extended, kernel.reshape(kernel.shape[0], kernel...  37 us
    ppermute x8, waiting for transfers between devices, halving_sum(): chunk = keep + lax.ppermute(give, axis, pairs)  24.8 us
    ppermute x8, waiting for transfers between devices, butterfly_sum(): values = values + lax.ppermute(values, axis, pairs)  23 us
    ppermute x8, waiting for transfers between devices, halving_sum(): other = lax.ppermute(chunk, axis, pairs)  19.5 us
    ppermute x2, starting transfers between devices, with_halo(): lax.ppermute(lax.slice_in_dim(block, 0, width, axis=dim), axis, backward)  14.9 us
    pallas_call x1, Pallas kernels, kernel_terms(): pl.pallas_call(body, grid=(channels // lanes,), in_specs=[pl.BlockSpec((r...  14.7 us
    conv_general_dilated x3, local copies, waits for them, and re-layouts, depthwise(): lax.conv_general_dilated(extended, kernel.reshape(kernel.shape[0], kernel...  14.1 us
    ppermute x2, waiting for transfers between devices, with_halo(): lax.ppermute(lax.slice_in_dim(block, block.shape[dim] - width, None, axis...  13.4 us
  transfers between devices with their start and end apart: 28, of which 25 were waited for; matrix products, arithmetic and copies ran while one was open for 7% of the time, Pallas kernels for 0%

profile of v2, /device:TPU:28, one launch (start us, length us, event | category | flops | bytes accessed | tf_op | source)
XLA Modules:
  0.0 256.3 jit_solution(17945850352785829695)
XLA Ops:
  0.7 1.5 fusion.39
  2.2 2.1 collective-permute-start
  4.2 7.9 %collective-permute-start.1 = (bf16[1,3,64,1536]{3,2,1,0:T(8,128)(2,1)S(1)}, bf16[1,3,64,1536]{3,2,1,0:T(8,128)(2,1)S(1)}, u32[]{:S(2)}, u32[]{:S(2)}) collective-permute-start(bf16[1,3,64,1536]{3,2,1,0:T(8,128)(2,1)S(1)} %get-tuple-element.21), channel_id=1, source_target_pairs={{1,0},{2,1},{3,2},{4,3},{5,4},{6,5},{7,6},{8,7},{9,8},{10,9},{11,1... | collective-permute-start | bytes 1769480 | tf_op jit(solution)/shard_map/ppermute | solution.py:16
  12.1 5.6 %collective-permute-done = bf16[1,3,64,1536]{3,2,1,0:T(8,128)(2,1)S(1)} collective-permute-done((bf16[1,3,64,1536]{3,2,1,0:T(8,128)(2,1)S(1)}, bf16[1,3,64,1536]{3,2,1,0:T(8,128)(2,1)S(1)}, u32[]{:S(2)}, u32[]{:S(2)}) %collective-permute-start) | collective-permute-done | bytes 589856 | tf_op jit(solution)/shard_map/ppermute | solution.py:13
  17.9 1.6 collective-permute-done.1
  19.6 21.5 %fusion.5 = f32[1,8,64,1536]{3,0,2,1:T(1,128)S(1)} fusion(bf16[1,14,64,1536]{3,2,1,0:T(8,128)(2,1)S(1)} %constant_dynamic-update-slice_fusion, bf16[7,7,1,1536]{3,1,0,2:T(8,128)(2,1)S(1)} %bitcast.37), kind=kOutput, calls=%fused_computation.7 | convolution fusion | flops 75005952 | bytes 6048768 | tf_op jit(solution)/shard_map/conv_general_dilated | solution.py:78
  43.6 1.2 collective-permute-done.2
  44.8 3.6 %collective-permute-done.3 = f32[1,1536]{1,0:T(1,128)S(1)} collective-permute-done((f32[1,1536]{1,0:T(1,128)S(1)}, f32[1,1536]{1,0:T(1,128)S(1)}, u32[]{:S(2)}, u32[]{:S(2)}) %collective-permute-start.3) | collective-permute-done | bytes 6176 | tf_op jit(solution)/shard_map/ppermute | solution.py:30
  48.5 3.3 %collective-permute-start.4 = (f32[1,1536]{1,0:T(1,128)S(1)}, f32[1,1536]{1,0:T(1,128)S(1)}, u32[]{:S(2)}, u32[]{:S(2)}) collective-permute-start(f32[1,1536]{1,0:T(1,128)S(1)} %add.151), channel_id=1, source_target_pairs={{0,4},{1,5},{2,6},{3,7},{4,0},{5,1},{6,2},{7,3},{8,12},{9,13},{10,... | collective-permute-start | bytes 18440 | tf_op jit(solution)/shard_map/ppermute | solution.py:30
  51.7 1.6 collective-permute-done.4
  53.4 3.9 %collective-permute-start.5 = (f32[1,1536]{1,0:T(1,128)S(1)}, f32[1,1536]{1,0:T(1,128)S(1)}, u32[]{:S(2)}, u32[]{:S(2)}) collective-permute-start(f32[1,1536]{1,0:T(1,128)S(1)} %add.152), channel_id=1, source_target_pairs={{0,8},{1,9},{2,10},{3,11},{4,12},{5,13},{6,14},{7,15},{8,0},{9,1},... | collective-permute-start | bytes 18440 | tf_op jit(solution)/shard_map/ppermute | solution.py:30
  57.3 3.7 %collective-permute-done.5 = f32[1,1536]{1,0:T(1,128)S(1)} collective-permute-done((f32[1,1536]{1,0:T(1,128)S(1)}, f32[1,1536]{1,0:T(1,128)S(1)}, u32[]{:S(2)}, u32[]{:S(2)}) %collective-permute-start.5) | collective-permute-done | bytes 6176 | tf_op jit(solution)/shard_map/ppermute | solution.py:30
  61.0 1.3 collective-permute-start.6
  62.4 3.9 %collective-permute-done.6 = f32[1,1536]{1,0:T(1,128)S(1)} collective-permute-done((f32[1,1536]{1,0:T(1,128)S(1)}, f32[1,1536]{1,0:T(1,128)S(1)}, u32[]{:S(2)}, u32[]{:S(2)}) %collective-permute-start.6) | collective-permute-done | bytes 6176 | tf_op jit(solution)/shard_map/ppermute | solution.py:30
  66.6 1.3 collective-permute-start.7
  67.9 3.8 %collective-permute-done.7 = f32[8,2560]{1,0:T(8,128)S(1)} collective-permute-done((f32[8,2560]{1,0:T(8,128)S(1)}, f32[8,2560]{1,0:T(8,128)S(1)}, u32[]{:S(2)}, u32[]{:S(2)}) %collective-permute-start.7) | collective-permute-done | bytes 81952 | tf_op jit(solution)/shard_map/ppermute | solution.py:30
  72.8 5.2 %collective-permute-done.8 = f32[8,2560]{1,0:T(8,128)S(1)} collective-permute-done((f32[8,2560]{1,0:T(8,128)S(1)}, f32[8,2560]{1,0:T(8,128)S(1)}, u32[]{:S(2)}, u32[]{:S(2)}) %collective-permute-start.8) | collective-permute-done | bytes 81952 | tf_op jit(solution)/shard_map/ppermute | solution.py:30
  78.0 1.0 collective-permute-start.9
  79.0 5.3 %bitcast_convert_fusion.x_ref = f32[14,70,1536]{2,1,0:T(8,128)} fusion(bf16[1,14,64,1536]{3,2,1,0:T(8,128)(2,1)} %copy-done.7), kind=kLoop, calls=%fused_computation.17 | loop fusion | flops 1505280 | bytes 8773632 | tf_op jit(solution)/shard_map/squeeze | solution.py:184
  84.4 1.4 multiply_reduce_fusion.5
  88.8 3.8 %convolution_reduce_fusion = f32[1536]{0:T(1024)S(1)} fusion(bf16[1536,1024]{1,0:T(8,128)(2,1)S(1)} %copy-done, f32[8,1024]{1,0:T(8,128)S(1)} %get-tuple-element.27, s32[]{:T(128)S(6)} %select_n.233, f32[8,1024]{1,0:T(8,128)S(1)} %get-tuple-element.31, f32[1]{0:T(128)} %dynamic-slice.2, f32[1]{0:T(128)} %dynamic-slice.1), kind=kOutput, calls=%fused_computation.23 | convolution fusion | flops 18877440 | bytes 3160076 | tf_op jit(solution)/shard_map/dot_general | solution.py:175
  94.6 2.5 fusion.46.g_ref
  97.1 14.7 %shard_map.111 = f32[7,7,1536]{2,1,0:T(8,128)} custom-call(f32[8,64,1536]{2,1,0:T(8,128)} %fusion.46.g_ref, f32[14,70,1536]{2,1,0:T(8,128)} %bitcast_convert_fusion.x_ref), custom_call_target="tpu_custom_call" | custom-call | tf_op jit(solution)/shard_map/pallas_call | solution.py:103
  111.8 1.0 reshape.156
  113.6 1.7 collective-permute-done.12
  116.9 2.0 collective-permute-start.13
  118.9 2.7 %collective-permute-done.13 = f32[18816]{0:T(1024)S(1)} collective-permute-done((f32[18816]{0:T(1024)S(1)}, f32[18816]{0:T(1024)S(1)}, u32[]{:S(2)}, u32[]{:S(2)}) %collective-permute-start.13) | collective-permute-done | bytes 75296 | tf_op jit(solution)/shard_map/ppermute | solution.py:57
  121.5 1.0 select_add_fusion.1
  122.6 2.7 %collective-permute-start.14 = (f32[9408]{0:T(1024)S(1)}, f32[9408]{0:T(1024)S(1)}, u32[]{:S(2)}, u32[]{:S(2)}) collective-permute-start(f32[9408]{0:T(1024)S(1)} %slice_select_fusion.2), channel_id=1, source_target_pairs={{0,4},{1,5},{2,6},{3,7},{4,0},{5,1},{6,2},{7,3},{8,12},{9,13},{10,... | collective-permute-start | bytes 112904 | tf_op jit(solution)/shard_map/ppermute | solution.py:57
  125.3 2.3 collective-permute-done.14
  127.8 3.2 %collective-permute-start.15 = (f32[4704]{0:T(1024)S(1)}, f32[4704]{0:T(1024)S(1)}, u32[]{:S(2)}, u32[]{:S(2)}) collective-permute-start(f32[4704]{0:T(1024)S(1)} %slice_select_fusion.3), channel_id=1, source_target_pairs={{0,8},{1,9},{2,10},{3,11},{4,12},{5,13},{6,14},{7,15},{8,0},{9,1},... | collective-permute-start | bytes 56456 | tf_op jit(solution)/shard_map/ppermute | solution.py:57
  130.9 4.5 %collective-permute-done.15 = f32[4704]{0:T(1024)S(1)} collective-permute-done((f32[4704]{0:T(1024)S(1)}, f32[4704]{0:T(1024)S(1)}, u32[]{:S(2)}, u32[]{:S(2)}) %collective-permute-start.15) | collective-permute-done | bytes 18848 | tf_op jit(solution)/shard_map/ppermute | solution.py:57
  135.6 1.0 collective-permute-start.16
  136.6 4.3 %collective-permute-done.16 = f32[2352]{0:T(1024)S(1)} collective-permute-done((f32[2352]{0:T(1024)S(1)}, f32[2352]{0:T(1024)S(1)}, u32[]{:S(2)}, u32[]{:S(2)}) %collective-permute-start.16) | collective-permute-done | bytes 9440 | tf_op jit(solution)/shard_map/ppermute | solution.py:57
  141.0 1.0 collective-permute-start.17
  142.0 2.7 %collective-permute-done.17 = f32[1176]{0:T(1024)S(1)} collective-permute-done((f32[1176]{0:T(1024)S(1)}, f32[1176]{0:T(1024)S(1)}, u32[]{:S(2)}, u32[]{:S(2)}) %collective-permute-start.17) | collective-permute-done | bytes 4736 | tf_op jit(solution)/shard_map/ppermute | solution.py:57
  145.6 4.3 %collective-permute-done.18 = f32[588]{0:T(1024)S(1)} collective-permute-done((f32[588]{0:T(1024)S(1)}, f32[588]{0:T(1024)S(1)}, u32[]{:S(2)}, u32[]{:S(2)}) %collective-permute-start.18) | collective-permute-done | bytes 2384 | tf_op jit(solution)/shard_map/ppermute | solution.py:57
  150.1 1.3 collective-permute-start.19
  151.4 2.3 collective-permute-done.19
  153.8 1.3 collective-permute-start.20
  155.1 2.3 collective-permute-done.20
  157.4 1.0 collective-permute-start.21
  158.5 4.3 %collective-permute-done.21 = f32[588]{0:T(1024)S(1)} collective-permute-done((f32[588]{0:T(1024)S(1)}, f32[588]{0:T(1024)S(1)}, u32[]{:S(2)}, u32[]{:S(2)}) %collective-permute-start.21) | collective-permute-done | bytes 2384 | tf_op jit(solution)/shard_map/ppermute | solution.py:61
  162.9 1.0 collective-permute-start.22
  163.8 2.7 %collective-permute-done.22 = f32[1176]{0:T(1024)S(1)} collective-permute-done((f32[1176]{0:T(1024)S(1)}, f32[1176]{0:T(1024)S(1)}, u32[]{:S(2)}, u32[]{:S(2)}) %collective-permute-start.22) | collective-permute-done | bytes 4736 | tf_op jit(solution)/shard_map/ppermute | solution.py:61
  166.6 1.0 collective-permute-start.23
  167.6 4.3 %collective-permute-done.23 = f32[2352]{0:T(1024)S(1)} collective-permute-done((f32[2352]{0:T(1024)S(1)}, f32[2352]{0:T(1024)S(1)}, u32[]{:S(2)}, u32[]{:S(2)}) %collective-permute-start.23) | collective-permute-done | bytes 9440 | tf_op jit(solution)/shard_map/ppermute | solution.py:61
  171.9 3.2 %collective-permute-start.24 = (f32[4704]{0:T(1024)S(1)}, f32[4704]{0:T(1024)S(1)}, u32[]{:S(2)}, u32[]{:S(2)}) collective-permute-start(f32[4704]{0:T(1024)S(1)} %maximum_select_fusion.4), channel_id=1, source_target_pairs={{0,8},{1,9},{2,10},{3,11},{4,12},{5,13},{6,14},{7,15},{8,0},{9,1},... | collective-permute-start | bytes 56456 | tf_op jit(solution)/shard_map/ppermute | solution.py:61
  175.1 6.1 %rev.3 = f32[7,7,1536]{2,1,0:T(8,128)} reverse(bf16[7,7,1536]{2,1,0:T(8,128)(2,1)} %param.9), dimensions={0,1} | reverse | bytes 451584 | tf_op jit(solution)/shard_map/rev | solution.py:182
  181.3 1.5 collective-permute-start.25
  183.7 2.6 %collective-permute-done.25 = f32[9408]{0:T(1024)S(1)} collective-permute-done((f32[9408]{0:T(1024)S(1)}, f32[9408]{0:T(1024)S(1)}, u32[]{:S(2)}, u32[]{:S(2)}) %collective-permute-start.25) | collective-permute-done | bytes 37664 | tf_op jit(solution)/shard_map/ppermute | solution.py:61
  186.4 1.1 collective-permute-start.26
  187.6 3.2 %collective-permute-done.26 = f32[18816]{0:T(1024)S(1)} collective-permute-done((f32[18816]{0:T(1024)S(1)}, f32[18816]{0:T(1024)S(1)}, u32[]{:S(2)}, u32[]{:S(2)}) %collective-permute-start.26) | collective-permute-done | bytes 75296 | tf_op jit(solution)/shard_map/ppermute | solution.py:61
  192.5 2.4 collective-permute-start.10
  194.9 7.0 %collective-permute-start.11 = (f32[1,3,64,1536]{3,2,1,0:T(8,128)S(1)}, f32[1,3,64,1536]{3,2,1,0:T(8,128)}, u32[]{:S(2)}, u32[]{:S(2)}) collective-permute-start(f32[1,3,64,1536]{3,2,1,0:T(8,128)S(1)} %get-tuple-element.20), channel_id=1, source_target_pairs={{1,0},{2,1},{3,2},{4,3},{5,4},{6,5},{7,6},{8,7},{9,8},{10,9},{11,1... | collective-permute-start | bytes 3538952 | tf_op jit(solution)/shard_map/ppermute | solution.py:16
  202.0 1.9 fusion.17
  206.0 7.7 %collective-permute-done.10 = f32[1,3,64,1536]{3,2,1,0:T(8,128)} collective-permute-done((f32[1,3,64,1536]{3,2,1,0:T(8,128)S(1)}, f32[1,3,64,1536]{3,2,1,0:T(8,128)}, u32[]{:S(2)}, u32[]{:S(2)}) %collective-permute-start.10) | collective-permute-done | bytes 1179680 | tf_op jit(solution)/shard_map/ppermute | solution.py:13
  213.8 1.7 collective-permute-done.11
  215.4 3.1 %maximum_bitcast_fusion = f32[14,1,64,1536]{3,2,0,1:T(8,128)S(1)} fusion(f32[1,3,64,1536]{3,2,1,0:T(8,128)} %collective-permute-done.11, f32[1,8,64,1536]{3,2,1,0:T(8,128)} %copy-done.5, f32[1,3,64,1536]{3,2,1,0:T(8,128)} %collective-permute-done.10), kind=kLoop, calls=%fused_computation.6 | loop fusion | flops 2752512 | bytes 11010048 | tf_op jit(solution)/shard_map/concatenate | solution.py:17
  218.5 3.5 %pad.6 = f32[14,1,72,1536]{3,2,0,1:T(8,128)} pad(f32[14,1,64,1536]{3,2,0,1:T(8,128)S(1)} %maximum_bitcast_fusion, f32[]{:T(128)} %constant.169.clone.1), padding=0_0x0_0x3_5x0_0 | pad | bytes 11698180 | tf_op jit(solution)/shard_map/concatenate | solution.py:17
  222.0 10.3 %reshape.159 = f32[14,1,8,9,1536]{4,1,3,2,0:T(1,128)} reshape(f32[14,1,72,1536]{3,2,0,1:T(8,128)} %pad.6) | data formatting | bytes 12386304 | tf_op jit(solution)/shard_map/conv_general_dilated | solution.py:78
  232.3 3.2 %copy.22 = f32[14,1,8,9,1536]{4,2,3,0,1:T(8,128)S(1)} copy(f32[14,1,8,9,1536]{4,1,3,2,0:T(1,128)} %reshape.159) | data formatting | bytes 12386304 | tf_op jit(solution)/shard_map/conv_general_dilated | solution.py:78
  236.6 15.6 %select_convert_fusion = bf16[8,8,9,1536]{3,1,2,0:T(8,128)(2,1)S(1)} fusion(f32[14,1,7,6,1536]{4,2,3,0,1:T(8,128)S(1)} %slice.94, f32[14,1,8,9,1536]{4,2,3,0,1:T(8,128)S(1)} %copy.22, pred[8,9]{0,1:T(8,128)(4,1)S(1)} %copy-done.17, f32[7,7,1,1536]{3,1,0,2:T(8,128)S(1)} %bitcast.36), kind=kOutput, calls=%fused_computation.11 | convolution fusion | flops 529735680 | bytes 11876424 | tf_op jit(solution)/shard_map/conv_general_dilated | solution.py:78
  252.8 1.6 copy.25
  (112 shorter events, 18.1 us)
Async XLA Ops:
  0.6 83.8 %copy-start = (bf16[1536,1024]{1,0:T(8,128)(2,1)S(1)}, bf16[1536,1024]{1,0:T(8,128)(2,1)}, u32[]{:S(2)}) copy-start(bf16[1536,1024]{1,0:T(8,128)(2,1)} %param.13) | copy-start | bytes 9437188
  0.6 17.1 %copy-start.6 = (bf16[1,8,64,1536]{3,2,1,0:T(8,128)(2,1)S(1)}, bf16[1,8,64,1536]{3,2,1,0:T(8,128)(2,1)}, u32[]{:S(2)}) copy-start(bf16[1,8,64,1536]{3,2,1,0:T(8,128)(2,1)} %param.8) | copy-start | bytes 4718596
  2.1 17.4 %copy-start.11 = (bf16[7,7,1536]{2,1,0:T(8,128)(2,1)S(1)}, bf16[7,7,1536]{2,1,0:T(8,128)(2,1)}, u32[]{:S(2)}) copy-start(bf16[7,7,1536]{2,1,0:T(8,128)(2,1)} %param.9) | copy-start | bytes 451588
  2.2 15.6 %collective-permute-start = (bf16[1,3,64,1536]{3,2,1,0:T(8,128)(2,1)S(1)}, bf16[1,3,64,1536]{3,2,1,0:T(8,128)(2,1)S(1)}, u32[]{:S(2)}, u32[]{:S(2)}) collective-permute-start(bf16[1,3,64,1536]{3,2,1,0:T(8,128)(2,1)S(1)} %get-tuple-element.22), channel_id=1, source_target_pairs={{0,1},{1,2},{2,3},{3,4},{4,5},{5,6},{6,7},{7,8},{8,9},{9,10},{10,1... | collective-permute-start | bytes 1769480 | tf_op jit(solution)/shard_map/ppermute | solution.py:13
  4.2 15.3 %collective-permute-start.1 = (bf16[1,3,64,1536]{3,2,1,0:T(8,128)(2,1)S(1)}, bf16[1,3,64,1536]{3,2,1,0:T(8,128)(2,1)S(1)}, u32[]{:S(2)}, u32[]{:S(2)}) collective-permute-start(bf16[1,3,64,1536]{3,2,1,0:T(8,128)(2,1)S(1)} %get-tuple-element.21), channel_id=1, source_target_pairs={{1,0},{2,1},{3,2},{4,3},{5,4},{6,5},{7,6},{8,7},{9,8},{10,9},{11,1... | collective-permute-start | bytes 1769480 | tf_op jit(solution)/shard_map/ppermute | solution.py:16
  19.5 21.5 %copy-start.7 = (bf16[1,14,64,1536]{3,2,1,0:T(8,128)(2,1)}, bf16[1,14,64,1536]{3,2,1,0:T(8,128)(2,1)S(1)}, u32[]{:S(2)}) copy-start(bf16[1,14,64,1536]{3,2,1,0:T(8,128)(2,1)S(1)} %constant_dynamic-update-slice_fusion) | copy-start | bytes 8257540
  19.5 21.5 %copy-start.10 = (f32[1536]{0:T(1024)S(1)}, f32[1536]{0:T(1024)}, u32[]{:S(2)}) copy-start(f32[1536]{0:T(1024)} %param.10) | copy-start | bytes 18436
  41.0 1.7 copy-start.2
  41.1 1.7 copy-start.12
  41.1 1.7 copy-start.14
  41.4 24.9 %copy-start.13 = (f32[1,1024]{1,0:T(1,128)S(1)}, f32[1,1024]{1,0:T(1,128)}, u32[]{:S(2)}) copy-start(f32[1,1024]{1,0:T(1,128)} %param.14) | copy-start | bytes 12292
  43.5 1.3 collective-permute-start.2
  44.7 3.7 %collective-permute-start.3 = (f32[1,1536]{1,0:T(1,128)S(1)}, f32[1,1536]{1,0:T(1,128)S(1)}, u32[]{:S(2)}, u32[]{:S(2)}) collective-permute-start(f32[1,1536]{1,0:T(1,128)S(1)} %reshape_add_fusion), channel_id=1, source_target_pairs={{0,2},{1,3},{2,0},{3,1},{4,6},{5,7},{6,4},{7,5},{8,10},{9,11},{10,... | collective-permute-start | bytes 18440 | tf_op jit(solution)/shard_map/ppermute | solution.py:30
  48.5 4.9 %collective-permute-start.4 = (f32[1,1536]{1,0:T(1,128)S(1)}, f32[1,1536]{1,0:T(1,128)S(1)}, u32[]{:S(2)}, u32[]{:S(2)}) collective-permute-start(f32[1,1536]{1,0:T(1,128)S(1)} %add.151), channel_id=1, source_target_pairs={{0,4},{1,5},{2,6},{3,7},{4,0},{5,1},{6,2},{7,3},{8,12},{9,13},{10,... | collective-permute-start | bytes 18440 | tf_op jit(solution)/shard_map/ppermute | solution.py:30
  53.4 7.6 %collective-permute-start.5 = (f32[1,1536]{1,0:T(1,128)S(1)}, f32[1,1536]{1,0:T(1,128)S(1)}, u32[]{:S(2)}, u32[]{:S(2)}) collective-permute-start(f32[1,1536]{1,0:T(1,128)S(1)} %add.152), channel_id=1, source_target_pairs={{0,8},{1,9},{2,10},{3,11},{4,12},{5,13},{6,14},{7,15},{8,0},{9,1},... | collective-permute-start | bytes 18440 | tf_op jit(solution)/shard_map/ppermute | solution.py:30
  61.0 5.2 %collective-permute-start.6 = (f32[1,1536]{1,0:T(1,128)S(1)}, f32[1,1536]{1,0:T(1,128)S(1)}, u32[]{:S(2)}, u32[]{:S(2)}) collective-permute-start(f32[1,1536]{1,0:T(1,128)S(1)} %add.153), channel_id=1, source_target_pairs={{0,16},{1,17},{2,18},{3,19},{4,20},{5,21},{6,22},{7,23},{8,24},{9,... | collective-permute-start | bytes 18440 | tf_op jit(solution)/shard_map/ppermute | solution.py:30
  66.6 5.1 %collective-permute-start.7 = (f32[8,2560]{1,0:T(8,128)S(1)}, f32[8,2560]{1,0:T(8,128)S(1)}, u32[]{:S(2)}, u32[]{:S(2)}) collective-permute-start(f32[8,2560]{1,0:T(8,128)S(1)} %dynamic_update_slice.5), channel_id=1, source_target_pairs={{0,32},{32,0},{64,96},{96,64},{128,160},{160,128},{192,224},{224,1... | collective-permute-start | bytes 245768 | tf_op jit(solution)/shard_map/ppermute | solution.py:30
  71.9 6.0 %collective-permute-start.8 = (f32[8,2560]{1,0:T(8,128)S(1)}, f32[8,2560]{1,0:T(8,128)S(1)}, u32[]{:S(2)}, u32[]{:S(2)}) collective-permute-start(f32[8,2560]{1,0:T(8,128)S(1)} %add.156), channel_id=1, source_target_pairs={{0,64},{32,96},{64,0},{96,32},{128,192},{160,224},{192,128},{224,1... | collective-permute-start | bytes 245768 | tf_op jit(solution)/shard_map/ppermute | solution.py:30
  78.0 6.3 %collective-permute-start.9 = (f32[8,2560]{1,0:T(8,128)S(1)}, f32[8,2560]{1,0:T(8,128)S(1)}, u32[]{:S(2)}, u32[]{:S(2)}) collective-permute-start(f32[8,2560]{1,0:T(8,128)S(1)} %add.157), channel_id=1, source_target_pairs={{0,128},{32,160},{64,192},{96,224},{128,0},{160,32},{192,64},{224,... | collective-permute-start | bytes 245768 | tf_op jit(solution)/shard_map/ppermute | solution.py:30
  84.4 8.8 %copy-start.3 = (f32[1,8,64,1536]{3,0,2,1:T(1,128)S(1)}, f32[1,8,64,1536]{3,0,2,1:T(1,128)}, u32[]{:S(2)}) copy-start(f32[1,8,64,1536]{3,0,2,1:T(1,128)} %copy-done.2) | copy-start | bytes 9437188
  85.9 0.7 copy-start.15
  92.6 2.0 copy-start.4
  113.6 1.7 collective-permute-start.12
  116.2 0.7 copy-start.8
  116.9 4.6 %collective-permute-start.13 = (f32[18816]{0:T(1024)S(1)}, f32[18816]{0:T(1024)S(1)}, u32[]{:S(2)}, u32[]{:S(2)}) collective-permute-start(f32[18816]{0:T(1024)S(1)} %slice_select_fusion.1), channel_id=1, source_target_pairs={{0,2},{1,3},{2,0},{3,1},{4,6},{5,7},{6,4},{7,5},{8,10},{9,11},{10,... | collective-permute-start | bytes 225800 | tf_op jit(solution)/shard_map/ppermute | solution.py:57
  122.6 5.0 %collective-permute-start.14 = (f32[9408]{0:T(1024)S(1)}, f32[9408]{0:T(1024)S(1)}, u32[]{:S(2)}, u32[]{:S(2)}) collective-permute-start(f32[9408]{0:T(1024)S(1)} %slice_select_fusion.2), channel_id=1, source_target_pairs={{0,4},{1,5},{2,6},{3,7},{4,0},{5,1},{6,2},{7,3},{8,12},{9,13},{10,... | collective-permute-start | bytes 112904 | tf_op jit(solution)/shard_map/ppermute | solution.py:57
  127.8 7.7 %collective-permute-start.15 = (f32[4704]{0:T(1024)S(1)}, f32[4704]{0:T(1024)S(1)}, u32[]{:S(2)}, u32[]{:S(2)}) collective-permute-start(f32[4704]{0:T(1024)S(1)} %slice_select_fusion.3), channel_id=1, source_target_pairs={{0,8},{1,9},{2,10},{3,11},{4,12},{5,13},{6,14},{7,15},{8,0},{9,1},... | collective-permute-start | bytes 56456 | tf_op jit(solution)/shard_map/ppermute | solution.py:57
  135.6 5.2 %collective-permute-start.16 = (f32[2352]{0:T(1024)S(1)}, f32[2352]{0:T(1024)S(1)}, u32[]{:S(2)}, u32[]{:S(2)}) collective-permute-start(f32[2352]{0:T(1024)S(1)} %slice_select_fusion.4), channel_id=1, source_target_pairs={{0,16},{1,17},{2,18},{3,19},{4,20},{5,21},{6,22},{7,23},{8,24},{9,... | collective-permute-start | bytes 28232 | tf_op jit(solution)/shard_map/ppermute | solution.py:57
  141.0 3.7 %collective-permute-start.17 = (f32[1176]{0:T(1024)S(1)}, f32[1176]{0:T(1024)S(1)}, u32[]{:S(2)}, u32[]{:S(2)}) collective-permute-start(f32[1176]{0:T(1024)S(1)} %slice_select_fusion.5), channel_id=1, source_target_pairs={{0,32},{32,0},{64,96},{96,64},{128,160},{160,128},{192,224},{224,1... | collective-permute-start | bytes 14120 | tf_op jit(solution)/shard_map/ppermute | solution.py:57
  144.8 5.1 %collective-permute-start.18 = (f32[588]{0:T(1024)S(1)}, f32[588]{0:T(1024)S(1)}, u32[]{:S(2)}, u32[]{:S(2)}) collective-permute-start(f32[588]{0:T(1024)S(1)} %slice_select_fusion.6), channel_id=1, source_target_pairs={{0,64},{32,96},{64,0},{96,32},{128,192},{160,224},{192,128},{224,1... | collective-permute-start | bytes 7064 | tf_op jit(solution)/shard_map/ppermute | solution.py:57
  150.1 3.6 %collective-permute-start.19 = (f32[294]{0:T(512)S(1)}, f32[294]{0:T(512)S(1)}, u32[]{:S(2)}, u32[]{:S(2)}) collective-permute-start(f32[294]{0:T(512)S(1)} %slice_select_fusion.7), channel_id=1, source_target_pairs={{0,128},{32,160},{64,192},{96,224},{128,0},{160,32},{192,64},{224,... | collective-permute-start | bytes 3536 | tf_op jit(solution)/shard_map/ppermute | solution.py:57
  153.8 3.6 %collective-permute-start.20 = (f32[294]{0:T(512)S(1)}, f32[294]{0:T(512)S(1)}, u32[]{:S(2)}, u32[]{:S(2)}) collective-permute-start(f32[294]{0:T(512)S(1)} %select_add_fusion.7), channel_id=1, source_target_pairs={{0,128},{32,160},{64,192},{96,224},{128,0},{160,32},{192,64},{224,... | collective-permute-start | bytes 3536 | tf_op jit(solution)/shard_map/ppermute | solution.py:61
  157.4 5.4 %collective-permute-start.21 = (f32[588]{0:T(1024)S(1)}, f32[588]{0:T(1024)S(1)}, u32[]{:S(2)}, u32[]{:S(2)}) collective-permute-start(f32[588]{0:T(1024)S(1)} %maximum_select_fusion.7), channel_id=1, source_target_pairs={{0,64},{32,96},{64,0},{96,32},{128,192},{160,224},{192,128},{224,1... | collective-permute-start | bytes 7064 | tf_op jit(solution)/shard_map/ppermute | solution.py:61
  162.9 3.7 %collective-permute-start.22 = (f32[1176]{0:T(1024)S(1)}, f32[1176]{0:T(1024)S(1)}, u32[]{:S(2)}, u32[]{:S(2)}) collective-permute-start(f32[1176]{0:T(1024)S(1)} %maximum_select_fusion.6), channel_id=1, source_target_pairs={{0,32},{32,0},{64,96},{96,64},{128,160},{160,128},{192,224},{224,1... | collective-permute-start | bytes 14120 | tf_op jit(solution)/shard_map/ppermute | solution.py:61
  166.6 5.2 %collective-permute-start.23 = (f32[2352]{0:T(1024)S(1)}, f32[2352]{0:T(1024)S(1)}, u32[]{:S(2)}, u32[]{:S(2)}) collective-permute-start(f32[2352]{0:T(1024)S(1)} %maximum_select_fusion.5), channel_id=1, source_target_pairs={{0,16},{1,17},{2,18},{3,19},{4,20},{5,21},{6,22},{7,23},{8,24},{9,... | collective-permute-start | bytes 28232 | tf_op jit(solution)/shard_map/ppermute | solution.py:61
  171.9 9.3 %collective-permute-start.24 = (f32[4704]{0:T(1024)S(1)}, f32[4704]{0:T(1024)S(1)}, u32[]{:S(2)}, u32[]{:S(2)}) collective-permute-start(f32[4704]{0:T(1024)S(1)} %maximum_select_fusion.4), channel_id=1, source_target_pairs={{0,8},{1,9},{2,10},{3,11},{4,12},{5,13},{6,14},{7,15},{8,0},{9,1},... | collective-permute-start | bytes 56456 | tf_op jit(solution)/shard_map/ppermute | solution.py:61
  181.3 5.0 %collective-permute-start.25 = (f32[9408]{0:T(1024)S(1)}, f32[9408]{0:T(1024)S(1)}, u32[]{:S(2)}, u32[]{:S(2)}) collective-permute-start(f32[9408]{0:T(1024)S(1)} %maximum_select_fusion.3), channel_id=1, source_target_pairs={{0,4},{1,5},{2,6},{3,7},{4,0},{5,1},{6,2},{7,3},{8,12},{9,13},{10,... | collective-permute-start | bytes 112904 | tf_op jit(solution)/shard_map/ppermute | solution.py:61
  183.6 3.8 %copy-start.5 = (f32[1,8,64,1536]{3,2,1,0:T(8,128)}, f32[1,8,64,1536]{3,2,1,0:T(8,128)S(1)}, u32[]{:S(2)}) copy-start(f32[1,8,64,1536]{3,2,1,0:T(8,128)S(1)} %subtract_multiply_fusion) | copy-start | bytes 9437188
  183.6 7.7 %copy-start.16 = (f32[8]{0:T(128)S(1)}, f32[8]{0:T(128)}, u32[]{:S(2)}) copy-start(f32[8]{0:T(128)} %copy-done.15) | copy-start | bytes 100
  186.4 4.5 %collective-permute-start.26 = (f32[18816]{0:T(1024)S(1)}, f32[18816]{0:T(1024)S(1)}, u32[]{:S(2)}, u32[]{:S(2)}) collective-permute-start(f32[18816]{0:T(1024)S(1)} %maximum_select_fusion.2), channel_id=1, source_target_pairs={{0,2},{1,3},{2,0},{3,1},{4,6},{5,7},{6,4},{7,5},{8,10},{9,11},{10,... | collective-permute-start | bytes 225800 | tf_op jit(solution)/shard_map/ppermute | solution.py:61
  190.9 14.3 %collective-permute-start.27 = (f32[37632]{0:T(1024)S(1)}, f32[37632]{0:T(1024)S(1)}, u32[]{:S(2)}, u32[]{:S(2)}) collective-permute-start(f32[37632]{0:T(1024)S(1)} %maximum_select_fusion.1), channel_id=1, source_target_pairs={{0,1},{1,0},{2,3},{3,2},{4,5},{5,4},{6,7},{7,6},{8,9},{9,8},{10,11... | collective-permute-start | bytes 451592 | tf_op jit(solution)/shard_map/ppermute | solution.py:61
  192.5 21.2 %collective-permute-start.10 = (f32[1,3,64,1536]{3,2,1,0:T(8,128)S(1)}, f32[1,3,64,1536]{3,2,1,0:T(8,128)}, u32[]{:S(2)}, u32[]{:S(2)}) collective-permute-start(f32[1,3,64,1536]{3,2,1,0:T(8,128)S(1)} %get-tuple-element.19), channel_id=1, source_target_pairs={{0,1},{1,2},{2,3},{3,4},{4,5},{5,6},{6,7},{7,8},{8,9},{9,10},{10,1... | collective-permute-start | bytes 3538952 | tf_op jit(solution)/shard_map/ppermute | solution.py:13
  194.9 20.5 %collective-permute-start.11 = (f32[1,3,64,1536]{3,2,1,0:T(8,128)S(1)}, f32[1,3,64,1536]{3,2,1,0:T(8,128)}, u32[]{:S(2)}, u32[]{:S(2)}) collective-permute-start(f32[1,3,64,1536]{3,2,1,0:T(8,128)S(1)} %get-tuple-element.20), channel_id=1, source_target_pairs={{1,0},{2,1},{3,2},{4,3},{5,4},{6,5},{7,6},{8,7},{9,8},{10,9},{11,1... | collective-permute-start | bytes 3538952 | tf_op jit(solution)/shard_map/ppermute | solution.py:16
  235.6 1.0 copy-start.9
  235.6 1.0 copy-start.17
  252.7 2.5 copy-start.1

commit v3 on v2

--- a/solution.py
+++ b/solution.py
@@ -111,6 +111,30 @@
         out_shape=jax.ShapeDtypeStruct((side, side, channels), jnp.float32),
     )(grad_rows, padded)
 
+def input_terms(padded, kernel, row_count, lanes=128):
+    side = kernel.shape[0]
+    col_count = padded.shape[1] - side + 1
+    channels = padded.shape[2]
+
+    def body(x_ref, k_ref, o_ref):
+        for h in range(row_count):
+            acc = jnp.zeros((col_count, lanes), jnp.float32)
+            for a in range(side):
+                for d in range(side):
+                    acc = acc + k_ref[a, pl.ds(d, 1), :] * x_ref[h + a, pl.ds(d, col_count), :]
+            o_ref[h] = acc.astype(o_ref.dtype)
+
+    return pl.pallas_call(
+        body,
+        grid=(channels // lanes,),
+        in_specs=[
+            pl.BlockSpec(padded.shape[:2] + (lanes,), lambda i: (0, 0, i)),
+            pl.BlockSpec((side, side, lanes), lambda i: (0, 0, i)),
+        ],
+        out_specs=pl.BlockSpec((row_count, col_count, lanes), lambda i: (0, 0, i)),
+        out_shape=jax.ShapeDtypeStruct((row_count, col_count, channels), jnp.bfloat16),
+    )(padded, kernel)
+
 def logsum(scores, axis):
     highest = jnp.max(scores, axis=axis, keepdims=True)
     return jnp.squeeze(highest, axis) + jnp.log(jnp.sum(jnp.exp(scores - highest), axis=axis))
@@ -178,8 +202,10 @@
     spread_term = jnp.mean(weight_rows * normed, axis=-1, keepdims=True)
     grad_own = inv_dev * (weight_rows - weight_mean - normed * spread_term)
     grad_wide = with_halo(grad_own, (("space", 1),), reach_rows)
-    input_grad = depthwise(
-        grad_wide, kernel_float[::-1, ::-1], reach_rows, precision=lax.Precision.HIGHEST
+    grad_pad = jnp.pad(grad_wide, ((0, 0), (0, 0), (reach_rows, reach_rows), (0, 0)))
+    flipped = kernel_float[::-1, ::-1]
+    input_grad = jnp.stack(
+        [input_terms(grad_pad[image], flipped, row_count) for image in range(batch_dev)]
     )
     kernel_part = kernel_terms(grad_own[0], padded_all[0], reach_rows)
     for image in range(1, batch_dev):

time: 260 us -> 241 us (0.927)
  local copies, waits for them, and re-layouts: 35.1 us -> 15.6 us
  matrix products: 43.4 us -> 27.8 us
  Pallas kernels: 14.7 us -> 28.2 us
  other arithmetic: 21.7 us -> 28.1 us
  waiting for transfers between devices: 83.8 us -> 80 us
    conv_general_dilated x2 -> x1, matrix products: 37 us -> 21.5 us  [depthwise(): lax.conv_general_dilated(extended, kernel.reshape(kernel.shape[0], kernel...]
    conv_general_dilated x3 -> x0, local copies, waits for them, and re-layouts: 14.1 us -> none  [depthwise(): lax.conv_general_dilated(extended, kernel.reshape(kernel.shape[0], kernel...]
    pallas_call x0 -> x1, Pallas kernels: none -> 13.5 us  [input_terms(): pl.pallas_call(body, grid=(channels // lanes,), in_specs=[pl.BlockSpec(pa...]
    squeeze x0 -> x1, other arithmetic: none -> 4.68 us  [shards(): grad_pad[image]]
    concatenate x2 -> x1, local copies, waits for them, and re-layouts: 3.5 us -> 0.04 us  [with_halo(): block = jnp.concatenate([low, block, high], axis=dim)]
    ppermute x8, waiting for transfers between devices: 19.5 us -> 16.2 us  [halving_sum(): other = lax.ppermute(chunk, axis, pairs)]
    concatenate x1 -> x0, other arithmetic: 3.12 us -> none  [with_halo(): block = jnp.concatenate([low, block, high], axis=dim)]
    unnamed x39 -> x32, local copies, waits for them, and re-layouts: 4.52 us -> 1.68 us
  transfers between devices with their start and end apart: 28 -> 28, of which waited for: 25 -> 25; matrix products, arithmetic and copies ran while one was open for 7% -> 9% of each run, Pallas kernels for 0% -> 0%
where the time goes in v3:
time: 241 us; the launch traced here: 237 us
  waiting for transfers between devices  80 us (33%)
  starting transfers between devices  52.3 us (22%)
  Pallas kernels  28.2 us (12%)
  other arithmetic  28.1 us (12%)
  matrix products  27.8 us (12%)
  local copies, waits for them, and re-layouts  15.6 us (6%)
  between operations  4.83 us (2%)
    ppermute x8, waiting for transfers between devices, halving_sum(): chunk = keep + lax.ppermute(give, axis, pairs)  24.8 us
    ppermute x8, waiting for transfers between devices, butterfly_sum(): values = values + lax.ppermute(values, axis, pairs)  23 us
    conv_general_dilated x1, matrix products, depthwise(): lax.conv_general_dilated(extended, kernel.reshape(kernel.shape[0], kernel...  21.5 us
    ppermute x8, waiting for transfers between devices, halving_sum(): other = lax.ppermute(chunk, axis, pairs)  16.2 us
    pallas_call x1, Pallas kernels, kernel_terms(): pl.pallas_call(body, grid=(channels // lanes,), in_specs=[pl.BlockSpec((r...  14.7 us
    ppermute x2, starting transfers between devices, with_halo(): lax.ppermute(lax.slice_in_dim(block, 0, width, axis=dim), axis, backward)  14.7 us
    pallas_call x1, Pallas kernels, input_terms(): pl.pallas_call(body, grid=(channels // lanes,), in_specs=[pl.BlockSpec(pa...  13.5 us
    ppermute x2, waiting for transfers between devices, with_halo(): lax.ppermute(lax.slice_in_dim(block, block.shape[dim] - width, None, axis...  12.7 us
  transfers between devices with their start and end apart: 28, of which 25 were waited for; matrix products, arithmetic and copies ran while one was open for 9% of the time, Pallas kernels for 0%

profile of v3, /device:TPU:28, one launch (start us, length us, event | category | flops | bytes accessed | tf_op | source)
XLA Modules:
  0.0 237.0 jit_solution(14379552376099827187)
XLA Ops:
  0.7 1.5 fusion.28
  2.1 2.1 collective-permute-start
  4.2 7.9 %collective-permute-start.1 = (bf16[1,3,64,1536]{3,2,1,0:T(8,128)(2,1)S(1)}, bf16[1,3,64,1536]{3,2,1,0:T(8,128)(2,1)S(1)}, u32[]{:S(2)}, u32[]{:S(2)}) collective-permute-start(bf16[1,3,64,1536]{3,2,1,0:T(8,128)(2,1)S(1)} %get-tuple-element.17), channel_id=1, source_target_pairs={{1,0},{2,1},{3,2},{4,3},{5,4},{6,5},{7,6},{8,7},{9,8},{10,9},{11,1... | collective-permute-start | bytes 1769480 | tf_op jit(solution)/shard_map/ppermute | solution.py:16
  12.1 5.6 %collective-permute-done = bf16[1,3,64,1536]{3,2,1,0:T(8,128)(2,1)S(1)} collective-permute-done((bf16[1,3,64,1536]{3,2,1,0:T(8,128)(2,1)S(1)}, bf16[1,3,64,1536]{3,2,1,0:T(8,128)(2,1)S(1)}, u32[]{:S(2)}, u32[]{:S(2)}) %collective-permute-start) | collective-permute-done | bytes 589856 | tf_op jit(solution)/shard_map/ppermute | solution.py:13
  17.9 1.6 collective-permute-done.1
  19.6 21.5 %fusion.2 = f32[1,8,64,1536]{3,0,2,1:T(1,128)S(1)} fusion(bf16[1,14,64,1536]{3,2,1,0:T(8,128)(2,1)S(1)} %constant_dynamic-update-slice_fusion, bf16[7,7,1,1536]{3,1,0,2:T(8,128)(2,1)S(1)} %bitcast.24), kind=kOutput, calls=%fused_computation.6 | convolution fusion | flops 75005952 | bytes 6048768 | tf_op jit(solution)/shard_map/conv_general_dilated | solution.py:78
  43.5 1.2 collective-permute-done.2
  44.8 3.6 %collective-permute-done.3 = f32[1,1536]{1,0:T(1,128)S(1)} collective-permute-done((f32[1,1536]{1,0:T(1,128)S(1)}, f32[1,1536]{1,0:T(1,128)S(1)}, u32[]{:S(2)}, u32[]{:S(2)}) %collective-permute-start.3) | collective-permute-done | bytes 6176 | tf_op jit(solution)/shard_map/ppermute | solution.py:30
  48.4 3.3 %collective-permute-start.4 = (f32[1,1536]{1,0:T(1,128)S(1)}, f32[1,1536]{1,0:T(1,128)S(1)}, u32[]{:S(2)}, u32[]{:S(2)}) collective-permute-start(f32[1,1536]{1,0:T(1,128)S(1)} %add.153), channel_id=1, source_target_pairs={{0,4},{1,5},{2,6},{3,7},{4,0},{5,1},{6,2},{7,3},{8,12},{9,13},{10,... | collective-permute-start | bytes 18440 | tf_op jit(solution)/shard_map/ppermute | solution.py:30
  51.7 1.6 collective-permute-done.4
  53.4 3.9 %collective-permute-start.5 = (f32[1,1536]{1,0:T(1,128)S(1)}, f32[1,1536]{1,0:T(1,128)S(1)}, u32[]{:S(2)}, u32[]{:S(2)}) collective-permute-start(f32[1,1536]{1,0:T(1,128)S(1)} %add.154), channel_id=1, source_target_pairs={{0,8},{1,9},{2,10},{3,11},{4,12},{5,13},{6,14},{7,15},{8,0},{9,1},... | collective-permute-start | bytes 18440 | tf_op jit(solution)/shard_map/ppermute | solution.py:30
  57.3 3.7 %collective-permute-done.5 = f32[1,1536]{1,0:T(1,128)S(1)} collective-permute-done((f32[1,1536]{1,0:T(1,128)S(1)}, f32[1,1536]{1,0:T(1,128)S(1)}, u32[]{:S(2)}, u32[]{:S(2)}) %collective-permute-start.5) | collective-permute-done | bytes 6176 | tf_op jit(solution)/shard_map/ppermute | solution.py:30
  61.0 1.3 collective-permute-start.6
  62.3 3.9 %collective-permute-done.6 = f32[1,1536]{1,0:T(1,128)S(1)} collective-permute-done((f32[1,1536]{1,0:T(1,128)S(1)}, f32[1,1536]{1,0:T(1,128)S(1)}, u32[]{:S(2)}, u32[]{:S(2)}) %collective-permute-start.6) | collective-permute-done | bytes 6176 | tf_op jit(solution)/shard_map/ppermute | solution.py:30
  66.5 1.3 collective-permute-start.7
  67.8 3.8 %collective-permute-done.7 = f32[8,2560]{1,0:T(8,128)S(1)} collective-permute-done((f32[8,2560]{1,0:T(8,128)S(1)}, f32[8,2560]{1,0:T(8,128)S(1)}, u32[]{:S(2)}, u32[]{:S(2)}) %collective-permute-start.7) | collective-permute-done | bytes 81952 | tf_op jit(solution)/shard_map/ppermute | solution.py:30
  72.8 5.2 %collective-permute-done.8 = f32[8,2560]{1,0:T(8,128)S(1)} collective-permute-done((f32[8,2560]{1,0:T(8,128)S(1)}, f32[8,2560]{1,0:T(8,128)S(1)}, u32[]{:S(2)}, u32[]{:S(2)}) %collective-permute-start.8) | collective-permute-done | bytes 81952 | tf_op jit(solution)/shard_map/ppermute | solution.py:30
  78.0 1.0 collective-permute-start.9
  79.0 5.3 %bitcast_convert_fusion.x_ref = f32[14,70,1536]{2,1,0:T(8,128)} fusion(bf16[1,14,64,1536]{3,2,1,0:T(8,128)(2,1)} %copy-done.5), kind=kLoop, calls=%fused_computation.13 | loop fusion | flops 1505280 | bytes 8773632 | tf_op jit(solution)/shard_map/squeeze | solution.py:210
  84.4 1.4 multiply_reduce_fusion.5
  88.8 3.8 %convolution_reduce_fusion = f32[1536]{0:T(1024)S(1)} fusion(bf16[1536,1024]{1,0:T(8,128)(2,1)S(1)} %copy-done, f32[8,1024]{1,0:T(8,128)S(1)} %get-tuple-element.23, s32[]{:T(128)S(6)} %select_n.233, f32[8,1024]{1,0:T(8,128)S(1)} %get-tuple-element.27, f32[1]{0:T(128)} %dynamic-slice.2, f32[1]{0:T(128)} %dynamic-slice.1), kind=kOutput, calls=%fused_computation.18 | convolution fusion | flops 18877440 | bytes 3160076 | tf_op jit(solution)/shard_map/dot_general | solution.py:199
  94.6 4.3 %fusion.35.g_ref = f32[8,64,1536]{2,1,0:T(8,128)} fusion(f32[8,64]{1,0:T(8,128)S(1)} %broadcast_multiply_fusion, f32[8,64]{1,0:T(8,128)S(1)} %broadcast_multiply_fusion.1, f32[1536]{0:T(1024)S(1)} %copy-done.8, f32[1,8,64,1536]{3,0,2,1:T(1,128)} %copy-done.1, f32[1536]{0:T(1024)S(1)} %broadcast_subtract_fusion, f32[8,64]{1,0:T(8,128)S(1)} %add_rsqrt_fusion), kind=kLoop, calls=%fused_computation.96 | loop fusion | flops 4718592 | bytes 6309888 | tf_op jit(solution)/shard_map/squeeze | solution.py:210
  98.9 14.7 %shard_map.112 = f32[7,7,1536]{2,1,0:T(8,128)} custom-call(f32[8,64,1536]{2,1,0:T(8,128)} %fusion.35.g_ref, f32[14,70,1536]{2,1,0:T(8,128)} %bitcast_convert_fusion.x_ref), custom_call_target="tpu_custom_call" | custom-call | tf_op jit(solution)/shard_map/pallas_call | solution.py:103
  113.6 1.0 reshape.152
  115.3 1.7 collective-permute-done.12
  117.1 0.9 select_add_fusion
  118.7 2.0 collective-permute-start.13
  120.7 2.7 %collective-permute-done.13 = f32[18816]{0:T(1024)S(1)} collective-permute-done((f32[18816]{0:T(1024)S(1)}, f32[18816]{0:T(1024)S(1)}, u32[]{:S(2)}, u32[]{:S(2)}) %collective-permute-start.13) | collective-permute-done | bytes 75296 | tf_op jit(solution)/shard_map/ppermute | solution.py:57
  123.3 1.0 select_add_fusion.1
  124.4 2.7 %collective-permute-start.14 = (f32[9408]{0:T(1024)S(1)}, f32[9408]{0:T(1024)S(1)}, u32[]{:S(2)}, u32[]{:S(2)}) collective-permute-start(f32[9408]{0:T(1024)S(1)} %slice_select_fusion.2), channel_id=1, source_target_pairs={{0,4},{1,5},{2,6},{3,7},{4,0},{5,1},{6,2},{7,3},{8,12},{9,13},{10,... | collective-permute-start | bytes 112904 | tf_op jit(solution)/shard_map/ppermute | solution.py:57
  127.1 2.3 collective-permute-done.14
  129.5 3.2 %collective-permute-start.15 = (f32[4704]{0:T(1024)S(1)}, f32[4704]{0:T(1024)S(1)}, u32[]{:S(2)}, u32[]{:S(2)}) collective-permute-start(f32[4704]{0:T(1024)S(1)} %slice_select_fusion.3), channel_id=1, source_target_pairs={{0,8},{1,9},{2,10},{3,11},{4,12},{5,13},{6,14},{7,15},{8,0},{9,1},... | collective-permute-start | bytes 56456 | tf_op jit(solution)/shard_map/ppermute | solution.py:57
  132.7 4.5 %collective-permute-done.15 = f32[4704]{0:T(1024)S(1)} collective-permute-done((f32[4704]{0:T(1024)S(1)}, f32[4704]{0:T(1024)S(1)}, u32[]{:S(2)}, u32[]{:S(2)}) %collective-permute-start.15) | collective-permute-done | bytes 18848 | tf_op jit(solution)/shard_map/ppermute | solution.py:57
  137.4 1.0 collective-permute-start.16
  138.4 4.3 %collective-permute-done.16 = f32[2352]{0:T(1024)S(1)} collective-permute-done((f32[2352]{0:T(1024)S(1)}, f32[2352]{0:T(1024)S(1)}, u32[]{:S(2)}, u32[]{:S(2)}) %collective-permute-start.16) | collective-permute-done | bytes 9440 | tf_op jit(solution)/shard_map/ppermute | solution.py:57
  142.8 1.0 collective-permute-start.17
  143.7 2.7 %collective-permute-done.17 = f32[1176]{0:T(1024)S(1)} collective-permute-done((f32[1176]{0:T(1024)S(1)}, f32[1176]{0:T(1024)S(1)}, u32[]{:S(2)}, u32[]{:S(2)}) %collective-permute-start.17) | collective-permute-done | bytes 4736 | tf_op jit(solution)/shard_map/ppermute | solution.py:57
  146.6 0.8 collective-permute-start.18
  147.4 4.3 %collective-permute-done.18 = f32[588]{0:T(1024)S(1)} collective-permute-done((f32[588]{0:T(1024)S(1)}, f32[588]{0:T(1024)S(1)}, u32[]{:S(2)}, u32[]{:S(2)}) %collective-permute-start.18) | collective-permute-done | bytes 2384 | tf_op jit(solution)/shard_map/ppermute | solution.py:57
  151.9 1.3 collective-permute-start.19
  153.2 2.3 collective-permute-done.19
  155.6 1.3 collective-permute-start.20
  156.8 2.3 collective-permute-done.20
  159.2 1.0 collective-permute-start.21
  160.3 4.3 %collective-permute-done.21 = f32[588]{0:T(1024)S(1)} collective-permute-done((f32[588]{0:T(1024)S(1)}, f32[588]{0:T(1024)S(1)}, u32[]{:S(2)}, u32[]{:S(2)}) %collective-permute-start.21) | collective-permute-done | bytes 2384 | tf_op jit(solution)/shard_map/ppermute | solution.py:61
  164.7 1.0 collective-permute-start.22
  165.6 2.7 %collective-permute-done.22 = f32[1176]{0:T(1024)S(1)} collective-permute-done((f32[1176]{0:T(1024)S(1)}, f32[1176]{0:T(1024)S(1)}, u32[]{:S(2)}, u32[]{:S(2)}) %collective-permute-start.22) | collective-permute-done | bytes 4736 | tf_op jit(solution)/shard_map/ppermute | solution.py:61
  168.4 1.0 collective-permute-start.23
  169.4 4.3 %collective-permute-done.23 = f32[2352]{0:T(1024)S(1)} collective-permute-done((f32[2352]{0:T(1024)S(1)}, f32[2352]{0:T(1024)S(1)}, u32[]{:S(2)}, u32[]{:S(2)}) %collective-permute-start.23) | collective-permute-done | bytes 9440 | tf_op jit(solution)/shard_map/ppermute | solution.py:61
  173.7 3.2 %collective-permute-start.24 = (f32[4704]{0:T(1024)S(1)}, f32[4704]{0:T(1024)S(1)}, u32[]{:S(2)}, u32[]{:S(2)}) collective-permute-start(f32[4704]{0:T(1024)S(1)} %maximum_select_fusion.4), channel_id=1, source_target_pairs={{0,8},{1,9},{2,10},{3,11},{4,12},{5,13},{6,14},{7,15},{8,0},{9,1},... | collective-permute-start | bytes 56456 | tf_op jit(solution)/shard_map/ppermute | solution.py:61
  176.9 6.1 %rev.3.k_ref = f32[7,7,1536]{2,1,0:T(8,128)} reverse(bf16[7,7,1536]{2,1,0:T(8,128)(2,1)} %param.9), dimensions={0,1} | reverse | bytes 451584 | tf_op jit(solution)/shard_map/rev | solution.py:206
  183.1 1.5 collective-permute-start.25
  184.6 2.7 %subtract_multiply_fusion = f32[1,8,64,1536]{3,2,1,0:T(8,128)S(1)} fusion(f32[1,8,64,1536]{3,0,2,1:T(1,128)} %copy-done.1, f32[8,64]{1,0:T(8,128)S(1)} %broadcast_multiply_fusion, f32[1536]{0:T(1024)S(1)} %broadcast_subtract_fusion, f32[8,64]{1,0:T(8,128)S(1)} %add_rsqrt_fusion, f32[8,64]{1,0:T(8,128)S(1)} %broadcast_multiply_fusion.1, f32[1536]{0:T(1024)S(1)} %copy-done.8), kind=kLoop, calls=%fused_computation.9 | loop fusion | flops 4718592 | bytes 6309888 | tf_op jit(solution)/shard_map/mul | solution.py:203
  188.2 1.1 collective-permute-start.26
  189.3 1.6 fusion.27
  190.8 1.8 collective-permute-done.26
  194.4 2.4 %collective-permute-start.10 = (f32[1,3,64,1536]{3,2,1,0:T(8,128)}, f32[1,3,64,1536]{3,2,1,0:T(8,128)}, u32[]{:S(2)}, u32[]{:S(2)}) collective-permute-start(f32[1,3,64,1536]{3,2,1,0:T(8,128)} %get-tuple-element.15), channel_id=1, source_target_pairs={{0,1},{1,2},{2,3},{3,4},{4,5},{5,6},{6,7},{7,8},{8,9},{9,10},{10,1... | collective-permute-start | bytes 3538952 | tf_op jit(solution)/shard_map/ppermute | solution.py:13
  196.8 6.8 %collective-permute-start.11 = (f32[1,3,64,1536]{3,2,1,0:T(8,128)}, f32[1,3,64,1536]{3,2,1,0:T(8,128)}, u32[]{:S(2)}, u32[]{:S(2)}) collective-permute-start(f32[1,3,64,1536]{3,2,1,0:T(8,128)} %get-tuple-element.16), channel_id=1, source_target_pairs={{1,0},{2,1},{3,2},{4,3},{5,4},{6,5},{7,6},{8,7},{9,8},{10,9},{11,1... | collective-permute-start | bytes 3538952 | tf_op jit(solution)/shard_map/ppermute | solution.py:16
  203.6 1.9 fusion.9
  206.8 1.2 fusion.5
  208.8 7.1 %collective-permute-done.10 = f32[1,3,64,1536]{3,2,1,0:T(8,128)} collective-permute-done((f32[1,3,64,1536]{3,2,1,0:T(8,128)}, f32[1,3,64,1536]{3,2,1,0:T(8,128)}, u32[]{:S(2)}, u32[]{:S(2)}) %collective-permute-start.10) | collective-permute-done | bytes 1179680 | tf_op jit(solution)/shard_map/ppermute | solution.py:13
  215.9 1.8 collective-permute-done.11
  217.6 4.7 %fusion.x_ref = f32[14,70,1536]{2,1,0:T(8,128)} fusion(f32[1,3,64,1536]{3,2,1,0:T(8,128)} %collective-permute-done.11, f32[1,8,64,1536]{3,2,1,0:T(8,128)} %copy-done.3, f32[1,3,64,1536]{3,2,1,0:T(8,128)} %collective-permute-done.10), kind=kLoop, calls=%fused_computation.3 | loop fusion | flops 12042240 | bytes 11526144 | tf_op jit(solution)/shard_map/squeeze | solution.py:208
  222.3 13.5 %shard_map.111 = bf16[8,64,1536]{2,1,0:T(8,128)(2,1)} custom-call(f32[14,70,1536]{2,1,0:T(8,128)} %fusion.x_ref, f32[7,7,1536]{2,1,0:T(8,128)} %rev.3.k_ref), custom_call_target="tpu_custom_call" | custom-call | tf_op jit(solution)/shard_map/pallas_call | solution.py:127
  (99 shorter events, 13.9 us)
Async XLA Ops:
  0.6 83.8 %copy-start = (bf16[1536,1024]{1,0:T(8,128)(2,1)S(1)}, bf16[1536,1024]{1,0:T(8,128)(2,1)}, u32[]{:S(2)}) copy-start(bf16[1536,1024]{1,0:T(8,128)(2,1)} %param.13) | copy-start | bytes 9437188
  0.6 17.1 %copy-start.4 = (bf16[1,8,64,1536]{3,2,1,0:T(8,128)(2,1)S(1)}, bf16[1,8,64,1536]{3,2,1,0:T(8,128)(2,1)}, u32[]{:S(2)}) copy-start(bf16[1,8,64,1536]{3,2,1,0:T(8,128)(2,1)} %param.8) | copy-start | bytes 4718596
  2.1 17.4 %copy-start.9 = (bf16[7,7,1536]{2,1,0:T(8,128)(2,1)S(1)}, bf16[7,7,1536]{2,1,0:T(8,128)(2,1)}, u32[]{:S(2)}) copy-start(bf16[7,7,1536]{2,1,0:T(8,128)(2,1)} %param.9) | copy-start | bytes 451588
  2.1 15.6 %collective-permute-start = (bf16[1,3,64,1536]{3,2,1,0:T(8,128)(2,1)S(1)}, bf16[1,3,64,1536]{3,2,1,0:T(8,128)(2,1)S(1)}, u32[]{:S(2)}, u32[]{:S(2)}) collective-permute-start(bf16[1,3,64,1536]{3,2,1,0:T(8,128)(2,1)S(1)} %get-tuple-element.18), channel_id=1, source_target_pairs={{0,1},{1,2},{2,3},{3,4},{4,5},{5,6},{6,7},{7,8},{8,9},{9,10},{10,1... | collective-permute-start | bytes 1769480 | tf_op jit(solution)/shard_map/ppermute | solution.py:13
  4.2 15.3 %collective-permute-start.1 = (bf16[1,3,64,1536]{3,2,1,0:T(8,128)(2,1)S(1)}, bf16[1,3,64,1536]{3,2,1,0:T(8,128)(2,1)S(1)}, u32[]{:S(2)}, u32[]{:S(2)}) collective-permute-start(bf16[1,3,64,1536]{3,2,1,0:T(8,128)(2,1)S(1)} %get-tuple-element.17), channel_id=1, source_target_pairs={{1,0},{2,1},{3,2},{4,3},{5,4},{6,5},{7,6},{8,7},{9,8},{10,9},{11,1... | collective-permute-start | bytes 1769480 | tf_op jit(solution)/shard_map/ppermute | solution.py:16
  19.5 21.5 %copy-start.5 = (bf16[1,14,64,1536]{3,2,1,0:T(8,128)(2,1)}, bf16[1,14,64,1536]{3,2,1,0:T(8,128)(2,1)S(1)}, u32[]{:S(2)}) copy-start(bf16[1,14,64,1536]{3,2,1,0:T(8,128)(2,1)S(1)} %constant_dynamic-update-slice_fusion) | copy-start | bytes 8257540
  19.5 21.5 %copy-start.8 = (f32[1536]{0:T(1024)S(1)}, f32[1536]{0:T(1024)}, u32[]{:S(2)}) copy-start(f32[1536]{0:T(1024)} %param.10) | copy-start | bytes 18436
  41.0 1.7 copy-start.1
  41.1 1.7 copy-start.10
  41.1 1.7 copy-start.12
  41.4 24.9 %copy-start.11 = (f32[1,1024]{1,0:T(1,128)S(1)}, f32[1,1024]{1,0:T(1,128)}, u32[]{:S(2)}) copy-start(f32[1,1024]{1,0:T(1,128)} %param.14) | copy-start | bytes 12292
  43.4 1.3 collective-permute-start.2
  44.7 3.7 %collective-permute-start.3 = (f32[1,1536]{1,0:T(1,128)S(1)}, f32[1,1536]{1,0:T(1,128)S(1)}, u32[]{:S(2)}, u32[]{:S(2)}) collective-permute-start(f32[1,1536]{1,0:T(1,128)S(1)} %reshape_add_fusion), channel_id=1, source_target_pairs={{0,2},{1,3},{2,0},{3,1},{4,6},{5,7},{6,4},{7,5},{8,10},{9,11},{10,... | collective-permute-start | bytes 18440 | tf_op jit(solution)/shard_map/ppermute | solution.py:30
  48.4 4.9 %collective-permute-start.4 = (f32[1,1536]{1,0:T(1,128)S(1)}, f32[1,1536]{1,0:T(1,128)S(1)}, u32[]{:S(2)}, u32[]{:S(2)}) collective-permute-start(f32[1,1536]{1,0:T(1,128)S(1)} %add.153), channel_id=1, source_target_pairs={{0,4},{1,5},{2,6},{3,7},{4,0},{5,1},{6,2},{7,3},{8,12},{9,13},{10,... | collective-permute-start | bytes 18440 | tf_op jit(solution)/shard_map/ppermute | solution.py:30
  53.4 7.6 %collective-permute-start.5 = (f32[1,1536]{1,0:T(1,128)S(1)}, f32[1,1536]{1,0:T(1,128)S(1)}, u32[]{:S(2)}, u32[]{:S(2)}) collective-permute-start(f32[1,1536]{1,0:T(1,128)S(1)} %add.154), channel_id=1, source_target_pairs={{0,8},{1,9},{2,10},{3,11},{4,12},{5,13},{6,14},{7,15},{8,0},{9,1},... | collective-permute-start | bytes 18440 | tf_op jit(solution)/shard_map/ppermute | solution.py:30
  61.0 5.2 %collective-permute-start.6 = (f32[1,1536]{1,0:T(1,128)S(1)}, f32[1,1536]{1,0:T(1,128)S(1)}, u32[]{:S(2)}, u32[]{:S(2)}) collective-permute-start(f32[1,1536]{1,0:T(1,128)S(1)} %add.155), channel_id=1, source_target_pairs={{0,16},{1,17},{2,18},{3,19},{4,20},{5,21},{6,22},{7,23},{8,24},{9,... | collective-permute-start | bytes 18440 | tf_op jit(solution)/shard_map/ppermute | solution.py:30
  66.5 5.1 %collective-permute-start.7 = (f32[8,2560]{1,0:T(8,128)S(1)}, f32[8,2560]{1,0:T(8,128)S(1)}, u32[]{:S(2)}, u32[]{:S(2)}) collective-permute-start(f32[8,2560]{1,0:T(8,128)S(1)} %dynamic_update_slice.5), channel_id=1, source_target_pairs={{0,32},{32,0},{64,96},{96,64},{128,160},{160,128},{192,224},{224,1... | collective-permute-start | bytes 245768 | tf_op jit(solution)/shard_map/ppermute | solution.py:30
  71.9 6.0 %collective-permute-start.8 = (f32[8,2560]{1,0:T(8,128)S(1)}, f32[8,2560]{1,0:T(8,128)S(1)}, u32[]{:S(2)}, u32[]{:S(2)}) collective-permute-start(f32[8,2560]{1,0:T(8,128)S(1)} %add.158), channel_id=1, source_target_pairs={{0,64},{32,96},{64,0},{96,32},{128,192},{160,224},{192,128},{224,1... | collective-permute-start | bytes 245768 | tf_op jit(solution)/shard_map/ppermute | solution.py:30
  78.0 6.3 %collective-permute-start.9 = (f32[8,2560]{1,0:T(8,128)S(1)}, f32[8,2560]{1,0:T(8,128)S(1)}, u32[]{:S(2)}, u32[]{:S(2)}) collective-permute-start(f32[8,2560]{1,0:T(8,128)S(1)} %add.159), channel_id=1, source_target_pairs={{0,128},{32,160},{64,192},{96,224},{128,0},{160,32},{192,64},{224,... | collective-permute-start | bytes 245768 | tf_op jit(solution)/shard_map/ppermute | solution.py:30
  84.4 8.8 %copy-start.2 = (f32[1,8,64,1536]{3,0,2,1:T(1,128)S(1)}, f32[1,8,64,1536]{3,0,2,1:T(1,128)}, u32[]{:S(2)}) copy-start(f32[1,8,64,1536]{3,0,2,1:T(1,128)} %copy-done.1) | copy-start | bytes 9437188
  85.9 0.7 copy-start.13
  115.3 1.7 collective-permute-start.12
  118.0 0.7 copy-start.6
  118.7 4.6 %collective-permute-start.13 = (f32[18816]{0:T(1024)S(1)}, f32[18816]{0:T(1024)S(1)}, u32[]{:S(2)}, u32[]{:S(2)}) collective-permute-start(f32[18816]{0:T(1024)S(1)} %slice_select_fusion.1), channel_id=1, source_target_pairs={{0,2},{1,3},{2,0},{3,1},{4,6},{5,7},{6,4},{7,5},{8,10},{9,11},{10,... | collective-permute-start | bytes 225800 | tf_op jit(solution)/shard_map/ppermute | solution.py:57
  124.4 5.0 %collective-permute-start.14 = (f32[9408]{0:T(1024)S(1)}, f32[9408]{0:T(1024)S(1)}, u32[]{:S(2)}, u32[]{:S(2)}) collective-permute-start(f32[9408]{0:T(1024)S(1)} %slice_select_fusion.2), channel_id=1, source_target_pairs={{0,4},{1,5},{2,6},{3,7},{4,0},{5,1},{6,2},{7,3},{8,12},{9,13},{10,... | collective-permute-start | bytes 112904 | tf_op jit(solution)/shard_map/ppermute | solution.py:57
  129.5 7.7 %collective-permute-start.15 = (f32[4704]{0:T(1024)S(1)}, f32[4704]{0:T(1024)S(1)}, u32[]{:S(2)}, u32[]{:S(2)}) collective-permute-start(f32[4704]{0:T(1024)S(1)} %slice_select_fusion.3), channel_id=1, source_target_pairs={{0,8},{1,9},{2,10},{3,11},{4,12},{5,13},{6,14},{7,15},{8,0},{9,1},... | collective-permute-start | bytes 56456 | tf_op jit(solution)/shard_map/ppermute | solution.py:57
  137.4 5.2 %collective-permute-start.16 = (f32[2352]{0:T(1024)S(1)}, f32[2352]{0:T(1024)S(1)}, u32[]{:S(2)}, u32[]{:S(2)}) collective-permute-start(f32[2352]{0:T(1024)S(1)} %slice_select_fusion.4), channel_id=1, source_target_pairs={{0,16},{1,17},{2,18},{3,19},{4,20},{5,21},{6,22},{7,23},{8,24},{9,... | collective-permute-start | bytes 28232 | tf_op jit(solution)/shard_map/ppermute | solution.py:57
  142.8 3.7 %collective-permute-start.17 = (f32[1176]{0:T(1024)S(1)}, f32[1176]{0:T(1024)S(1)}, u32[]{:S(2)}, u32[]{:S(2)}) collective-permute-start(f32[1176]{0:T(1024)S(1)} %slice_select_fusion.5), channel_id=1, source_target_pairs={{0,32},{32,0},{64,96},{96,64},{128,160},{160,128},{192,224},{224,1... | collective-permute-start | bytes 14120 | tf_op jit(solution)/shard_map/ppermute | solution.py:57
  146.6 5.1 %collective-permute-start.18 = (f32[588]{0:T(1024)S(1)}, f32[588]{0:T(1024)S(1)}, u32[]{:S(2)}, u32[]{:S(2)}) collective-permute-start(f32[588]{0:T(1024)S(1)} %slice_select_fusion.6), channel_id=1, source_target_pairs={{0,64},{32,96},{64,0},{96,32},{128,192},{160,224},{192,128},{224,1... | collective-permute-start | bytes 7064 | tf_op jit(solution)/shard_map/ppermute | solution.py:57
  151.9 3.6 %collective-permute-start.19 = (f32[294]{0:T(512)S(1)}, f32[294]{0:T(512)S(1)}, u32[]{:S(2)}, u32[]{:S(2)}) collective-permute-start(f32[294]{0:T(512)S(1)} %slice_select_fusion.7), channel_id=1, source_target_pairs={{0,128},{32,160},{64,192},{96,224},{128,0},{160,32},{192,64},{224,... | collective-permute-start | bytes 3536 | tf_op jit(solution)/shard_map/ppermute | solution.py:57
  155.6 3.6 %collective-permute-start.20 = (f32[294]{0:T(512)S(1)}, f32[294]{0:T(512)S(1)}, u32[]{:S(2)}, u32[]{:S(2)}) collective-permute-start(f32[294]{0:T(512)S(1)} %select_add_fusion.7), channel_id=1, source_target_pairs={{0,128},{32,160},{64,192},{96,224},{128,0},{160,32},{192,64},{224,... | collective-permute-start | bytes 3536 | tf_op jit(solution)/shard_map/ppermute | solution.py:61
  159.2 5.4 %collective-permute-start.21 = (f32[588]{0:T(1024)S(1)}, f32[588]{0:T(1024)S(1)}, u32[]{:S(2)}, u32[]{:S(2)}) collective-permute-start(f32[588]{0:T(1024)S(1)} %maximum_select_fusion.7), channel_id=1, source_target_pairs={{0,64},{32,96},{64,0},{96,32},{128,192},{160,224},{192,128},{224,1... | collective-permute-start | bytes 7064 | tf_op jit(solution)/shard_map/ppermute | solution.py:61
  164.7 3.7 %collective-permute-start.22 = (f32[1176]{0:T(1024)S(1)}, f32[1176]{0:T(1024)S(1)}, u32[]{:S(2)}, u32[]{:S(2)}) collective-permute-start(f32[1176]{0:T(1024)S(1)} %maximum_select_fusion.6), channel_id=1, source_target_pairs={{0,32},{32,0},{64,96},{96,64},{128,160},{160,128},{192,224},{224,1... | collective-permute-start | bytes 14120 | tf_op jit(solution)/shard_map/ppermute | solution.py:61
  168.4 5.2 %collective-permute-start.23 = (f32[2352]{0:T(1024)S(1)}, f32[2352]{0:T(1024)S(1)}, u32[]{:S(2)}, u32[]{:S(2)}) collective-permute-start(f32[2352]{0:T(1024)S(1)} %maximum_select_fusion.5), channel_id=1, source_target_pairs={{0,16},{1,17},{2,18},{3,19},{4,20},{5,21},{6,22},{7,23},{8,24},{9,... | collective-permute-start | bytes 28232 | tf_op jit(solution)/shard_map/ppermute | solution.py:61
  173.7 9.3 %collective-permute-start.24 = (f32[4704]{0:T(1024)S(1)}, f32[4704]{0:T(1024)S(1)}, u32[]{:S(2)}, u32[]{:S(2)}) collective-permute-start(f32[4704]{0:T(1024)S(1)} %maximum_select_fusion.4), channel_id=1, source_target_pairs={{0,8},{1,9},{2,10},{3,11},{4,12},{5,13},{6,14},{7,15},{8,0},{9,1},... | collective-permute-start | bytes 56456 | tf_op jit(solution)/shard_map/ppermute | solution.py:61
  183.1 5.0 %collective-permute-start.25 = (f32[9408]{0:T(1024)S(1)}, f32[9408]{0:T(1024)S(1)}, u32[]{:S(2)}, u32[]{:S(2)}) collective-permute-start(f32[9408]{0:T(1024)S(1)} %maximum_select_fusion.3), channel_id=1, source_target_pairs={{0,4},{1,5},{2,6},{3,7},{4,0},{5,1},{6,2},{7,3},{8,12},{9,13},{10,... | collective-permute-start | bytes 112904 | tf_op jit(solution)/shard_map/ppermute | solution.py:61
  187.3 2.0 copy-start.3
  187.3 5.9 %copy-start.14 = (f32[8]{0:T(128)S(1)}, f32[8]{0:T(128)}, u32[]{:S(2)}) copy-start(f32[8]{0:T(128)} %copy-done.13) | copy-start | bytes 100
  188.2 4.5 %collective-permute-start.26 = (f32[18816]{0:T(1024)S(1)}, f32[18816]{0:T(1024)S(1)}, u32[]{:S(2)}, u32[]{:S(2)}) collective-permute-start(f32[18816]{0:T(1024)S(1)} %maximum_select_fusion.2), channel_id=1, source_target_pairs={{0,2},{1,3},{2,0},{3,1},{4,6},{5,7},{6,4},{7,5},{8,10},{9,11},{10,... | collective-permute-start | bytes 225800 | tf_op jit(solution)/shard_map/ppermute | solution.py:61
  192.7 14.1 %copy-start.7 = (f32[37632]{0:T(1024)}, f32[37632]{0:T(1024)S(1)}, u32[]{:S(2)}) copy-start(f32[37632]{0:T(1024)S(1)} %maximum_select_fusion.1) | copy-start | bytes 451588
  192.7 14.1 %collective-permute-start.27 = (f32[37632]{0:T(1024)S(1)}, f32[37632]{0:T(1024)}, u32[]{:S(2)}, u32[]{:S(2)}) collective-permute-start(f32[37632]{0:T(1024)S(1)} %maximum_select_fusion.1), channel_id=1, source_target_pairs={{0,1},{1,0},{2,3},{3,2},{4,5},{5,4},{6,7},{7,6},{8,9},{9,8},{10,11... | collective-permute-start | bytes 451592 | tf_op jit(solution)/shard_map/ppermute | solution.py:61
  194.4 21.4 %collective-permute-start.10 = (f32[1,3,64,1536]{3,2,1,0:T(8,128)}, f32[1,3,64,1536]{3,2,1,0:T(8,128)}, u32[]{:S(2)}, u32[]{:S(2)}) collective-permute-start(f32[1,3,64,1536]{3,2,1,0:T(8,128)} %get-tuple-element.15), channel_id=1, source_target_pairs={{0,1},{1,2},{2,3},{3,4},{4,5},{5,6},{6,7},{7,8},{8,9},{9,10},{10,1... | collective-permute-start | bytes 3538952 | tf_op jit(solution)/shard_map/ppermute | solution.py:13
  196.8 20.8 %collective-permute-start.11 = (f32[1,3,64,1536]{3,2,1,0:T(8,128)}, f32[1,3,64,1536]{3,2,1,0:T(8,128)}, u32[]{:S(2)}, u32[]{:S(2)}) collective-permute-start(f32[1,3,64,1536]{3,2,1,0:T(8,128)} %get-tuple-element.16), channel_id=1, source_target_pairs={{1,0},{2,1},{3,2},{4,3},{5,4},{6,5},{7,6},{8,7},{9,8},{10,9},{11,1... | collective-permute-start | bytes 3538952 | tf_op jit(solution)/shard_map/ppermute | solution.py:16

commit v4 on v3

--- a/solution.py
+++ b/solution.py
@@ -32,7 +32,7 @@
     return values
 
 
-def halving_sum(values, axes):
+def halving_sum(values, axes, split_steps):
     steps = []
     for axis in axes:
         count = lax.axis_size(axis)
@@ -42,12 +42,13 @@
         while step < count:
             steps.append((axis, count, step))
             step *= 2
-    parts = 1 << len(steps)
+    split_steps = min(split_steps, len(steps))
+    parts = 1 << split_steps
     flat = values.reshape(-1)
     size = flat.shape[0]
     padded_size = -(-size // parts) * parts
     chunk = jnp.pad(flat, (0, padded_size - size))
-    for axis, count, step in steps:
+    for axis, count, step in steps[:split_steps]:
         pairs = [(i, i ^ step) for i in range(count)]
         upper = (lax.axis_index(axis) // step) % 2 == 1
         half = chunk.shape[0] // 2
@@ -55,7 +56,10 @@
         keep = jnp.where(upper, high, low)
         give = jnp.where(upper, low, high)
         chunk = keep + lax.ppermute(give, axis, pairs)
-    for axis, count, step in reversed(steps):
+    for axis, count, step in steps[split_steps:]:
+        pairs = [(i, i ^ step) for i in range(count)]
+        chunk = chunk + lax.ppermute(chunk, axis, pairs)
+    for axis, count, step in reversed(steps[:split_steps]):
         pairs = [(i, i ^ step) for i in range(count)]
         upper = (lax.axis_index(axis) // step) % 2 == 1
         other = lax.ppermute(chunk, axis, pairs)
@@ -210,7 +214,8 @@
     kernel_part = kernel_terms(grad_own[0], padded_all[0], reach_rows)
     for image in range(1, batch_dev):
         kernel_part = kernel_part + kernel_terms(grad_own[image], padded_all[image], reach_rows)
-    kernel_grad = halving_sum(kernel_part, ("space", "dp")) / pixel_count
+    kernel_part, input_grad = lax.optimization_barrier((kernel_part, input_grad))
+    kernel_grad = halving_sum(kernel_part, ("space", "dp"), 3) / pixel_count
     return (loss, input_grad.astype(jnp.bfloat16), kernel_grad, text_grad)
 
 

time: 241 us -> 213 us (0.88)
  waiting for transfers between devices: 80 us -> 67 us
  starting transfers between devices: 52.3 us -> 41.5 us
  other arithmetic: 28.1 us -> 25.2 us
    ppermute x0 -> x5, waiting for transfers between devices: none -> 21.2 us  [halving_sum(): chunk = chunk + lax.ppermute(chunk, axis, pairs)]
    ppermute x8 -> x3, waiting for transfers between devices: 24.8 us -> 6.78 us  [halving_sum(): chunk = keep + lax.ppermute(give, axis, pairs)]
    ppermute x8 -> x3, waiting for transfers between devices: 16.2 us -> 5.07 us  [halving_sum(): other = lax.ppermute(chunk, axis, pairs)]
    ppermute x2, waiting for transfers between devices: 12.7 us -> 5.63 us  [with_halo(): lax.ppermute(lax.slice_in_dim(block, block.shape[dim] - width, None, axis...]
    ppermute x8 -> x3, starting transfers between devices: 11.9 us -> 5.78 us  [halving_sum(): chunk = keep + lax.ppermute(give, axis, pairs)]
    ppermute x0 -> x5, starting transfers between devices: none -> 5.82 us  [halving_sum(): chunk = chunk + lax.ppermute(chunk, axis, pairs)]
    ppermute x8 -> x3, starting transfers between devices: 10.1 us -> 4.41 us  [halving_sum(): other = lax.ppermute(chunk, axis, pairs)]
    ppermute x2, starting transfers between devices: 14.7 us -> 9.79 us  [with_halo(): lax.ppermute(lax.slice_in_dim(block, 0, width, axis=dim), axis, backward)]
  transfers between devices with their start and end apart: 28 -> 23, of which waited for: 25 -> 20; matrix products, arithmetic and copies ran while one was open for 9% -> 7% of each run, Pallas kernels for 0% -> 7%
where the time goes in v4:
time: 213 us; the launch traced here: 209 us
  waiting for transfers between devices  67 us (31%)
  starting transfers between devices  41.5 us (19%)
  Pallas kernels  28.2 us (13%)
  matrix products  27.8 us (13%)
  other arithmetic  25.2 us (12%)
  local copies, waits for them, and re-layouts  15 us (7%)
  between operations  4.8 us (2%)
    ppermute x8, waiting for transfers between devices, butterfly_sum(): values = values + lax.ppermute(values, axis, pairs)  26.7 us
    conv_general_dilated x1, matrix products, depthwise(): lax.conv_general_dilated(extended, kernel.reshape(kernel.shape[0], kernel...  21.5 us
    ppermute x5, waiting for transfers between devices, halving_sum(): chunk = chunk + lax.ppermute(chunk, axis, pairs)  21.2 us
    pallas_call x1, Pallas kernels, kernel_terms(): pl.pallas_call(body, grid=(channels // lanes,), in_specs=[pl.BlockSpec((r...  14.7 us
    pallas_call x1, Pallas kernels, input_terms(): pl.pallas_call(body, grid=(channels // lanes,), in_specs=[pl.BlockSpec(pa...  13.5 us
    ppermute x8, starting transfers between devices, butterfly_sum(): values = values + lax.ppermute(values, axis, pairs)  11.2 us
    ppermute x2, starting transfers between devices, with_halo(): lax.ppermute(lax.slice_in_dim(block, 0, width, axis=dim), axis, backward)  9.79 us
    squeeze x2, other arithmetic, shards(): kernel_part = kernel_terms(grad_own[0], padded_all[0], reach_rows)  7.87 us
  transfers between devices with their start and end apart: 23, of which 20 were waited for; matrix products, arithmetic and copies ran while one was open for 7% of the time, Pallas kernels for 7%

profile of v4, /device:TPU:28, one launch (start us, length us, event | category | flops | bytes accessed | tf_op | source)
XLA Modules:
  0.0 209.5 jit_solution(15935355750973436119)
XLA Ops:
  0.7 1.5 fusion.28
  2.1 2.1 collective-permute-start
  4.2 7.9 %collective-permute-start.1 = (bf16[1,3,64,1536]{3,2,1,0:T(8,128)(2,1)S(1)}, bf16[1,3,64,1536]{3,2,1,0:T(8,128)(2,1)S(1)}, u32[]{:S(2)}, u32[]{:S(2)}) collective-permute-start(bf16[1,3,64,1536]{3,2,1,0:T(8,128)(2,1)S(1)} %get-tuple-element.21), channel_id=1, source_target_pairs={{1,0},{2,1},{3,2},{4,3},{5,4},{6,5},{7,6},{8,7},{9,8},{10,9},{11,1... | collective-permute-start | bytes 1769480 | tf_op jit(solution)/shard_map/ppermute | solution.py:16
  12.1 5.6 %collective-permute-done = bf16[1,3,64,1536]{3,2,1,0:T(8,128)(2,1)S(1)} collective-permute-done((bf16[1,3,64,1536]{3,2,1,0:T(8,128)(2,1)S(1)}, bf16[1,3,64,1536]{3,2,1,0:T(8,128)(2,1)S(1)}, u32[]{:S(2)}, u32[]{:S(2)}) %collective-permute-start) | collective-permute-done | bytes 589856 | tf_op jit(solution)/shard_map/ppermute | solution.py:13
  17.9 1.6 collective-permute-done.1
  19.6 21.5 %fusion.2 = f32[1,8,64,1536]{3,0,2,1:T(1,128)S(1)} fusion(bf16[1,14,64,1536]{3,2,1,0:T(8,128)(2,1)S(1)} %constant_dynamic-update-slice_fusion, bf16[7,7,1,1536]{3,1,0,2:T(8,128)(2,1)S(1)} %bitcast.24), kind=kOutput, calls=%fused_computation.6 | convolution fusion | flops 75005952 | bytes 6048768 | tf_op jit(solution)/shard_map/conv_general_dilated | solution.py:82
  41.9 0.8 copy-done.1
  42.7 0.7 add_reduce_fusion
  43.5 1.2 collective-permute-done.2
  44.8 3.6 %collective-permute-done.3 = f32[1,1536]{1,0:T(1,128)S(1)} collective-permute-done((f32[1,1536]{1,0:T(1,128)S(1)}, f32[1,1536]{1,0:T(1,128)S(1)}, u32[]{:S(2)}, u32[]{:S(2)}) %collective-permute-start.3) | collective-permute-done | bytes 6176 | tf_op jit(solution)/shard_map/ppermute | solution.py:30
  48.4 3.3 %collective-permute-start.4 = (f32[1,1536]{1,0:T(1,128)S(1)}, f32[1,1536]{1,0:T(1,128)S(1)}, u32[]{:S(2)}, u32[]{:S(2)}) collective-permute-start(f32[1,1536]{1,0:T(1,128)S(1)} %add.128), channel_id=1, source_target_pairs={{0,4},{1,5},{2,6},{3,7},{4,0},{5,1},{6,2},{7,3},{8,12},{9,13},{10,... | collective-permute-start | bytes 18440 | tf_op jit(solution)/shard_map/ppermute | solution.py:30
  51.7 1.6 collective-permute-done.4
  53.3 3.9 %collective-permute-start.5 = (f32[1,1536]{1,0:T(1,128)S(1)}, f32[1,1536]{1,0:T(1,128)S(1)}, u32[]{:S(2)}, u32[]{:S(2)}) collective-permute-start(f32[1,1536]{1,0:T(1,128)S(1)} %add.129), channel_id=1, source_target_pairs={{0,8},{1,9},{2,10},{3,11},{4,12},{5,13},{6,14},{7,15},{8,0},{9,1},... | collective-permute-start | bytes 18440 | tf_op jit(solution)/shard_map/ppermute | solution.py:30
  57.3 3.7 %collective-permute-done.5 = f32[1,1536]{1,0:T(1,128)S(1)} collective-permute-done((f32[1,1536]{1,0:T(1,128)S(1)}, f32[1,1536]{1,0:T(1,128)S(1)}, u32[]{:S(2)}, u32[]{:S(2)}) %collective-permute-start.5) | collective-permute-done | bytes 6176 | tf_op jit(solution)/shard_map/ppermute | solution.py:30
  61.0 1.3 collective-permute-start.6
  62.3 3.9 %collective-permute-done.6 = f32[1,1536]{1,0:T(1,128)S(1)} collective-permute-done((f32[1,1536]{1,0:T(1,128)S(1)}, f32[1,1536]{1,0:T(1,128)S(1)}, u32[]{:S(2)}, u32[]{:S(2)}) %collective-permute-start.6) | collective-permute-done | bytes 6176 | tf_op jit(solution)/shard_map/ppermute | solution.py:30
  66.5 1.3 collective-permute-start.7
  67.8 3.8 %collective-permute-done.7 = f32[8,2560]{1,0:T(8,128)S(1)} collective-permute-done((f32[8,2560]{1,0:T(8,128)S(1)}, f32[8,2560]{1,0:T(8,128)S(1)}, u32[]{:S(2)}, u32[]{:S(2)}) %collective-permute-start.7) | collective-permute-done | bytes 81952 | tf_op jit(solution)/shard_map/ppermute | solution.py:30
  72.1 5.8 %collective-permute-done.8 = f32[8,2560]{1,0:T(8,128)S(1)} collective-permute-done((f32[8,2560]{1,0:T(8,128)S(1)}, f32[8,2560]{1,0:T(8,128)S(1)}, u32[]{:S(2)}, u32[]{:S(2)}) %collective-permute-start.8) | collective-permute-done | bytes 81952 | tf_op jit(solution)/shard_map/ppermute | solution.py:30
  77.9 1.0 collective-permute-start.9
  79.6 3.0 %collective-permute-done.9 = f32[8,2560]{1,0:T(8,128)S(1)} collective-permute-done((f32[8,2560]{1,0:T(8,128)S(1)}, f32[8,2560]{1,0:T(8,128)S(1)}, u32[]{:S(2)}, u32[]{:S(2)}) %collective-permute-start.9) | collective-permute-done | bytes 81952 | tf_op jit(solution)/shard_map/ppermute | solution.py:30
  82.8 1.4 multiply_reduce_fusion.5
  85.4 0.7 subtract_reduce_fusion
  87.1 3.8 %convolution_reduce_fusion = f32[1536]{0:T(1024)S(1)} fusion(bf16[1536,1024]{1,0:T(8,128)(2,1)S(1)} %copy-done, f32[8,1024]{1,0:T(8,128)S(1)} %get-tuple-element.27, s32[]{:T(128)S(6)} %select_n.95, f32[8,1024]{1,0:T(8,128)S(1)} %get-tuple-element.31, f32[1]{0:T(128)} %dynamic-slice.2, f32[1]{0:T(128)} %dynamic-slice.1), kind=kOutput, calls=%fused_computation.18 | convolution fusion | flops 18877440 | bytes 3160076 | tf_op jit(solution)/shard_map/dot_general | solution.py:203
  91.6 0.7 multiply_reduce_fusion
  92.9 2.7 %subtract_multiply_fusion = f32[1,8,64,1536]{3,2,1,0:T(8,128)S(1)} fusion(f32[1,8,64,1536]{3,0,2,1:T(1,128)} %copy-done.1, f32[8,64]{1,0:T(8,128)S(1)} %broadcast_multiply_fusion, f32[1536]{0:T(1024)S(1)} %broadcast_subtract_fusion, f32[8,64]{1,0:T(8,128)S(1)} %add_rsqrt_fusion, f32[8,64]{1,0:T(8,128)S(1)} %broadcast_multiply_fusion.1, f32[1536]{0:T(1024)S(1)} %copy-done.9), kind=kLoop, calls=%fused_computation.9 | loop fusion | flops 4718592 | bytes 6309888 | tf_op jit(solution)/shard_map/mul | solution.py:207
  95.6 1.7 copy-done.4
  97.3 1.6 fusion.27
  98.9 1.9 collective-permute-start.11
  100.8 2.4 %collective-permute-start.10 = (f32[1,3,64,1536]{3,2,1,0:T(8,128)}, f32[1,3,64,1536]{3,2,1,0:T(8,128)}, u32[]{:S(2)}, u32[]{:S(2)}) collective-permute-start(f32[1,3,64,1536]{3,2,1,0:T(8,128)} %get-tuple-element.19), channel_id=1, source_target_pairs={{0,1},{1,2},{2,3},{3,4},{4,5},{5,6},{6,7},{7,8},{8,9},{9,10},{10,1... | collective-permute-start | bytes 3538952 | tf_op jit(solution)/shard_map/ppermute | solution.py:13
  103.2 3.8 %rev.3.k_ref = f32[7,7,1536]{2,1,0:T(8,128)} reverse(bf16[7,7,1536]{2,1,0:T(8,128)(2,1)S(1)} %copy-done.10), dimensions={0,1} | reverse | bytes 451584 | tf_op jit(solution)/shard_map/rev | solution.py:210
  107.1 5.4 %bitcast_convert_fusion.x_ref = f32[14,70,1536]{2,1,0:T(8,128)} fusion(bf16[1,14,64,1536]{3,2,1,0:T(8,128)(2,1)} %copy-done.6), kind=kLoop, calls=%fused_computation.13 | loop fusion | flops 1505280 | bytes 8773632 | tf_op jit(solution)/shard_map/squeeze | solution.py:214
  112.5 2.5 %fusion.35.g_ref = f32[8,64,1536]{2,1,0:T(8,128)} fusion(f32[8,64]{1,0:T(8,128)S(1)} %broadcast_multiply_fusion, f32[8,64]{1,0:T(8,128)S(1)} %broadcast_multiply_fusion.1, f32[1536]{0:T(1024)S(1)} %copy-done.9, f32[1,8,64,1536]{3,0,2,1:T(1,128)S(1)} %copy-done.3, f32[1536]{0:T(1024)S(1)} %broadcast_subtract_fusion, f32[8,64]{1,0:T(8,128)S(1)} %add_rsqrt_fusion), kind=kLoop, calls=%fused_computation.81 | loop fusion | flops 4718592 | bytes 6309888 | tf_op jit(solution)/shard_map/squeeze | solution.py:214
  114.9 14.7 %shard_map.111 = f32[7,7,1536]{2,1,0:T(8,128)} custom-call(f32[8,64,1536]{2,1,0:T(8,128)} %fusion.35.g_ref, f32[14,70,1536]{2,1,0:T(8,128)} %bitcast_convert_fusion.x_ref), custom_call_target="tpu_custom_call" | custom-call | tf_op jit(solution)/shard_map/pallas_call | solution.py:107
  129.6 4.7 %fusion.x_ref = f32[14,70,1536]{2,1,0:T(8,128)} fusion(f32[1,3,64,1536]{3,2,1,0:T(8,128)} %collective-permute-done.11, f32[1,8,64,1536]{3,2,1,0:T(8,128)} %copy-done.4, f32[1,3,64,1536]{3,2,1,0:T(8,128)} %collective-permute-done.10), kind=kLoop, calls=%fused_computation.3 | loop fusion | flops 12042240 | bytes 11526144 | tf_op jit(solution)/shard_map/squeeze | solution.py:212
  134.3 13.5 %shard_map.112 = bf16[8,64,1536]{2,1,0:T(8,128)(2,1)} custom-call(f32[14,70,1536]{2,1,0:T(8,128)} %fusion.x_ref, f32[7,7,1536]{2,1,0:T(8,128)} %rev.3.k_ref), custom_call_target="tpu_custom_call" | custom-call | tf_op jit(solution)/shard_map/pallas_call | solution.py:131
  147.9 1.0 reshape.152
  148.9 0.7 slice_select_fusion
  149.6 1.5 collective-permute-start.12
  151.1 1.4 collective-permute-done.12
  152.4 0.9 select_add_fusion
  153.4 0.7 copy-done.7
  154.1 1.6 collective-permute-start.13
  155.6 3.2 %collective-permute-done.13 = f32[18816]{0:T(1024)S(1)} collective-permute-done((f32[18816]{0:T(1024)S(1)}, f32[18816]{0:T(1024)S(1)}, u32[]{:S(2)}, u32[]{:S(2)}) %collective-permute-start.13) | collective-permute-done | bytes 75296 | tf_op jit(solution)/shard_map/ppermute | solution.py:58
  158.8 1.0 select_add_fusion.1
  159.8 2.7 %collective-permute-start.14 = (f32[9408]{0:T(1024)S(1)}, f32[9408]{0:T(1024)S(1)}, u32[]{:S(2)}, u32[]{:S(2)}) collective-permute-start(f32[9408]{0:T(1024)S(1)} %slice_select_fusion.2), channel_id=1, source_target_pairs={{0,4},{1,5},{2,6},{3,7},{4,0},{5,1},{6,2},{7,3},{8,12},{9,13},{10,... | collective-permute-start | bytes 112904 | tf_op jit(solution)/shard_map/ppermute | solution.py:58
  162.6 2.3 %collective-permute-done.14 = f32[9408]{0:T(1024)S(1)} collective-permute-done((f32[9408]{0:T(1024)S(1)}, f32[9408]{0:T(1024)S(1)}, u32[]{:S(2)}, u32[]{:S(2)}) %collective-permute-start.14) | collective-permute-done | bytes 37664 | tf_op jit(solution)/shard_map/ppermute | solution.py:58
  164.9 2.4 %collective-permute-start.15 = (f32[9408]{0:T(1024)S(1)}, f32[9408]{0:T(1024)S(1)}, u32[]{:S(2)}, u32[]{:S(2)}) collective-permute-start(f32[9408]{0:T(1024)S(1)} %select_add_fusion.2), channel_id=1, source_target_pairs={{0,8},{1,9},{2,10},{3,11},{4,12},{5,13},{6,14},{7,15},{8,0},{9,1},... | collective-permute-start | bytes 112904 | tf_op jit(solution)/shard_map/ppermute | solution.py:61
  167.3 5.6 %collective-permute-done.15 = f32[9408]{0:T(1024)S(1)} collective-permute-done((f32[9408]{0:T(1024)S(1)}, f32[9408]{0:T(1024)S(1)}, u32[]{:S(2)}, u32[]{:S(2)}) %collective-permute-start.15) | collective-permute-done | bytes 37664 | tf_op jit(solution)/shard_map/ppermute | solution.py:61
  172.9 1.2 collective-permute-start.16
  174.2 4.3 %collective-permute-done.16 = f32[9408]{0:T(1024)S(1)} collective-permute-done((f32[9408]{0:T(1024)S(1)}, f32[9408]{0:T(1024)S(1)}, u32[]{:S(2)}, u32[]{:S(2)}) %collective-permute-start.16) | collective-permute-done | bytes 37664 | tf_op jit(solution)/shard_map/ppermute | solution.py:61
  178.4 0.7 collective-permute-start.17
  179.2 3.3 %collective-permute-done.17 = f32[9408]{0:T(1024)S(1)} collective-permute-done((f32[9408]{0:T(1024)S(1)}, f32[9408]{0:T(1024)S(1)}, u32[]{:S(2)}, u32[]{:S(2)}) %collective-permute-start.17) | collective-permute-done | bytes 37664 | tf_op jit(solution)/shard_map/ppermute | solution.py:61
  183.0 4.9 %collective-permute-done.18 = f32[9408]{0:T(1024)S(1)} collective-permute-done((f32[9408]{0:T(1024)S(1)}, f32[9408]{0:T(1024)S(1)}, u32[]{:S(2)}, u32[]{:S(2)}) %collective-permute-start.18) | collective-permute-done | bytes 37664 | tf_op jit(solution)/shard_map/ppermute | solution.py:61
  188.0 0.9 collective-permute-start.19
  188.8 3.1 %collective-permute-done.19 = f32[9408]{0:T(1024)S(1)} collective-permute-done((f32[9408]{0:T(1024)S(1)}, f32[9408]{0:T(1024)S(1)}, u32[]{:S(2)}, u32[]{:S(2)}) %collective-permute-start.19) | collective-permute-done | bytes 37664 | tf_op jit(solution)/shard_map/ppermute | solution.py:61
  192.0 2.8 %collective-permute-start.20 = (f32[9408]{0:T(1024)S(1)}, f32[9408]{0:T(1024)S(1)}, u32[]{:S(2)}, u32[]{:S(2)}) collective-permute-start(f32[9408]{0:T(1024)S(1)} %add.150), channel_id=1, source_target_pairs={{0,4},{1,5},{2,6},{3,7},{4,0},{5,1},{6,2},{7,3},{8,12},{9,13},{10,... | collective-permute-start | bytes 112904 | tf_op jit(solution)/shard_map/ppermute | solution.py:65
  194.8 2.1 %collective-permute-done.20 = f32[9408]{0:T(1024)S(1)} collective-permute-done((f32[9408]{0:T(1024)S(1)}, f32[9408]{0:T(1024)S(1)}, u32[]{:S(2)}, u32[]{:S(2)}) %collective-permute-start.20) | collective-permute-done | bytes 37664 | tf_op jit(solution)/shard_map/ppermute | solution.py:65
  197.0 1.5 collective-permute-start.21
  198.5 3.0 %collective-permute-done.21 = f32[18816]{0:T(1024)S(1)} collective-permute-done((f32[18816]{0:T(1024)S(1)}, f32[18816]{0:T(1024)S(1)}, u32[]{:S(2)}, u32[]{:S(2)}) %collective-permute-start.21) | collective-permute-done | bytes 75296 | tf_op jit(solution)/shard_map/ppermute | solution.py:65
  202.0 0.6 dynamic-slice.4
  204.5 1.9 fusion.9
  206.4 1.2 fusion.5
  207.6 0.8 div.96
  (77 shorter events, 6.9 us)
Async XLA Ops:
  0.6 82.1 %copy-start = (bf16[1536,1024]{1,0:T(8,128)(2,1)S(1)}, bf16[1536,1024]{1,0:T(8,128)(2,1)}, u32[]{:S(2)}) copy-start(bf16[1536,1024]{1,0:T(8,128)(2,1)} %param.13) | copy-start | bytes 9437188
  0.6 17.1 %copy-start.5 = (bf16[1,8,64,1536]{3,2,1,0:T(8,128)(2,1)S(1)}, bf16[1,8,64,1536]{3,2,1,0:T(8,128)(2,1)}, u32[]{:S(2)}) copy-start(bf16[1,8,64,1536]{3,2,1,0:T(8,128)(2,1)} %param.8) | copy-start | bytes 4718596
  2.1 17.4 %copy-start.10 = (bf16[7,7,1536]{2,1,0:T(8,128)(2,1)S(1)}, bf16[7,7,1536]{2,1,0:T(8,128)(2,1)}, u32[]{:S(2)}) copy-start(bf16[7,7,1536]{2,1,0:T(8,128)(2,1)} %param.9) | copy-start | bytes 451588
  2.1 15.6 %collective-permute-start = (bf16[1,3,64,1536]{3,2,1,0:T(8,128)(2,1)S(1)}, bf16[1,3,64,1536]{3,2,1,0:T(8,128)(2,1)S(1)}, u32[]{:S(2)}, u32[]{:S(2)}) collective-permute-start(bf16[1,3,64,1536]{3,2,1,0:T(8,128)(2,1)S(1)} %get-tuple-element.22), channel_id=1, source_target_pairs={{0,1},{1,2},{2,3},{3,4},{4,5},{5,6},{6,7},{7,8},{8,9},{9,10},{10,1... | collective-permute-start | bytes 1769480 | tf_op jit(solution)/shard_map/ppermute | solution.py:13
  4.2 15.3 %collective-permute-start.1 = (bf16[1,3,64,1536]{3,2,1,0:T(8,128)(2,1)S(1)}, bf16[1,3,64,1536]{3,2,1,0:T(8,128)(2,1)S(1)}, u32[]{:S(2)}, u32[]{:S(2)}) collective-permute-start(bf16[1,3,64,1536]{3,2,1,0:T(8,128)(2,1)S(1)} %get-tuple-element.21), channel_id=1, source_target_pairs={{1,0},{2,1},{3,2},{4,3},{5,4},{6,5},{7,6},{8,7},{9,8},{10,9},{11,1... | collective-permute-start | bytes 1769480 | tf_op jit(solution)/shard_map/ppermute | solution.py:16
  19.5 21.5 %copy-start.6 = (bf16[1,14,64,1536]{3,2,1,0:T(8,128)(2,1)}, bf16[1,14,64,1536]{3,2,1,0:T(8,128)(2,1)S(1)}, u32[]{:S(2)}) copy-start(bf16[1,14,64,1536]{3,2,1,0:T(8,128)(2,1)S(1)} %constant_dynamic-update-slice_fusion) | copy-start | bytes 8257540
  19.5 21.5 %copy-start.9 = (f32[1536]{0:T(1024)S(1)}, f32[1536]{0:T(1024)}, u32[]{:S(2)}) copy-start(f32[1536]{0:T(1024)} %param.10) | copy-start | bytes 18436
  41.0 1.6 copy-start.1
  41.1 1.6 copy-start.11
  41.1 1.6 copy-start.13
  41.4 24.8 %copy-start.12 = (f32[1,1024]{1,0:T(1,128)S(1)}, f32[1,1024]{1,0:T(1,128)}, u32[]{:S(2)}) copy-start(f32[1,1024]{1,0:T(1,128)} %param.14) | copy-start | bytes 12292
  43.4 1.3 collective-permute-start.2
  44.7 3.7 %collective-permute-start.3 = (f32[1,1536]{1,0:T(1,128)S(1)}, f32[1,1536]{1,0:T(1,128)S(1)}, u32[]{:S(2)}, u32[]{:S(2)}) collective-permute-start(f32[1,1536]{1,0:T(1,128)S(1)} %reshape_add_fusion), channel_id=1, source_target_pairs={{0,2},{1,3},{2,0},{3,1},{4,6},{5,7},{6,4},{7,5},{8,10},{9,11},{10,... | collective-permute-start | bytes 18440 | tf_op jit(solution)/shard_map/ppermute | solution.py:30
  48.4 4.9 %collective-permute-start.4 = (f32[1,1536]{1,0:T(1,128)S(1)}, f32[1,1536]{1,0:T(1,128)S(1)}, u32[]{:S(2)}, u32[]{:S(2)}) collective-permute-start(f32[1,1536]{1,0:T(1,128)S(1)} %add.128), channel_id=1, source_target_pairs={{0,4},{1,5},{2,6},{3,7},{4,0},{5,1},{6,2},{7,3},{8,12},{9,13},{10,... | collective-permute-start | bytes 18440 | tf_op jit(solution)/shard_map/ppermute | solution.py:30
  53.3 7.6 %collective-permute-start.5 = (f32[1,1536]{1,0:T(1,128)S(1)}, f32[1,1536]{1,0:T(1,128)S(1)}, u32[]{:S(2)}, u32[]{:S(2)}) collective-permute-start(f32[1,1536]{1,0:T(1,128)S(1)} %add.129), channel_id=1, source_target_pairs={{0,8},{1,9},{2,10},{3,11},{4,12},{5,13},{6,14},{7,15},{8,0},{9,1},... | collective-permute-start | bytes 18440 | tf_op jit(solution)/shard_map/ppermute | solution.py:30
  61.0 5.2 %collective-permute-start.6 = (f32[1,1536]{1,0:T(1,128)S(1)}, f32[1,1536]{1,0:T(1,128)S(1)}, u32[]{:S(2)}, u32[]{:S(2)}) collective-permute-start(f32[1,1536]{1,0:T(1,128)S(1)} %add.130), channel_id=1, source_target_pairs={{0,16},{1,17},{2,18},{3,19},{4,20},{5,21},{6,22},{7,23},{8,24},{9,... | collective-permute-start | bytes 18440 | tf_op jit(solution)/shard_map/ppermute | solution.py:30
  66.5 5.1 %collective-permute-start.7 = (f32[8,2560]{1,0:T(8,128)S(1)}, f32[8,2560]{1,0:T(8,128)S(1)}, u32[]{:S(2)}, u32[]{:S(2)}) collective-permute-start(f32[8,2560]{1,0:T(8,128)S(1)} %dynamic_update_slice.5), channel_id=1, source_target_pairs={{0,32},{32,0},{64,96},{96,64},{128,160},{160,128},{192,224},{224,1... | collective-permute-start | bytes 245768 | tf_op jit(solution)/shard_map/ppermute | solution.py:30
  71.9 6.0 %collective-permute-start.8 = (f32[8,2560]{1,0:T(8,128)S(1)}, f32[8,2560]{1,0:T(8,128)S(1)}, u32[]{:S(2)}, u32[]{:S(2)}) collective-permute-start(f32[8,2560]{1,0:T(8,128)S(1)} %add.133), channel_id=1, source_target_pairs={{0,64},{32,96},{64,0},{96,32},{128,192},{160,224},{192,128},{224,1... | collective-permute-start | bytes 245768 | tf_op jit(solution)/shard_map/ppermute | solution.py:30
  77.9 4.7 %collective-permute-start.9 = (f32[8,2560]{1,0:T(8,128)S(1)}, f32[8,2560]{1,0:T(8,128)S(1)}, u32[]{:S(2)}, u32[]{:S(2)}) collective-permute-start(f32[8,2560]{1,0:T(8,128)S(1)} %add.134), channel_id=1, source_target_pairs={{0,128},{32,160},{64,192},{96,224},{128,0},{160,32},{192,64},{224,... | collective-permute-start | bytes 245768 | tf_op jit(solution)/shard_map/ppermute | solution.py:30
  82.8 8.8 %copy-start.2 = (f32[1,8,64,1536]{3,0,2,1:T(1,128)S(1)}, f32[1,8,64,1536]{3,0,2,1:T(1,128)}, u32[]{:S(2)}) copy-start(f32[1,8,64,1536]{3,0,2,1:T(1,128)} %copy-done.1) | copy-start | bytes 9437188
  95.6 1.7 copy-start.4
  98.9 30.7 %collective-permute-start.11 = (f32[1,3,64,1536]{3,2,1,0:T(8,128)}, f32[1,3,64,1536]{3,2,1,0:T(8,128)}, u32[]{:S(2)}, u32[]{:S(2)}) collective-permute-start(f32[1,3,64,1536]{3,2,1,0:T(8,128)} %get-tuple-element.20), channel_id=1, source_target_pairs={{1,0},{2,1},{3,2},{4,3},{5,4},{6,5},{7,6},{8,7},{9,8},{10,9},{11,1... | collective-permute-start | bytes 3538952 | tf_op jit(solution)/shard_map/ppermute | solution.py:16
  100.8 28.8 %collective-permute-start.10 = (f32[1,3,64,1536]{3,2,1,0:T(8,128)}, f32[1,3,64,1536]{3,2,1,0:T(8,128)}, u32[]{:S(2)}, u32[]{:S(2)}) collective-permute-start(f32[1,3,64,1536]{3,2,1,0:T(8,128)} %get-tuple-element.19), channel_id=1, source_target_pairs={{0,1},{1,2},{2,3},{3,4},{4,5},{5,6},{6,7},{7,8},{8,9},{9,10},{10,1... | collective-permute-start | bytes 3538952 | tf_op jit(solution)/shard_map/ppermute | solution.py:13
  107.1 5.4 %copy-start.3 = (f32[1,8,64,1536]{3,0,2,1:T(1,128)S(1)}, f32[1,8,64,1536]{3,0,2,1:T(1,128)}, u32[]{:S(2)}) copy-start(f32[1,8,64,1536]{3,0,2,1:T(1,128)} %copy-done.1) | copy-start | bytes 9437188
  149.6 2.9 %collective-permute-start.12 = (f32[37632]{0:T(1024)}, f32[37632]{0:T(1024)}, u32[]{:S(2)}, u32[]{:S(2)}) collective-permute-start(f32[37632]{0:T(1024)} %slice_select_fusion), channel_id=1, source_target_pairs={{0,1},{1,0},{2,3},{3,2},{4,5},{5,4},{6,7},{7,6},{8,9},{9,8},{10,11... | collective-permute-start | bytes 451592 | tf_op jit(solution)/shard_map/ppermute | solution.py:58
  153.4 0.7 copy-start.7
  154.1 4.7 %collective-permute-start.13 = (f32[18816]{0:T(1024)S(1)}, f32[18816]{0:T(1024)S(1)}, u32[]{:S(2)}, u32[]{:S(2)}) collective-permute-start(f32[18816]{0:T(1024)S(1)} %slice_select_fusion.1), channel_id=1, source_target_pairs={{0,2},{1,3},{2,0},{3,1},{4,6},{5,7},{6,4},{7,5},{8,10},{9,11},{10,... | collective-permute-start | bytes 225800 | tf_op jit(solution)/shard_map/ppermute | solution.py:58
  159.8 5.0 %collective-permute-start.14 = (f32[9408]{0:T(1024)S(1)}, f32[9408]{0:T(1024)S(1)}, u32[]{:S(2)}, u32[]{:S(2)}) collective-permute-start(f32[9408]{0:T(1024)S(1)} %slice_select_fusion.2), channel_id=1, source_target_pairs={{0,4},{1,5},{2,6},{3,7},{4,0},{5,1},{6,2},{7,3},{8,12},{9,13},{10,... | collective-permute-start | bytes 112904 | tf_op jit(solution)/shard_map/ppermute | solution.py:58
  164.9 8.0 %collective-permute-start.15 = (f32[9408]{0:T(1024)S(1)}, f32[9408]{0:T(1024)S(1)}, u32[]{:S(2)}, u32[]{:S(2)}) collective-permute-start(f32[9408]{0:T(1024)S(1)} %select_add_fusion.2), channel_id=1, source_target_pairs={{0,8},{1,9},{2,10},{3,11},{4,12},{5,13},{6,14},{7,15},{8,0},{9,1},... | collective-permute-start | bytes 112904 | tf_op jit(solution)/shard_map/ppermute | solution.py:61
  172.9 5.5 %collective-permute-start.16 = (f32[9408]{0:T(1024)S(1)}, f32[9408]{0:T(1024)S(1)}, u32[]{:S(2)}, u32[]{:S(2)}) collective-permute-start(f32[9408]{0:T(1024)S(1)} %add.146), channel_id=1, source_target_pairs={{0,16},{1,17},{2,18},{3,19},{4,20},{5,21},{6,22},{7,23},{8,24},{9,... | collective-permute-start | bytes 112904 | tf_op jit(solution)/shard_map/ppermute | solution.py:61
  178.4 4.0 %collective-permute-start.17 = (f32[9408]{0:T(1024)S(1)}, f32[9408]{0:T(1024)S(1)}, u32[]{:S(2)}, u32[]{:S(2)}) collective-permute-start(f32[9408]{0:T(1024)S(1)} %add.147), channel_id=1, source_target_pairs={{0,32},{32,0},{64,96},{96,64},{128,160},{160,128},{192,224},{224,1... | collective-permute-start | bytes 112904 | tf_op jit(solution)/shard_map/ppermute | solution.py:61
  182.5 5.5 %collective-permute-start.18 = (f32[9408]{0:T(1024)S(1)}, f32[9408]{0:T(1024)S(1)}, u32[]{:S(2)}, u32[]{:S(2)}) collective-permute-start(f32[9408]{0:T(1024)S(1)} %add.148), channel_id=1, source_target_pairs={{0,64},{32,96},{64,0},{96,32},{128,192},{160,224},{192,128},{224,1... | collective-permute-start | bytes 112904 | tf_op jit(solution)/shard_map/ppermute | solution.py:61
  188.0 4.0 %collective-permute-start.19 = (f32[9408]{0:T(1024)S(1)}, f32[9408]{0:T(1024)S(1)}, u32[]{:S(2)}, u32[]{:S(2)}) collective-permute-start(f32[9408]{0:T(1024)S(1)} %add.149), channel_id=1, source_target_pairs={{0,128},{32,160},{64,192},{96,224},{128,0},{160,32},{192,64},{224,... | collective-permute-start | bytes 112904 | tf_op jit(solution)/shard_map/ppermute | solution.py:61
  192.0 4.9 %collective-permute-start.20 = (f32[9408]{0:T(1024)S(1)}, f32[9408]{0:T(1024)S(1)}, u32[]{:S(2)}, u32[]{:S(2)}) collective-permute-start(f32[9408]{0:T(1024)S(1)} %add.150), channel_id=1, source_target_pairs={{0,4},{1,5},{2,6},{3,7},{4,0},{5,1},{6,2},{7,3},{8,12},{9,13},{10,... | collective-permute-start | bytes 112904 | tf_op jit(solution)/shard_map/ppermute | solution.py:65
  197.0 4.5 %collective-permute-start.21 = (f32[18816]{0:T(1024)S(1)}, f32[18816]{0:T(1024)S(1)}, u32[]{:S(2)}, u32[]{:S(2)}) collective-permute-start(f32[18816]{0:T(1024)S(1)} %maximum_select_fusion.2), channel_id=1, source_target_pairs={{0,2},{1,3},{2,0},{3,1},{4,6},{5,7},{6,4},{7,5},{8,10},{9,11},{10,... | collective-permute-start | bytes 225800 | tf_op jit(solution)/shard_map/ppermute | solution.py:65
  201.5 4.9 %copy-start.8 = (f32[37632]{0:T(1024)}, f32[37632]{0:T(1024)S(1)}, u32[]{:S(2)}) copy-start(f32[37632]{0:T(1024)S(1)} %maximum_select_fusion.1) | copy-start | bytes 451588
  201.5 4.9 %collective-permute-start.22 = (f32[37632]{0:T(1024)S(1)}, f32[37632]{0:T(1024)}, u32[]{:S(2)}, u32[]{:S(2)}) collective-permute-start(f32[37632]{0:T(1024)S(1)} %maximum_select_fusion.1), channel_id=1, source_target_pairs={{0,1},{1,0},{2,3},{3,2},{4,5},{5,4},{6,7},{7,6},{8,9},{9,8},{10,11... | collective-permute-start | bytes 451592 | tf_op jit(solution)/shard_map/ppermute | solution.py:65

commit v5 on v4

--- a/solution.py
+++ b/solution.py
@@ -18,7 +18,8 @@
     return block
 
 
-def butterfly_sum(values, axes):
+def butterfly_sum(values, axes, riders=None):
+    riders_done = None
     for axis in axes:
         count = lax.axis_size(axis)
         if count & (count - 1):
@@ -27,12 +28,17 @@
         step = 1
         while step < count:
             pairs = [(i, i ^ step) for i in range(count)]
-            values = values + lax.ppermute(values, axis, pairs)
+            received = lax.ppermute(values, axis, pairs)
+            if riders is not None:
+                received, riders = lax.optimization_barrier((received, riders))
+                riders_done = riders
+                riders = None
+            values = values + received
             step *= 2
-    return values
-
-
-def halving_sum(values, axes, split_steps):
+    return values if riders_done is None else (values, riders_done)
+
+
+def halving_sum(values, axes, split_steps, riders):
     steps = []
     for axis in axes:
         count = lax.axis_size(axis)
@@ -43,6 +49,7 @@
             steps.append((axis, count, step))
             step *= 2
     split_steps = min(split_steps, len(steps))
+    riders_done = None
     parts = 1 << split_steps
     flat = values.reshape(-1)
     size = flat.shape[0]
@@ -55,7 +62,11 @@
         low, high = chunk[:half], chunk[half:]
         keep = jnp.where(upper, high, low)
         give = jnp.where(upper, low, high)
-        chunk = keep + lax.ppermute(give, axis, pairs)
+        received = lax.ppermute(give, axis, pairs)
+        if riders is not None:
+            received, riders_done = lax.optimization_barrier((received, riders))
+            riders = None
+        chunk = keep + received
     for axis, count, step in steps[split_steps:]:
         pairs = [(i, i ^ step) for i in range(count)]
         chunk = chunk + lax.ppermute(chunk, axis, pairs)
@@ -66,7 +77,7 @@
         chunk = jnp.where(
             upper, jnp.concatenate([other, chunk]), jnp.concatenate([chunk, other])
         )
-    return chunk[:size].reshape(values.shape)
+    return chunk[:size].reshape(values.shape), riders_done
 
 
 def normalize(values):
@@ -125,7 +136,8 @@
             acc = jnp.zeros((col_count, lanes), jnp.float32)
             for a in range(side):
                 for d in range(side):
-                    acc = acc + k_ref[a, pl.ds(d, 1), :] * x_ref[h + a, pl.ds(d, col_count), :]
+                    weight = k_ref[side - 1 - a, pl.ds(side - 1 - d, 1), :]
+                    acc = acc + weight * x_ref[h + a, pl.ds(d, col_count), :]
             o_ref[h] = acc.astype(o_ref.dtype)
 
     return pl.pallas_call(
@@ -160,7 +172,7 @@
     )
     normed, inv_dev = normalize(conv_out)
     pool_part = jnp.sum(normed * ln_gain + ln_shift, axis=(1, 2))
-    pool_sum = butterfly_sum(pool_part, ("space",))
+    pool_sum, padded_all = butterfly_sum(pool_part, ("space",), riders=padded_all)
     first_row = lax.axis_index("dp") * batch_dev
     packed = jnp.concatenate([pool_sum, text], axis=1)
     table = lax.dynamic_update_slice(
@@ -207,15 +219,14 @@
     grad_own = inv_dev * (weight_rows - weight_mean - normed * spread_term)
     grad_wide = with_halo(grad_own, (("space", 1),), reach_rows)
     grad_pad = jnp.pad(grad_wide, ((0, 0), (0, 0), (reach_rows, reach_rows), (0, 0)))
-    flipped = kernel_float[::-1, ::-1]
     input_grad = jnp.stack(
-        [input_terms(grad_pad[image], flipped, row_count) for image in range(batch_dev)]
+        [input_terms(grad_pad[image], kernel_float, row_count) for image in range(batch_dev)]
     )
     kernel_part = kernel_terms(grad_own[0], padded_all[0], reach_rows)
     for image in range(1, batch_dev):
         kernel_part = kernel_part + kernel_terms(grad_own[image], padded_all[image], reach_rows)
-    kernel_part, input_grad = lax.optimization_barrier((kernel_part, input_grad))
-    kernel_grad = halving_sum(kernel_part, ("space", "dp"), 3) / pixel_count
+    kernel_sum, input_grad = halving_sum(kernel_part, ("space", "dp"), 3, riders=input_grad)
+    kernel_grad = kernel_sum / pixel_count
     return (loss, input_grad.astype(jnp.bfloat16), kernel_grad, text_grad)
 
 

time: 213 us -> 202 us (0.948)
  waiting for transfers between devices: 67 us -> 61.4 us
  local copies, waits for them, and re-layouts: 15 us -> 9.46 us
  starting transfers between devices: 41.5 us -> 43.8 us
    squeeze x2 -> x1, other arithmetic: 7.87 us -> 2.46 us  [shards(): kernel_part = kernel_terms(grad_own[0], padded_all[0], reach_rows)]
    ppermute x11, waiting for transfers between devices: 33.5 us -> 29.6 us  [the longest x8 24.5 us: butterfly_sum(): received = lax.ppermute(values, axis, pairs)]
    rev x1 -> x0, local copies, waits for them, and re-layouts: 3.82 us -> none  [shards(): flipped = kernel_float[::-1, ::-1]]
    pad x0 -> x1, other arithmetic: none -> 3.52 us  [shards(): jnp.pad(extended.astype(jnp.float32), ((0, 0), (0, 0), (reach_rows, reach...]
  transfers between devices with their start and end apart: 23 -> 23, of which waited for: 20 -> 18; matrix products, arithmetic and copies ran while one was open for 7% -> 8% of each run, Pallas kernels for 7% -> 14%
where the time goes in v5:
time: 202 us; the launch traced here: 199 us
  waiting for transfers between devices  61.4 us (30%)
  starting transfers between devices  43.8 us (22%)
  Pallas kernels  28.2 us (14%)
  matrix products  27.7 us (14%)
  other arithmetic  24 us (12%)
  local copies, waits for them, and re-layouts  9.46 us (5%)
  between operations  4.73 us (2%)
    ppermute x8, waiting for transfers between devices, butterfly_sum(): received = lax.ppermute(values, axis, pairs)  24.5 us
    conv_general_dilated x1, matrix products, depthwise(): lax.conv_general_dilated(extended, kernel.reshape(kernel.shape[0], kernel...  21.5 us
    ppermute x5, waiting for transfers between devices, halving_sum(): chunk = chunk + lax.ppermute(chunk, axis, pairs)  19.6 us
    pallas_call x1, Pallas kernels, kernel_terms(): pl.pallas_call(body, grid=(channels // lanes,), in_specs=[pl.BlockSpec((r...  14.7 us
    pallas_call x1, Pallas kernels, input_terms(): pl.pallas_call(body, grid=(channels // lanes,), in_specs=[pl.BlockSpec(pa...  13.5 us
    ppermute x8, starting transfers between devices, butterfly_sum(): received = lax.ppermute(values, axis, pairs)  11.6 us
    ppermute x2, starting transfers between devices, with_halo(): lax.ppermute(lax.slice_in_dim(block, 0, width, axis=dim), axis, backward)  10 us
    ppermute x5, starting transfers between devices, halving_sum(): chunk = chunk + lax.ppermute(chunk, axis, pairs)  7.39 us
  transfers between devices with their start and end apart: 23, of which 18 were waited for; matrix products, arithmetic and copies ran while one was open for 8% of the time, Pallas kernels for 14%

profile of v5, /device:TPU:28, one launch (start us, length us, event | category | flops | bytes accessed | tf_op | source)
XLA Modules:
  0.0 199.2 jit_solution(6317318882483734660)
XLA Ops:
  0.7 1.5 fusion.28
  2.1 2.1 %collective-permute-start = (bf16[1,3,64,1536]{3,2,1,0:T(8,128)(2,1)S(1)}, bf16[1,3,64,1536]{3,2,1,0:T(8,128)(2,1)S(1)}, u32[]{:S(2)}, u32[]{:S(2)}) collective-permute-start(bf16[1,3,64,1536]{3,2,1,0:T(8,128)(2,1)S(1)} %get-tuple-element.26), channel_id=1, source_target_pairs={{0,1},{1,2},{2,3},{3,4},{4,5},{5,6},{6,7},{7,8},{8,9},{9,10},{10,1... | collective-permute-start | bytes 1769480 | tf_op jit(solution)/shard_map/ppermute | solution.py:13
  4.2 7.9 %collective-permute-start.1 = (bf16[1,3,64,1536]{3,2,1,0:T(8,128)(2,1)S(1)}, bf16[1,3,64,1536]{3,2,1,0:T(8,128)(2,1)S(1)}, u32[]{:S(2)}, u32[]{:S(2)}) collective-permute-start(bf16[1,3,64,1536]{3,2,1,0:T(8,128)(2,1)S(1)} %get-tuple-element.25), channel_id=1, source_target_pairs={{1,0},{2,1},{3,2},{4,3},{5,4},{6,5},{7,6},{8,7},{9,8},{10,9},{11,1... | collective-permute-start | bytes 1769480 | tf_op jit(solution)/shard_map/ppermute | solution.py:16
  12.1 5.6 %collective-permute-done = bf16[1,3,64,1536]{3,2,1,0:T(8,128)(2,1)S(1)} collective-permute-done((bf16[1,3,64,1536]{3,2,1,0:T(8,128)(2,1)S(1)}, bf16[1,3,64,1536]{3,2,1,0:T(8,128)(2,1)S(1)}, u32[]{:S(2)}, u32[]{:S(2)}) %collective-permute-start) | collective-permute-done | bytes 589856 | tf_op jit(solution)/shard_map/ppermute | solution.py:13
  17.9 1.6 collective-permute-done.1
  19.5 21.5 %fusion.2 = f32[1,8,64,1536]{3,0,2,1:T(1,128)S(1)} fusion(bf16[1,14,64,1536]{3,2,1,0:T(8,128)(2,1)S(1)} %constant_dynamic-update-slice_fusion, bf16[7,7,1,1536]{3,1,0,2:T(8,128)(2,1)S(1)} %bitcast.23), kind=kOutput, calls=%fused_computation.6 | convolution fusion | flops 75005952 | bytes 6048768 | tf_op jit(solution)/shard_map/conv_general_dilated | solution.py:93
  41.9 0.8 copy-done.1
  42.6 0.7 add_reduce_fusion
  43.5 3.5 %pad_convert_fusion = f32[1,14,70,1536]{3,2,1,0:T(8,128)} fusion(bf16[1,14,64,1536]{3,2,1,0:T(8,128)(2,1)S(1)} %constant_dynamic-update-slice_fusion), kind=kLoop, calls=%fused_computation.13 | loop fusion | flops 1505280 | bytes 8773632 | tf_op jit(solution)/shard_map/jit(_pad)/pad | solution.py:167
  47.1 3.6 %collective-permute-done.3 = f32[1,1536]{1,0:T(1,128)S(1)} collective-permute-done((f32[1,1536]{1,0:T(1,128)S(1)}, f32[1,1536]{1,0:T(1,128)S(1)}, u32[]{:S(2)}, u32[]{:S(2)}) %collective-permute-start.3) | collective-permute-done | bytes 6176 | tf_op jit(solution)/shard_map/ppermute | solution.py:31
  50.7 3.6 %collective-permute-start.4 = (f32[1,1536]{1,0:T(1,128)S(1)}, f32[1,1536]{1,0:T(1,128)S(1)}, u32[]{:S(2)}, u32[]{:S(2)}) collective-permute-start(f32[1,1536]{1,0:T(1,128)S(1)} %add.128), channel_id=1, source_target_pairs={{0,4},{1,5},{2,6},{3,7},{4,0},{5,1},{6,2},{7,3},{8,12},{9,13},{10,... | collective-permute-start | bytes 18440 | tf_op jit(solution)/shard_map/ppermute | solution.py:31
  54.3 1.6 collective-permute-done.4
  56.0 3.7 %collective-permute-start.5 = (f32[1,1536]{1,0:T(1,128)S(1)}, f32[1,1536]{1,0:T(1,128)S(1)}, u32[]{:S(2)}, u32[]{:S(2)}) collective-permute-start(f32[1,1536]{1,0:T(1,128)S(1)} %add.129), channel_id=1, source_target_pairs={{0,8},{1,9},{2,10},{3,11},{4,12},{5,13},{6,14},{7,15},{8,0},{9,1},... | collective-permute-start | bytes 18440 | tf_op jit(solution)/shard_map/ppermute | solution.py:31
  59.7 3.9 %collective-permute-done.5 = f32[1,1536]{1,0:T(1,128)S(1)} collective-permute-done((f32[1,1536]{1,0:T(1,128)S(1)}, f32[1,1536]{1,0:T(1,128)S(1)}, u32[]{:S(2)}, u32[]{:S(2)}) %collective-permute-start.5) | collective-permute-done | bytes 6176 | tf_op jit(solution)/shard_map/ppermute | solution.py:31
  63.6 1.3 collective-permute-start.6
  64.9 3.9 %collective-permute-done.6 = f32[1,1536]{1,0:T(1,128)S(1)} collective-permute-done((f32[1,1536]{1,0:T(1,128)S(1)}, f32[1,1536]{1,0:T(1,128)S(1)}, u32[]{:S(2)}, u32[]{:S(2)}) %collective-permute-start.6) | collective-permute-done | bytes 6176 | tf_op jit(solution)/shard_map/ppermute | solution.py:31
  69.1 1.3 collective-permute-start.7
  70.4 3.7 %collective-permute-done.7 = f32[8,2560]{1,0:T(8,128)S(1)} collective-permute-done((f32[8,2560]{1,0:T(8,128)S(1)}, f32[8,2560]{1,0:T(8,128)S(1)}, u32[]{:S(2)}, u32[]{:S(2)}) %collective-permute-start.7) | collective-permute-done | bytes 81952 | tf_op jit(solution)/shard_map/ppermute | solution.py:31
  74.9 5.5 %collective-permute-done.8 = f32[8,2560]{1,0:T(8,128)S(1)} collective-permute-done((f32[8,2560]{1,0:T(8,128)S(1)}, f32[8,2560]{1,0:T(8,128)S(1)}, u32[]{:S(2)}, u32[]{:S(2)}) %collective-permute-start.8) | collective-permute-done | bytes 81952 | tf_op jit(solution)/shard_map/ppermute | solution.py:31
  80.4 1.0 collective-permute-start.9
  81.4 0.8 convert_element_type.20.k_ref
  82.8 2.3 %collective-permute-done.9 = f32[8,2560]{1,0:T(8,128)S(1)} collective-permute-done((f32[8,2560]{1,0:T(8,128)S(1)}, f32[8,2560]{1,0:T(8,128)S(1)}, u32[]{:S(2)}, u32[]{:S(2)}) %collective-permute-start.9) | collective-permute-done | bytes 81952 | tf_op jit(solution)/shard_map/ppermute | solution.py:31
  85.3 1.4 multiply_reduce_fusion.5
  87.9 0.6 subtract_reduce_fusion
  89.5 3.7 %convolution_reduce_fusion = f32[1536]{0:T(1024)S(1)} fusion(bf16[1536,1024]{1,0:T(8,128)(2,1)S(1)} %copy-done, f32[8,1024]{1,0:T(8,128)S(1)} %get-tuple-element.31, s32[]{:T(128)S(6)} %select_n.95, f32[8,1024]{1,0:T(8,128)S(1)} %get-tuple-element.35, f32[1]{0:T(128)} %dynamic-slice.2, f32[1]{0:T(128)} %dynamic-slice.1), kind=kOutput, calls=%fused_computation.18 | convolution fusion | flops 18877440 | bytes 3160076 | tf_op jit(solution)/shard_map/dot_general | solution.py:215
  93.2 0.6 fusion.26
  93.8 0.7 multiply_reduce_fusion
  95.2 2.7 %subtract_multiply_fusion = f32[1,8,64,1536]{3,2,1,0:T(8,128)S(1)} fusion(f32[1,8,64,1536]{3,0,2,1:T(1,128)} %copy-done.1, f32[8,64]{1,0:T(8,128)S(1)} %broadcast_multiply_fusion, f32[1536]{0:T(1024)S(1)} %broadcast_subtract_fusion, f32[8,64]{1,0:T(8,128)S(1)} %add_rsqrt_fusion, f32[8,64]{1,0:T(8,128)S(1)} %broadcast_multiply_fusion.1, f32[1536]{0:T(1024)S(1)} %copy-done.8), kind=kLoop, calls=%fused_computation.9 | loop fusion | flops 4718592 | bytes 6309888 | tf_op jit(solution)/shard_map/mul | solution.py:219
  97.9 1.6 fusion.27
  99.5 2.2 %collective-permute-start.12 = (f32[1,3,64,1536]{3,2,1,0:T(8,128)}, f32[1,3,64,1536]{3,2,1,0:T(8,128)}, u32[]{:S(2)}, u32[]{:S(2)}) collective-permute-start(f32[1,3,64,1536]{3,2,1,0:T(8,128)} %get-tuple-element.24), channel_id=1, source_target_pairs={{1,0},{2,1},{3,2},{4,3},{5,4},{6,5},{7,6},{8,7},{9,8},{10,9},{11,1... | collective-permute-start | bytes 3538952 | tf_op jit(solution)/shard_map/ppermute | solution.py:16
  101.7 2.4 %collective-permute-start.11 = (f32[1,3,64,1536]{3,2,1,0:T(8,128)}, f32[1,3,64,1536]{3,2,1,0:T(8,128)}, u32[]{:S(2)}, u32[]{:S(2)}) collective-permute-start(f32[1,3,64,1536]{3,2,1,0:T(8,128)} %get-tuple-element.23), channel_id=1, source_target_pairs={{0,1},{1,2},{2,3},{3,4},{4,5},{5,6},{6,7},{7,8},{8,9},{9,10},{10,1... | collective-permute-start | bytes 3538952 | tf_op jit(solution)/shard_map/ppermute | solution.py:13
  104.1 2.5 %fusion.35.g_ref = f32[8,64,1536]{2,1,0:T(8,128)} fusion(f32[8,64]{1,0:T(8,128)S(1)} %broadcast_multiply_fusion, f32[8,64]{1,0:T(8,128)S(1)} %broadcast_multiply_fusion.1, f32[1536]{0:T(1024)S(1)} %copy-done.8, f32[1,8,64,1536]{3,0,2,1:T(1,128)S(1)} %copy-done.3, f32[1536]{0:T(1024)S(1)} %broadcast_subtract_fusion, f32[8,64]{1,0:T(8,128)S(1)} %add_rsqrt_fusion), kind=kLoop, calls=%fused_computation.81 | loop fusion | flops 4718592 | bytes 6309888 | tf_op jit(solution)/shard_map/squeeze | solution.py:225
  106.6 14.7 %shard_map.111 = f32[7,7,1536]{2,1,0:T(8,128)} custom-call(f32[8,64,1536]{2,1,0:T(8,128)} %fusion.35.g_ref, f32[14,70,1536]{2,1,0:T(8,128)} %bitcast.21), custom_call_target="tpu_custom_call" | custom-call | tf_op jit(solution)/shard_map/pallas_call | solution.py:118
  121.3 1.0 reshape.152
  122.3 0.7 slice_select_fusion
  123.0 1.4 collective-permute-start.10
  124.4 4.7 %fusion.x_ref = f32[14,70,1536]{2,1,0:T(8,128)} fusion(f32[1,3,64,1536]{3,2,1,0:T(8,128)} %collective-permute-done.12, f32[1,8,64,1536]{3,2,1,0:T(8,128)} %copy-done.4, f32[1,3,64,1536]{3,2,1,0:T(8,128)} %collective-permute-done.11), kind=kLoop, calls=%fused_computation.3 | loop fusion | flops 12042240 | bytes 11526144 | tf_op jit(solution)/shard_map/squeeze | solution.py:223
  129.0 13.5 %shard_map.112 = bf16[8,64,1536]{2,1,0:T(8,128)(2,1)} custom-call(f32[14,70,1536]{2,1,0:T(8,128)} %fusion.x_ref, f32[7,7,1536]{2,1,0:T(8,128)} %convert_element_type.20.k_ref), custom_call_target="tpu_custom_call" | custom-call | tf_op jit(solution)/shard_map/pallas_call | solution.py:143
  142.5 0.9 select_add_fusion
  143.5 0.7 copy-done.6
  144.2 1.6 collective-permute-start.13
  145.7 2.9 %collective-permute-done.13 = f32[18816]{0:T(1024)S(1)} collective-permute-done((f32[18816]{0:T(1024)S(1)}, f32[18816]{0:T(1024)S(1)}, u32[]{:S(2)}, u32[]{:S(2)}) %collective-permute-start.13) | collective-permute-done | bytes 75296 | tf_op jit(solution)/shard_map/ppermute | solution.py:65
  148.6 1.0 select_add_fusion.1
  149.7 2.9 %collective-permute-start.14 = (f32[9408]{0:T(1024)S(1)}, f32[9408]{0:T(1024)S(1)}, u32[]{:S(2)}, u32[]{:S(2)}) collective-permute-start(f32[9408]{0:T(1024)S(1)} %slice_select_fusion.2), channel_id=1, source_target_pairs={{0,4},{1,5},{2,6},{3,7},{4,0},{5,1},{6,2},{7,3},{8,12},{9,13},{10,... | collective-permute-start | bytes 112904 | tf_op jit(solution)/shard_map/ppermute | solution.py:65
  152.6 2.1 %collective-permute-done.14 = f32[9408]{0:T(1024)S(1)} collective-permute-done((f32[9408]{0:T(1024)S(1)}, f32[9408]{0:T(1024)S(1)}, u32[]{:S(2)}, u32[]{:S(2)}) %collective-permute-start.14) | collective-permute-done | bytes 37664 | tf_op jit(solution)/shard_map/ppermute | solution.py:65
  154.8 2.6 %collective-permute-start.15 = (f32[9408]{0:T(1024)S(1)}, f32[9408]{0:T(1024)S(1)}, u32[]{:S(2)}, u32[]{:S(2)}) collective-permute-start(f32[9408]{0:T(1024)S(1)} %select_add_fusion.2), channel_id=1, source_target_pairs={{0,8},{1,9},{2,10},{3,11},{4,12},{5,13},{6,14},{7,15},{8,0},{9,1},... | collective-permute-start | bytes 112904 | tf_op jit(solution)/shard_map/ppermute | solution.py:72
  157.4 5.4 %collective-permute-done.15 = f32[9408]{0:T(1024)S(1)} collective-permute-done((f32[9408]{0:T(1024)S(1)}, f32[9408]{0:T(1024)S(1)}, u32[]{:S(2)}, u32[]{:S(2)}) %collective-permute-start.15) | collective-permute-done | bytes 37664 | tf_op jit(solution)/shard_map/ppermute | solution.py:72
  162.8 1.8 collective-permute-start.16
  164.5 3.7 %collective-permute-done.16 = f32[9408]{0:T(1024)S(1)} collective-permute-done((f32[9408]{0:T(1024)S(1)}, f32[9408]{0:T(1024)S(1)}, u32[]{:S(2)}, u32[]{:S(2)}) %collective-permute-start.16) | collective-permute-done | bytes 37664 | tf_op jit(solution)/shard_map/ppermute | solution.py:72
  168.3 1.1 collective-permute-start.17
  169.4 2.9 %collective-permute-done.17 = f32[9408]{0:T(1024)S(1)} collective-permute-done((f32[9408]{0:T(1024)S(1)}, f32[9408]{0:T(1024)S(1)}, u32[]{:S(2)}, u32[]{:S(2)}) %collective-permute-start.17) | collective-permute-done | bytes 37664 | tf_op jit(solution)/shard_map/ppermute | solution.py:72
  172.3 1.2 collective-permute-start.18
  173.6 4.3 %collective-permute-done.18 = f32[9408]{0:T(1024)S(1)} collective-permute-done((f32[9408]{0:T(1024)S(1)}, f32[9408]{0:T(1024)S(1)}, u32[]{:S(2)}, u32[]{:S(2)}) %collective-permute-start.18) | collective-permute-done | bytes 37664 | tf_op jit(solution)/shard_map/ppermute | solution.py:72
  177.8 0.7 collective-permute-start.19
  178.6 3.3 %collective-permute-done.19 = f32[9408]{0:T(1024)S(1)} collective-permute-done((f32[9408]{0:T(1024)S(1)}, f32[9408]{0:T(1024)S(1)}, u32[]{:S(2)}, u32[]{:S(2)}) %collective-permute-start.19) | collective-permute-done | bytes 37664 | tf_op jit(solution)/shard_map/ppermute | solution.py:72
  181.8 2.8 %collective-permute-start.20 = (f32[9408]{0:T(1024)S(1)}, f32[9408]{0:T(1024)S(1)}, u32[]{:S(2)}, u32[]{:S(2)}) collective-permute-start(f32[9408]{0:T(1024)S(1)} %add.150), channel_id=1, source_target_pairs={{0,4},{1,5},{2,6},{3,7},{4,0},{5,1},{6,2},{7,3},{8,12},{9,13},{10,... | collective-permute-start | bytes 112904 | tf_op jit(solution)/shard_map/ppermute | solution.py:76
  184.6 2.1 %collective-permute-done.20 = f32[9408]{0:T(1024)S(1)} collective-permute-done((f32[9408]{0:T(1024)S(1)}, f32[9408]{0:T(1024)S(1)}, u32[]{:S(2)}, u32[]{:S(2)}) %collective-permute-start.20) | collective-permute-done | bytes 37664 | tf_op jit(solution)/shard_map/ppermute | solution.py:76
  186.8 1.5 collective-permute-start.21
  188.4 2.9 %collective-permute-done.21 = f32[18816]{0:T(1024)S(1)} collective-permute-done((f32[18816]{0:T(1024)S(1)}, f32[18816]{0:T(1024)S(1)}, u32[]{:S(2)}, u32[]{:S(2)}) %collective-permute-start.21) | collective-permute-done | bytes 75296 | tf_op jit(solution)/shard_map/ppermute | solution.py:76
  191.8 0.6 dynamic-slice.4
  192.5 0.6 dynamic-slice.3
  194.3 1.9 fusion.9
  196.2 1.2 fusion.5
  197.3 0.8 div.96
  (75 shorter events, 5.4 us)
Async XLA Ops:
  0.6 84.6 %copy-start = (bf16[1536,1024]{1,0:T(8,128)(2,1)S(1)}, bf16[1536,1024]{1,0:T(8,128)(2,1)}, u32[]{:S(2)}) copy-start(bf16[1536,1024]{1,0:T(8,128)(2,1)} %param.13) | copy-start | bytes 9437188
  0.6 17.1 %copy-start.5 = (bf16[1,8,64,1536]{3,2,1,0:T(8,128)(2,1)S(1)}, bf16[1,8,64,1536]{3,2,1,0:T(8,128)(2,1)}, u32[]{:S(2)}) copy-start(bf16[1,8,64,1536]{3,2,1,0:T(8,128)(2,1)} %param.8) | copy-start | bytes 4718596
  2.1 17.4 %copy-start.9 = (bf16[7,7,1536]{2,1,0:T(8,128)(2,1)S(1)}, bf16[7,7,1536]{2,1,0:T(8,128)(2,1)}, u32[]{:S(2)}) copy-start(bf16[7,7,1536]{2,1,0:T(8,128)(2,1)} %param.9) | copy-start | bytes 451588
  2.1 15.6 %collective-permute-start = (bf16[1,3,64,1536]{3,2,1,0:T(8,128)(2,1)S(1)}, bf16[1,3,64,1536]{3,2,1,0:T(8,128)(2,1)S(1)}, u32[]{:S(2)}, u32[]{:S(2)}) collective-permute-start(bf16[1,3,64,1536]{3,2,1,0:T(8,128)(2,1)S(1)} %get-tuple-element.26), channel_id=1, source_target_pairs={{0,1},{1,2},{2,3},{3,4},{4,5},{5,6},{6,7},{7,8},{8,9},{9,10},{10,1... | collective-permute-start | bytes 1769480 | tf_op jit(solution)/shard_map/ppermute | solution.py:13
  4.2 15.3 %collective-permute-start.1 = (bf16[1,3,64,1536]{3,2,1,0:T(8,128)(2,1)S(1)}, bf16[1,3,64,1536]{3,2,1,0:T(8,128)(2,1)S(1)}, u32[]{:S(2)}, u32[]{:S(2)}) collective-permute-start(bf16[1,3,64,1536]{3,2,1,0:T(8,128)(2,1)S(1)} %get-tuple-element.25), channel_id=1, source_target_pairs={{1,0},{2,1},{3,2},{4,3},{5,4},{6,5},{7,6},{8,7},{9,8},{10,9},{11,1... | collective-permute-start | bytes 1769480 | tf_op jit(solution)/shard_map/ppermute | solution.py:16
  19.5 21.5 %copy-start.8 = (f32[1536]{0:T(1024)S(1)}, f32[1536]{0:T(1024)}, u32[]{:S(2)}) copy-start(f32[1536]{0:T(1024)} %param.10) | copy-start | bytes 18436
  41.0 1.6 copy-start.1
  41.0 1.6 copy-start.10
  41.0 1.6 copy-start.12
  43.3 25.5 %copy-start.11 = (f32[1,1024]{1,0:T(1,128)S(1)}, f32[1,1024]{1,0:T(1,128)}, u32[]{:S(2)}) copy-start(f32[1,1024]{1,0:T(1,128)} %param.14) | copy-start | bytes 12292
  43.4 3.6 %collective-permute-start.2 = (f32[1,1536]{1,0:T(1,128)S(1)}, f32[1,1536]{1,0:T(1,128)S(1)}, u32[]{:S(2)}, u32[]{:S(2)}) collective-permute-start(f32[1,1536]{1,0:T(1,128)S(1)} %reduce_sum.131), channel_id=1, source_target_pairs={{0,1},{1,0},{2,3},{3,2},{4,5},{5,4},{6,7},{7,6},{8,9},{9,8},{10,11... | collective-permute-start | bytes 18440 | tf_op jit(solution)/shard_map/ppermute | solution.py:31
  47.0 3.7 %collective-permute-start.3 = (f32[1,1536]{1,0:T(1,128)S(1)}, f32[1,1536]{1,0:T(1,128)S(1)}, u32[]{:S(2)}, u32[]{:S(2)}) collective-permute-start(f32[1,1536]{1,0:T(1,128)S(1)} %reshape_add_fusion), channel_id=1, source_target_pairs={{0,2},{1,3},{2,0},{3,1},{4,6},{5,7},{6,4},{7,5},{8,10},{9,11},{10,... | collective-permute-start | bytes 18440 | tf_op jit(solution)/shard_map/ppermute | solution.py:31
  50.7 5.2 %collective-permute-start.4 = (f32[1,1536]{1,0:T(1,128)S(1)}, f32[1,1536]{1,0:T(1,128)S(1)}, u32[]{:S(2)}, u32[]{:S(2)}) collective-permute-start(f32[1,1536]{1,0:T(1,128)S(1)} %add.128), channel_id=1, source_target_pairs={{0,4},{1,5},{2,6},{3,7},{4,0},{5,1},{6,2},{7,3},{8,12},{9,13},{10,... | collective-permute-start | bytes 18440 | tf_op jit(solution)/shard_map/ppermute | solution.py:31
  56.0 7.6 %collective-permute-start.5 = (f32[1,1536]{1,0:T(1,128)S(1)}, f32[1,1536]{1,0:T(1,128)S(1)}, u32[]{:S(2)}, u32[]{:S(2)}) collective-permute-start(f32[1,1536]{1,0:T(1,128)S(1)} %add.129), channel_id=1, source_target_pairs={{0,8},{1,9},{2,10},{3,11},{4,12},{5,13},{6,14},{7,15},{8,0},{9,1},... | collective-permute-start | bytes 18440 | tf_op jit(solution)/shard_map/ppermute | solution.py:31
  63.6 5.2 %collective-permute-start.6 = (f32[1,1536]{1,0:T(1,128)S(1)}, f32[1,1536]{1,0:T(1,128)S(1)}, u32[]{:S(2)}, u32[]{:S(2)}) collective-permute-start(f32[1,1536]{1,0:T(1,128)S(1)} %add.130), channel_id=1, source_target_pairs={{0,16},{1,17},{2,18},{3,19},{4,20},{5,21},{6,22},{7,23},{8,24},{9,... | collective-permute-start | bytes 18440 | tf_op jit(solution)/shard_map/ppermute | solution.py:31
  69.1 4.9 %collective-permute-start.7 = (f32[8,2560]{1,0:T(8,128)S(1)}, f32[8,2560]{1,0:T(8,128)S(1)}, u32[]{:S(2)}, u32[]{:S(2)}) collective-permute-start(f32[8,2560]{1,0:T(8,128)S(1)} %dynamic_update_slice.5), channel_id=1, source_target_pairs={{0,32},{32,0},{64,96},{96,64},{128,160},{160,128},{192,224},{224,1... | collective-permute-start | bytes 245768 | tf_op jit(solution)/shard_map/ppermute | solution.py:31
  74.4 6.0 %collective-permute-start.8 = (f32[8,2560]{1,0:T(8,128)S(1)}, f32[8,2560]{1,0:T(8,128)S(1)}, u32[]{:S(2)}, u32[]{:S(2)}) collective-permute-start(f32[8,2560]{1,0:T(8,128)S(1)} %add.133), channel_id=1, source_target_pairs={{0,64},{32,96},{64,0},{96,32},{128,192},{160,224},{192,128},{224,1... | collective-permute-start | bytes 245768 | tf_op jit(solution)/shard_map/ppermute | solution.py:31
  80.4 4.7 %collective-permute-start.9 = (f32[8,2560]{1,0:T(8,128)S(1)}, f32[8,2560]{1,0:T(8,128)S(1)}, u32[]{:S(2)}, u32[]{:S(2)}) collective-permute-start(f32[8,2560]{1,0:T(8,128)S(1)} %add.134), channel_id=1, source_target_pairs={{0,128},{32,160},{64,192},{96,224},{128,0},{160,32},{192,64},{224,... | collective-permute-start | bytes 245768 | tf_op jit(solution)/shard_map/ppermute | solution.py:31
  85.3 8.6 %copy-start.2 = (f32[1,8,64,1536]{3,0,2,1:T(1,128)S(1)}, f32[1,8,64,1536]{3,0,2,1:T(1,128)}, u32[]{:S(2)}) copy-start(f32[1,8,64,1536]{3,0,2,1:T(1,128)} %copy-done.1) | copy-start | bytes 9437188
  97.9 8.7 %copy-start.4 = (f32[1,8,64,1536]{3,2,1,0:T(8,128)}, f32[1,8,64,1536]{3,2,1,0:T(8,128)S(1)}, u32[]{:S(2)}) copy-start(f32[1,8,64,1536]{3,2,1,0:T(8,128)S(1)} %subtract_multiply_fusion) | copy-start | bytes 9437188
  97.9 6.2 %copy-start.3 = (f32[1,8,64,1536]{3,0,2,1:T(1,128)S(1)}, f32[1,8,64,1536]{3,0,2,1:T(1,128)}, u32[]{:S(2)}) copy-start(f32[1,8,64,1536]{3,0,2,1:T(1,128)} %copy-done.1) | copy-start | bytes 9437188
  99.5 24.8 %collective-permute-start.12 = (f32[1,3,64,1536]{3,2,1,0:T(8,128)}, f32[1,3,64,1536]{3,2,1,0:T(8,128)}, u32[]{:S(2)}, u32[]{:S(2)}) collective-permute-start(f32[1,3,64,1536]{3,2,1,0:T(8,128)} %get-tuple-element.24), channel_id=1, source_target_pairs={{1,0},{2,1},{3,2},{4,3},{5,4},{6,5},{7,6},{8,7},{9,8},{10,9},{11,1... | collective-permute-start | bytes 3538952 | tf_op jit(solution)/shard_map/ppermute | solution.py:16
  101.7 22.7 %collective-permute-start.11 = (f32[1,3,64,1536]{3,2,1,0:T(8,128)}, f32[1,3,64,1536]{3,2,1,0:T(8,128)}, u32[]{:S(2)}, u32[]{:S(2)}) collective-permute-start(f32[1,3,64,1536]{3,2,1,0:T(8,128)} %get-tuple-element.23), channel_id=1, source_target_pairs={{0,1},{1,2},{2,3},{3,4},{4,5},{5,6},{6,7},{7,8},{8,9},{9,10},{10,1... | collective-permute-start | bytes 3538952 | tf_op jit(solution)/shard_map/ppermute | solution.py:13
  123.0 19.6 %collective-permute-start.10 = (f32[37632]{0:T(1024)}, f32[37632]{0:T(1024)}, u32[]{:S(2)}, u32[]{:S(2)}) collective-permute-start(f32[37632]{0:T(1024)} %slice_select_fusion), channel_id=1, source_target_pairs={{0,1},{1,0},{2,3},{3,2},{4,5},{5,4},{6,7},{7,6},{8,9},{9,8},{10,11... | collective-permute-start | bytes 451592 | tf_op jit(solution)/shard_map/ppermute | solution.py:65
  143.5 0.7 copy-start.6
  144.2 4.5 %collective-permute-start.13 = (f32[18816]{0:T(1024)S(1)}, f32[18816]{0:T(1024)S(1)}, u32[]{:S(2)}, u32[]{:S(2)}) collective-permute-start(f32[18816]{0:T(1024)S(1)} %slice_select_fusion.1), channel_id=1, source_target_pairs={{0,2},{1,3},{2,0},{3,1},{4,6},{5,7},{6,4},{7,5},{8,10},{9,11},{10,... | collective-permute-start | bytes 225800 | tf_op jit(solution)/shard_map/ppermute | solution.py:65
  149.7 5.0 %collective-permute-start.14 = (f32[9408]{0:T(1024)S(1)}, f32[9408]{0:T(1024)S(1)}, u32[]{:S(2)}, u32[]{:S(2)}) collective-permute-start(f32[9408]{0:T(1024)S(1)} %slice_select_fusion.2), channel_id=1, source_target_pairs={{0,4},{1,5},{2,6},{3,7},{4,0},{5,1},{6,2},{7,3},{8,12},{9,13},{10,... | collective-permute-start | bytes 112904 | tf_op jit(solution)/shard_map/ppermute | solution.py:65
  154.8 8.0 %collective-permute-start.15 = (f32[9408]{0:T(1024)S(1)}, f32[9408]{0:T(1024)S(1)}, u32[]{:S(2)}, u32[]{:S(2)}) collective-permute-start(f32[9408]{0:T(1024)S(1)} %select_add_fusion.2), channel_id=1, source_target_pairs={{0,8},{1,9},{2,10},{3,11},{4,12},{5,13},{6,14},{7,15},{8,0},{9,1},... | collective-permute-start | bytes 112904 | tf_op jit(solution)/shard_map/ppermute | solution.py:72
  162.8 5.5 %collective-permute-start.16 = (f32[9408]{0:T(1024)S(1)}, f32[9408]{0:T(1024)S(1)}, u32[]{:S(2)}, u32[]{:S(2)}) collective-permute-start(f32[9408]{0:T(1024)S(1)} %add.146), channel_id=1, source_target_pairs={{0,16},{1,17},{2,18},{3,19},{4,20},{5,21},{6,22},{7,23},{8,24},{9,... | collective-permute-start | bytes 112904 | tf_op jit(solution)/shard_map/ppermute | solution.py:72
  168.3 4.0 %collective-permute-start.17 = (f32[9408]{0:T(1024)S(1)}, f32[9408]{0:T(1024)S(1)}, u32[]{:S(2)}, u32[]{:S(2)}) collective-permute-start(f32[9408]{0:T(1024)S(1)} %add.147), channel_id=1, source_target_pairs={{0,32},{32,0},{64,96},{96,64},{128,160},{160,128},{192,224},{224,1... | collective-permute-start | bytes 112904 | tf_op jit(solution)/shard_map/ppermute | solution.py:72
  172.3 5.5 %collective-permute-start.18 = (f32[9408]{0:T(1024)S(1)}, f32[9408]{0:T(1024)S(1)}, u32[]{:S(2)}, u32[]{:S(2)}) collective-permute-start(f32[9408]{0:T(1024)S(1)} %add.148), channel_id=1, source_target_pairs={{0,64},{32,96},{64,0},{96,32},{128,192},{160,224},{192,128},{224,1... | collective-permute-start | bytes 112904 | tf_op jit(solution)/shard_map/ppermute | solution.py:72
  177.8 4.0 %collective-permute-start.19 = (f32[9408]{0:T(1024)S(1)}, f32[9408]{0:T(1024)S(1)}, u32[]{:S(2)}, u32[]{:S(2)}) collective-permute-start(f32[9408]{0:T(1024)S(1)} %add.149), channel_id=1, source_target_pairs={{0,128},{32,160},{64,192},{96,224},{128,0},{160,32},{192,64},{224,... | collective-permute-start | bytes 112904 | tf_op jit(solution)/shard_map/ppermute | solution.py:72
  181.8 4.9 %collective-permute-start.20 = (f32[9408]{0:T(1024)S(1)}, f32[9408]{0:T(1024)S(1)}, u32[]{:S(2)}, u32[]{:S(2)}) collective-permute-start(f32[9408]{0:T(1024)S(1)} %add.150), channel_id=1, source_target_pairs={{0,4},{1,5},{2,6},{3,7},{4,0},{5,1},{6,2},{7,3},{8,12},{9,13},{10,... | collective-permute-start | bytes 112904 | tf_op jit(solution)/shard_map/ppermute | solution.py:76
  186.8 4.5 %collective-permute-start.21 = (f32[18816]{0:T(1024)S(1)}, f32[18816]{0:T(1024)S(1)}, u32[]{:S(2)}, u32[]{:S(2)}) collective-permute-start(f32[18816]{0:T(1024)S(1)} %maximum_select_fusion.2), channel_id=1, source_target_pairs={{0,2},{1,3},{2,0},{3,1},{4,6},{5,7},{6,4},{7,5},{8,10},{9,11},{10,... | collective-permute-start | bytes 225800 | tf_op jit(solution)/shard_map/ppermute | solution.py:76
  191.3 4.8 %copy-start.7 = (f32[37632]{0:T(1024)}, f32[37632]{0:T(1024)S(1)}, u32[]{:S(2)}) copy-start(f32[37632]{0:T(1024)S(1)} %maximum_select_fusion.1) | copy-start | bytes 451588
  191.4 4.8 %collective-permute-start.22 = (f32[37632]{0:T(1024)S(1)}, f32[37632]{0:T(1024)}, u32[]{:S(2)}, u32[]{:S(2)}) collective-permute-start(f32[37632]{0:T(1024)S(1)} %maximum_select_fusion.1), channel_id=1, source_target_pairs={{0,1},{1,0},{2,3},{3,2},{4,5},{5,4},{6,7},{7,6},{8,9},{9,8},{10,11... | collective-permute-start | bytes 451592 | tf_op jit(solution)/shard_map/ppermute | solution.py:76

commit v6 on v5

--- a/solution.py
+++ b/solution.py
@@ -49,7 +49,7 @@
             steps.append((axis, count, step))
             step *= 2
     split_steps = min(split_steps, len(steps))
-    riders_done = None
+    riders_done = []
     parts = 1 << split_steps
     flat = values.reshape(-1)
     size = flat.shape[0]
@@ -63,9 +63,9 @@
         keep = jnp.where(upper, high, low)
         give = jnp.where(upper, low, high)
         received = lax.ppermute(give, axis, pairs)
-        if riders is not None:
-            received, riders_done = lax.optimization_barrier((received, riders))
-            riders = None
+        if len(riders_done) < len(riders):
+            received, rider = lax.optimization_barrier((received, riders[len(riders_done)]))
+            riders_done.append(rider)
         chunk = keep + received
     for axis, count, step in steps[split_steps:]:
         pairs = [(i, i ^ step) for i in range(count)]
@@ -126,7 +126,7 @@
         out_shape=jax.ShapeDtypeStruct((side, side, channels), jnp.float32),
     )(grad_rows, padded)
 
-def input_terms(padded, kernel, row_count, lanes=128):
+def input_terms(padded, kernel, row_count, first_block, block_count, lanes=128):
     side = kernel.shape[0]
     col_count = padded.shape[1] - side + 1
     channels = padded.shape[2]
@@ -142,13 +142,13 @@
 
     return pl.pallas_call(
         body,
-        grid=(channels // lanes,),
+        grid=(block_count,),
         in_specs=[
-            pl.BlockSpec(padded.shape[:2] + (lanes,), lambda i: (0, 0, i)),
-            pl.BlockSpec((side, side, lanes), lambda i: (0, 0, i)),
+            pl.BlockSpec(padded.shape[:2] + (lanes,), lambda i: (0, 0, i + first_block)),
+            pl.BlockSpec((side, side, lanes), lambda i: (0, 0, i + first_block)),
         ],
         out_specs=pl.BlockSpec((row_count, col_count, lanes), lambda i: (0, 0, i)),
-        out_shape=jax.ShapeDtypeStruct((row_count, col_count, channels), jnp.bfloat16),
+        out_shape=jax.ShapeDtypeStruct((row_count, col_count, block_count * lanes), jnp.bfloat16),
     )(padded, kernel)
 
 def logsum(scores, axis):
@@ -219,13 +219,19 @@
     grad_own = inv_dev * (weight_rows - weight_mean - normed * spread_term)
     grad_wide = with_halo(grad_own, (("space", 1),), reach_rows)
     grad_pad = jnp.pad(grad_wide, ((0, 0), (0, 0), (reach_rows, reach_rows), (0, 0)))
-    input_grad = jnp.stack(
-        [input_terms(grad_pad[image], kernel_float, row_count) for image in range(batch_dev)]
-    )
+    blocks = channels // 128
+    halves = ((0, blocks // 2), (blocks // 2, blocks - blocks // 2))
+    input_parts = [
+        [input_terms(grad_pad[image], kernel_float, row_count, *half) for image in range(batch_dev)]
+        for half in halves
+    ]
     kernel_part = kernel_terms(grad_own[0], padded_all[0], reach_rows)
     for image in range(1, batch_dev):
         kernel_part = kernel_part + kernel_terms(grad_own[image], padded_all[image], reach_rows)
-    kernel_sum, input_grad = halving_sum(kernel_part, ("space", "dp"), 3, riders=input_grad)
+    kernel_sum, input_parts = halving_sum(kernel_part, ("space", "dp"), 3, input_parts)
+    input_grad = jnp.stack(
+        [jnp.concatenate([half[image] for half in input_parts], axis=-1) for image in range(batch_dev)]
+    )
     kernel_grad = kernel_sum / pixel_count
     return (loss, input_grad.astype(jnp.bfloat16), kernel_grad, text_grad)
 

time: 202 us -> 198 us (0.980)
  starting transfers between devices: 43.8 us -> 39.7 us
  waiting for transfers between devices: 61.4 us -> 58.7 us
    another operation x0 -> x1, other arithmetic: none -> 2.63 us  [shards(): jnp.stack([jnp.concatenate([half[image] for half in input_parts], axis=-1...]
    ppermute x3, waiting for transfers between devices: 5.04 us -> 2.92 us  [halving_sum(): other = lax.ppermute(chunk, axis, pairs)]
    ppermute x3, starting transfers between devices: 4.44 us -> 2.36 us  [halving_sum(): other = lax.ppermute(chunk, axis, pairs)]
    pallas_call x1 -> x2, Pallas kernels: 13.5 us -> 15.1 us  [input_terms(): pl.pallas_call(body, grid=(block_count,), in_specs=[pl.BlockSpec(padded.s...]
  transfers between devices with their start and end apart: 23 -> 23, of which waited for: 18 -> 17; matrix products, arithmetic and copies ran while one was open for 8% -> 10% of each run, Pallas kernels for 14% -> 15%
where the time goes in v6:
time: 198 us; the launch traced here: 195 us
  waiting for transfers between devices  58.7 us (30%)
  starting transfers between devices  39.7 us (20%)
  Pallas kernels  29.8 us (15%)
  matrix products  27.7 us (14%)
  other arithmetic  25.2 us (13%)
  local copies, waits for them, and re-layouts  9.38 us (5%)
  between operations  4.73 us (2%)
    ppermute x8, waiting for transfers between devices, butterfly_sum(): received = lax.ppermute(values, axis, pairs)  24.5 us
    conv_general_dilated x1, matrix products, depthwise(): lax.conv_general_dilated(extended, kernel.reshape(kernel.shape[0], kernel...  21.5 us
    ppermute x5, waiting for transfers between devices, halving_sum(): chunk = chunk + lax.ppermute(chunk, axis, pairs)  20.4 us
    pallas_call x2, Pallas kernels, input_terms(): pl.pallas_call(body, grid=(block_count,), in_specs=[pl.BlockSpec(padded.s...  15.1 us
    pallas_call x1, Pallas kernels, kernel_terms(): pl.pallas_call(body, grid=(channels // lanes,), in_specs=[pl.BlockSpec((r...  14.7 us
    ppermute x8, starting transfers between devices, butterfly_sum(): received = lax.ppermute(values, axis, pairs)  11.6 us
    ppermute x2, starting transfers between devices, with_halo(): lax.ppermute(lax.slice_in_dim(block, 0, width, axis=dim), axis, backward)  10 us
    ppermute x5, starting transfers between devices, halving_sum(): chunk = chunk + lax.ppermute(chunk, axis, pairs)  6.59 us
  transfers between devices with their start and end apart: 23, of which 17 were waited for; matrix products, arithmetic and copies ran while one was open for 10% of the time, Pallas kernels for 15%

profile of v6, /device:TPU:28, one launch (start us, length us, event | category | flops | bytes accessed | tf_op | source)
XLA Modules:
  0.0 195.2 jit_solution(9014403643450695209)
XLA Ops:
  0.7 1.5 fusion.28
  2.1 2.1 %collective-permute-start = (bf16[1,3,64,1536]{3,2,1,0:T(8,128)(2,1)S(1)}, bf16[1,3,64,1536]{3,2,1,0:T(8,128)(2,1)S(1)}, u32[]{:S(2)}, u32[]{:S(2)}) collective-permute-start(bf16[1,3,64,1536]{3,2,1,0:T(8,128)(2,1)S(1)} %get-tuple-element.30), channel_id=1, source_target_pairs={{0,1},{1,2},{2,3},{3,4},{4,5},{5,6},{6,7},{7,8},{8,9},{9,10},{10,1... | collective-permute-start | bytes 1769480 | tf_op jit(solution)/shard_map/ppermute | solution.py:13
  4.2 7.9 %collective-permute-start.1 = (bf16[1,3,64,1536]{3,2,1,0:T(8,128)(2,1)S(1)}, bf16[1,3,64,1536]{3,2,1,0:T(8,128)(2,1)S(1)}, u32[]{:S(2)}, u32[]{:S(2)}) collective-permute-start(bf16[1,3,64,1536]{3,2,1,0:T(8,128)(2,1)S(1)} %get-tuple-element.29), channel_id=1, source_target_pairs={{1,0},{2,1},{3,2},{4,3},{5,4},{6,5},{7,6},{8,7},{9,8},{10,9},{11,1... | collective-permute-start | bytes 1769480 | tf_op jit(solution)/shard_map/ppermute | solution.py:16
  12.1 5.6 %collective-permute-done = bf16[1,3,64,1536]{3,2,1,0:T(8,128)(2,1)S(1)} collective-permute-done((bf16[1,3,64,1536]{3,2,1,0:T(8,128)(2,1)S(1)}, bf16[1,3,64,1536]{3,2,1,0:T(8,128)(2,1)S(1)}, u32[]{:S(2)}, u32[]{:S(2)}) %collective-permute-start) | collective-permute-done | bytes 589856 | tf_op jit(solution)/shard_map/ppermute | solution.py:13
  17.9 1.6 collective-permute-done.1
  19.5 21.5 %fusion.2 = f32[1,8,64,1536]{3,0,2,1:T(1,128)S(1)} fusion(bf16[1,14,64,1536]{3,2,1,0:T(8,128)(2,1)S(1)} %constant_dynamic-update-slice_fusion, bf16[7,7,1,1536]{3,1,0,2:T(8,128)(2,1)S(1)} %bitcast.23), kind=kOutput, calls=%fused_computation.6 | convolution fusion | flops 75005952 | bytes 6048768 | tf_op jit(solution)/shard_map/conv_general_dilated | solution.py:93
  41.9 0.8 copy-done.1
  42.6 0.7 add_reduce_fusion
  43.5 3.5 %pad_convert_fusion = f32[1,14,70,1536]{3,2,1,0:T(8,128)} fusion(bf16[1,14,64,1536]{3,2,1,0:T(8,128)(2,1)S(1)} %constant_dynamic-update-slice_fusion), kind=kLoop, calls=%fused_computation.13 | loop fusion | flops 1505280 | bytes 8773632 | tf_op jit(solution)/shard_map/jit(_pad)/pad | solution.py:167
  47.1 3.6 %collective-permute-done.3 = f32[1,1536]{1,0:T(1,128)S(1)} collective-permute-done((f32[1,1536]{1,0:T(1,128)S(1)}, f32[1,1536]{1,0:T(1,128)S(1)}, u32[]{:S(2)}, u32[]{:S(2)}) %collective-permute-start.3) | collective-permute-done | bytes 6176 | tf_op jit(solution)/shard_map/ppermute | solution.py:31
  50.7 3.6 %collective-permute-start.4 = (f32[1,1536]{1,0:T(1,128)S(1)}, f32[1,1536]{1,0:T(1,128)S(1)}, u32[]{:S(2)}, u32[]{:S(2)}) collective-permute-start(f32[1,1536]{1,0:T(1,128)S(1)} %add.128), channel_id=1, source_target_pairs={{0,4},{1,5},{2,6},{3,7},{4,0},{5,1},{6,2},{7,3},{8,12},{9,13},{10,... | collective-permute-start | bytes 18440 | tf_op jit(solution)/shard_map/ppermute | solution.py:31
  54.3 1.6 collective-permute-done.4
  56.0 3.7 %collective-permute-start.5 = (f32[1,1536]{1,0:T(1,128)S(1)}, f32[1,1536]{1,0:T(1,128)S(1)}, u32[]{:S(2)}, u32[]{:S(2)}) collective-permute-start(f32[1,1536]{1,0:T(1,128)S(1)} %add.129), channel_id=1, source_target_pairs={{0,8},{1,9},{2,10},{3,11},{4,12},{5,13},{6,14},{7,15},{8,0},{9,1},... | collective-permute-start | bytes 18440 | tf_op jit(solution)/shard_map/ppermute | solution.py:31
  59.7 3.9 %collective-permute-done.5 = f32[1,1536]{1,0:T(1,128)S(1)} collective-permute-done((f32[1,1536]{1,0:T(1,128)S(1)}, f32[1,1536]{1,0:T(1,128)S(1)}, u32[]{:S(2)}, u32[]{:S(2)}) %collective-permute-start.5) | collective-permute-done | bytes 6176 | tf_op jit(solution)/shard_map/ppermute | solution.py:31
  63.6 1.3 collective-permute-start.6
  64.9 3.9 %collective-permute-done.6 = f32[1,1536]{1,0:T(1,128)S(1)} collective-permute-done((f32[1,1536]{1,0:T(1,128)S(1)}, f32[1,1536]{1,0:T(1,128)S(1)}, u32[]{:S(2)}, u32[]{:S(2)}) %collective-permute-start.6) | collective-permute-done | bytes 6176 | tf_op jit(solution)/shard_map/ppermute | solution.py:31
  69.1 1.3 collective-permute-start.7
  70.4 3.7 %collective-permute-done.7 = f32[8,2560]{1,0:T(8,128)S(1)} collective-permute-done((f32[8,2560]{1,0:T(8,128)S(1)}, f32[8,2560]{1,0:T(8,128)S(1)}, u32[]{:S(2)}, u32[]{:S(2)}) %collective-permute-start.7) | collective-permute-done | bytes 81952 | tf_op jit(solution)/shard_map/ppermute | solution.py:31
  74.9 5.5 %collective-permute-done.8 = f32[8,2560]{1,0:T(8,128)S(1)} collective-permute-done((f32[8,2560]{1,0:T(8,128)S(1)}, f32[8,2560]{1,0:T(8,128)S(1)}, u32[]{:S(2)}, u32[]{:S(2)}) %collective-permute-start.8) | collective-permute-done | bytes 81952 | tf_op jit(solution)/shard_map/ppermute | solution.py:31
  80.4 1.0 collective-permute-start.9
  81.4 0.8 convert_element_type.20.k_ref
  82.8 2.3 %collective-permute-done.9 = f32[8,2560]{1,0:T(8,128)S(1)} collective-permute-done((f32[8,2560]{1,0:T(8,128)S(1)}, f32[8,2560]{1,0:T(8,128)S(1)}, u32[]{:S(2)}, u32[]{:S(2)}) %collective-permute-start.9) | collective-permute-done | bytes 81952 | tf_op jit(solution)/shard_map/ppermute | solution.py:31
  85.3 1.4 multiply_reduce_fusion.5
  86.7 0.6 dynamic-slice.2
  87.9 0.6 subtract_reduce_fusion
  89.5 3.7 %convolution_reduce_fusion = f32[1536]{0:T(1024)S(1)} fusion(bf16[1536,1024]{1,0:T(8,128)(2,1)S(1)} %copy-done, f32[8,1024]{1,0:T(8,128)S(1)} %get-tuple-element.35, s32[]{:T(128)S(6)} %select_n.95, f32[8,1024]{1,0:T(8,128)S(1)} %get-tuple-element.39, f32[1]{0:T(128)} %dynamic-slice.2, f32[1]{0:T(128)} %dynamic-slice.1), kind=kOutput, calls=%fused_computation.19 | convolution fusion | flops 18877440 | bytes 3160076 | tf_op jit(solution)/shard_map/dot_general | solution.py:215
  93.2 0.6 fusion.26
  93.8 0.7 multiply_reduce_fusion
  95.2 2.7 %subtract_multiply_fusion = f32[1,8,64,1536]{3,2,1,0:T(8,128)S(1)} fusion(f32[1,8,64,1536]{3,0,2,1:T(1,128)} %copy-done.1, f32[8,64]{1,0:T(8,128)S(1)} %broadcast_multiply_fusion, f32[1536]{0:T(1024)S(1)} %broadcast_subtract_fusion, f32[8,64]{1,0:T(8,128)S(1)} %add_rsqrt_fusion, f32[8,64]{1,0:T(8,128)S(1)} %broadcast_multiply_fusion.1, f32[1536]{0:T(1024)S(1)} %copy-done.8), kind=kLoop, calls=%fused_computation.9 | loop fusion | flops 4718592 | bytes 6309888 | tf_op jit(solution)/shard_map/mul | solution.py:219
  97.9 1.6 fusion.27
  99.5 2.2 %collective-permute-start.12 = (f32[1,3,64,1536]{3,2,1,0:T(8,128)}, f32[1,3,64,1536]{3,2,1,0:T(8,128)}, u32[]{:S(2)}, u32[]{:S(2)}) collective-permute-start(f32[1,3,64,1536]{3,2,1,0:T(8,128)} %get-tuple-element.28), channel_id=1, source_target_pairs={{1,0},{2,1},{3,2},{4,3},{5,4},{6,5},{7,6},{8,7},{9,8},{10,9},{11,1... | collective-permute-start | bytes 3538952 | tf_op jit(solution)/shard_map/ppermute | solution.py:16
  101.7 2.4 %collective-permute-start.11 = (f32[1,3,64,1536]{3,2,1,0:T(8,128)}, f32[1,3,64,1536]{3,2,1,0:T(8,128)}, u32[]{:S(2)}, u32[]{:S(2)}) collective-permute-start(f32[1,3,64,1536]{3,2,1,0:T(8,128)} %get-tuple-element.27), channel_id=1, source_target_pairs={{0,1},{1,2},{2,3},{3,4},{4,5},{5,6},{6,7},{7,8},{8,9},{9,10},{10,1... | collective-permute-start | bytes 3538952 | tf_op jit(solution)/shard_map/ppermute | solution.py:13
  104.1 2.5 %fusion.35.g_ref = f32[8,64,1536]{2,1,0:T(8,128)} fusion(f32[8,64]{1,0:T(8,128)S(1)} %broadcast_multiply_fusion, f32[8,64]{1,0:T(8,128)S(1)} %broadcast_multiply_fusion.1, f32[1536]{0:T(1024)S(1)} %copy-done.8, f32[1,8,64,1536]{3,0,2,1:T(1,128)S(1)} %copy-done.3, f32[1536]{0:T(1024)S(1)} %broadcast_subtract_fusion, f32[8,64]{1,0:T(8,128)S(1)} %add_rsqrt_fusion), kind=kLoop, calls=%fused_computation.82 | loop fusion | flops 4718592 | bytes 6309888 | tf_op jit(solution)/shard_map/squeeze | solution.py:228
  106.6 14.7 %shard_map.111 = f32[7,7,1536]{2,1,0:T(8,128)} custom-call(f32[8,64,1536]{2,1,0:T(8,128)} %fusion.35.g_ref, f32[14,70,1536]{2,1,0:T(8,128)} %bitcast.22), custom_call_target="tpu_custom_call" | custom-call | tf_op jit(solution)/shard_map/pallas_call | solution.py:118
  121.3 1.0 reshape.152
  122.3 0.7 slice_select_fusion
  123.0 1.4 collective-permute-start.10
  124.4 4.7 %fusion.x_ref = f32[14,70,1536]{2,1,0:T(8,128)} fusion(f32[1,3,64,1536]{3,2,1,0:T(8,128)} %collective-permute-done.12, f32[1,8,64,1536]{3,2,1,0:T(8,128)} %copy-done.4, f32[1,3,64,1536]{3,2,1,0:T(8,128)} %collective-permute-done.11), kind=kLoop, calls=%fused_computation.3 | loop fusion | flops 12042240 | bytes 11526144 | tf_op jit(solution)/shard_map/squeeze | solution.py:225
  129.0 7.5 %shard_map.112 = bf16[8,64,768]{2,1,0:T(8,128)(2,1)} custom-call(f32[14,70,1536]{2,1,0:T(8,128)} %fusion.x_ref, f32[7,7,1536]{2,1,0:T(8,128)} %convert_element_type.20.k_ref), custom_call_target="tpu_custom_call" | custom-call | tf_op jit(solution)/shard_map/pallas_call | solution.py:143
  136.6 0.9 select_add_fusion
  137.5 0.7 copy-done.6
  138.2 0.6 slice_select_fusion.1
  138.8 1.5 collective-permute-start.13
  140.3 7.6 %shard_map.113 = bf16[8,64,768]{2,1,0:T(8,128)(2,1)} custom-call(f32[14,70,1536]{2,1,0:T(8,128)} %fusion.x_ref, f32[7,7,1536]{2,1,0:T(8,128)} %convert_element_type.20.k_ref), custom_call_target="tpu_custom_call" | custom-call | tf_op jit(solution)/shard_map/pallas_call | solution.py:143
  148.0 1.8 collective-permute-start.14
  149.8 3.6 %collective-permute-done.14 = f32[9408]{0:T(1024)S(1)} collective-permute-done((f32[9408]{0:T(1024)S(1)}, f32[9408]{0:T(1024)S(1)}, u32[]{:S(2)}, u32[]{:S(2)}) %collective-permute-start.14) | collective-permute-done | bytes 37664 | tf_op jit(solution)/shard_map/ppermute | solution.py:65
  153.5 1.7 collective-permute-start.15
  155.2 6.3 %collective-permute-done.15 = f32[9408]{0:T(1024)S(1)} collective-permute-done((f32[9408]{0:T(1024)S(1)}, f32[9408]{0:T(1024)S(1)}, u32[]{:S(2)}, u32[]{:S(2)}) %collective-permute-start.15) | collective-permute-done | bytes 37664 | tf_op jit(solution)/shard_map/ppermute | solution.py:72
  161.5 1.7 collective-permute-start.16
  163.2 3.8 %collective-permute-done.16 = f32[9408]{0:T(1024)S(1)} collective-permute-done((f32[9408]{0:T(1024)S(1)}, f32[9408]{0:T(1024)S(1)}, u32[]{:S(2)}, u32[]{:S(2)}) %collective-permute-start.16) | collective-permute-done | bytes 37664 | tf_op jit(solution)/shard_map/ppermute | solution.py:72
  167.0 1.1 collective-permute-start.17
  168.1 2.9 %collective-permute-done.17 = f32[9408]{0:T(1024)S(1)} collective-permute-done((f32[9408]{0:T(1024)S(1)}, f32[9408]{0:T(1024)S(1)}, u32[]{:S(2)}, u32[]{:S(2)}) %collective-permute-start.17) | collective-permute-done | bytes 37664 | tf_op jit(solution)/shard_map/ppermute | solution.py:72
  171.0 1.0 collective-permute-start.18
  172.0 4.5 %collective-permute-done.18 = f32[9408]{0:T(1024)S(1)} collective-permute-done((f32[9408]{0:T(1024)S(1)}, f32[9408]{0:T(1024)S(1)}, u32[]{:S(2)}, u32[]{:S(2)}) %collective-permute-start.18) | collective-permute-done | bytes 37664 | tf_op jit(solution)/shard_map/ppermute | solution.py:72
  176.5 1.2 collective-permute-start.19
  177.7 2.8 %collective-permute-done.19 = f32[9408]{0:T(1024)S(1)} collective-permute-done((f32[9408]{0:T(1024)S(1)}, f32[9408]{0:T(1024)S(1)}, u32[]{:S(2)}, u32[]{:S(2)}) %collective-permute-start.19) | collective-permute-done | bytes 37664 | tf_op jit(solution)/shard_map/ppermute | solution.py:72
  180.5 1.3 collective-permute-start.20
  182.2 0.6 dynamic-slice.4
  184.6 1.3 collective-permute-done.20
  186.0 1.0 collective-permute-start.21
  187.0 1.9 fusion.9
  188.9 1.6 collective-permute-done.21
  190.6 2.6 %maximum_bitcast_fusion = bf16[1,8,64,1536]{3,2,1,0:T(8,128)(2,1)} fusion(bf16[8,64,768]{2,1,0:T(8,128)(2,1)} %shard_map.113, bf16[8,64,768]{2,1,0:T(8,128)(2,1)} %shard_map.112), kind=kLoop, calls=%fused_computation.16 | loop fusion | flops 3145728 | bytes 3145728 | tf_op jit(solution)/shard_map/stack | solution.py:232
  193.3 0.8 div.96
  (77 shorter events, 5.5 us)
Async XLA Ops:
  0.6 84.6 %copy-start = (bf16[1536,1024]{1,0:T(8,128)(2,1)S(1)}, bf16[1536,1024]{1,0:T(8,128)(2,1)}, u32[]{:S(2)}) copy-start(bf16[1536,1024]{1,0:T(8,128)(2,1)} %param.13) | copy-start | bytes 9437188
  0.6 17.1 %copy-start.5 = (bf16[1,8,64,1536]{3,2,1,0:T(8,128)(2,1)S(1)}, bf16[1,8,64,1536]{3,2,1,0:T(8,128)(2,1)}, u32[]{:S(2)}) copy-start(bf16[1,8,64,1536]{3,2,1,0:T(8,128)(2,1)} %param.8) | copy-start | bytes 4718596
  2.1 17.4 %copy-start.9 = (bf16[7,7,1536]{2,1,0:T(8,128)(2,1)S(1)}, bf16[7,7,1536]{2,1,0:T(8,128)(2,1)}, u32[]{:S(2)}) copy-start(bf16[7,7,1536]{2,1,0:T(8,128)(2,1)} %param.9) | copy-start | bytes 451588
  2.1 15.6 %collective-permute-start = (bf16[1,3,64,1536]{3,2,1,0:T(8,128)(2,1)S(1)}, bf16[1,3,64,1536]{3,2,1,0:T(8,128)(2,1)S(1)}, u32[]{:S(2)}, u32[]{:S(2)}) collective-permute-start(bf16[1,3,64,1536]{3,2,1,0:T(8,128)(2,1)S(1)} %get-tuple-element.30), channel_id=1, source_target_pairs={{0,1},{1,2},{2,3},{3,4},{4,5},{5,6},{6,7},{7,8},{8,9},{9,10},{10,1... | collective-permute-start | bytes 1769480 | tf_op jit(solution)/shard_map/ppermute | solution.py:13
  4.2 15.3 %collective-permute-start.1 = (bf16[1,3,64,1536]{3,2,1,0:T(8,128)(2,1)S(1)}, bf16[1,3,64,1536]{3,2,1,0:T(8,128)(2,1)S(1)}, u32[]{:S(2)}, u32[]{:S(2)}) collective-permute-start(bf16[1,3,64,1536]{3,2,1,0:T(8,128)(2,1)S(1)} %get-tuple-element.29), channel_id=1, source_target_pairs={{1,0},{2,1},{3,2},{4,3},{5,4},{6,5},{7,6},{8,7},{9,8},{10,9},{11,1... | collective-permute-start | bytes 1769480 | tf_op jit(solution)/shard_map/ppermute | solution.py:16
  19.5 21.5 %copy-start.8 = (f32[1536]{0:T(1024)S(1)}, f32[1536]{0:T(1024)}, u32[]{:S(2)}) copy-start(f32[1536]{0:T(1024)} %param.10) | copy-start | bytes 18436
  41.0 1.6 copy-start.1
  41.0 1.6 copy-start.10
  41.0 1.6 copy-start.12
  43.3 25.5 %copy-start.11 = (f32[1,1024]{1,0:T(1,128)S(1)}, f32[1,1024]{1,0:T(1,128)}, u32[]{:S(2)}) copy-start(f32[1,1024]{1,0:T(1,128)} %param.14) | copy-start | bytes 12292
  43.4 3.6 %collective-permute-start.2 = (f32[1,1536]{1,0:T(1,128)S(1)}, f32[1,1536]{1,0:T(1,128)S(1)}, u32[]{:S(2)}, u32[]{:S(2)}) collective-permute-start(f32[1,1536]{1,0:T(1,128)S(1)} %reduce_sum.131), channel_id=1, source_target_pairs={{0,1},{1,0},{2,3},{3,2},{4,5},{5,4},{6,7},{7,6},{8,9},{9,8},{10,11... | collective-permute-start | bytes 18440 | tf_op jit(solution)/shard_map/ppermute | solution.py:31
  47.0 3.7 %collective-permute-start.3 = (f32[1,1536]{1,0:T(1,128)S(1)}, f32[1,1536]{1,0:T(1,128)S(1)}, u32[]{:S(2)}, u32[]{:S(2)}) collective-permute-start(f32[1,1536]{1,0:T(1,128)S(1)} %reshape_add_fusion), channel_id=1, source_target_pairs={{0,2},{1,3},{2,0},{3,1},{4,6},{5,7},{6,4},{7,5},{8,10},{9,11},{10,... | collective-permute-start | bytes 18440 | tf_op jit(solution)/shard_map/ppermute | solution.py:31
  50.7 5.2 %collective-permute-start.4 = (f32[1,1536]{1,0:T(1,128)S(1)}, f32[1,1536]{1,0:T(1,128)S(1)}, u32[]{:S(2)}, u32[]{:S(2)}) collective-permute-start(f32[1,1536]{1,0:T(1,128)S(1)} %add.128), channel_id=1, source_target_pairs={{0,4},{1,5},{2,6},{3,7},{4,0},{5,1},{6,2},{7,3},{8,12},{9,13},{10,... | collective-permute-start | bytes 18440 | tf_op jit(solution)/shard_map/ppermute | solution.py:31
  56.0 7.6 %collective-permute-start.5 = (f32[1,1536]{1,0:T(1,128)S(1)}, f32[1,1536]{1,0:T(1,128)S(1)}, u32[]{:S(2)}, u32[]{:S(2)}) collective-permute-start(f32[1,1536]{1,0:T(1,128)S(1)} %add.129), channel_id=1, source_target_pairs={{0,8},{1,9},{2,10},{3,11},{4,12},{5,13},{6,14},{7,15},{8,0},{9,1},... | collective-permute-start | bytes 18440 | tf_op jit(solution)/shard_map/ppermute | solution.py:31
  63.6 5.2 %collective-permute-start.6 = (f32[1,1536]{1,0:T(1,128)S(1)}, f32[1,1536]{1,0:T(1,128)S(1)}, u32[]{:S(2)}, u32[]{:S(2)}) collective-permute-start(f32[1,1536]{1,0:T(1,128)S(1)} %add.130), channel_id=1, source_target_pairs={{0,16},{1,17},{2,18},{3,19},{4,20},{5,21},{6,22},{7,23},{8,24},{9,... | collective-permute-start | bytes 18440 | tf_op jit(solution)/shard_map/ppermute | solution.py:31
  69.1 4.9 %collective-permute-start.7 = (f32[8,2560]{1,0:T(8,128)S(1)}, f32[8,2560]{1,0:T(8,128)S(1)}, u32[]{:S(2)}, u32[]{:S(2)}) collective-permute-start(f32[8,2560]{1,0:T(8,128)S(1)} %dynamic_update_slice.5), channel_id=1, source_target_pairs={{0,32},{32,0},{64,96},{96,64},{128,160},{160,128},{192,224},{224,1... | collective-permute-start | bytes 245768 | tf_op jit(solution)/shard_map/ppermute | solution.py:31
  74.4 6.0 %collective-permute-start.8 = (f32[8,2560]{1,0:T(8,128)S(1)}, f32[8,2560]{1,0:T(8,128)S(1)}, u32[]{:S(2)}, u32[]{:S(2)}) collective-permute-start(f32[8,2560]{1,0:T(8,128)S(1)} %add.133), channel_id=1, source_target_pairs={{0,64},{32,96},{64,0},{96,32},{128,192},{160,224},{192,128},{224,1... | collective-permute-start | bytes 245768 | tf_op jit(solution)/shard_map/ppermute | solution.py:31
  80.4 4.7 %collective-permute-start.9 = (f32[8,2560]{1,0:T(8,128)S(1)}, f32[8,2560]{1,0:T(8,128)S(1)}, u32[]{:S(2)}, u32[]{:S(2)}) collective-permute-start(f32[8,2560]{1,0:T(8,128)S(1)} %add.134), channel_id=1, source_target_pairs={{0,128},{32,160},{64,192},{96,224},{128,0},{160,32},{192,64},{224,... | collective-permute-start | bytes 245768 | tf_op jit(solution)/shard_map/ppermute | solution.py:31
  85.3 8.6 %copy-start.2 = (f32[1,8,64,1536]{3,0,2,1:T(1,128)S(1)}, f32[1,8,64,1536]{3,0,2,1:T(1,128)}, u32[]{:S(2)}) copy-start(f32[1,8,64,1536]{3,0,2,1:T(1,128)} %copy-done.1) | copy-start | bytes 9437188
  97.9 8.7 %copy-start.4 = (f32[1,8,64,1536]{3,2,1,0:T(8,128)}, f32[1,8,64,1536]{3,2,1,0:T(8,128)S(1)}, u32[]{:S(2)}) copy-start(f32[1,8,64,1536]{3,2,1,0:T(8,128)S(1)} %subtract_multiply_fusion) | copy-start | bytes 9437188
  97.9 6.2 %copy-start.3 = (f32[1,8,64,1536]{3,0,2,1:T(1,128)S(1)}, f32[1,8,64,1536]{3,0,2,1:T(1,128)}, u32[]{:S(2)}) copy-start(f32[1,8,64,1536]{3,0,2,1:T(1,128)} %copy-done.1) | copy-start | bytes 9437188
  99.5 24.8 %collective-permute-start.12 = (f32[1,3,64,1536]{3,2,1,0:T(8,128)}, f32[1,3,64,1536]{3,2,1,0:T(8,128)}, u32[]{:S(2)}, u32[]{:S(2)}) collective-permute-start(f32[1,3,64,1536]{3,2,1,0:T(8,128)} %get-tuple-element.28), channel_id=1, source_target_pairs={{1,0},{2,1},{3,2},{4,3},{5,4},{6,5},{7,6},{8,7},{9,8},{10,9},{11,1... | collective-permute-start | bytes 3538952 | tf_op jit(solution)/shard_map/ppermute | solution.py:16
  101.7 22.7 %collective-permute-start.11 = (f32[1,3,64,1536]{3,2,1,0:T(8,128)}, f32[1,3,64,1536]{3,2,1,0:T(8,128)}, u32[]{:S(2)}, u32[]{:S(2)}) collective-permute-start(f32[1,3,64,1536]{3,2,1,0:T(8,128)} %get-tuple-element.27), channel_id=1, source_target_pairs={{0,1},{1,2},{2,3},{3,4},{4,5},{5,6},{6,7},{7,8},{8,9},{9,10},{10,1... | collective-permute-start | bytes 3538952 | tf_op jit(solution)/shard_map/ppermute | solution.py:13
  123.0 13.6 %collective-permute-start.10 = (f32[37632]{0:T(1024)}, f32[37632]{0:T(1024)}, u32[]{:S(2)}, u32[]{:S(2)}) collective-permute-start(f32[37632]{0:T(1024)} %slice_select_fusion), channel_id=1, source_target_pairs={{0,1},{1,0},{2,3},{3,2},{4,5},{5,4},{6,7},{7,6},{8,9},{9,8},{10,11... | collective-permute-start | bytes 451592 | tf_op jit(solution)/shard_map/ppermute | solution.py:65
  137.5 0.7 copy-start.6
  138.8 9.0 %collective-permute-start.13 = (f32[18816]{0:T(1024)}, f32[18816]{0:T(1024)S(1)}, u32[]{:S(2)}, u32[]{:S(2)}) collective-permute-start(f32[18816]{0:T(1024)} %slice_select_fusion.1), channel_id=1, source_target_pairs={{0,2},{1,3},{2,0},{3,1},{4,6},{5,7},{6,4},{7,5},{8,10},{9,11},{10,... | collective-permute-start | bytes 225800 | tf_op jit(solution)/shard_map/ppermute | solution.py:65
  140.3 7.6 %copy-start.7 = (f32[37632]{0:T(1024)S(1)}, f32[37632]{0:T(1024)}, u32[]{:S(2)}) copy-start(f32[37632]{0:T(1024)} %copy-done.6) | copy-start | bytes 451588
  148.0 5.4 %collective-permute-start.14 = (f32[9408]{0:T(1024)S(1)}, f32[9408]{0:T(1024)S(1)}, u32[]{:S(2)}, u32[]{:S(2)}) collective-permute-start(f32[9408]{0:T(1024)S(1)} %slice_select_fusion.2), channel_id=1, source_target_pairs={{0,4},{1,5},{2,6},{3,7},{4,0},{5,1},{6,2},{7,3},{8,12},{9,13},{10,... | collective-permute-start | bytes 112904 | tf_op jit(solution)/shard_map/ppermute | solution.py:65
  153.5 8.0 %collective-permute-start.15 = (f32[9408]{0:T(1024)S(1)}, f32[9408]{0:T(1024)S(1)}, u32[]{:S(2)}, u32[]{:S(2)}) collective-permute-start(f32[9408]{0:T(1024)S(1)} %select_add_fusion.2), channel_id=1, source_target_pairs={{0,8},{1,9},{2,10},{3,11},{4,12},{5,13},{6,14},{7,15},{8,0},{9,1},... | collective-permute-start | bytes 112904 | tf_op jit(solution)/shard_map/ppermute | solution.py:72
  161.5 5.5 %collective-permute-start.16 = (f32[9408]{0:T(1024)S(1)}, f32[9408]{0:T(1024)S(1)}, u32[]{:S(2)}, u32[]{:S(2)}) collective-permute-start(f32[9408]{0:T(1024)S(1)} %add.146), channel_id=1, source_target_pairs={{0,16},{1,17},{2,18},{3,19},{4,20},{5,21},{6,22},{7,23},{8,24},{9,... | collective-permute-start | bytes 112904 | tf_op jit(solution)/shard_map/ppermute | solution.py:72
  167.0 4.0 %collective-permute-start.17 = (f32[9408]{0:T(1024)S(1)}, f32[9408]{0:T(1024)S(1)}, u32[]{:S(2)}, u32[]{:S(2)}) collective-permute-start(f32[9408]{0:T(1024)S(1)} %add.147), channel_id=1, source_target_pairs={{0,32},{32,0},{64,96},{96,64},{128,160},{160,128},{192,224},{224,1... | collective-permute-start | bytes 112904 | tf_op jit(solution)/shard_map/ppermute | solution.py:72
  171.0 5.5 %collective-permute-start.18 = (f32[9408]{0:T(1024)S(1)}, f32[9408]{0:T(1024)S(1)}, u32[]{:S(2)}, u32[]{:S(2)}) collective-permute-start(f32[9408]{0:T(1024)S(1)} %add.148), channel_id=1, source_target_pairs={{0,64},{32,96},{64,0},{96,32},{128,192},{160,224},{192,128},{224,1... | collective-permute-start | bytes 112904 | tf_op jit(solution)/shard_map/ppermute | solution.py:72
  176.5 4.0 %collective-permute-start.19 = (f32[9408]{0:T(1024)S(1)}, f32[9408]{0:T(1024)S(1)}, u32[]{:S(2)}, u32[]{:S(2)}) collective-permute-start(f32[9408]{0:T(1024)S(1)} %add.149), channel_id=1, source_target_pairs={{0,128},{32,160},{64,192},{96,224},{128,0},{160,32},{192,64},{224,... | collective-permute-start | bytes 112904 | tf_op jit(solution)/shard_map/ppermute | solution.py:72
  180.5 5.3 %collective-permute-start.20 = (f32[9408]{0:T(1024)S(1)}, f32[9408]{0:T(1024)S(1)}, u32[]{:S(2)}, u32[]{:S(2)}) collective-permute-start(f32[9408]{0:T(1024)S(1)} %add.150), channel_id=1, source_target_pairs={{0,4},{1,5},{2,6},{3,7},{4,0},{5,1},{6,2},{7,3},{8,12},{9,13},{10,... | collective-permute-start | bytes 112904 | tf_op jit(solution)/shard_map/ppermute | solution.py:76
  186.0 4.5 %collective-permute-start.21 = (f32[18816]{0:T(1024)S(1)}, f32[18816]{0:T(1024)S(1)}, u32[]{:S(2)}, u32[]{:S(2)}) collective-permute-start(f32[18816]{0:T(1024)S(1)} %maximum_select_fusion.2), channel_id=1, source_target_pairs={{0,2},{1,3},{2,0},{3,1},{4,6},{5,7},{6,4},{7,5},{8,10},{9,11},{10,... | collective-permute-start | bytes 225800 | tf_op jit(solution)/shard_map/ppermute | solution.py:76
  190.5 2.7 %collective-permute-start.22 = (f32[37632]{0:T(1024)S(1)}, f32[37632]{0:T(1024)S(1)}, u32[]{:S(2)}, u32[]{:S(2)}) collective-permute-start(f32[37632]{0:T(1024)S(1)} %maximum_select_fusion.1), channel_id=1, source_target_pairs={{0,1},{1,0},{2,3},{3,2},{4,5},{5,4},{6,7},{7,6},{8,9},{9,8},{10,11... | collective-permute-start | bytes 451592 | tf_op jit(solution)/shard_map/ppermute | solution.py:76

commit v7 on v6

--- a/solution.py
+++ b/solution.py
@@ -64,7 +64,10 @@
         give = jnp.where(upper, low, high)
         received = lax.ppermute(give, axis, pairs)
         if len(riders_done) < len(riders):
-            received, rider = lax.optimization_barrier((received, riders[len(riders_done)]))
+            rider = riders[len(riders_done)]
+            if callable(rider):
+                rider = rider(riders_done)
+            received, rider = lax.optimization_barrier((received, rider))
             riders_done.append(rider)
         chunk = keep + received
     for axis, count, step in steps[split_steps:]:
@@ -228,10 +231,15 @@
     kernel_part = kernel_terms(grad_own[0], padded_all[0], reach_rows)
     for image in range(1, batch_dev):
         kernel_part = kernel_part + kernel_terms(grad_own[image], padded_all[image], reach_rows)
-    kernel_sum, input_parts = halving_sum(kernel_part, ("space", "dp"), 3, input_parts)
-    input_grad = jnp.stack(
-        [jnp.concatenate([half[image] for half in input_parts], axis=-1) for image in range(batch_dev)]
-    )
+    def join(done):
+        return jnp.stack(
+            [jnp.concatenate([half[image] for half in done], axis=-1) for image in range(batch_dev)]
+        )
+
+    kernel_sum, riders_done = halving_sum(
+        kernel_part, ("space", "dp"), 3, input_parts + [join]
+    )
+    input_grad = riders_done[-1]
     kernel_grad = kernel_sum / pixel_count
     return (loss, input_grad.astype(jnp.bfloat16), kernel_grad, text_grad)
 

time: 198 us -> 201 us (1.015)
  waiting for transfers between devices: 58.7 us -> 61.6 us
    ppermute x3, waiting for transfers between devices: 2.92 us -> 8.19 us  [halving_sum(): other = lax.ppermute(chunk, axis, pairs)]
    ppermute x3, waiting for transfers between devices: 3.63 us -> 1 us  [halving_sum(): received = lax.ppermute(give, axis, pairs)]
where the time goes in v7:
time: 201 us; the launch traced here: 199 us
  waiting for transfers between devices  61.6 us (31%)
  starting transfers between devices  39 us (19%)
  Pallas kernels  29.8 us (15%)
  matrix products  27.7 us (14%)
  other arithmetic  26.3 us (13%)
  local copies, waits for them, and re-layouts  9.46 us (5%)
  between operations  4.74 us (2%)
    ppermute x8, waiting for transfers between devices, butterfly_sum(): received = lax.ppermute(values, axis, pairs)  24.5 us
    conv_general_dilated x1, matrix products, depthwise(): lax.conv_general_dilated(extended, kernel.reshape(kernel.shape[0], kernel...  21.5 us
    ppermute x5, waiting for transfers between devices, halving_sum(): chunk = chunk + lax.ppermute(chunk, axis, pairs)  20.7 us
    pallas_call x2, Pallas kernels, input_terms(): pl.pallas_call(body, grid=(block_count,), in_specs=[pl.BlockSpec(padded.s...  15.1 us
    pallas_call x1, Pallas kernels, kernel_terms(): pl.pallas_call(body, grid=(channels // lanes,), in_specs=[pl.BlockSpec((r...  14.7 us
    ppermute x8, starting transfers between devices, butterfly_sum(): received = lax.ppermute(values, axis, pairs)  11.6 us
    ppermute x2, starting transfers between devices, with_halo(): lax.ppermute(lax.slice_in_dim(block, 0, width, axis=dim), axis, backward)  10 us
    ppermute x3, waiting for transfers between devices, halving_sum(): other = lax.ppermute(chunk, axis, pairs)  8.19 us
  transfers between devices with their start and end apart: 23, of which 17 were waited for; matrix products, arithmetic and copies ran while one was open for 10% of the time, Pallas kernels for 15%

profile of v7, /device:TPU:28, one launch (start us, length us, event | category | flops | bytes accessed | tf_op | source)
XLA Modules:
  0.0 198.6 jit_solution(18134008989419755057)
XLA Ops:
  0.7 1.5 fusion.28
  2.1 2.1 %collective-permute-start = (bf16[1,3,64,1536]{3,2,1,0:T(8,128)(2,1)S(1)}, bf16[1,3,64,1536]{3,2,1,0:T(8,128)(2,1)S(1)}, u32[]{:S(2)}, u32[]{:S(2)}) collective-permute-start(bf16[1,3,64,1536]{3,2,1,0:T(8,128)(2,1)S(1)} %get-tuple-element.34), channel_id=1, source_target_pairs={{0,1},{1,2},{2,3},{3,4},{4,5},{5,6},{6,7},{7,8},{8,9},{9,10},{10,1... | collective-permute-start | bytes 1769480 | tf_op jit(solution)/shard_map/ppermute | solution.py:13
  4.2 7.9 %collective-permute-start.1 = (bf16[1,3,64,1536]{3,2,1,0:T(8,128)(2,1)S(1)}, bf16[1,3,64,1536]{3,2,1,0:T(8,128)(2,1)S(1)}, u32[]{:S(2)}, u32[]{:S(2)}) collective-permute-start(bf16[1,3,64,1536]{3,2,1,0:T(8,128)(2,1)S(1)} %get-tuple-element.33), channel_id=1, source_target_pairs={{1,0},{2,1},{3,2},{4,3},{5,4},{6,5},{7,6},{8,7},{9,8},{10,9},{11,1... | collective-permute-start | bytes 1769480 | tf_op jit(solution)/shard_map/ppermute | solution.py:16
  12.1 5.6 %collective-permute-done = bf16[1,3,64,1536]{3,2,1,0:T(8,128)(2,1)S(1)} collective-permute-done((bf16[1,3,64,1536]{3,2,1,0:T(8,128)(2,1)S(1)}, bf16[1,3,64,1536]{3,2,1,0:T(8,128)(2,1)S(1)}, u32[]{:S(2)}, u32[]{:S(2)}) %collective-permute-start) | collective-permute-done | bytes 589856 | tf_op jit(solution)/shard_map/ppermute | solution.py:13
  17.9 1.6 collective-permute-done.1
  19.5 21.5 %fusion.2 = f32[1,8,64,1536]{3,0,2,1:T(1,128)S(1)} fusion(bf16[1,14,64,1536]{3,2,1,0:T(8,128)(2,1)S(1)} %constant_dynamic-update-slice_fusion, bf16[7,7,1,1536]{3,1,0,2:T(8,128)(2,1)S(1)} %bitcast.23), kind=kOutput, calls=%fused_computation.6 | convolution fusion | flops 75005952 | bytes 6048768 | tf_op jit(solution)/shard_map/conv_general_dilated | solution.py:96
  41.9 0.8 copy-done.1
  42.6 0.7 add_reduce_fusion
  43.5 3.5 %pad_convert_fusion = f32[1,14,70,1536]{3,2,1,0:T(8,128)} fusion(bf16[1,14,64,1536]{3,2,1,0:T(8,128)(2,1)S(1)} %constant_dynamic-update-slice_fusion), kind=kLoop, calls=%fused_computation.13 | loop fusion | flops 1505280 | bytes 8773632 | tf_op jit(solution)/shard_map/jit(_pad)/pad | solution.py:170
  47.1 3.6 %collective-permute-done.3 = f32[1,1536]{1,0:T(1,128)S(1)} collective-permute-done((f32[1,1536]{1,0:T(1,128)S(1)}, f32[1,1536]{1,0:T(1,128)S(1)}, u32[]{:S(2)}, u32[]{:S(2)}) %collective-permute-start.3) | collective-permute-done | bytes 6176 | tf_op jit(solution)/shard_map/ppermute | solution.py:31
  50.7 3.6 %collective-permute-start.4 = (f32[1,1536]{1,0:T(1,128)S(1)}, f32[1,1536]{1,0:T(1,128)S(1)}, u32[]{:S(2)}, u32[]{:S(2)}) collective-permute-start(f32[1,1536]{1,0:T(1,128)S(1)} %add.128), channel_id=1, source_target_pairs={{0,4},{1,5},{2,6},{3,7},{4,0},{5,1},{6,2},{7,3},{8,12},{9,13},{10,... | collective-permute-start | bytes 18440 | tf_op jit(solution)/shard_map/ppermute | solution.py:31
  54.3 1.6 collective-permute-done.4
  56.0 3.7 %collective-permute-start.5 = (f32[1,1536]{1,0:T(1,128)S(1)}, f32[1,1536]{1,0:T(1,128)S(1)}, u32[]{:S(2)}, u32[]{:S(2)}) collective-permute-start(f32[1,1536]{1,0:T(1,128)S(1)} %add.129), channel_id=1, source_target_pairs={{0,8},{1,9},{2,10},{3,11},{4,12},{5,13},{6,14},{7,15},{8,0},{9,1},... | collective-permute-start | bytes 18440 | tf_op jit(solution)/shard_map/ppermute | solution.py:31
  59.7 3.9 %collective-permute-done.5 = f32[1,1536]{1,0:T(1,128)S(1)} collective-permute-done((f32[1,1536]{1,0:T(1,128)S(1)}, f32[1,1536]{1,0:T(1,128)S(1)}, u32[]{:S(2)}, u32[]{:S(2)}) %collective-permute-start.5) | collective-permute-done | bytes 6176 | tf_op jit(solution)/shard_map/ppermute | solution.py:31
  63.6 1.3 collective-permute-start.6
  64.9 3.9 %collective-permute-done.6 = f32[1,1536]{1,0:T(1,128)S(1)} collective-permute-done((f32[1,1536]{1,0:T(1,128)S(1)}, f32[1,1536]{1,0:T(1,128)S(1)}, u32[]{:S(2)}, u32[]{:S(2)}) %collective-permute-start.6) | collective-permute-done | bytes 6176 | tf_op jit(solution)/shard_map/ppermute | solution.py:31
  69.1 1.3 collective-permute-start.7
  70.4 3.7 %collective-permute-done.7 = f32[8,2560]{1,0:T(8,128)S(1)} collective-permute-done((f32[8,2560]{1,0:T(8,128)S(1)}, f32[8,2560]{1,0:T(8,128)S(1)}, u32[]{:S(2)}, u32[]{:S(2)}) %collective-permute-start.7) | collective-permute-done | bytes 81952 | tf_op jit(solution)/shard_map/ppermute | solution.py:31
  74.9 5.5 %collective-permute-done.8 = f32[8,2560]{1,0:T(8,128)S(1)} collective-permute-done((f32[8,2560]{1,0:T(8,128)S(1)}, f32[8,2560]{1,0:T(8,128)S(1)}, u32[]{:S(2)}, u32[]{:S(2)}) %collective-permute-start.8) | collective-permute-done | bytes 81952 | tf_op jit(solution)/shard_map/ppermute | solution.py:31
  80.4 1.0 collective-permute-start.9
  81.4 0.8 convert_element_type.20.k_ref
  82.8 2.3 %collective-permute-done.9 = f32[8,2560]{1,0:T(8,128)S(1)} collective-permute-done((f32[8,2560]{1,0:T(8,128)S(1)}, f32[8,2560]{1,0:T(8,128)S(1)}, u32[]{:S(2)}, u32[]{:S(2)}) %collective-permute-start.9) | collective-permute-done | bytes 81952 | tf_op jit(solution)/shard_map/ppermute | solution.py:31
  85.3 1.4 multiply_reduce_fusion.5
  87.9 0.6 subtract_reduce_fusion
  89.5 3.7 %convolution_reduce_fusion = f32[1536]{0:T(1024)S(1)} fusion(bf16[1536,1024]{1,0:T(8,128)(2,1)S(1)} %copy-done, f32[8,1024]{1,0:T(8,128)S(1)} %get-tuple-element.39, s32[]{:T(128)S(6)} %select_n.95, f32[8,1024]{1,0:T(8,128)S(1)} %get-tuple-element.43, f32[1]{0:T(128)} %dynamic-slice.2, f32[1]{0:T(128)} %dynamic-slice.1), kind=kOutput, calls=%fused_computation.19 | convolution fusion | flops 18877440 | bytes 3160076 | tf_op jit(solution)/shard_map/dot_general | solution.py:218
  93.2 0.6 fusion.26
  93.8 0.7 multiply_reduce_fusion
  95.2 2.7 %subtract_multiply_fusion = f32[1,8,64,1536]{3,2,1,0:T(8,128)S(1)} fusion(f32[1,8,64,1536]{3,0,2,1:T(1,128)} %copy-done.1, f32[8,64]{1,0:T(8,128)S(1)} %broadcast_multiply_fusion, f32[1536]{0:T(1024)S(1)} %broadcast_subtract_fusion, f32[8,64]{1,0:T(8,128)S(1)} %add_rsqrt_fusion, f32[8,64]{1,0:T(8,128)S(1)} %broadcast_multiply_fusion.1, f32[1536]{0:T(1024)S(1)} %copy-done.9), kind=kLoop, calls=%fused_computation.9 | loop fusion | flops 4718592 | bytes 6309888 | tf_op jit(solution)/shard_map/mul | solution.py:222
  97.9 1.6 fusion.27
  99.5 2.2 %collective-permute-start.12 = (f32[1,3,64,1536]{3,2,1,0:T(8,128)}, f32[1,3,64,1536]{3,2,1,0:T(8,128)}, u32[]{:S(2)}, u32[]{:S(2)}) collective-permute-start(f32[1,3,64,1536]{3,2,1,0:T(8,128)} %get-tuple-element.32), channel_id=1, source_target_pairs={{1,0},{2,1},{3,2},{4,3},{5,4},{6,5},{7,6},{8,7},{9,8},{10,9},{11,1... | collective-permute-start | bytes 3538952 | tf_op jit(solution)/shard_map/ppermute | solution.py:16
  101.7 2.4 %collective-permute-start.11 = (f32[1,3,64,1536]{3,2,1,0:T(8,128)}, f32[1,3,64,1536]{3,2,1,0:T(8,128)}, u32[]{:S(2)}, u32[]{:S(2)}) collective-permute-start(f32[1,3,64,1536]{3,2,1,0:T(8,128)} %get-tuple-element.31), channel_id=1, source_target_pairs={{0,1},{1,2},{2,3},{3,4},{4,5},{5,6},{6,7},{7,8},{8,9},{9,10},{10,1... | collective-permute-start | bytes 3538952 | tf_op jit(solution)/shard_map/ppermute | solution.py:13
  104.1 2.5 %fusion.35.g_ref = f32[8,64,1536]{2,1,0:T(8,128)} fusion(f32[8,64]{1,0:T(8,128)S(1)} %broadcast_multiply_fusion, f32[8,64]{1,0:T(8,128)S(1)} %broadcast_multiply_fusion.1, f32[1536]{0:T(1024)S(1)} %copy-done.9, f32[1,8,64,1536]{3,0,2,1:T(1,128)S(1)} %copy-done.3, f32[1536]{0:T(1024)S(1)} %broadcast_subtract_fusion, f32[8,64]{1,0:T(8,128)S(1)} %add_rsqrt_fusion), kind=kLoop, calls=%fused_computation.82 | loop fusion | flops 4718592 | bytes 6309888 | tf_op jit(solution)/shard_map/squeeze | solution.py:231
  106.6 14.7 %shard_map.111 = f32[7,7,1536]{2,1,0:T(8,128)} custom-call(f32[8,64,1536]{2,1,0:T(8,128)} %fusion.35.g_ref, f32[14,70,1536]{2,1,0:T(8,128)} %bitcast.22), custom_call_target="tpu_custom_call" | custom-call | tf_op jit(solution)/shard_map/pallas_call | solution.py:121
  121.3 1.0 reshape.152
  122.3 0.7 slice_select_fusion
  123.0 1.4 collective-permute-start.10
  124.4 4.7 %fusion.x_ref = f32[14,70,1536]{2,1,0:T(8,128)} fusion(f32[1,3,64,1536]{3,2,1,0:T(8,128)} %collective-permute-done.12, f32[1,8,64,1536]{3,2,1,0:T(8,128)} %copy-done.4, f32[1,3,64,1536]{3,2,1,0:T(8,128)} %collective-permute-done.11), kind=kLoop, calls=%fused_computation.3 | loop fusion | flops 12042240 | bytes 11526144 | tf_op jit(solution)/shard_map/squeeze | solution.py:228
  129.0 7.5 %shard_map.112 = bf16[8,64,768]{2,1,0:T(8,128)(2,1)} custom-call(f32[14,70,1536]{2,1,0:T(8,128)} %fusion.x_ref, f32[7,7,1536]{2,1,0:T(8,128)} %convert_element_type.20.k_ref), custom_call_target="tpu_custom_call" | custom-call | tf_op jit(solution)/shard_map/pallas_call | solution.py:146
  136.6 0.9 select_add_fusion
  137.5 0.7 copy-done.6
  138.2 0.6 slice_select_fusion.1
  138.8 1.5 collective-permute-start.13
  140.3 7.6 %shard_map.113 = bf16[8,64,768]{2,1,0:T(8,128)(2,1)} custom-call(f32[14,70,1536]{2,1,0:T(8,128)} %fusion.x_ref, f32[7,7,1536]{2,1,0:T(8,128)} %convert_element_type.20.k_ref), custom_call_target="tpu_custom_call" | custom-call | tf_op jit(solution)/shard_map/pallas_call | solution.py:146
  148.0 1.8 collective-permute-start.14
  149.8 2.6 %maximum_bitcast_fusion = bf16[1,8,64,1536]{3,2,1,0:T(8,128)(2,1)} fusion(bf16[8,64,768]{2,1,0:T(8,128)(2,1)} %shard_map.113, bf16[8,64,768]{2,1,0:T(8,128)(2,1)} %shard_map.112), kind=kLoop, calls=%fused_computation.16 | loop fusion | flops 3145728 | bytes 3145728 | tf_op jit(solution)/shard_map/stack | solution.py:235
  152.4 1.0 collective-permute-done.14
  153.5 1.7 collective-permute-start.15
  155.2 6.3 %collective-permute-done.15 = f32[9408]{0:T(1024)S(1)} collective-permute-done((f32[9408]{0:T(1024)S(1)}, f32[9408]{0:T(1024)S(1)}, u32[]{:S(2)}, u32[]{:S(2)}) %collective-permute-start.15) | collective-permute-done | bytes 37664 | tf_op jit(solution)/shard_map/ppermute | solution.py:75
  161.5 1.7 collective-permute-start.16
  163.2 3.8 %collective-permute-done.16 = f32[9408]{0:T(1024)S(1)} collective-permute-done((f32[9408]{0:T(1024)S(1)}, f32[9408]{0:T(1024)S(1)}, u32[]{:S(2)}, u32[]{:S(2)}) %collective-permute-start.16) | collective-permute-done | bytes 37664 | tf_op jit(solution)/shard_map/ppermute | solution.py:75
  167.0 1.1 collective-permute-start.17
  168.1 3.2 %collective-permute-done.17 = f32[9408]{0:T(1024)S(1)} collective-permute-done((f32[9408]{0:T(1024)S(1)}, f32[9408]{0:T(1024)S(1)}, u32[]{:S(2)}, u32[]{:S(2)}) %collective-permute-start.17) | collective-permute-done | bytes 37664 | tf_op jit(solution)/shard_map/ppermute | solution.py:75
  171.2 1.1 collective-permute-start.18
  172.4 4.4 %collective-permute-done.18 = f32[9408]{0:T(1024)S(1)} collective-permute-done((f32[9408]{0:T(1024)S(1)}, f32[9408]{0:T(1024)S(1)}, u32[]{:S(2)}, u32[]{:S(2)}) %collective-permute-start.18) | collective-permute-done | bytes 37664 | tf_op jit(solution)/shard_map/ppermute | solution.py:75
  176.8 1.0 collective-permute-start.19
  177.7 3.0 %collective-permute-done.19 = f32[9408]{0:T(1024)S(1)} collective-permute-done((f32[9408]{0:T(1024)S(1)}, f32[9408]{0:T(1024)S(1)}, u32[]{:S(2)}, u32[]{:S(2)}) %collective-permute-start.19) | collective-permute-done | bytes 37664 | tf_op jit(solution)/shard_map/ppermute | solution.py:75
  180.8 1.1 collective-permute-start.20
  181.8 4.3 %collective-permute-done.20 = f32[9408]{0:T(1024)S(1)} collective-permute-done((f32[9408]{0:T(1024)S(1)}, f32[9408]{0:T(1024)S(1)}, u32[]{:S(2)}, u32[]{:S(2)}) %collective-permute-start.20) | collective-permute-done | bytes 37664 | tf_op jit(solution)/shard_map/ppermute | solution.py:79
  186.8 3.9 %collective-permute-done.21 = f32[18816]{0:T(1024)S(1)} collective-permute-done((f32[18816]{0:T(1024)S(1)}, f32[18816]{0:T(1024)S(1)}, u32[]{:S(2)}, u32[]{:S(2)}) %collective-permute-start.21) | collective-permute-done | bytes 75296 | tf_op jit(solution)/shard_map/ppermute | solution.py:79
  191.2 0.6 dynamic-slice.4
  191.8 0.6 dynamic-slice.3
  193.6 1.9 fusion.9
  195.5 1.2 fusion.5
  196.7 0.8 div.96
  (79 shorter events, 6.0 us)
Async XLA Ops:
  0.6 84.6 %copy-start = (bf16[1536,1024]{1,0:T(8,128)(2,1)S(1)}, bf16[1536,1024]{1,0:T(8,128)(2,1)}, u32[]{:S(2)}) copy-start(bf16[1536,1024]{1,0:T(8,128)(2,1)} %param.13) | copy-start | bytes 9437188
  0.6 17.1 %copy-start.5 = (bf16[1,8,64,1536]{3,2,1,0:T(8,128)(2,1)S(1)}, bf16[1,8,64,1536]{3,2,1,0:T(8,128)(2,1)}, u32[]{:S(2)}) copy-start(bf16[1,8,64,1536]{3,2,1,0:T(8,128)(2,1)} %param.8) | copy-start | bytes 4718596
  2.1 17.4 %copy-start.10 = (bf16[7,7,1536]{2,1,0:T(8,128)(2,1)S(1)}, bf16[7,7,1536]{2,1,0:T(8,128)(2,1)}, u32[]{:S(2)}) copy-start(bf16[7,7,1536]{2,1,0:T(8,128)(2,1)} %param.9) | copy-start | bytes 451588
  2.1 15.6 %collective-permute-start = (bf16[1,3,64,1536]{3,2,1,0:T(8,128)(2,1)S(1)}, bf16[1,3,64,1536]{3,2,1,0:T(8,128)(2,1)S(1)}, u32[]{:S(2)}, u32[]{:S(2)}) collective-permute-start(bf16[1,3,64,1536]{3,2,1,0:T(8,128)(2,1)S(1)} %get-tuple-element.34), channel_id=1, source_target_pairs={{0,1},{1,2},{2,3},{3,4},{4,5},{5,6},{6,7},{7,8},{8,9},{9,10},{10,1... | collective-permute-start | bytes 1769480 | tf_op jit(solution)/shard_map/ppermute | solution.py:13
  4.2 15.3 %collective-permute-start.1 = (bf16[1,3,64,1536]{3,2,1,0:T(8,128)(2,1)S(1)}, bf16[1,3,64,1536]{3,2,1,0:T(8,128)(2,1)S(1)}, u32[]{:S(2)}, u32[]{:S(2)}) collective-permute-start(bf16[1,3,64,1536]{3,2,1,0:T(8,128)(2,1)S(1)} %get-tuple-element.33), channel_id=1, source_target_pairs={{1,0},{2,1},{3,2},{4,3},{5,4},{6,5},{7,6},{8,7},{9,8},{10,9},{11,1... | collective-permute-start | bytes 1769480 | tf_op jit(solution)/shard_map/ppermute | solution.py:16
  19.5 21.5 %copy-start.9 = (f32[1536]{0:T(1024)S(1)}, f32[1536]{0:T(1024)}, u32[]{:S(2)}) copy-start(f32[1536]{0:T(1024)} %param.10) | copy-start | bytes 18436
  41.0 1.6 copy-start.1
  41.0 1.6 copy-start.11
  41.0 1.6 copy-start.13
  43.3 25.5 %copy-start.12 = (f32[1,1024]{1,0:T(1,128)S(1)}, f32[1,1024]{1,0:T(1,128)}, u32[]{:S(2)}) copy-start(f32[1,1024]{1,0:T(1,128)} %param.14) | copy-start | bytes 12292
  43.4 3.6 %collective-permute-start.2 = (f32[1,1536]{1,0:T(1,128)S(1)}, f32[1,1536]{1,0:T(1,128)S(1)}, u32[]{:S(2)}, u32[]{:S(2)}) collective-permute-start(f32[1,1536]{1,0:T(1,128)S(1)} %reduce_sum.131), channel_id=1, source_target_pairs={{0,1},{1,0},{2,3},{3,2},{4,5},{5,4},{6,7},{7,6},{8,9},{9,8},{10,11... | collective-permute-start | bytes 18440 | tf_op jit(solution)/shard_map/ppermute | solution.py:31
  47.0 3.7 %collective-permute-start.3 = (f32[1,1536]{1,0:T(1,128)S(1)}, f32[1,1536]{1,0:T(1,128)S(1)}, u32[]{:S(2)}, u32[]{:S(2)}) collective-permute-start(f32[1,1536]{1,0:T(1,128)S(1)} %reshape_add_fusion), channel_id=1, source_target_pairs={{0,2},{1,3},{2,0},{3,1},{4,6},{5,7},{6,4},{7,5},{8,10},{9,11},{10,... | collective-permute-start | bytes 18440 | tf_op jit(solution)/shard_map/ppermute | solution.py:31
  50.7 5.2 %collective-permute-start.4 = (f32[1,1536]{1,0:T(1,128)S(1)}, f32[1,1536]{1,0:T(1,128)S(1)}, u32[]{:S(2)}, u32[]{:S(2)}) collective-permute-start(f32[1,1536]{1,0:T(1,128)S(1)} %add.128), channel_id=1, source_target_pairs={{0,4},{1,5},{2,6},{3,7},{4,0},{5,1},{6,2},{7,3},{8,12},{9,13},{10,... | collective-permute-start | bytes 18440 | tf_op jit(solution)/shard_map/ppermute | solution.py:31
  56.0 7.6 %collective-permute-start.5 = (f32[1,1536]{1,0:T(1,128)S(1)}, f32[1,1536]{1,0:T(1,128)S(1)}, u32[]{:S(2)}, u32[]{:S(2)}) collective-permute-start(f32[1,1536]{1,0:T(1,128)S(1)} %add.129), channel_id=1, source_target_pairs={{0,8},{1,9},{2,10},{3,11},{4,12},{5,13},{6,14},{7,15},{8,0},{9,1},... | collective-permute-start | bytes 18440 | tf_op jit(solution)/shard_map/ppermute | solution.py:31
  63.6 5.2 %collective-permute-start.6 = (f32[1,1536]{1,0:T(1,128)S(1)}, f32[1,1536]{1,0:T(1,128)S(1)}, u32[]{:S(2)}, u32[]{:S(2)}) collective-permute-start(f32[1,1536]{1,0:T(1,128)S(1)} %add.130), channel_id=1, source_target_pairs={{0,16},{1,17},{2,18},{3,19},{4,20},{5,21},{6,22},{7,23},{8,24},{9,... | collective-permute-start | bytes 18440 | tf_op jit(solution)/shard_map/ppermute | solution.py:31
  69.1 4.9 %collective-permute-start.7 = (f32[8,2560]{1,0:T(8,128)S(1)}, f32[8,2560]{1,0:T(8,128)S(1)}, u32[]{:S(2)}, u32[]{:S(2)}) collective-permute-start(f32[8,2560]{1,0:T(8,128)S(1)} %dynamic_update_slice.5), channel_id=1, source_target_pairs={{0,32},{32,0},{64,96},{96,64},{128,160},{160,128},{192,224},{224,1... | collective-permute-start | bytes 245768 | tf_op jit(solution)/shard_map/ppermute | solution.py:31
  74.4 6.0 %collective-permute-start.8 = (f32[8,2560]{1,0:T(8,128)S(1)}, f32[8,2560]{1,0:T(8,128)S(1)}, u32[]{:S(2)}, u32[]{:S(2)}) collective-permute-start(f32[8,2560]{1,0:T(8,128)S(1)} %add.133), channel_id=1, source_target_pairs={{0,64},{32,96},{64,0},{96,32},{128,192},{160,224},{192,128},{224,1... | collective-permute-start | bytes 245768 | tf_op jit(solution)/shard_map/ppermute | solution.py:31
  80.4 4.7 %collective-permute-start.9 = (f32[8,2560]{1,0:T(8,128)S(1)}, f32[8,2560]{1,0:T(8,128)S(1)}, u32[]{:S(2)}, u32[]{:S(2)}) collective-permute-start(f32[8,2560]{1,0:T(8,128)S(1)} %add.134), channel_id=1, source_target_pairs={{0,128},{32,160},{64,192},{96,224},{128,0},{160,32},{192,64},{224,... | collective-permute-start | bytes 245768 | tf_op jit(solution)/shard_map/ppermute | solution.py:31
  85.3 8.6 %copy-start.2 = (f32[1,8,64,1536]{3,0,2,1:T(1,128)S(1)}, f32[1,8,64,1536]{3,0,2,1:T(1,128)}, u32[]{:S(2)}) copy-start(f32[1,8,64,1536]{3,0,2,1:T(1,128)} %copy-done.1) | copy-start | bytes 9437188
  97.9 8.7 %copy-start.4 = (f32[1,8,64,1536]{3,2,1,0:T(8,128)}, f32[1,8,64,1536]{3,2,1,0:T(8,128)S(1)}, u32[]{:S(2)}) copy-start(f32[1,8,64,1536]{3,2,1,0:T(8,128)S(1)} %subtract_multiply_fusion) | copy-start | bytes 9437188
  97.9 6.2 %copy-start.3 = (f32[1,8,64,1536]{3,0,2,1:T(1,128)S(1)}, f32[1,8,64,1536]{3,0,2,1:T(1,128)}, u32[]{:S(2)}) copy-start(f32[1,8,64,1536]{3,0,2,1:T(1,128)} %copy-done.1) | copy-start | bytes 9437188
  99.5 24.8 %collective-permute-start.12 = (f32[1,3,64,1536]{3,2,1,0:T(8,128)}, f32[1,3,64,1536]{3,2,1,0:T(8,128)}, u32[]{:S(2)}, u32[]{:S(2)}) collective-permute-start(f32[1,3,64,1536]{3,2,1,0:T(8,128)} %get-tuple-element.32), channel_id=1, source_target_pairs={{1,0},{2,1},{3,2},{4,3},{5,4},{6,5},{7,6},{8,7},{9,8},{10,9},{11,1... | collective-permute-start | bytes 3538952 | tf_op jit(solution)/shard_map/ppermute | solution.py:16
  101.7 22.7 %collective-permute-start.11 = (f32[1,3,64,1536]{3,2,1,0:T(8,128)}, f32[1,3,64,1536]{3,2,1,0:T(8,128)}, u32[]{:S(2)}, u32[]{:S(2)}) collective-permute-start(f32[1,3,64,1536]{3,2,1,0:T(8,128)} %get-tuple-element.31), channel_id=1, source_target_pairs={{0,1},{1,2},{2,3},{3,4},{4,5},{5,6},{6,7},{7,8},{8,9},{9,10},{10,1... | collective-permute-start | bytes 3538952 | tf_op jit(solution)/shard_map/ppermute | solution.py:13
  123.0 13.6 %collective-permute-start.10 = (f32[37632]{0:T(1024)}, f32[37632]{0:T(1024)}, u32[]{:S(2)}, u32[]{:S(2)}) collective-permute-start(f32[37632]{0:T(1024)} %slice_select_fusion), channel_id=1, source_target_pairs={{0,1},{1,0},{2,3},{3,2},{4,5},{5,4},{6,7},{7,6},{8,9},{9,8},{10,11... | collective-permute-start | bytes 451592 | tf_op jit(solution)/shard_map/ppermute | solution.py:65
  137.5 0.7 copy-start.6
  138.8 9.0 %collective-permute-start.13 = (f32[18816]{0:T(1024)}, f32[18816]{0:T(1024)S(1)}, u32[]{:S(2)}, u32[]{:S(2)}) collective-permute-start(f32[18816]{0:T(1024)} %slice_select_fusion.1), channel_id=1, source_target_pairs={{0,2},{1,3},{2,0},{3,1},{4,6},{5,7},{6,4},{7,5},{8,10},{9,11},{10,... | collective-permute-start | bytes 225800 | tf_op jit(solution)/shard_map/ppermute | solution.py:65
  140.3 7.6 %copy-start.7 = (f32[37632]{0:T(1024)S(1)}, f32[37632]{0:T(1024)}, u32[]{:S(2)}) copy-start(f32[37632]{0:T(1024)} %copy-done.6) | copy-start | bytes 451588
  148.0 5.4 %collective-permute-start.14 = (f32[9408]{0:T(1024)S(1)}, f32[9408]{0:T(1024)S(1)}, u32[]{:S(2)}, u32[]{:S(2)}) collective-permute-start(f32[9408]{0:T(1024)S(1)} %slice_select_fusion.2), channel_id=1, source_target_pairs={{0,4},{1,5},{2,6},{3,7},{4,0},{5,1},{6,2},{7,3},{8,12},{9,13},{10,... | collective-permute-start | bytes 112904 | tf_op jit(solution)/shard_map/ppermute | solution.py:65
  153.5 8.0 %collective-permute-start.15 = (f32[9408]{0:T(1024)S(1)}, f32[9408]{0:T(1024)S(1)}, u32[]{:S(2)}, u32[]{:S(2)}) collective-permute-start(f32[9408]{0:T(1024)S(1)} %select_add_fusion.2), channel_id=1, source_target_pairs={{0,8},{1,9},{2,10},{3,11},{4,12},{5,13},{6,14},{7,15},{8,0},{9,1},... | collective-permute-start | bytes 112904 | tf_op jit(solution)/shard_map/ppermute | solution.py:75
  161.5 5.5 %collective-permute-start.16 = (f32[9408]{0:T(1024)S(1)}, f32[9408]{0:T(1024)S(1)}, u32[]{:S(2)}, u32[]{:S(2)}) collective-permute-start(f32[9408]{0:T(1024)S(1)} %add.146), channel_id=1, source_target_pairs={{0,16},{1,17},{2,18},{3,19},{4,20},{5,21},{6,22},{7,23},{8,24},{9,... | collective-permute-start | bytes 112904 | tf_op jit(solution)/shard_map/ppermute | solution.py:75
  167.0 4.2 %collective-permute-start.17 = (f32[9408]{0:T(1024)S(1)}, f32[9408]{0:T(1024)S(1)}, u32[]{:S(2)}, u32[]{:S(2)}) collective-permute-start(f32[9408]{0:T(1024)S(1)} %add.147), channel_id=1, source_target_pairs={{0,32},{32,0},{64,96},{96,64},{128,160},{160,128},{192,224},{224,1... | collective-permute-start | bytes 112904 | tf_op jit(solution)/shard_map/ppermute | solution.py:75
  171.2 5.5 %collective-permute-start.18 = (f32[9408]{0:T(1024)S(1)}, f32[9408]{0:T(1024)S(1)}, u32[]{:S(2)}, u32[]{:S(2)}) collective-permute-start(f32[9408]{0:T(1024)S(1)} %add.148), channel_id=1, source_target_pairs={{0,64},{32,96},{64,0},{96,32},{128,192},{160,224},{192,128},{224,1... | collective-permute-start | bytes 112904 | tf_op jit(solution)/shard_map/ppermute | solution.py:75
  176.8 4.0 %collective-permute-start.19 = (f32[9408]{0:T(1024)S(1)}, f32[9408]{0:T(1024)S(1)}, u32[]{:S(2)}, u32[]{:S(2)}) collective-permute-start(f32[9408]{0:T(1024)S(1)} %add.149), channel_id=1, source_target_pairs={{0,128},{32,160},{64,192},{96,224},{128,0},{160,32},{192,64},{224,... | collective-permute-start | bytes 112904 | tf_op jit(solution)/shard_map/ppermute | solution.py:75
  180.8 5.3 %collective-permute-start.20 = (f32[9408]{0:T(1024)S(1)}, f32[9408]{0:T(1024)S(1)}, u32[]{:S(2)}, u32[]{:S(2)}) collective-permute-start(f32[9408]{0:T(1024)S(1)} %add.150), channel_id=1, source_target_pairs={{0,4},{1,5},{2,6},{3,7},{4,0},{5,1},{6,2},{7,3},{8,12},{9,13},{10,... | collective-permute-start | bytes 112904 | tf_op jit(solution)/shard_map/ppermute | solution.py:79
  186.2 4.5 %collective-permute-start.21 = (f32[18816]{0:T(1024)S(1)}, f32[18816]{0:T(1024)S(1)}, u32[]{:S(2)}, u32[]{:S(2)}) collective-permute-start(f32[18816]{0:T(1024)S(1)} %maximum_select_fusion.2), channel_id=1, source_target_pairs={{0,2},{1,3},{2,0},{3,1},{4,6},{5,7},{6,4},{7,5},{8,10},{9,11},{10,... | collective-permute-start | bytes 225800 | tf_op jit(solution)/shard_map/ppermute | solution.py:79
  190.7 4.8 %copy-start.8 = (f32[37632]{0:T(1024)}, f32[37632]{0:T(1024)S(1)}, u32[]{:S(2)}) copy-start(f32[37632]{0:T(1024)S(1)} %maximum_select_fusion.1) | copy-start | bytes 451588
  190.7 4.8 %collective-permute-start.22 = (f32[37632]{0:T(1024)S(1)}, f32[37632]{0:T(1024)}, u32[]{:S(2)}, u32[]{:S(2)}) collective-permute-start(f32[37632]{0:T(1024)S(1)} %maximum_select_fusion.1), channel_id=1, source_target_pairs={{0,1},{1,0},{2,3},{3,2},{4,5},{5,4},{6,7},{7,6},{8,9},{9,8},{10,11... | collective-permute-start | bytes 451592 | tf_op jit(solution)/shard_map/ppermute | solution.py:79

commit v8 on v6

--- a/solution.py
+++ b/solution.py
@@ -101,7 +101,7 @@
     )
 
 
-def kernel_terms(grad_rows, padded, reach, lanes=128):
+def kernel_terms(grad_rows, padded, reach, scale, lanes=128):
     row_count, col_count, channels = grad_rows.shape
     side = 2 * reach + 1
     groups = col_count // 8
@@ -113,7 +113,7 @@
                 for h in range(row_count):
                     prod = g_ref[h] * x_ref[h + a, pl.ds(d, col_count), :]
                     acc = acc + prod.reshape(groups, 8, lanes).sum(axis=0)
-                o_ref[a, pl.ds(d, 1), :] = acc.sum(axis=0, keepdims=True)
+                o_ref[a, pl.ds(d, 1), :] = acc.sum(axis=0, keepdims=True) * scale
 
     return pl.pallas_call(
         body,
@@ -225,14 +225,18 @@
         [input_terms(grad_pad[image], kernel_float, row_count, *half) for image in range(batch_dev)]
         for half in halves
     ]
-    kernel_part = kernel_terms(grad_own[0], padded_all[0], reach_rows)
+    kernel_part = kernel_terms(grad_own[0], padded_all[0], reach_rows, 1.0 / pixel_count)
     for image in range(1, batch_dev):
-        kernel_part = kernel_part + kernel_terms(grad_own[image], padded_all[image], reach_rows)
-    kernel_sum, input_parts = halving_sum(kernel_part, ("space", "dp"), 3, input_parts)
+        kernel_part = kernel_part + kernel_terms(
+            grad_own[image], padded_all[image], reach_rows, 1.0 / pixel_count
+        )
+    kernel_grad, riders_done = halving_sum(
+        kernel_part, ("space", "dp"), 3, input_parts + [text_grad]
+    )
+    input_parts, text_grad = riders_done[:2], riders_done[2]
     input_grad = jnp.stack(
         [jnp.concatenate([half[image] for half in input_parts], axis=-1) for image in range(batch_dev)]
     )
-    kernel_grad = kernel_sum / pixel_count
     return (loss, input_grad.astype(jnp.bfloat16), kernel_grad, text_grad)
 
 

time: 198 us -> 200 us (1.010)
    ppermute x3, waiting for transfers between devices: 2.92 us -> 5.73 us  [halving_sum(): other = lax.ppermute(chunk, axis, pairs)]
where the time goes in v8:
time: 200 us; the launch traced here: 196 us
  waiting for transfers between devices  59.6 us (30%)
  starting transfers between devices  39.8 us (20%)
  Pallas kernels  29.8 us (15%)
  matrix products  27.8 us (14%)
  other arithmetic  25.2 us (13%)
  local copies, waits for them, and re-layouts  9.44 us (5%)
  between operations  4.76 us (2%)
    ppermute x8, waiting for transfers between devices, butterfly_sum(): received = lax.ppermute(values, axis, pairs)  24.5 us
    conv_general_dilated x1, matrix products, depthwise(): lax.conv_general_dilated(extended, kernel.reshape(kernel.shape[0], kernel...  21.5 us
    ppermute x5, waiting for transfers between devices, halving_sum(): chunk = chunk + lax.ppermute(chunk, axis, pairs)  20.5 us
    pallas_call x2, Pallas kernels, input_terms(): pl.pallas_call(body, grid=(block_count,), in_specs=[pl.BlockSpec(padded.s...  15.1 us
    pallas_call x1, Pallas kernels, kernel_terms(): pl.pallas_call(body, grid=(channels // lanes,), in_specs=[pl.BlockSpec((r...  14.7 us
    ppermute x8, starting transfers between devices, butterfly_sum(): received = lax.ppermute(values, axis, pairs)  11.6 us
    ppermute x2, starting transfers between devices, with_halo(): lax.ppermute(lax.slice_in_dim(block, 0, width, axis=dim), axis, backward)  10 us
    ppermute x5, starting transfers between devices, halving_sum(): chunk = chunk + lax.ppermute(chunk, axis, pairs)  6.56 us
  transfers between devices with their start and end apart: 23, of which 17 were waited for; matrix products, arithmetic and copies ran while one was open for 10% of the time, Pallas kernels for 15%

profile of v8, /device:TPU:28, one launch (start us, length us, event | category | flops | bytes accessed | tf_op | source)
XLA Modules:
  0.0 196.5 jit_solution(732396442133957913)
XLA Ops:
  0.7 1.5 fusion.27
  2.1 2.1 %collective-permute-start = (bf16[1,3,64,1536]{3,2,1,0:T(8,128)(2,1)S(1)}, bf16[1,3,64,1536]{3,2,1,0:T(8,128)(2,1)S(1)}, u32[]{:S(2)}, u32[]{:S(2)}) collective-permute-start(bf16[1,3,64,1536]{3,2,1,0:T(8,128)(2,1)S(1)} %get-tuple-element.34), channel_id=1, source_target_pairs={{0,1},{1,2},{2,3},{3,4},{4,5},{5,6},{6,7},{7,8},{8,9},{9,10},{10,1... | collective-permute-start | bytes 1769480 | tf_op jit(solution)/shard_map/ppermute | solution.py:13
  4.2 7.9 %collective-permute-start.1 = (bf16[1,3,64,1536]{3,2,1,0:T(8,128)(2,1)S(1)}, bf16[1,3,64,1536]{3,2,1,0:T(8,128)(2,1)S(1)}, u32[]{:S(2)}, u32[]{:S(2)}) collective-permute-start(bf16[1,3,64,1536]{3,2,1,0:T(8,128)(2,1)S(1)} %get-tuple-element.33), channel_id=1, source_target_pairs={{1,0},{2,1},{3,2},{4,3},{5,4},{6,5},{7,6},{8,7},{9,8},{10,9},{11,1... | collective-permute-start | bytes 1769480 | tf_op jit(solution)/shard_map/ppermute | solution.py:16
  12.1 5.6 %collective-permute-done = bf16[1,3,64,1536]{3,2,1,0:T(8,128)(2,1)S(1)} collective-permute-done((bf16[1,3,64,1536]{3,2,1,0:T(8,128)(2,1)S(1)}, bf16[1,3,64,1536]{3,2,1,0:T(8,128)(2,1)S(1)}, u32[]{:S(2)}, u32[]{:S(2)}) %collective-permute-start) | collective-permute-done | bytes 589856 | tf_op jit(solution)/shard_map/ppermute | solution.py:13
  17.9 1.6 collective-permute-done.1
  19.5 21.5 %fusion.2 = f32[1,8,64,1536]{3,0,2,1:T(1,128)S(1)} fusion(bf16[1,14,64,1536]{3,2,1,0:T(8,128)(2,1)S(1)} %constant_dynamic-update-slice_fusion, bf16[7,7,1,1536]{3,1,0,2:T(8,128)(2,1)S(1)} %bitcast.23), kind=kOutput, calls=%fused_computation.6 | convolution fusion | flops 75005952 | bytes 6048768 | tf_op jit(solution)/shard_map/conv_general_dilated | solution.py:93
  41.9 0.8 copy-done.1
  42.6 0.7 add_reduce_fusion
  43.5 3.5 %pad_convert_fusion = f32[1,14,70,1536]{3,2,1,0:T(8,128)} fusion(bf16[1,14,64,1536]{3,2,1,0:T(8,128)(2,1)S(1)} %constant_dynamic-update-slice_fusion), kind=kLoop, calls=%fused_computation.13 | loop fusion | flops 1505280 | bytes 8773632 | tf_op jit(solution)/shard_map/jit(_pad)/pad | solution.py:167
  47.1 3.6 %collective-permute-done.3 = f32[1,1536]{1,0:T(1,128)S(1)} collective-permute-done((f32[1,1536]{1,0:T(1,128)S(1)}, f32[1,1536]{1,0:T(1,128)S(1)}, u32[]{:S(2)}, u32[]{:S(2)}) %collective-permute-start.3) | collective-permute-done | bytes 6176 | tf_op jit(solution)/shard_map/ppermute | solution.py:31
  50.7 3.6 %collective-permute-start.4 = (f32[1,1536]{1,0:T(1,128)S(1)}, f32[1,1536]{1,0:T(1,128)S(1)}, u32[]{:S(2)}, u32[]{:S(2)}) collective-permute-start(f32[1,1536]{1,0:T(1,128)S(1)} %add.128), channel_id=1, source_target_pairs={{0,4},{1,5},{2,6},{3,7},{4,0},{5,1},{6,2},{7,3},{8,12},{9,13},{10,... | collective-permute-start | bytes 18440 | tf_op jit(solution)/shard_map/ppermute | solution.py:31
  54.3 1.6 collective-permute-done.4
  56.0 3.7 %collective-permute-start.5 = (f32[1,1536]{1,0:T(1,128)S(1)}, f32[1,1536]{1,0:T(1,128)S(1)}, u32[]{:S(2)}, u32[]{:S(2)}) collective-permute-start(f32[1,1536]{1,0:T(1,128)S(1)} %add.129), channel_id=1, source_target_pairs={{0,8},{1,9},{2,10},{3,11},{4,12},{5,13},{6,14},{7,15},{8,0},{9,1},... | collective-permute-start | bytes 18440 | tf_op jit(solution)/shard_map/ppermute | solution.py:31
  59.7 3.9 %collective-permute-done.5 = f32[1,1536]{1,0:T(1,128)S(1)} collective-permute-done((f32[1,1536]{1,0:T(1,128)S(1)}, f32[1,1536]{1,0:T(1,128)S(1)}, u32[]{:S(2)}, u32[]{:S(2)}) %collective-permute-start.5) | collective-permute-done | bytes 6176 | tf_op jit(solution)/shard_map/ppermute | solution.py:31
  63.6 1.3 collective-permute-start.6
  64.9 3.9 %collective-permute-done.6 = f32[1,1536]{1,0:T(1,128)S(1)} collective-permute-done((f32[1,1536]{1,0:T(1,128)S(1)}, f32[1,1536]{1,0:T(1,128)S(1)}, u32[]{:S(2)}, u32[]{:S(2)}) %collective-permute-start.6) | collective-permute-done | bytes 6176 | tf_op jit(solution)/shard_map/ppermute | solution.py:31
  69.1 1.3 collective-permute-start.7
  70.4 3.7 %collective-permute-done.7 = f32[8,2560]{1,0:T(8,128)S(1)} collective-permute-done((f32[8,2560]{1,0:T(8,128)S(1)}, f32[8,2560]{1,0:T(8,128)S(1)}, u32[]{:S(2)}, u32[]{:S(2)}) %collective-permute-start.7) | collective-permute-done | bytes 81952 | tf_op jit(solution)/shard_map/ppermute | solution.py:31
  74.9 5.5 %collective-permute-done.8 = f32[8,2560]{1,0:T(8,128)S(1)} collective-permute-done((f32[8,2560]{1,0:T(8,128)S(1)}, f32[8,2560]{1,0:T(8,128)S(1)}, u32[]{:S(2)}, u32[]{:S(2)}) %collective-permute-start.8) | collective-permute-done | bytes 81952 | tf_op jit(solution)/shard_map/ppermute | solution.py:31
  80.4 1.0 collective-permute-start.9
  81.4 0.8 convert_element_type.20.k_ref
  82.8 2.3 %collective-permute-done.9 = f32[8,2560]{1,0:T(8,128)S(1)} collective-permute-done((f32[8,2560]{1,0:T(8,128)S(1)}, f32[8,2560]{1,0:T(8,128)S(1)}, u32[]{:S(2)}, u32[]{:S(2)}) %collective-permute-start.9) | collective-permute-done | bytes 81952 | tf_op jit(solution)/shard_map/ppermute | solution.py:31
  85.3 1.4 multiply_reduce_fusion.5
  86.7 0.6 dynamic-slice.2
  87.9 0.7 subtract_reduce_fusion
  89.6 3.8 %convolution_reduce_fusion = f32[1536]{0:T(1024)S(1)} fusion(bf16[1536,1024]{1,0:T(8,128)(2,1)S(1)} %copy-done, f32[8,1024]{1,0:T(8,128)S(1)} %get-tuple-element.39, s32[]{:T(128)S(6)} %select_n.97, f32[8,1024]{1,0:T(8,128)S(1)} %get-tuple-element.43, f32[1]{0:T(128)} %dynamic-slice.2, f32[1]{0:T(128)} %dynamic-slice.1), kind=kOutput, calls=%fused_computation.19 | convolution fusion | flops 18877440 | bytes 3160076 | tf_op jit(solution)/shard_map/dot_general | solution.py:215
  93.4 0.6 fusion.25
  94.0 0.7 multiply_reduce_fusion
  95.4 2.7 %subtract_multiply_fusion = f32[1,8,64,1536]{3,2,1,0:T(8,128)S(1)} fusion(f32[1,8,64,1536]{3,0,2,1:T(1,128)} %copy-done.1, f32[8,64]{1,0:T(8,128)S(1)} %broadcast_multiply_fusion, f32[1536]{0:T(1024)S(1)} %broadcast_subtract_fusion, f32[8,64]{1,0:T(8,128)S(1)} %add_rsqrt_fusion, f32[8,64]{1,0:T(8,128)S(1)} %broadcast_multiply_fusion.1, f32[1536]{0:T(1024)S(1)} %copy-done.8), kind=kLoop, calls=%fused_computation.9 | loop fusion | flops 4718592 | bytes 6309888 | tf_op jit(solution)/shard_map/mul | solution.py:219
  98.1 1.6 fusion.26
  99.7 2.2 %collective-permute-start.12 = (f32[1,3,64,1536]{3,2,1,0:T(8,128)}, f32[1,3,64,1536]{3,2,1,0:T(8,128)}, u32[]{:S(2)}, u32[]{:S(2)}) collective-permute-start(f32[1,3,64,1536]{3,2,1,0:T(8,128)} %get-tuple-element.32), channel_id=1, source_target_pairs={{1,0},{2,1},{3,2},{4,3},{5,4},{6,5},{7,6},{8,7},{9,8},{10,9},{11,1... | collective-permute-start | bytes 3538952 | tf_op jit(solution)/shard_map/ppermute | solution.py:16
  101.9 2.4 %collective-permute-start.11 = (f32[1,3,64,1536]{3,2,1,0:T(8,128)}, f32[1,3,64,1536]{3,2,1,0:T(8,128)}, u32[]{:S(2)}, u32[]{:S(2)}) collective-permute-start(f32[1,3,64,1536]{3,2,1,0:T(8,128)} %get-tuple-element.31), channel_id=1, source_target_pairs={{0,1},{1,2},{2,3},{3,4},{4,5},{5,6},{6,7},{7,8},{8,9},{9,10},{10,1... | collective-permute-start | bytes 3538952 | tf_op jit(solution)/shard_map/ppermute | solution.py:13
  104.3 2.5 %fusion.34.g_ref = f32[8,64,1536]{2,1,0:T(8,128)} fusion(f32[8,64]{1,0:T(8,128)S(1)} %broadcast_multiply_fusion, f32[8,64]{1,0:T(8,128)S(1)} %broadcast_multiply_fusion.1, f32[1536]{0:T(1024)S(1)} %copy-done.8, f32[1,8,64,1536]{3,0,2,1:T(1,128)S(1)} %copy-done.3, f32[1536]{0:T(1024)S(1)} %broadcast_subtract_fusion, f32[8,64]{1,0:T(8,128)S(1)} %add_rsqrt_fusion), kind=kLoop, calls=%fused_computation.81 | loop fusion | flops 4718592 | bytes 6309888 | tf_op jit(solution)/shard_map/squeeze | solution.py:228
  106.8 14.7 %shard_map.111 = f32[7,7,1536]{2,1,0:T(8,128)} custom-call(f32[8,64,1536]{2,1,0:T(8,128)} %fusion.34.g_ref, f32[14,70,1536]{2,1,0:T(8,128)} %bitcast.22), custom_call_target="tpu_custom_call" | custom-call | tf_op jit(solution)/shard_map/pallas_call | solution.py:118
  121.4 1.0 reshape.150
  122.5 0.7 slice_select_fusion
  123.1 1.4 collective-permute-start.10
  124.5 4.7 %fusion.x_ref = f32[14,70,1536]{2,1,0:T(8,128)} fusion(f32[1,3,64,1536]{3,2,1,0:T(8,128)} %collective-permute-done.12, f32[1,8,64,1536]{3,2,1,0:T(8,128)} %copy-done.4, f32[1,3,64,1536]{3,2,1,0:T(8,128)} %collective-permute-done.11), kind=kLoop, calls=%fused_computation.3 | loop fusion | flops 12042240 | bytes 11526144 | tf_op jit(solution)/shard_map/squeeze | solution.py:225
  129.2 7.5 %shard_map.112 = bf16[8,64,768]{2,1,0:T(8,128)(2,1)} custom-call(f32[14,70,1536]{2,1,0:T(8,128)} %fusion.x_ref, f32[7,7,1536]{2,1,0:T(8,128)} %convert_element_type.20.k_ref), custom_call_target="tpu_custom_call" | custom-call | tf_op jit(solution)/shard_map/pallas_call | solution.py:143
  136.7 0.9 select_add_fusion
  137.7 0.7 copy-done.6
  138.3 0.6 slice_select_fusion.1
  139.0 1.5 collective-permute-start.13
  141.4 0.6 dynamic-slice.3
  142.0 7.6 %shard_map.113 = bf16[8,64,768]{2,1,0:T(8,128)(2,1)} custom-call(f32[14,70,1536]{2,1,0:T(8,128)} %fusion.x_ref, f32[7,7,1536]{2,1,0:T(8,128)} %convert_element_type.20.k_ref), custom_call_target="tpu_custom_call" | custom-call | tf_op jit(solution)/shard_map/pallas_call | solution.py:143
  149.7 1.8 collective-permute-start.14
  151.5 1.9 fusion.8
  153.4 1.7 collective-permute-done.14
  155.2 1.7 collective-permute-start.15
  156.9 6.3 %collective-permute-done.15 = f32[9408]{0:T(1024)S(1)} collective-permute-done((f32[9408]{0:T(1024)S(1)}, f32[9408]{0:T(1024)S(1)}, u32[]{:S(2)}, u32[]{:S(2)}) %collective-permute-start.15) | collective-permute-done | bytes 37664 | tf_op jit(solution)/shard_map/ppermute | solution.py:72
  163.2 1.7 collective-permute-start.16
  164.9 3.8 %collective-permute-done.16 = f32[9408]{0:T(1024)S(1)} collective-permute-done((f32[9408]{0:T(1024)S(1)}, f32[9408]{0:T(1024)S(1)}, u32[]{:S(2)}, u32[]{:S(2)}) %collective-permute-start.16) | collective-permute-done | bytes 37664 | tf_op jit(solution)/shard_map/ppermute | solution.py:72
  168.7 1.1 collective-permute-start.17
  169.8 3.0 %collective-permute-done.17 = f32[9408]{0:T(1024)S(1)} collective-permute-done((f32[9408]{0:T(1024)S(1)}, f32[9408]{0:T(1024)S(1)}, u32[]{:S(2)}, u32[]{:S(2)}) %collective-permute-start.17) | collective-permute-done | bytes 37664 | tf_op jit(solution)/shard_map/ppermute | solution.py:72
  172.7 1.0 collective-permute-start.18
  173.7 4.5 %collective-permute-done.18 = f32[9408]{0:T(1024)S(1)} collective-permute-done((f32[9408]{0:T(1024)S(1)}, f32[9408]{0:T(1024)S(1)}, u32[]{:S(2)}, u32[]{:S(2)}) %collective-permute-start.18) | collective-permute-done | bytes 37664 | tf_op jit(solution)/shard_map/ppermute | solution.py:72
  178.3 1.2 collective-permute-start.19
  179.4 2.8 %collective-permute-done.19 = f32[9408]{0:T(1024)S(1)} collective-permute-done((f32[9408]{0:T(1024)S(1)}, f32[9408]{0:T(1024)S(1)}, u32[]{:S(2)}, u32[]{:S(2)}) %collective-permute-start.19) | collective-permute-done | bytes 37664 | tf_op jit(solution)/shard_map/ppermute | solution.py:72
  182.3 1.3 collective-permute-start.20
  183.5 3.6 %collective-permute-done.20 = f32[9408]{0:T(1024)S(1)} collective-permute-done((f32[9408]{0:T(1024)S(1)}, f32[9408]{0:T(1024)S(1)}, u32[]{:S(2)}, u32[]{:S(2)}) %collective-permute-start.20) | collective-permute-done | bytes 37664 | tf_op jit(solution)/shard_map/ppermute | solution.py:76
  187.3 1.2 collective-permute-start.21
  189.7 2.1 %collective-permute-done.21 = f32[18816]{0:T(1024)S(1)} collective-permute-done((f32[18816]{0:T(1024)S(1)}, f32[18816]{0:T(1024)S(1)}, u32[]{:S(2)}, u32[]{:S(2)}) %collective-permute-start.21) | collective-permute-done | bytes 75296 | tf_op jit(solution)/shard_map/ppermute | solution.py:76
  191.9 2.6 %maximum_bitcast_fusion = bf16[1,8,64,1536]{3,2,1,0:T(8,128)(2,1)} fusion(bf16[8,64,768]{2,1,0:T(8,128)(2,1)} %shard_map.113, bf16[8,64,768]{2,1,0:T(8,128)(2,1)} %shard_map.112), kind=kLoop, calls=%fused_computation.16 | loop fusion | flops 3145728 | bytes 3145728 | tf_op jit(solution)/shard_map/stack | solution.py:237
  194.6 0.8 select_n.118
  (77 shorter events, 5.5 us)
Async XLA Ops:
  0.6 84.6 %copy-start = (bf16[1536,1024]{1,0:T(8,128)(2,1)S(1)}, bf16[1536,1024]{1,0:T(8,128)(2,1)}, u32[]{:S(2)}) copy-start(bf16[1536,1024]{1,0:T(8,128)(2,1)} %param.13) | copy-start | bytes 9437188
  0.6 17.1 %copy-start.5 = (bf16[1,8,64,1536]{3,2,1,0:T(8,128)(2,1)S(1)}, bf16[1,8,64,1536]{3,2,1,0:T(8,128)(2,1)}, u32[]{:S(2)}) copy-start(bf16[1,8,64,1536]{3,2,1,0:T(8,128)(2,1)} %param.8) | copy-start | bytes 4718596
  2.1 17.4 %copy-start.9 = (bf16[7,7,1536]{2,1,0:T(8,128)(2,1)S(1)}, bf16[7,7,1536]{2,1,0:T(8,128)(2,1)}, u32[]{:S(2)}) copy-start(bf16[7,7,1536]{2,1,0:T(8,128)(2,1)} %param.9) | copy-start | bytes 451588
  2.1 15.6 %collective-permute-start = (bf16[1,3,64,1536]{3,2,1,0:T(8,128)(2,1)S(1)}, bf16[1,3,64,1536]{3,2,1,0:T(8,128)(2,1)S(1)}, u32[]{:S(2)}, u32[]{:S(2)}) collective-permute-start(bf16[1,3,64,1536]{3,2,1,0:T(8,128)(2,1)S(1)} %get-tuple-element.34), channel_id=1, source_target_pairs={{0,1},{1,2},{2,3},{3,4},{4,5},{5,6},{6,7},{7,8},{8,9},{9,10},{10,1... | collective-permute-start | bytes 1769480 | tf_op jit(solution)/shard_map/ppermute | solution.py:13
  4.2 15.3 %collective-permute-start.1 = (bf16[1,3,64,1536]{3,2,1,0:T(8,128)(2,1)S(1)}, bf16[1,3,64,1536]{3,2,1,0:T(8,128)(2,1)S(1)}, u32[]{:S(2)}, u32[]{:S(2)}) collective-permute-start(bf16[1,3,64,1536]{3,2,1,0:T(8,128)(2,1)S(1)} %get-tuple-element.33), channel_id=1, source_target_pairs={{1,0},{2,1},{3,2},{4,3},{5,4},{6,5},{7,6},{8,7},{9,8},{10,9},{11,1... | collective-permute-start | bytes 1769480 | tf_op jit(solution)/shard_map/ppermute | solution.py:16
  19.5 21.5 %copy-start.8 = (f32[1536]{0:T(1024)S(1)}, f32[1536]{0:T(1024)}, u32[]{:S(2)}) copy-start(f32[1536]{0:T(1024)} %param.10) | copy-start | bytes 18436
  41.0 1.6 copy-start.1
  41.0 1.6 copy-start.10
  41.0 1.6 copy-start.12
  43.3 25.5 %copy-start.11 = (f32[1,1024]{1,0:T(1,128)S(1)}, f32[1,1024]{1,0:T(1,128)}, u32[]{:S(2)}) copy-start(f32[1,1024]{1,0:T(1,128)} %param.14) | copy-start | bytes 12292
  43.4 3.6 %collective-permute-start.2 = (f32[1,1536]{1,0:T(1,128)S(1)}, f32[1,1536]{1,0:T(1,128)S(1)}, u32[]{:S(2)}, u32[]{:S(2)}) collective-permute-start(f32[1,1536]{1,0:T(1,128)S(1)} %reduce_sum.131), channel_id=1, source_target_pairs={{0,1},{1,0},{2,3},{3,2},{4,5},{5,4},{6,7},{7,6},{8,9},{9,8},{10,11... | collective-permute-start | bytes 18440 | tf_op jit(solution)/shard_map/ppermute | solution.py:31
  47.0 3.7 %collective-permute-start.3 = (f32[1,1536]{1,0:T(1,128)S(1)}, f32[1,1536]{1,0:T(1,128)S(1)}, u32[]{:S(2)}, u32[]{:S(2)}) collective-permute-start(f32[1,1536]{1,0:T(1,128)S(1)} %reshape_add_fusion), channel_id=1, source_target_pairs={{0,2},{1,3},{2,0},{3,1},{4,6},{5,7},{6,4},{7,5},{8,10},{9,11},{10,... | collective-permute-start | bytes 18440 | tf_op jit(solution)/shard_map/ppermute | solution.py:31
  50.7 5.2 %collective-permute-start.4 = (f32[1,1536]{1,0:T(1,128)S(1)}, f32[1,1536]{1,0:T(1,128)S(1)}, u32[]{:S(2)}, u32[]{:S(2)}) collective-permute-start(f32[1,1536]{1,0:T(1,128)S(1)} %add.128), channel_id=1, source_target_pairs={{0,4},{1,5},{2,6},{3,7},{4,0},{5,1},{6,2},{7,3},{8,12},{9,13},{10,... | collective-permute-start | bytes 18440 | tf_op jit(solution)/shard_map/ppermute | solution.py:31
  56.0 7.6 %collective-permute-start.5 = (f32[1,1536]{1,0:T(1,128)S(1)}, f32[1,1536]{1,0:T(1,128)S(1)}, u32[]{:S(2)}, u32[]{:S(2)}) collective-permute-start(f32[1,1536]{1,0:T(1,128)S(1)} %add.129), channel_id=1, source_target_pairs={{0,8},{1,9},{2,10},{3,11},{4,12},{5,13},{6,14},{7,15},{8,0},{9,1},... | collective-permute-start | bytes 18440 | tf_op jit(solution)/shard_map/ppermute | solution.py:31
  63.6 5.2 %collective-permute-start.6 = (f32[1,1536]{1,0:T(1,128)S(1)}, f32[1,1536]{1,0:T(1,128)S(1)}, u32[]{:S(2)}, u32[]{:S(2)}) collective-permute-start(f32[1,1536]{1,0:T(1,128)S(1)} %add.130), channel_id=1, source_target_pairs={{0,16},{1,17},{2,18},{3,19},{4,20},{5,21},{6,22},{7,23},{8,24},{9,... | collective-permute-start | bytes 18440 | tf_op jit(solution)/shard_map/ppermute | solution.py:31
  69.1 4.9 %collective-permute-start.7 = (f32[8,2560]{1,0:T(8,128)S(1)}, f32[8,2560]{1,0:T(8,128)S(1)}, u32[]{:S(2)}, u32[]{:S(2)}) collective-permute-start(f32[8,2560]{1,0:T(8,128)S(1)} %dynamic_update_slice.5), channel_id=1, source_target_pairs={{0,32},{32,0},{64,96},{96,64},{128,160},{160,128},{192,224},{224,1... | collective-permute-start | bytes 245768 | tf_op jit(solution)/shard_map/ppermute | solution.py:31
  74.4 6.0 %collective-permute-start.8 = (f32[8,2560]{1,0:T(8,128)S(1)}, f32[8,2560]{1,0:T(8,128)S(1)}, u32[]{:S(2)}, u32[]{:S(2)}) collective-permute-start(f32[8,2560]{1,0:T(8,128)S(1)} %add.133), channel_id=1, source_target_pairs={{0,64},{32,96},{64,0},{96,32},{128,192},{160,224},{192,128},{224,1... | collective-permute-start | bytes 245768 | tf_op jit(solution)/shard_map/ppermute | solution.py:31
  80.4 4.7 %collective-permute-start.9 = (f32[8,2560]{1,0:T(8,128)S(1)}, f32[8,2560]{1,0:T(8,128)S(1)}, u32[]{:S(2)}, u32[]{:S(2)}) collective-permute-start(f32[8,2560]{1,0:T(8,128)S(1)} %add.134), channel_id=1, source_target_pairs={{0,128},{32,160},{64,192},{96,224},{128,0},{160,32},{192,64},{224,... | collective-permute-start | bytes 245768 | tf_op jit(solution)/shard_map/ppermute | solution.py:31
  85.3 8.8 %copy-start.2 = (f32[1,8,64,1536]{3,0,2,1:T(1,128)S(1)}, f32[1,8,64,1536]{3,0,2,1:T(1,128)}, u32[]{:S(2)}) copy-start(f32[1,8,64,1536]{3,0,2,1:T(1,128)} %copy-done.1) | copy-start | bytes 9437188
  98.1 8.7 %copy-start.4 = (f32[1,8,64,1536]{3,2,1,0:T(8,128)}, f32[1,8,64,1536]{3,2,1,0:T(8,128)S(1)}, u32[]{:S(2)}) copy-start(f32[1,8,64,1536]{3,2,1,0:T(8,128)S(1)} %subtract_multiply_fusion) | copy-start | bytes 9437188
  98.1 6.2 %copy-start.3 = (f32[1,8,64,1536]{3,0,2,1:T(1,128)S(1)}, f32[1,8,64,1536]{3,0,2,1:T(1,128)}, u32[]{:S(2)}) copy-start(f32[1,8,64,1536]{3,0,2,1:T(1,128)} %copy-done.1) | copy-start | bytes 9437188
  99.7 24.8 %collective-permute-start.12 = (f32[1,3,64,1536]{3,2,1,0:T(8,128)}, f32[1,3,64,1536]{3,2,1,0:T(8,128)}, u32[]{:S(2)}, u32[]{:S(2)}) collective-permute-start(f32[1,3,64,1536]{3,2,1,0:T(8,128)} %get-tuple-element.32), channel_id=1, source_target_pairs={{1,0},{2,1},{3,2},{4,3},{5,4},{6,5},{7,6},{8,7},{9,8},{10,9},{11,1... | collective-permute-start | bytes 3538952 | tf_op jit(solution)/shard_map/ppermute | solution.py:16
  101.9 22.6 %collective-permute-start.11 = (f32[1,3,64,1536]{3,2,1,0:T(8,128)}, f32[1,3,64,1536]{3,2,1,0:T(8,128)}, u32[]{:S(2)}, u32[]{:S(2)}) collective-permute-start(f32[1,3,64,1536]{3,2,1,0:T(8,128)} %get-tuple-element.31), channel_id=1, source_target_pairs={{0,1},{1,2},{2,3},{3,4},{4,5},{5,6},{6,7},{7,8},{8,9},{9,10},{10,1... | collective-permute-start | bytes 3538952 | tf_op jit(solution)/shard_map/ppermute | solution.py:13
  123.1 13.6 %collective-permute-start.10 = (f32[37632]{0:T(1024)}, f32[37632]{0:T(1024)}, u32[]{:S(2)}, u32[]{:S(2)}) collective-permute-start(f32[37632]{0:T(1024)} %slice_select_fusion), channel_id=1, source_target_pairs={{0,1},{1,0},{2,3},{3,2},{4,5},{5,4},{6,7},{7,6},{8,9},{9,8},{10,11... | collective-permute-start | bytes 451592 | tf_op jit(solution)/shard_map/ppermute | solution.py:65
  137.7 0.7 copy-start.6
  139.0 10.6 %collective-permute-start.13 = (f32[18816]{0:T(1024)}, f32[18816]{0:T(1024)S(1)}, u32[]{:S(2)}, u32[]{:S(2)}) collective-permute-start(f32[18816]{0:T(1024)} %slice_select_fusion.1), channel_id=1, source_target_pairs={{0,2},{1,3},{2,0},{3,1},{4,6},{5,7},{6,4},{7,5},{8,10},{9,11},{10,... | collective-permute-start | bytes 225800 | tf_op jit(solution)/shard_map/ppermute | solution.py:65
  142.0 7.6 %copy-start.7 = (f32[37632]{0:T(1024)S(1)}, f32[37632]{0:T(1024)}, u32[]{:S(2)}) copy-start(f32[37632]{0:T(1024)} %copy-done.6) | copy-start | bytes 451588
  149.7 5.4 %collective-permute-start.14 = (f32[9408]{0:T(1024)S(1)}, f32[9408]{0:T(1024)S(1)}, u32[]{:S(2)}, u32[]{:S(2)}) collective-permute-start(f32[9408]{0:T(1024)S(1)} %slice_select_fusion.2), channel_id=1, source_target_pairs={{0,4},{1,5},{2,6},{3,7},{4,0},{5,1},{6,2},{7,3},{8,12},{9,13},{10,... | collective-permute-start | bytes 112904 | tf_op jit(solution)/shard_map/ppermute | solution.py:65
  155.2 8.0 %collective-permute-start.15 = (f32[9408]{0:T(1024)S(1)}, f32[9408]{0:T(1024)S(1)}, u32[]{:S(2)}, u32[]{:S(2)}) collective-permute-start(f32[9408]{0:T(1024)S(1)} %select_add_fusion.2), channel_id=1, source_target_pairs={{0,8},{1,9},{2,10},{3,11},{4,12},{5,13},{6,14},{7,15},{8,0},{9,1},... | collective-permute-start | bytes 112904 | tf_op jit(solution)/shard_map/ppermute | solution.py:72
  163.2 5.5 %collective-permute-start.16 = (f32[9408]{0:T(1024)S(1)}, f32[9408]{0:T(1024)S(1)}, u32[]{:S(2)}, u32[]{:S(2)}) collective-permute-start(f32[9408]{0:T(1024)S(1)} %add.146), channel_id=1, source_target_pairs={{0,16},{1,17},{2,18},{3,19},{4,20},{5,21},{6,22},{7,23},{8,24},{9,... | collective-permute-start | bytes 112904 | tf_op jit(solution)/shard_map/ppermute | solution.py:72
  168.7 4.0 %collective-permute-start.17 = (f32[9408]{0:T(1024)S(1)}, f32[9408]{0:T(1024)S(1)}, u32[]{:S(2)}, u32[]{:S(2)}) collective-permute-start(f32[9408]{0:T(1024)S(1)} %add.147), channel_id=1, source_target_pairs={{0,32},{32,0},{64,96},{96,64},{128,160},{160,128},{192,224},{224,1... | collective-permute-start | bytes 112904 | tf_op jit(solution)/shard_map/ppermute | solution.py:72
  172.7 5.5 %collective-permute-start.18 = (f32[9408]{0:T(1024)S(1)}, f32[9408]{0:T(1024)S(1)}, u32[]{:S(2)}, u32[]{:S(2)}) collective-permute-start(f32[9408]{0:T(1024)S(1)} %add.148), channel_id=1, source_target_pairs={{0,64},{32,96},{64,0},{96,32},{128,192},{160,224},{192,128},{224,1... | collective-permute-start | bytes 112904 | tf_op jit(solution)/shard_map/ppermute | solution.py:72
  178.3 4.0 %collective-permute-start.19 = (f32[9408]{0:T(1024)S(1)}, f32[9408]{0:T(1024)S(1)}, u32[]{:S(2)}, u32[]{:S(2)}) collective-permute-start(f32[9408]{0:T(1024)S(1)} %add.149), channel_id=1, source_target_pairs={{0,128},{32,160},{64,192},{96,224},{128,0},{160,32},{192,64},{224,... | collective-permute-start | bytes 112904 | tf_op jit(solution)/shard_map/ppermute | solution.py:72
  182.3 4.9 %collective-permute-start.20 = (f32[9408]{0:T(1024)S(1)}, f32[9408]{0:T(1024)S(1)}, u32[]{:S(2)}, u32[]{:S(2)}) collective-permute-start(f32[9408]{0:T(1024)S(1)} %add.150), channel_id=1, source_target_pairs={{0,4},{1,5},{2,6},{3,7},{4,0},{5,1},{6,2},{7,3},{8,12},{9,13},{10,... | collective-permute-start | bytes 112904 | tf_op jit(solution)/shard_map/ppermute | solution.py:76
  187.3 4.5 %collective-permute-start.21 = (f32[18816]{0:T(1024)S(1)}, f32[18816]{0:T(1024)S(1)}, u32[]{:S(2)}, u32[]{:S(2)}) collective-permute-start(f32[18816]{0:T(1024)S(1)} %maximum_select_fusion.2), channel_id=1, source_target_pairs={{0,2},{1,3},{2,0},{3,1},{4,6},{5,7},{6,4},{7,5},{8,10},{9,11},{10,... | collective-permute-start | bytes 225800 | tf_op jit(solution)/shard_map/ppermute | solution.py:76
  191.8 2.7 %collective-permute-start.22 = (f32[37632]{0:T(1024)S(1)}, f32[37632]{0:T(1024)S(1)}, u32[]{:S(2)}, u32[]{:S(2)}) collective-permute-start(f32[37632]{0:T(1024)S(1)} %maximum_select_fusion.1), channel_id=1, source_target_pairs={{0,1},{1,0},{2,3},{3,2},{4,5},{5,4},{6,7},{7,6},{8,9},{9,8},{10,11... | collective-permute-start | bytes 451592 | tf_op jit(solution)/shard_map/ppermute | solution.py:76

commit v9 on v6

--- a/solution.py
+++ b/solution.py
@@ -220,7 +220,8 @@
     grad_wide = with_halo(grad_own, (("space", 1),), reach_rows)
     grad_pad = jnp.pad(grad_wide, ((0, 0), (0, 0), (reach_rows, reach_rows), (0, 0)))
     blocks = channels // 128
-    halves = ((0, blocks // 2), (blocks // 2, blocks - blocks // 2))
+    cuts = [blocks * k // 3 for k in range(4)]
+    halves = [(cuts[k], cuts[k + 1] - cuts[k]) for k in range(3)]
     input_parts = [
         [input_terms(grad_pad[image], kernel_float, row_count, *half) for image in range(batch_dev)]
         for half in halves

time: 198 us -> 197 us (level)
  waiting for transfers between devices: 58.7 us -> 54.6 us
    ppermute x3, waiting for transfers between devices: 3.63 us -> 0.01 us  [halving_sum(): received = lax.ppermute(give, axis, pairs)]
    pallas_call x2 -> x3, Pallas kernels: 15.1 us -> 16.6 us  [input_terms(): pl.pallas_call(body, grid=(block_count,), in_specs=[pl.BlockSpec(padded.s...]
  transfers between devices with their start and end apart: 23 -> 23, of which waited for: 17 -> 16; matrix products, arithmetic and copies ran while one was open for 10% -> 10% of each run, Pallas kernels for 15% -> 16%
where the time goes in v9:
time: 197 us; the launch traced here: 194 us
  waiting for transfers between devices  54.6 us (28%)
  starting transfers between devices  40.5 us (21%)
  Pallas kernels  31.3 us (16%)
  matrix products  27.7 us (14%)
  other arithmetic  25.4 us (13%)
  local copies, waits for them, and re-layouts  9.38 us (5%)
  between operations  4.73 us (2%)
    ppermute x8, waiting for transfers between devices, butterfly_sum(): received = lax.ppermute(values, axis, pairs)  24.5 us
    conv_general_dilated x1, matrix products, depthwise(): lax.conv_general_dilated(extended, kernel.reshape(kernel.shape[0], kernel...  21.5 us
    ppermute x5, waiting for transfers between devices, halving_sum(): chunk = chunk + lax.ppermute(chunk, axis, pairs)  21 us
    pallas_call x3, Pallas kernels, input_terms(): pl.pallas_call(body, grid=(block_count,), in_specs=[pl.BlockSpec(padded.s...  16.6 us
    pallas_call x1, Pallas kernels, kernel_terms(): pl.pallas_call(body, grid=(channels // lanes,), in_specs=[pl.BlockSpec((r...  14.7 us
    ppermute x8, starting transfers between devices, butterfly_sum(): received = lax.ppermute(values, axis, pairs)  11.6 us
    ppermute x2, starting transfers between devices, with_halo(): lax.ppermute(lax.slice_in_dim(block, 0, width, axis=dim), axis, backward)  10 us
    ppermute x5, starting transfers between devices, halving_sum(): chunk = chunk + lax.ppermute(chunk, axis, pairs)  6.46 us
  transfers between devices with their start and end apart: 23, of which 16 were waited for; matrix products, arithmetic and copies ran while one was open for 10% of the time, Pallas kernels for 16%

profile of v9, /device:TPU:28, one launch (start us, length us, event | category | flops | bytes accessed | tf_op | source)
XLA Modules:
  0.0 193.6 jit_solution(15597102948374647874)
XLA Ops:
  0.7 1.5 fusion.28
  2.1 2.1 %collective-permute-start = (bf16[1,3,64,1536]{3,2,1,0:T(8,128)(2,1)S(1)}, bf16[1,3,64,1536]{3,2,1,0:T(8,128)(2,1)S(1)}, u32[]{:S(2)}, u32[]{:S(2)}) collective-permute-start(bf16[1,3,64,1536]{3,2,1,0:T(8,128)(2,1)S(1)} %get-tuple-element.34), channel_id=1, source_target_pairs={{0,1},{1,2},{2,3},{3,4},{4,5},{5,6},{6,7},{7,8},{8,9},{9,10},{10,1... | collective-permute-start | bytes 1769480 | tf_op jit(solution)/shard_map/ppermute | solution.py:13
  4.2 7.9 %collective-permute-start.1 = (bf16[1,3,64,1536]{3,2,1,0:T(8,128)(2,1)S(1)}, bf16[1,3,64,1536]{3,2,1,0:T(8,128)(2,1)S(1)}, u32[]{:S(2)}, u32[]{:S(2)}) collective-permute-start(bf16[1,3,64,1536]{3,2,1,0:T(8,128)(2,1)S(1)} %get-tuple-element.33), channel_id=1, source_target_pairs={{1,0},{2,1},{3,2},{4,3},{5,4},{6,5},{7,6},{8,7},{9,8},{10,9},{11,1... | collective-permute-start | bytes 1769480 | tf_op jit(solution)/shard_map/ppermute | solution.py:16
  12.1 5.6 %collective-permute-done = bf16[1,3,64,1536]{3,2,1,0:T(8,128)(2,1)S(1)} collective-permute-done((bf16[1,3,64,1536]{3,2,1,0:T(8,128)(2,1)S(1)}, bf16[1,3,64,1536]{3,2,1,0:T(8,128)(2,1)S(1)}, u32[]{:S(2)}, u32[]{:S(2)}) %collective-permute-start) | collective-permute-done | bytes 589856 | tf_op jit(solution)/shard_map/ppermute | solution.py:13
  17.9 1.6 collective-permute-done.1
  19.5 21.5 %fusion.2 = f32[1,8,64,1536]{3,0,2,1:T(1,128)S(1)} fusion(bf16[1,14,64,1536]{3,2,1,0:T(8,128)(2,1)S(1)} %constant_dynamic-update-slice_fusion, bf16[7,7,1,1536]{3,1,0,2:T(8,128)(2,1)S(1)} %bitcast.23), kind=kOutput, calls=%fused_computation.6 | convolution fusion | flops 75005952 | bytes 6048768 | tf_op jit(solution)/shard_map/conv_general_dilated | solution.py:93
  41.9 0.8 copy-done.1
  42.6 0.7 add_reduce_fusion
  43.5 3.5 %pad_convert_fusion = f32[1,14,70,1536]{3,2,1,0:T(8,128)} fusion(bf16[1,14,64,1536]{3,2,1,0:T(8,128)(2,1)S(1)} %constant_dynamic-update-slice_fusion), kind=kLoop, calls=%fused_computation.13 | loop fusion | flops 1505280 | bytes 8773632 | tf_op jit(solution)/shard_map/jit(_pad)/pad | solution.py:167
  47.1 3.6 %collective-permute-done.3 = f32[1,1536]{1,0:T(1,128)S(1)} collective-permute-done((f32[1,1536]{1,0:T(1,128)S(1)}, f32[1,1536]{1,0:T(1,128)S(1)}, u32[]{:S(2)}, u32[]{:S(2)}) %collective-permute-start.3) | collective-permute-done | bytes 6176 | tf_op jit(solution)/shard_map/ppermute | solution.py:31
  50.7 3.6 %collective-permute-start.4 = (f32[1,1536]{1,0:T(1,128)S(1)}, f32[1,1536]{1,0:T(1,128)S(1)}, u32[]{:S(2)}, u32[]{:S(2)}) collective-permute-start(f32[1,1536]{1,0:T(1,128)S(1)} %add.128), channel_id=1, source_target_pairs={{0,4},{1,5},{2,6},{3,7},{4,0},{5,1},{6,2},{7,3},{8,12},{9,13},{10,... | collective-permute-start | bytes 18440 | tf_op jit(solution)/shard_map/ppermute | solution.py:31
  54.3 1.6 collective-permute-done.4
  56.0 3.7 %collective-permute-start.5 = (f32[1,1536]{1,0:T(1,128)S(1)}, f32[1,1536]{1,0:T(1,128)S(1)}, u32[]{:S(2)}, u32[]{:S(2)}) collective-permute-start(f32[1,1536]{1,0:T(1,128)S(1)} %add.129), channel_id=1, source_target_pairs={{0,8},{1,9},{2,10},{3,11},{4,12},{5,13},{6,14},{7,15},{8,0},{9,1},... | collective-permute-start | bytes 18440 | tf_op jit(solution)/shard_map/ppermute | solution.py:31
  59.7 3.9 %collective-permute-done.5 = f32[1,1536]{1,0:T(1,128)S(1)} collective-permute-done((f32[1,1536]{1,0:T(1,128)S(1)}, f32[1,1536]{1,0:T(1,128)S(1)}, u32[]{:S(2)}, u32[]{:S(2)}) %collective-permute-start.5) | collective-permute-done | bytes 6176 | tf_op jit(solution)/shard_map/ppermute | solution.py:31
  63.6 1.3 collective-permute-start.6
  64.9 3.9 %collective-permute-done.6 = f32[1,1536]{1,0:T(1,128)S(1)} collective-permute-done((f32[1,1536]{1,0:T(1,128)S(1)}, f32[1,1536]{1,0:T(1,128)S(1)}, u32[]{:S(2)}, u32[]{:S(2)}) %collective-permute-start.6) | collective-permute-done | bytes 6176 | tf_op jit(solution)/shard_map/ppermute | solution.py:31
  69.1 1.3 collective-permute-start.7
  70.4 3.7 %collective-permute-done.7 = f32[8,2560]{1,0:T(8,128)S(1)} collective-permute-done((f32[8,2560]{1,0:T(8,128)S(1)}, f32[8,2560]{1,0:T(8,128)S(1)}, u32[]{:S(2)}, u32[]{:S(2)}) %collective-permute-start.7) | collective-permute-done | bytes 81952 | tf_op jit(solution)/shard_map/ppermute | solution.py:31
  74.9 5.5 %collective-permute-done.8 = f32[8,2560]{1,0:T(8,128)S(1)} collective-permute-done((f32[8,2560]{1,0:T(8,128)S(1)}, f32[8,2560]{1,0:T(8,128)S(1)}, u32[]{:S(2)}, u32[]{:S(2)}) %collective-permute-start.8) | collective-permute-done | bytes 81952 | tf_op jit(solution)/shard_map/ppermute | solution.py:31
  80.4 1.0 collective-permute-start.9
  81.4 0.8 convert_element_type.20.k_ref
  82.8 2.3 %collective-permute-done.9 = f32[8,2560]{1,0:T(8,128)S(1)} collective-permute-done((f32[8,2560]{1,0:T(8,128)S(1)}, f32[8,2560]{1,0:T(8,128)S(1)}, u32[]{:S(2)}, u32[]{:S(2)}) %collective-permute-start.9) | collective-permute-done | bytes 81952 | tf_op jit(solution)/shard_map/ppermute | solution.py:31
  85.3 1.4 multiply_reduce_fusion.5
  86.7 0.6 dynamic-slice.2
  87.9 0.6 subtract_reduce_fusion
  89.5 3.7 %convolution_reduce_fusion = f32[1536]{0:T(1024)S(1)} fusion(bf16[1536,1024]{1,0:T(8,128)(2,1)S(1)} %copy-done, f32[8,1024]{1,0:T(8,128)S(1)} %get-tuple-element.39, s32[]{:T(128)S(6)} %select_n.95, f32[8,1024]{1,0:T(8,128)S(1)} %get-tuple-element.43, f32[1]{0:T(128)} %dynamic-slice.2, f32[1]{0:T(128)} %dynamic-slice.1), kind=kOutput, calls=%fused_computation.19 | convolution fusion | flops 18877440 | bytes 3160076 | tf_op jit(solution)/shard_map/dot_general | solution.py:215
  93.2 0.6 fusion.26
  93.8 0.7 multiply_reduce_fusion
  95.2 2.7 %subtract_multiply_fusion = f32[1,8,64,1536]{3,2,1,0:T(8,128)S(1)} fusion(f32[1,8,64,1536]{3,0,2,1:T(1,128)} %copy-done.1, f32[8,64]{1,0:T(8,128)S(1)} %broadcast_multiply_fusion, f32[1536]{0:T(1024)S(1)} %broadcast_subtract_fusion, f32[8,64]{1,0:T(8,128)S(1)} %add_rsqrt_fusion, f32[8,64]{1,0:T(8,128)S(1)} %broadcast_multiply_fusion.1, f32[1536]{0:T(1024)S(1)} %copy-done.8), kind=kLoop, calls=%fused_computation.9 | loop fusion | flops 4718592 | bytes 6309888 | tf_op jit(solution)/shard_map/mul | solution.py:219
  97.9 1.6 fusion.27
  99.5 2.2 %collective-permute-start.12 = (f32[1,3,64,1536]{3,2,1,0:T(8,128)}, f32[1,3,64,1536]{3,2,1,0:T(8,128)}, u32[]{:S(2)}, u32[]{:S(2)}) collective-permute-start(f32[1,3,64,1536]{3,2,1,0:T(8,128)} %get-tuple-element.32), channel_id=1, source_target_pairs={{1,0},{2,1},{3,2},{4,3},{5,4},{6,5},{7,6},{8,7},{9,8},{10,9},{11,1... | collective-permute-start | bytes 3538952 | tf_op jit(solution)/shard_map/ppermute | solution.py:16
  101.7 2.4 %collective-permute-start.11 = (f32[1,3,64,1536]{3,2,1,0:T(8,128)}, f32[1,3,64,1536]{3,2,1,0:T(8,128)}, u32[]{:S(2)}, u32[]{:S(2)}) collective-permute-start(f32[1,3,64,1536]{3,2,1,0:T(8,128)} %get-tuple-element.31), channel_id=1, source_target_pairs={{0,1},{1,2},{2,3},{3,4},{4,5},{5,6},{6,7},{7,8},{8,9},{9,10},{10,1... | collective-permute-start | bytes 3538952 | tf_op jit(solution)/shard_map/ppermute | solution.py:13
  104.1 2.5 %fusion.35.g_ref = f32[8,64,1536]{2,1,0:T(8,128)} fusion(f32[8,64]{1,0:T(8,128)S(1)} %broadcast_multiply_fusion, f32[8,64]{1,0:T(8,128)S(1)} %broadcast_multiply_fusion.1, f32[1536]{0:T(1024)S(1)} %copy-done.8, f32[1,8,64,1536]{3,0,2,1:T(1,128)S(1)} %copy-done.3, f32[1536]{0:T(1024)S(1)} %broadcast_subtract_fusion, f32[8,64]{1,0:T(8,128)S(1)} %add_rsqrt_fusion), kind=kLoop, calls=%fused_computation.82 | loop fusion | flops 4718592 | bytes 6309888 | tf_op jit(solution)/shard_map/squeeze | solution.py:229
  106.6 14.7 %shard_map.111 = f32[7,7,1536]{2,1,0:T(8,128)} custom-call(f32[8,64,1536]{2,1,0:T(8,128)} %fusion.35.g_ref, f32[14,70,1536]{2,1,0:T(8,128)} %bitcast.22), custom_call_target="tpu_custom_call" | custom-call | tf_op jit(solution)/shard_map/pallas_call | solution.py:118
  121.3 1.0 reshape.152
  122.3 0.7 slice_select_fusion
  123.0 1.4 collective-permute-start.10
  124.4 4.7 %fusion.x_ref = f32[14,70,1536]{2,1,0:T(8,128)} fusion(f32[1,3,64,1536]{3,2,1,0:T(8,128)} %collective-permute-done.12, f32[1,8,64,1536]{3,2,1,0:T(8,128)} %copy-done.4, f32[1,3,64,1536]{3,2,1,0:T(8,128)} %collective-permute-done.11), kind=kLoop, calls=%fused_computation.3 | loop fusion | flops 12042240 | bytes 11526144 | tf_op jit(solution)/shard_map/squeeze | solution.py:226
  129.0 5.5 %shard_map.112 = bf16[8,64,512]{2,1,0:T(8,128)(2,1)} custom-call(f32[14,70,1536]{2,1,0:T(8,128)} %fusion.x_ref, f32[7,7,1536]{2,1,0:T(8,128)} %convert_element_type.20.k_ref), custom_call_target="tpu_custom_call" | custom-call | tf_op jit(solution)/shard_map/pallas_call | solution.py:143
  134.6 0.9 select_add_fusion
  135.5 0.7 copy-done.6
  136.2 1.6 collective-permute-start.13
  137.7 5.5 %shard_map.113 = bf16[8,64,512]{2,1,0:T(8,128)(2,1)} custom-call(f32[14,70,1536]{2,1,0:T(8,128)} %fusion.x_ref, f32[7,7,1536]{2,1,0:T(8,128)} %convert_element_type.20.k_ref), custom_call_target="tpu_custom_call" | custom-call | tf_op jit(solution)/shard_map/pallas_call | solution.py:143
  143.3 0.9 select_add_fusion.1
  144.3 2.0 %collective-permute-start.14 = (f32[9408]{0:T(1024)S(1)}, f32[9408]{0:T(1024)S(1)}, u32[]{:S(2)}, u32[]{:S(2)}) collective-permute-start(f32[9408]{0:T(1024)S(1)} %slice_select_fusion.2), channel_id=1, source_target_pairs={{0,4},{1,5},{2,6},{3,7},{4,0},{5,1},{6,2},{7,3},{8,12},{9,13},{10,... | collective-permute-start | bytes 112904 | tf_op jit(solution)/shard_map/ppermute | solution.py:65
  146.3 5.5 %shard_map.114 = bf16[8,64,512]{2,1,0:T(8,128)(2,1)} custom-call(f32[14,70,1536]{2,1,0:T(8,128)} %fusion.x_ref, f32[7,7,1536]{2,1,0:T(8,128)} %convert_element_type.20.k_ref), custom_call_target="tpu_custom_call" | custom-call | tf_op jit(solution)/shard_map/pallas_call | solution.py:143
  151.9 2.5 %collective-permute-start.15 = (f32[9408]{0:T(1024)S(1)}, f32[9408]{0:T(1024)S(1)}, u32[]{:S(2)}, u32[]{:S(2)}) collective-permute-start(f32[9408]{0:T(1024)S(1)} %select_add_fusion.2), channel_id=1, source_target_pairs={{0,8},{1,9},{2,10},{3,11},{4,12},{5,13},{6,14},{7,15},{8,0},{9,1},... | collective-permute-start | bytes 112904 | tf_op jit(solution)/shard_map/ppermute | solution.py:72
  154.4 5.9 %collective-permute-done.15 = f32[9408]{0:T(1024)S(1)} collective-permute-done((f32[9408]{0:T(1024)S(1)}, f32[9408]{0:T(1024)S(1)}, u32[]{:S(2)}, u32[]{:S(2)}) %collective-permute-start.15) | collective-permute-done | bytes 37664 | tf_op jit(solution)/shard_map/ppermute | solution.py:72
  160.3 1.2 collective-permute-start.16
  161.6 4.3 %collective-permute-done.16 = f32[9408]{0:T(1024)S(1)} collective-permute-done((f32[9408]{0:T(1024)S(1)}, f32[9408]{0:T(1024)S(1)}, u32[]{:S(2)}, u32[]{:S(2)}) %collective-permute-start.16) | collective-permute-done | bytes 37664 | tf_op jit(solution)/shard_map/ppermute | solution.py:72
  165.9 1.2 collective-permute-start.17
  167.1 2.8 %collective-permute-done.17 = f32[9408]{0:T(1024)S(1)} collective-permute-done((f32[9408]{0:T(1024)S(1)}, f32[9408]{0:T(1024)S(1)}, u32[]{:S(2)}, u32[]{:S(2)}) %collective-permute-start.17) | collective-permute-done | bytes 37664 | tf_op jit(solution)/shard_map/ppermute | solution.py:72
  169.9 1.2 collective-permute-start.18
  171.1 4.3 %collective-permute-done.18 = f32[9408]{0:T(1024)S(1)} collective-permute-done((f32[9408]{0:T(1024)S(1)}, f32[9408]{0:T(1024)S(1)}, u32[]{:S(2)}, u32[]{:S(2)}) %collective-permute-start.18) | collective-permute-done | bytes 37664 | tf_op jit(solution)/shard_map/ppermute | solution.py:72
  175.7 3.7 %collective-permute-done.19 = f32[9408]{0:T(1024)S(1)} collective-permute-done((f32[9408]{0:T(1024)S(1)}, f32[9408]{0:T(1024)S(1)}, u32[]{:S(2)}, u32[]{:S(2)}) %collective-permute-start.19) | collective-permute-done | bytes 37664 | tf_op jit(solution)/shard_map/ppermute | solution.py:72
  179.4 1.0 collective-permute-start.20
  180.8 0.6 dynamic-slice.4
  181.4 0.6 dynamic-slice.3
  183.2 1.1 collective-permute-done.20
  184.4 1.8 collective-permute-start.21
  186.2 1.9 fusion.9
  188.1 0.7 collective-permute-done.21
  189.0 2.6 %maximum_bitcast_fusion = bf16[1,8,64,1536]{3,2,1,0:T(8,128)(2,1)} fusion(bf16[8,64,512]{2,1,0:T(8,128)(2,1)} %shard_map.114, bf16[8,64,512]{2,1,0:T(8,128)(2,1)} %shard_map.113, bf16[8,64,512]{2,1,0:T(8,128)(2,1)} %shard_map.112), kind=kLoop, calls=%fused_computation.16 | loop fusion | flops 4718592 | bytes 3145728 | tf_op jit(solution)/shard_map/stack | solution.py:233
  191.7 0.8 div.96
  (78 shorter events, 5.2 us)
Async XLA Ops:
  0.6 84.6 %copy-start = (bf16[1536,1024]{1,0:T(8,128)(2,1)S(1)}, bf16[1536,1024]{1,0:T(8,128)(2,1)}, u32[]{:S(2)}) copy-start(bf16[1536,1024]{1,0:T(8,128)(2,1)} %param.13) | copy-start | bytes 9437188
  0.6 17.1 %copy-start.5 = (bf16[1,8,64,1536]{3,2,1,0:T(8,128)(2,1)S(1)}, bf16[1,8,64,1536]{3,2,1,0:T(8,128)(2,1)}, u32[]{:S(2)}) copy-start(bf16[1,8,64,1536]{3,2,1,0:T(8,128)(2,1)} %param.8) | copy-start | bytes 4718596
  2.1 17.4 %copy-start.9 = (bf16[7,7,1536]{2,1,0:T(8,128)(2,1)S(1)}, bf16[7,7,1536]{2,1,0:T(8,128)(2,1)}, u32[]{:S(2)}) copy-start(bf16[7,7,1536]{2,1,0:T(8,128)(2,1)} %param.9) | copy-start | bytes 451588
  2.1 15.6 %collective-permute-start = (bf16[1,3,64,1536]{3,2,1,0:T(8,128)(2,1)S(1)}, bf16[1,3,64,1536]{3,2,1,0:T(8,128)(2,1)S(1)}, u32[]{:S(2)}, u32[]{:S(2)}) collective-permute-start(bf16[1,3,64,1536]{3,2,1,0:T(8,128)(2,1)S(1)} %get-tuple-element.34), channel_id=1, source_target_pairs={{0,1},{1,2},{2,3},{3,4},{4,5},{5,6},{6,7},{7,8},{8,9},{9,10},{10,1... | collective-permute-start | bytes 1769480 | tf_op jit(solution)/shard_map/ppermute | solution.py:13
  4.2 15.3 %collective-permute-start.1 = (bf16[1,3,64,1536]{3,2,1,0:T(8,128)(2,1)S(1)}, bf16[1,3,64,1536]{3,2,1,0:T(8,128)(2,1)S(1)}, u32[]{:S(2)}, u32[]{:S(2)}) collective-permute-start(bf16[1,3,64,1536]{3,2,1,0:T(8,128)(2,1)S(1)} %get-tuple-element.33), channel_id=1, source_target_pairs={{1,0},{2,1},{3,2},{4,3},{5,4},{6,5},{7,6},{8,7},{9,8},{10,9},{11,1... | collective-permute-start | bytes 1769480 | tf_op jit(solution)/shard_map/ppermute | solution.py:16
  19.5 21.5 %copy-start.8 = (f32[1536]{0:T(1024)S(1)}, f32[1536]{0:T(1024)}, u32[]{:S(2)}) copy-start(f32[1536]{0:T(1024)} %param.10) | copy-start | bytes 18436
  41.0 1.6 copy-start.1
  41.0 1.6 copy-start.10
  41.0 1.6 copy-start.12
  43.3 25.5 %copy-start.11 = (f32[1,1024]{1,0:T(1,128)S(1)}, f32[1,1024]{1,0:T(1,128)}, u32[]{:S(2)}) copy-start(f32[1,1024]{1,0:T(1,128)} %param.14) | copy-start | bytes 12292
  43.4 3.6 %collective-permute-start.2 = (f32[1,1536]{1,0:T(1,128)S(1)}, f32[1,1536]{1,0:T(1,128)S(1)}, u32[]{:S(2)}, u32[]{:S(2)}) collective-permute-start(f32[1,1536]{1,0:T(1,128)S(1)} %reduce_sum.131), channel_id=1, source_target_pairs={{0,1},{1,0},{2,3},{3,2},{4,5},{5,4},{6,7},{7,6},{8,9},{9,8},{10,11... | collective-permute-start | bytes 18440 | tf_op jit(solution)/shard_map/ppermute | solution.py:31
  47.0 3.7 %collective-permute-start.3 = (f32[1,1536]{1,0:T(1,128)S(1)}, f32[1,1536]{1,0:T(1,128)S(1)}, u32[]{:S(2)}, u32[]{:S(2)}) collective-permute-start(f32[1,1536]{1,0:T(1,128)S(1)} %reshape_add_fusion), channel_id=1, source_target_pairs={{0,2},{1,3},{2,0},{3,1},{4,6},{5,7},{6,4},{7,5},{8,10},{9,11},{10,... | collective-permute-start | bytes 18440 | tf_op jit(solution)/shard_map/ppermute | solution.py:31
  50.7 5.2 %collective-permute-start.4 = (f32[1,1536]{1,0:T(1,128)S(1)}, f32[1,1536]{1,0:T(1,128)S(1)}, u32[]{:S(2)}, u32[]{:S(2)}) collective-permute-start(f32[1,1536]{1,0:T(1,128)S(1)} %add.128), channel_id=1, source_target_pairs={{0,4},{1,5},{2,6},{3,7},{4,0},{5,1},{6,2},{7,3},{8,12},{9,13},{10,... | collective-permute-start | bytes 18440 | tf_op jit(solution)/shard_map/ppermute | solution.py:31
  56.0 7.6 %collective-permute-start.5 = (f32[1,1536]{1,0:T(1,128)S(1)}, f32[1,1536]{1,0:T(1,128)S(1)}, u32[]{:S(2)}, u32[]{:S(2)}) collective-permute-start(f32[1,1536]{1,0:T(1,128)S(1)} %add.129), channel_id=1, source_target_pairs={{0,8},{1,9},{2,10},{3,11},{4,12},{5,13},{6,14},{7,15},{8,0},{9,1},... | collective-permute-start | bytes 18440 | tf_op jit(solution)/shard_map/ppermute | solution.py:31
  63.6 5.2 %collective-permute-start.6 = (f32[1,1536]{1,0:T(1,128)S(1)}, f32[1,1536]{1,0:T(1,128)S(1)}, u32[]{:S(2)}, u32[]{:S(2)}) collective-permute-start(f32[1,1536]{1,0:T(1,128)S(1)} %add.130), channel_id=1, source_target_pairs={{0,16},{1,17},{2,18},{3,19},{4,20},{5,21},{6,22},{7,23},{8,24},{9,... | collective-permute-start | bytes 18440 | tf_op jit(solution)/shard_map/ppermute | solution.py:31
  69.1 4.9 %collective-permute-start.7 = (f32[8,2560]{1,0:T(8,128)S(1)}, f32[8,2560]{1,0:T(8,128)S(1)}, u32[]{:S(2)}, u32[]{:S(2)}) collective-permute-start(f32[8,2560]{1,0:T(8,128)S(1)} %dynamic_update_slice.5), channel_id=1, source_target_pairs={{0,32},{32,0},{64,96},{96,64},{128,160},{160,128},{192,224},{224,1... | collective-permute-start | bytes 245768 | tf_op jit(solution)/shard_map/ppermute | solution.py:31
  74.4 6.0 %collective-permute-start.8 = (f32[8,2560]{1,0:T(8,128)S(1)}, f32[8,2560]{1,0:T(8,128)S(1)}, u32[]{:S(2)}, u32[]{:S(2)}) collective-permute-start(f32[8,2560]{1,0:T(8,128)S(1)} %add.133), channel_id=1, source_target_pairs={{0,64},{32,96},{64,0},{96,32},{128,192},{160,224},{192,128},{224,1... | collective-permute-start | bytes 245768 | tf_op jit(solution)/shard_map/ppermute | solution.py:31
  80.4 4.7 %collective-permute-start.9 = (f32[8,2560]{1,0:T(8,128)S(1)}, f32[8,2560]{1,0:T(8,128)S(1)}, u32[]{:S(2)}, u32[]{:S(2)}) collective-permute-start(f32[8,2560]{1,0:T(8,128)S(1)} %add.134), channel_id=1, source_target_pairs={{0,128},{32,160},{64,192},{96,224},{128,0},{160,32},{192,64},{224,... | collective-permute-start | bytes 245768 | tf_op jit(solution)/shard_map/ppermute | solution.py:31
  85.3 8.6 %copy-start.2 = (f32[1,8,64,1536]{3,0,2,1:T(1,128)S(1)}, f32[1,8,64,1536]{3,0,2,1:T(1,128)}, u32[]{:S(2)}) copy-start(f32[1,8,64,1536]{3,0,2,1:T(1,128)} %copy-done.1) | copy-start | bytes 9437188
  97.9 8.7 %copy-start.4 = (f32[1,8,64,1536]{3,2,1,0:T(8,128)}, f32[1,8,64,1536]{3,2,1,0:T(8,128)S(1)}, u32[]{:S(2)}) copy-start(f32[1,8,64,1536]{3,2,1,0:T(8,128)S(1)} %subtract_multiply_fusion) | copy-start | bytes 9437188
  97.9 6.2 %copy-start.3 = (f32[1,8,64,1536]{3,0,2,1:T(1,128)S(1)}, f32[1,8,64,1536]{3,0,2,1:T(1,128)}, u32[]{:S(2)}) copy-start(f32[1,8,64,1536]{3,0,2,1:T(1,128)} %copy-done.1) | copy-start | bytes 9437188
  99.5 24.8 %collective-permute-start.12 = (f32[1,3,64,1536]{3,2,1,0:T(8,128)}, f32[1,3,64,1536]{3,2,1,0:T(8,128)}, u32[]{:S(2)}, u32[]{:S(2)}) collective-permute-start(f32[1,3,64,1536]{3,2,1,0:T(8,128)} %get-tuple-element.32), channel_id=1, source_target_pairs={{1,0},{2,1},{3,2},{4,3},{5,4},{6,5},{7,6},{8,7},{9,8},{10,9},{11,1... | collective-permute-start | bytes 3538952 | tf_op jit(solution)/shard_map/ppermute | solution.py:16
  101.7 22.7 %collective-permute-start.11 = (f32[1,3,64,1536]{3,2,1,0:T(8,128)}, f32[1,3,64,1536]{3,2,1,0:T(8,128)}, u32[]{:S(2)}, u32[]{:S(2)}) collective-permute-start(f32[1,3,64,1536]{3,2,1,0:T(8,128)} %get-tuple-element.31), channel_id=1, source_target_pairs={{0,1},{1,2},{2,3},{3,4},{4,5},{5,6},{6,7},{7,8},{8,9},{9,10},{10,1... | collective-permute-start | bytes 3538952 | tf_op jit(solution)/shard_map/ppermute | solution.py:13
  123.0 11.6 %collective-permute-start.10 = (f32[37632]{0:T(1024)}, f32[37632]{0:T(1024)}, u32[]{:S(2)}, u32[]{:S(2)}) collective-permute-start(f32[37632]{0:T(1024)} %slice_select_fusion), channel_id=1, source_target_pairs={{0,1},{1,0},{2,3},{3,2},{4,5},{5,4},{6,7},{7,6},{8,9},{9,8},{10,11... | collective-permute-start | bytes 451592 | tf_op jit(solution)/shard_map/ppermute | solution.py:65
  135.5 0.7 copy-start.6
  136.2 7.1 %collective-permute-start.13 = (f32[18816]{0:T(1024)S(1)}, f32[18816]{0:T(1024)}, u32[]{:S(2)}, u32[]{:S(2)}) collective-permute-start(f32[18816]{0:T(1024)S(1)} %slice_select_fusion.1), channel_id=1, source_target_pairs={{0,2},{1,3},{2,0},{3,1},{4,6},{5,7},{6,4},{7,5},{8,10},{9,11},{10,... | collective-permute-start | bytes 225800 | tf_op jit(solution)/shard_map/ppermute | solution.py:65
  137.7 5.5 %copy-start.7 = (f32[37632]{0:T(1024)S(1)}, f32[37632]{0:T(1024)}, u32[]{:S(2)}) copy-start(f32[37632]{0:T(1024)} %copy-done.6) | copy-start | bytes 451588
  144.3 7.5 %collective-permute-start.14 = (f32[9408]{0:T(1024)S(1)}, f32[9408]{0:T(1024)S(1)}, u32[]{:S(2)}, u32[]{:S(2)}) collective-permute-start(f32[9408]{0:T(1024)S(1)} %slice_select_fusion.2), channel_id=1, source_target_pairs={{0,4},{1,5},{2,6},{3,7},{4,0},{5,1},{6,2},{7,3},{8,12},{9,13},{10,... | collective-permute-start | bytes 112904 | tf_op jit(solution)/shard_map/ppermute | solution.py:65
  151.9 8.4 %collective-permute-start.15 = (f32[9408]{0:T(1024)S(1)}, f32[9408]{0:T(1024)S(1)}, u32[]{:S(2)}, u32[]{:S(2)}) collective-permute-start(f32[9408]{0:T(1024)S(1)} %select_add_fusion.2), channel_id=1, source_target_pairs={{0,8},{1,9},{2,10},{3,11},{4,12},{5,13},{6,14},{7,15},{8,0},{9,1},... | collective-permute-start | bytes 112904 | tf_op jit(solution)/shard_map/ppermute | solution.py:72
  160.3 5.5 %collective-permute-start.16 = (f32[9408]{0:T(1024)S(1)}, f32[9408]{0:T(1024)S(1)}, u32[]{:S(2)}, u32[]{:S(2)}) collective-permute-start(f32[9408]{0:T(1024)S(1)} %add.146), channel_id=1, source_target_pairs={{0,16},{1,17},{2,18},{3,19},{4,20},{5,21},{6,22},{7,23},{8,24},{9,... | collective-permute-start | bytes 112904 | tf_op jit(solution)/shard_map/ppermute | solution.py:72
  165.9 4.0 %collective-permute-start.17 = (f32[9408]{0:T(1024)S(1)}, f32[9408]{0:T(1024)S(1)}, u32[]{:S(2)}, u32[]{:S(2)}) collective-permute-start(f32[9408]{0:T(1024)S(1)} %add.147), channel_id=1, source_target_pairs={{0,32},{32,0},{64,96},{96,64},{128,160},{160,128},{192,224},{224,1... | collective-permute-start | bytes 112904 | tf_op jit(solution)/shard_map/ppermute | solution.py:72
  169.9 5.5 %collective-permute-start.18 = (f32[9408]{0:T(1024)S(1)}, f32[9408]{0:T(1024)S(1)}, u32[]{:S(2)}, u32[]{:S(2)}) collective-permute-start(f32[9408]{0:T(1024)S(1)} %add.148), channel_id=1, source_target_pairs={{0,64},{32,96},{64,0},{96,32},{128,192},{160,224},{192,128},{224,1... | collective-permute-start | bytes 112904 | tf_op jit(solution)/shard_map/ppermute | solution.py:72
  175.4 4.0 %collective-permute-start.19 = (f32[9408]{0:T(1024)S(1)}, f32[9408]{0:T(1024)S(1)}, u32[]{:S(2)}, u32[]{:S(2)}) collective-permute-start(f32[9408]{0:T(1024)S(1)} %add.149), channel_id=1, source_target_pairs={{0,128},{32,160},{64,192},{96,224},{128,0},{160,32},{192,64},{224,... | collective-permute-start | bytes 112904 | tf_op jit(solution)/shard_map/ppermute | solution.py:72
  179.4 4.9 %collective-permute-start.20 = (f32[9408]{0:T(1024)S(1)}, f32[9408]{0:T(1024)S(1)}, u32[]{:S(2)}, u32[]{:S(2)}) collective-permute-start(f32[9408]{0:T(1024)S(1)} %add.150), channel_id=1, source_target_pairs={{0,4},{1,5},{2,6},{3,7},{4,0},{5,1},{6,2},{7,3},{8,12},{9,13},{10,... | collective-permute-start | bytes 112904 | tf_op jit(solution)/shard_map/ppermute | solution.py:76
  184.4 4.5 %collective-permute-start.21 = (f32[18816]{0:T(1024)S(1)}, f32[18816]{0:T(1024)S(1)}, u32[]{:S(2)}, u32[]{:S(2)}) collective-permute-start(f32[18816]{0:T(1024)S(1)} %maximum_select_fusion.2), channel_id=1, source_target_pairs={{0,2},{1,3},{2,0},{3,1},{4,6},{5,7},{6,4},{7,5},{8,10},{9,11},{10,... | collective-permute-start | bytes 225800 | tf_op jit(solution)/shard_map/ppermute | solution.py:76
  188.9 2.7 %collective-permute-start.22 = (f32[37632]{0:T(1024)S(1)}, f32[37632]{0:T(1024)S(1)}, u32[]{:S(2)}, u32[]{:S(2)}) collective-permute-start(f32[37632]{0:T(1024)S(1)} %maximum_select_fusion.1), channel_id=1, source_target_pairs={{0,1},{1,0},{2,3},{3,2},{4,5},{5,4},{6,7},{7,6},{8,9},{9,8},{10,11... | collective-permute-start | bytes 451592 | tf_op jit(solution)/shard_map/ppermute | solution.py:76

commit v10 on v6

--- a/solution.py
+++ b/solution.py
@@ -151,6 +151,21 @@
         out_shape=jax.ShapeDtypeStruct((row_count, col_count, block_count * lanes), jnp.bfloat16),
     )(padded, kernel)
 
+def dot_exact(values, weights, contract):
+    high = lax.reduce_precision(values, exponent_bits=8, mantissa_bits=7)
+    rest = values - high
+    middle = lax.reduce_precision(rest, exponent_bits=8, mantissa_bits=7)
+    low = rest - middle
+    dims = (((1,), (contract,)), ((), ()))
+    parts = [
+        lax.dot_general(
+            part.astype(jnp.bfloat16), weights, dims, preferred_element_type=jnp.float32
+        )
+        for part in (high, middle, low)
+    ]
+    return parts[0] + (parts[1] + parts[2])
+
+
 def logsum(scores, axis):
     highest = jnp.max(scores, axis=axis, keepdims=True)
     return jnp.squeeze(highest, axis) + jnp.log(jnp.sum(jnp.exp(scores - highest), axis=axis))
@@ -181,8 +196,7 @@
     table = butterfly_sum(table, ("dp",))
     pooled = table[:, :channels] / pixel_count
     all_text = table[:, channels:]
-    proj_float = proj.astype(jnp.float32)
-    embedded = jnp.dot(pooled, proj_float, precision=lax.Precision.HIGHEST)
+    embedded = dot_exact(pooled, proj, 0)
     emb_norm = jnp.sqrt(jnp.sum(embedded * embedded, axis=-1, keepdims=True))
     unit_img = embedded / emb_norm
     text_norm = jnp.sqrt(jnp.sum(all_text * all_text, axis=-1, keepdims=True))
@@ -212,7 +226,7 @@
     ) / emb_norm
     text_grad = lax.dynamic_slice_in_dim(text_grad_all, first_row, batch_dev, axis=0)
     emb_grad = lax.dynamic_slice_in_dim(emb_grad_all, first_row, batch_dev, axis=0)
-    weighted = jnp.dot(emb_grad, proj_float.T, precision=lax.Precision.HIGHEST) * ln_gain
+    weighted = dot_exact(emb_grad, proj, 1) * ln_gain
     weight_rows = weighted[:, None, None, :]
     weight_mean = jnp.mean(weighted, axis=-1)[:, None, None, None]
     spread_term = jnp.mean(weight_rows * normed, axis=-1, keepdims=True)

time: 198 us -> 202 us (1.020)
  matrix products: 27.7 us -> 30.9 us
    dot_general x2 -> x6, matrix products: 5.18 us -> 8.34 us  [dot_exact(): lax.dot_general(part.astype(jnp.bfloat16), weights, dims, preferred_eleme...]
where the time goes in v10:
time: 202 us; the launch traced here: 199 us
  waiting for transfers between devices  58.7 us (29%)
  starting transfers between devices  39.9 us (20%)
  matrix products  30.9 us (15%)
  Pallas kernels  29.8 us (15%)
  other arithmetic  25.2 us (12%)
  local copies, waits for them, and re-layouts  9.38 us (5%)
  between operations  4.74 us (2%)
    ppermute x8, waiting for transfers between devices, butterfly_sum(): received = lax.ppermute(values, axis, pairs)  24.5 us
    conv_general_dilated x1, matrix products, depthwise(): lax.conv_general_dilated(extended, kernel.reshape(kernel.shape[0], kernel...  21.5 us
    ppermute x5, waiting for transfers between devices, halving_sum(): chunk = chunk + lax.ppermute(chunk, axis, pairs)  20.4 us
    pallas_call x2, Pallas kernels, input_terms(): pl.pallas_call(body, grid=(block_count,), in_specs=[pl.BlockSpec(padded.s...  15.1 us
    pallas_call x1, Pallas kernels, kernel_terms(): pl.pallas_call(body, grid=(channels // lanes,), in_specs=[pl.BlockSpec((r...  14.7 us
    ppermute x8, starting transfers between devices, butterfly_sum(): received = lax.ppermute(values, axis, pairs)  11.6 us
    ppermute x2, starting transfers between devices, with_halo(): lax.ppermute(lax.slice_in_dim(block, 0, width, axis=dim), axis, backward)  10 us
    dot_general x6, matrix products, dot_exact(): lax.dot_general(part.astype(jnp.bfloat16), weights, dims, preferred_eleme...  8.34 us
  transfers between devices with their start and end apart: 23, of which 17 were waited for; matrix products, arithmetic and copies ran while one was open for 10% of the time, Pallas kernels for 15%

profile of v10, /device:TPU:28, one launch (start us, length us, event | category | flops | bytes accessed | tf_op | source)
XLA Modules:
  0.0 198.6 jit_solution(1730063440346355808)
XLA Ops:
  0.7 1.5 fusion.41
  2.1 2.1 %collective-permute-start = (bf16[1,3,64,1536]{3,2,1,0:T(8,128)(2,1)S(1)}, bf16[1,3,64,1536]{3,2,1,0:T(8,128)(2,1)S(1)}, u32[]{:S(2)}, u32[]{:S(2)}) collective-permute-start(bf16[1,3,64,1536]{3,2,1,0:T(8,128)(2,1)S(1)} %get-tuple-element.30), channel_id=1, source_target_pairs={{0,1},{1,2},{2,3},{3,4},{4,5},{5,6},{6,7},{7,8},{8,9},{9,10},{10,1... | collective-permute-start | bytes 1769480 | tf_op jit(solution)/shard_map/ppermute | solution.py:13
  4.2 7.9 %collective-permute-start.1 = (bf16[1,3,64,1536]{3,2,1,0:T(8,128)(2,1)S(1)}, bf16[1,3,64,1536]{3,2,1,0:T(8,128)(2,1)S(1)}, u32[]{:S(2)}, u32[]{:S(2)}) collective-permute-start(bf16[1,3,64,1536]{3,2,1,0:T(8,128)(2,1)S(1)} %get-tuple-element.29), channel_id=1, source_target_pairs={{1,0},{2,1},{3,2},{4,3},{5,4},{6,5},{7,6},{8,7},{9,8},{10,9},{11,1... | collective-permute-start | bytes 1769480 | tf_op jit(solution)/shard_map/ppermute | solution.py:16
  12.1 5.6 %collective-permute-done = bf16[1,3,64,1536]{3,2,1,0:T(8,128)(2,1)S(1)} collective-permute-done((bf16[1,3,64,1536]{3,2,1,0:T(8,128)(2,1)S(1)}, bf16[1,3,64,1536]{3,2,1,0:T(8,128)(2,1)S(1)}, u32[]{:S(2)}, u32[]{:S(2)}) %collective-permute-start) | collective-permute-done | bytes 589856 | tf_op jit(solution)/shard_map/ppermute | solution.py:13
  17.9 1.6 collective-permute-done.1
  19.5 21.5 %fusion.2 = f32[1,8,64,1536]{3,0,2,1:T(1,128)S(1)} fusion(bf16[1,14,64,1536]{3,2,1,0:T(8,128)(2,1)S(1)} %constant_dynamic-update-slice_fusion, bf16[7,7,1,1536]{3,1,0,2:T(8,128)(2,1)S(1)} %bitcast.32), kind=kOutput, calls=%fused_computation.6 | convolution fusion | flops 75005952 | bytes 6048768 | tf_op jit(solution)/shard_map/conv_general_dilated | solution.py:93
  41.9 0.8 copy-done.1
  42.6 0.7 add_reduce_fusion
  43.5 3.5 %pad_convert_fusion = f32[1,14,70,1536]{3,2,1,0:T(8,128)} fusion(bf16[1,14,64,1536]{3,2,1,0:T(8,128)(2,1)S(1)} %constant_dynamic-update-slice_fusion), kind=kLoop, calls=%fused_computation.13 | loop fusion | flops 1505280 | bytes 8773632 | tf_op jit(solution)/shard_map/jit(_pad)/pad | solution.py:182
  47.1 3.6 %collective-permute-done.3 = f32[1,1536]{1,0:T(1,128)S(1)} collective-permute-done((f32[1,1536]{1,0:T(1,128)S(1)}, f32[1,1536]{1,0:T(1,128)S(1)}, u32[]{:S(2)}, u32[]{:S(2)}) %collective-permute-start.3) | collective-permute-done | bytes 6176 | tf_op jit(solution)/shard_map/ppermute | solution.py:31
  50.7 3.6 %collective-permute-start.4 = (f32[1,1536]{1,0:T(1,128)S(1)}, f32[1,1536]{1,0:T(1,128)S(1)}, u32[]{:S(2)}, u32[]{:S(2)}) collective-permute-start(f32[1,1536]{1,0:T(1,128)S(1)} %add.142), channel_id=1, source_target_pairs={{0,4},{1,5},{2,6},{3,7},{4,0},{5,1},{6,2},{7,3},{8,12},{9,13},{10,... | collective-permute-start | bytes 18440 | tf_op jit(solution)/shard_map/ppermute | solution.py:31
  54.3 1.6 collective-permute-done.4
  56.0 3.7 %collective-permute-start.5 = (f32[1,1536]{1,0:T(1,128)S(1)}, f32[1,1536]{1,0:T(1,128)S(1)}, u32[]{:S(2)}, u32[]{:S(2)}) collective-permute-start(f32[1,1536]{1,0:T(1,128)S(1)} %add.143), channel_id=1, source_target_pairs={{0,8},{1,9},{2,10},{3,11},{4,12},{5,13},{6,14},{7,15},{8,0},{9,1},... | collective-permute-start | bytes 18440 | tf_op jit(solution)/shard_map/ppermute | solution.py:31
  59.7 3.9 %collective-permute-done.5 = f32[1,1536]{1,0:T(1,128)S(1)} collective-permute-done((f32[1,1536]{1,0:T(1,128)S(1)}, f32[1,1536]{1,0:T(1,128)S(1)}, u32[]{:S(2)}, u32[]{:S(2)}) %collective-permute-start.5) | collective-permute-done | bytes 6176 | tf_op jit(solution)/shard_map/ppermute | solution.py:31
  63.6 1.3 collective-permute-start.6
  64.9 3.9 %collective-permute-done.6 = f32[1,1536]{1,0:T(1,128)S(1)} collective-permute-done((f32[1,1536]{1,0:T(1,128)S(1)}, f32[1,1536]{1,0:T(1,128)S(1)}, u32[]{:S(2)}, u32[]{:S(2)}) %collective-permute-start.6) | collective-permute-done | bytes 6176 | tf_op jit(solution)/shard_map/ppermute | solution.py:31
  69.1 1.3 collective-permute-start.7
  70.4 3.7 %collective-permute-done.7 = f32[8,2560]{1,0:T(8,128)S(1)} collective-permute-done((f32[8,2560]{1,0:T(8,128)S(1)}, f32[8,2560]{1,0:T(8,128)S(1)}, u32[]{:S(2)}, u32[]{:S(2)}) %collective-permute-start.7) | collective-permute-done | bytes 81952 | tf_op jit(solution)/shard_map/ppermute | solution.py:31
  74.9 5.5 %collective-permute-done.8 = f32[8,2560]{1,0:T(8,128)S(1)} collective-permute-done((f32[8,2560]{1,0:T(8,128)S(1)}, f32[8,2560]{1,0:T(8,128)S(1)}, u32[]{:S(2)}, u32[]{:S(2)}) %collective-permute-start.8) | collective-permute-done | bytes 81952 | tf_op jit(solution)/shard_map/ppermute | solution.py:31
  80.4 1.0 collective-permute-start.9
  81.4 0.8 convert_element_type.43.k_ref
  82.8 2.3 %collective-permute-done.9 = f32[8,2560]{1,0:T(8,128)S(1)} collective-permute-done((f32[8,2560]{1,0:T(8,128)S(1)}, f32[8,2560]{1,0:T(8,128)S(1)}, u32[]{:S(2)}, u32[]{:S(2)}) %collective-permute-start.9) | collective-permute-done | bytes 81952 | tf_op jit(solution)/shard_map/ppermute | solution.py:31
  86.3 0.6 multiply_reduce_fusion.5
  88.1 0.6 subtract_reduce_fusion
  89.7 2.1 %convolution_reduce_fusion.2 = f32[1536]{0:T(1024)S(1)} fusion(bf16[1536,1024]{1,0:T(8,128)(2,1)S(1)} %copy-done, f32[8,1024]{1,0:T(8,128)S(1)} %get-tuple-element.35, s32[]{:T(128)S(6)} %select_n.95, f32[8,1024]{1,0:T(8,128)S(1)} %get-tuple-element.39, f32[1]{0:T(128)} %dynamic-slice.2, f32[1]{0:T(128)} %dynamic-slice.1), kind=kOutput, calls=%fused_computation.23 | convolution fusion | flops 3150848 | bytes 3160076 | tf_op jit(solution)/shard_map/dot_general | solution.py:161
  91.9 2.4 %convolution_reduce_fusion.1 = f32[1536]{0:T(1024)S(1)} fusion(bf16[1536,1024]{1,0:T(8,128)(2,1)S(1)} %copy-done, f32[8,1024]{1,0:T(8,128)S(1)} %get-tuple-element.35, s32[]{:T(128)S(6)} %select_n.95, f32[8,1024]{1,0:T(8,128)S(1)} %get-tuple-element.39, f32[1]{0:T(128)} %dynamic-slice.2, f32[1]{0:T(128)} %dynamic-slice.1), kind=kOutput, calls=%fused_computation.22 | convolution fusion | flops 3152896 | bytes 3160076 | tf_op jit(solution)/shard_map/dot_general | solution.py:161
  94.3 2.1 %convolution_reduce_fusion = f32[1536]{0:T(1024)S(1)} fusion(bf16[1536,1024]{1,0:T(8,128)(2,1)S(1)} %copy-done, f32[8,1024]{1,0:T(8,128)S(1)} %get-tuple-element.35, s32[]{:T(128)S(6)} %select_n.95, f32[8,1024]{1,0:T(8,128)S(1)} %get-tuple-element.39, f32[1]{0:T(128)} %dynamic-slice.2, f32[1]{0:T(128)} %dynamic-slice.1), kind=kOutput, calls=%fused_computation.21 | convolution fusion | flops 3153920 | bytes 3160076 | tf_op jit(solution)/shard_map/dot_general | solution.py:161
  96.4 0.6 fusion.39
  97.0 0.7 multiply_reduce_fusion
  98.4 2.7 %subtract_multiply_fusion = f32[1,8,64,1536]{3,2,1,0:T(8,128)S(1)} fusion(f32[1,8,64,1536]{3,0,2,1:T(1,128)} %copy-done.1, f32[8,64]{1,0:T(8,128)S(1)} %broadcast_multiply_fusion, f32[1536]{0:T(1024)S(1)} %broadcast_subtract_fusion, f32[8,64]{1,0:T(8,128)S(1)} %add_rsqrt_fusion, f32[8,64]{1,0:T(8,128)S(1)} %broadcast_multiply_fusion.1, f32[1536]{0:T(1024)S(1)} %copy-done.8), kind=kLoop, calls=%fused_computation.9 | loop fusion | flops 4718592 | bytes 6309888 | tf_op jit(solution)/shard_map/mul | solution.py:233
  101.1 1.6 fusion.40
  102.7 2.2 %collective-permute-start.12 = (f32[1,3,64,1536]{3,2,1,0:T(8,128)}, f32[1,3,64,1536]{3,2,1,0:T(8,128)}, u32[]{:S(2)}, u32[]{:S(2)}) collective-permute-start(f32[1,3,64,1536]{3,2,1,0:T(8,128)} %get-tuple-element.28), channel_id=1, source_target_pairs={{1,0},{2,1},{3,2},{4,3},{5,4},{6,5},{7,6},{8,7},{9,8},{10,9},{11,1... | collective-permute-start | bytes 3538952 | tf_op jit(solution)/shard_map/ppermute | solution.py:16
  104.9 2.4 %collective-permute-start.11 = (f32[1,3,64,1536]{3,2,1,0:T(8,128)}, f32[1,3,64,1536]{3,2,1,0:T(8,128)}, u32[]{:S(2)}, u32[]{:S(2)}) collective-permute-start(f32[1,3,64,1536]{3,2,1,0:T(8,128)} %get-tuple-element.27), channel_id=1, source_target_pairs={{0,1},{1,2},{2,3},{3,4},{4,5},{5,6},{6,7},{7,8},{8,9},{9,10},{10,1... | collective-permute-start | bytes 3538952 | tf_op jit(solution)/shard_map/ppermute | solution.py:13
  107.3 2.5 %fusion.52.g_ref = f32[8,64,1536]{2,1,0:T(8,128)} fusion(f32[8,64]{1,0:T(8,128)S(1)} %broadcast_multiply_fusion, f32[8,64]{1,0:T(8,128)S(1)} %broadcast_multiply_fusion.1, f32[1536]{0:T(1024)S(1)} %copy-done.8, f32[1,8,64,1536]{3,0,2,1:T(1,128)S(1)} %copy-done.3, f32[1536]{0:T(1024)S(1)} %broadcast_subtract_fusion, f32[8,64]{1,0:T(8,128)S(1)} %add_rsqrt_fusion), kind=kLoop, calls=%fused_computation.101 | loop fusion | flops 4718592 | bytes 6309888 | tf_op jit(solution)/shard_map/squeeze | solution.py:242
  109.8 14.7 %shard_map.111 = f32[7,7,1536]{2,1,0:T(8,128)} custom-call(f32[8,64,1536]{2,1,0:T(8,128)} %fusion.52.g_ref, f32[14,70,1536]{2,1,0:T(8,128)} %bitcast.31), custom_call_target="tpu_custom_call" | custom-call | tf_op jit(solution)/shard_map/pallas_call | solution.py:118
  124.5 1.0 reshape.164
  125.5 0.7 slice_select_fusion
  126.2 1.4 collective-permute-start.10
  127.5 4.7 %fusion.x_ref = f32[14,70,1536]{2,1,0:T(8,128)} fusion(f32[1,3,64,1536]{3,2,1,0:T(8,128)} %collective-permute-done.12, f32[1,8,64,1536]{3,2,1,0:T(8,128)} %copy-done.4, f32[1,3,64,1536]{3,2,1,0:T(8,128)} %collective-permute-done.11), kind=kLoop, calls=%fused_computation.3 | loop fusion | flops 12042240 | bytes 11526144 | tf_op jit(solution)/shard_map/squeeze | solution.py:239
  132.2 7.5 %shard_map.112 = bf16[8,64,768]{2,1,0:T(8,128)(2,1)} custom-call(f32[14,70,1536]{2,1,0:T(8,128)} %fusion.x_ref, f32[7,7,1536]{2,1,0:T(8,128)} %convert_element_type.43.k_ref), custom_call_target="tpu_custom_call" | custom-call | tf_op jit(solution)/shard_map/pallas_call | solution.py:143
  139.8 0.9 select_add_fusion
  140.7 0.7 copy-done.6
  141.4 0.6 slice_select_fusion.1
  142.0 1.5 collective-permute-start.13
  143.5 7.6 %shard_map.113 = bf16[8,64,768]{2,1,0:T(8,128)(2,1)} custom-call(f32[14,70,1536]{2,1,0:T(8,128)} %fusion.x_ref, f32[7,7,1536]{2,1,0:T(8,128)} %convert_element_type.43.k_ref), custom_call_target="tpu_custom_call" | custom-call | tf_op jit(solution)/shard_map/pallas_call | solution.py:143
  151.2 1.8 collective-permute-start.14
  153.0 3.6 %collective-permute-done.14 = f32[9408]{0:T(1024)S(1)} collective-permute-done((f32[9408]{0:T(1024)S(1)}, f32[9408]{0:T(1024)S(1)}, u32[]{:S(2)}, u32[]{:S(2)}) %collective-permute-start.14) | collective-permute-done | bytes 37664 | tf_op jit(solution)/shard_map/ppermute | solution.py:65
  156.7 1.9 collective-permute-start.15
  158.6 6.3 %collective-permute-done.15 = f32[9408]{0:T(1024)S(1)} collective-permute-done((f32[9408]{0:T(1024)S(1)}, f32[9408]{0:T(1024)S(1)}, u32[]{:S(2)}, u32[]{:S(2)}) %collective-permute-start.15) | collective-permute-done | bytes 37664 | tf_op jit(solution)/shard_map/ppermute | solution.py:72
  164.9 1.7 collective-permute-start.16
  166.6 3.8 %collective-permute-done.16 = f32[9408]{0:T(1024)S(1)} collective-permute-done((f32[9408]{0:T(1024)S(1)}, f32[9408]{0:T(1024)S(1)}, u32[]{:S(2)}, u32[]{:S(2)}) %collective-permute-start.16) | collective-permute-done | bytes 37664 | tf_op jit(solution)/shard_map/ppermute | solution.py:72
  170.4 1.1 collective-permute-start.17
  171.5 2.9 %collective-permute-done.17 = f32[9408]{0:T(1024)S(1)} collective-permute-done((f32[9408]{0:T(1024)S(1)}, f32[9408]{0:T(1024)S(1)}, u32[]{:S(2)}, u32[]{:S(2)}) %collective-permute-start.17) | collective-permute-done | bytes 37664 | tf_op jit(solution)/shard_map/ppermute | solution.py:72
  174.4 1.0 collective-permute-start.18
  175.4 4.5 %collective-permute-done.18 = f32[9408]{0:T(1024)S(1)} collective-permute-done((f32[9408]{0:T(1024)S(1)}, f32[9408]{0:T(1024)S(1)}, u32[]{:S(2)}, u32[]{:S(2)}) %collective-permute-start.18) | collective-permute-done | bytes 37664 | tf_op jit(solution)/shard_map/ppermute | solution.py:72
  179.9 1.2 collective-permute-start.19
  181.1 2.8 %collective-permute-done.19 = f32[9408]{0:T(1024)S(1)} collective-permute-done((f32[9408]{0:T(1024)S(1)}, f32[9408]{0:T(1024)S(1)}, u32[]{:S(2)}, u32[]{:S(2)}) %collective-permute-start.19) | collective-permute-done | bytes 37664 | tf_op jit(solution)/shard_map/ppermute | solution.py:72
  183.9 1.3 collective-permute-start.20
  188.0 1.3 collective-permute-done.20
  189.4 1.0 collective-permute-start.21
  190.4 1.9 fusion.22
  192.3 1.6 collective-permute-done.21
  194.0 2.6 %maximum_bitcast_fusion = bf16[1,8,64,1536]{3,2,1,0:T(8,128)(2,1)} fusion(bf16[8,64,768]{2,1,0:T(8,128)(2,1)} %shard_map.113, bf16[8,64,768]{2,1,0:T(8,128)(2,1)} %shard_map.112), kind=kLoop, calls=%fused_computation.16 | loop fusion | flops 3145728 | bytes 3145728 | tf_op jit(solution)/shard_map/stack | solution.py:246
  196.7 0.8 div.96
  (81 shorter events, 7.7 us)
Async XLA Ops:
  0.6 84.6 %copy-start = (bf16[1536,1024]{1,0:T(8,128)(2,1)S(1)}, bf16[1536,1024]{1,0:T(8,128)(2,1)}, u32[]{:S(2)}) copy-start(bf16[1536,1024]{1,0:T(8,128)(2,1)} %param.13) | copy-start | bytes 9437188
  0.6 17.1 %copy-start.5 = (bf16[1,8,64,1536]{3,2,1,0:T(8,128)(2,1)S(1)}, bf16[1,8,64,1536]{3,2,1,0:T(8,128)(2,1)}, u32[]{:S(2)}) copy-start(bf16[1,8,64,1536]{3,2,1,0:T(8,128)(2,1)} %param.8) | copy-start | bytes 4718596
  2.1 17.4 %copy-start.9 = (bf16[7,7,1536]{2,1,0:T(8,128)(2,1)S(1)}, bf16[7,7,1536]{2,1,0:T(8,128)(2,1)}, u32[]{:S(2)}) copy-start(bf16[7,7,1536]{2,1,0:T(8,128)(2,1)} %param.9) | copy-start | bytes 451588
  2.1 15.6 %collective-permute-start = (bf16[1,3,64,1536]{3,2,1,0:T(8,128)(2,1)S(1)}, bf16[1,3,64,1536]{3,2,1,0:T(8,128)(2,1)S(1)}, u32[]{:S(2)}, u32[]{:S(2)}) collective-permute-start(bf16[1,3,64,1536]{3,2,1,0:T(8,128)(2,1)S(1)} %get-tuple-element.30), channel_id=1, source_target_pairs={{0,1},{1,2},{2,3},{3,4},{4,5},{5,6},{6,7},{7,8},{8,9},{9,10},{10,1... | collective-permute-start | bytes 1769480 | tf_op jit(solution)/shard_map/ppermute | solution.py:13
  4.2 15.3 %collective-permute-start.1 = (bf16[1,3,64,1536]{3,2,1,0:T(8,128)(2,1)S(1)}, bf16[1,3,64,1536]{3,2,1,0:T(8,128)(2,1)S(1)}, u32[]{:S(2)}, u32[]{:S(2)}) collective-permute-start(bf16[1,3,64,1536]{3,2,1,0:T(8,128)(2,1)S(1)} %get-tuple-element.29), channel_id=1, source_target_pairs={{1,0},{2,1},{3,2},{4,3},{5,4},{6,5},{7,6},{8,7},{9,8},{10,9},{11,1... | collective-permute-start | bytes 1769480 | tf_op jit(solution)/shard_map/ppermute | solution.py:16
  19.5 21.5 %copy-start.8 = (f32[1536]{0:T(1024)S(1)}, f32[1536]{0:T(1024)}, u32[]{:S(2)}) copy-start(f32[1536]{0:T(1024)} %param.10) | copy-start | bytes 18436
  41.0 1.6 copy-start.1
  41.0 1.6 copy-start.10
  41.0 1.6 copy-start.12
  43.3 25.5 %copy-start.11 = (f32[1,1024]{1,0:T(1,128)S(1)}, f32[1,1024]{1,0:T(1,128)}, u32[]{:S(2)}) copy-start(f32[1,1024]{1,0:T(1,128)} %param.14) | copy-start | bytes 12292
  43.4 3.6 %collective-permute-start.2 = (f32[1,1536]{1,0:T(1,128)S(1)}, f32[1,1536]{1,0:T(1,128)S(1)}, u32[]{:S(2)}, u32[]{:S(2)}) collective-permute-start(f32[1,1536]{1,0:T(1,128)S(1)} %reduce_sum.131), channel_id=1, source_target_pairs={{0,1},{1,0},{2,3},{3,2},{4,5},{5,4},{6,7},{7,6},{8,9},{9,8},{10,11... | collective-permute-start | bytes 18440 | tf_op jit(solution)/shard_map/ppermute | solution.py:31
  47.0 3.7 %collective-permute-start.3 = (f32[1,1536]{1,0:T(1,128)S(1)}, f32[1,1536]{1,0:T(1,128)S(1)}, u32[]{:S(2)}, u32[]{:S(2)}) collective-permute-start(f32[1,1536]{1,0:T(1,128)S(1)} %reshape_add_fusion), channel_id=1, source_target_pairs={{0,2},{1,3},{2,0},{3,1},{4,6},{5,7},{6,4},{7,5},{8,10},{9,11},{10,... | collective-permute-start | bytes 18440 | tf_op jit(solution)/shard_map/ppermute | solution.py:31
  50.7 5.2 %collective-permute-start.4 = (f32[1,1536]{1,0:T(1,128)S(1)}, f32[1,1536]{1,0:T(1,128)S(1)}, u32[]{:S(2)}, u32[]{:S(2)}) collective-permute-start(f32[1,1536]{1,0:T(1,128)S(1)} %add.142), channel_id=1, source_target_pairs={{0,4},{1,5},{2,6},{3,7},{4,0},{5,1},{6,2},{7,3},{8,12},{9,13},{10,... | collective-permute-start | bytes 18440 | tf_op jit(solution)/shard_map/ppermute | solution.py:31
  56.0 7.6 %collective-permute-start.5 = (f32[1,1536]{1,0:T(1,128)S(1)}, f32[1,1536]{1,0:T(1,128)S(1)}, u32[]{:S(2)}, u32[]{:S(2)}) collective-permute-start(f32[1,1536]{1,0:T(1,128)S(1)} %add.143), channel_id=1, source_target_pairs={{0,8},{1,9},{2,10},{3,11},{4,12},{5,13},{6,14},{7,15},{8,0},{9,1},... | collective-permute-start | bytes 18440 | tf_op jit(solution)/shard_map/ppermute | solution.py:31
  63.6 5.2 %collective-permute-start.6 = (f32[1,1536]{1,0:T(1,128)S(1)}, f32[1,1536]{1,0:T(1,128)S(1)}, u32[]{:S(2)}, u32[]{:S(2)}) collective-permute-start(f32[1,1536]{1,0:T(1,128)S(1)} %add.144), channel_id=1, source_target_pairs={{0,16},{1,17},{2,18},{3,19},{4,20},{5,21},{6,22},{7,23},{8,24},{9,... | collective-permute-start | bytes 18440 | tf_op jit(solution)/shard_map/ppermute | solution.py:31
  69.1 4.9 %collective-permute-start.7 = (f32[8,2560]{1,0:T(8,128)S(1)}, f32[8,2560]{1,0:T(8,128)S(1)}, u32[]{:S(2)}, u32[]{:S(2)}) collective-permute-start(f32[8,2560]{1,0:T(8,128)S(1)} %dynamic_update_slice.5), channel_id=1, source_target_pairs={{0,32},{32,0},{64,96},{96,64},{128,160},{160,128},{192,224},{224,1... | collective-permute-start | bytes 245768 | tf_op jit(solution)/shard_map/ppermute | solution.py:31
  74.4 6.0 %collective-permute-start.8 = (f32[8,2560]{1,0:T(8,128)S(1)}, f32[8,2560]{1,0:T(8,128)S(1)}, u32[]{:S(2)}, u32[]{:S(2)}) collective-permute-start(f32[8,2560]{1,0:T(8,128)S(1)} %add.147), channel_id=1, source_target_pairs={{0,64},{32,96},{64,0},{96,32},{128,192},{160,224},{192,128},{224,1... | collective-permute-start | bytes 245768 | tf_op jit(solution)/shard_map/ppermute | solution.py:31
  80.4 4.7 %collective-permute-start.9 = (f32[8,2560]{1,0:T(8,128)S(1)}, f32[8,2560]{1,0:T(8,128)S(1)}, u32[]{:S(2)}, u32[]{:S(2)}) collective-permute-start(f32[8,2560]{1,0:T(8,128)S(1)} %add.148), channel_id=1, source_target_pairs={{0,128},{32,160},{64,192},{96,224},{128,0},{160,32},{192,64},{224,... | collective-permute-start | bytes 245768 | tf_op jit(solution)/shard_map/ppermute | solution.py:31
  91.8 5.2 %copy-start.2 = (f32[1,8,64,1536]{3,0,2,1:T(1,128)S(1)}, f32[1,8,64,1536]{3,0,2,1:T(1,128)}, u32[]{:S(2)}) copy-start(f32[1,8,64,1536]{3,0,2,1:T(1,128)} %copy-done.1) | copy-start | bytes 9437188
  101.1 8.7 %copy-start.4 = (f32[1,8,64,1536]{3,2,1,0:T(8,128)}, f32[1,8,64,1536]{3,2,1,0:T(8,128)S(1)}, u32[]{:S(2)}) copy-start(f32[1,8,64,1536]{3,2,1,0:T(8,128)S(1)} %subtract_multiply_fusion) | copy-start | bytes 9437188
  101.1 6.2 %copy-start.3 = (f32[1,8,64,1536]{3,0,2,1:T(1,128)S(1)}, f32[1,8,64,1536]{3,0,2,1:T(1,128)}, u32[]{:S(2)}) copy-start(f32[1,8,64,1536]{3,0,2,1:T(1,128)} %copy-done.1) | copy-start | bytes 9437188
  102.7 24.8 %collective-permute-start.12 = (f32[1,3,64,1536]{3,2,1,0:T(8,128)}, f32[1,3,64,1536]{3,2,1,0:T(8,128)}, u32[]{:S(2)}, u32[]{:S(2)}) collective-permute-start(f32[1,3,64,1536]{3,2,1,0:T(8,128)} %get-tuple-element.28), channel_id=1, source_target_pairs={{1,0},{2,1},{3,2},{4,3},{5,4},{6,5},{7,6},{8,7},{9,8},{10,9},{11,1... | collective-permute-start | bytes 3538952 | tf_op jit(solution)/shard_map/ppermute | solution.py:16
  104.9 22.7 %collective-permute-start.11 = (f32[1,3,64,1536]{3,2,1,0:T(8,128)}, f32[1,3,64,1536]{3,2,1,0:T(8,128)}, u32[]{:S(2)}, u32[]{:S(2)}) collective-permute-start(f32[1,3,64,1536]{3,2,1,0:T(8,128)} %get-tuple-element.27), channel_id=1, source_target_pairs={{0,1},{1,2},{2,3},{3,4},{4,5},{5,6},{6,7},{7,8},{8,9},{9,10},{10,1... | collective-permute-start | bytes 3538952 | tf_op jit(solution)/shard_map/ppermute | solution.py:13
  126.2 13.6 %collective-permute-start.10 = (f32[37632]{0:T(1024)}, f32[37632]{0:T(1024)}, u32[]{:S(2)}, u32[]{:S(2)}) collective-permute-start(f32[37632]{0:T(1024)} %slice_select_fusion), channel_id=1, source_target_pairs={{0,1},{1,0},{2,3},{3,2},{4,5},{5,4},{6,7},{7,6},{8,9},{9,8},{10,11... | collective-permute-start | bytes 451592 | tf_op jit(solution)/shard_map/ppermute | solution.py:65
  140.7 0.7 copy-start.6
  142.0 9.0 %collective-permute-start.13 = (f32[18816]{0:T(1024)}, f32[18816]{0:T(1024)S(1)}, u32[]{:S(2)}, u32[]{:S(2)}) collective-permute-start(f32[18816]{0:T(1024)} %slice_select_fusion.1), channel_id=1, source_target_pairs={{0,2},{1,3},{2,0},{3,1},{4,6},{5,7},{6,4},{7,5},{8,10},{9,11},{10,... | collective-permute-start | bytes 225800 | tf_op jit(solution)/shard_map/ppermute | solution.py:65
  143.5 7.6 %copy-start.7 = (f32[37632]{0:T(1024)S(1)}, f32[37632]{0:T(1024)}, u32[]{:S(2)}) copy-start(f32[37632]{0:T(1024)} %copy-done.6) | copy-start | bytes 451588
  151.2 5.4 %collective-permute-start.14 = (f32[9408]{0:T(1024)S(1)}, f32[9408]{0:T(1024)S(1)}, u32[]{:S(2)}, u32[]{:S(2)}) collective-permute-start(f32[9408]{0:T(1024)S(1)} %slice_select_fusion.2), channel_id=1, source_target_pairs={{0,4},{1,5},{2,6},{3,7},{4,0},{5,1},{6,2},{7,3},{8,12},{9,13},{10,... | collective-permute-start | bytes 112904 | tf_op jit(solution)/shard_map/ppermute | solution.py:65
  156.7 8.2 %collective-permute-start.15 = (f32[9408]{0:T(1024)S(1)}, f32[9408]{0:T(1024)S(1)}, u32[]{:S(2)}, u32[]{:S(2)}) collective-permute-start(f32[9408]{0:T(1024)S(1)} %select_add_fusion.2), channel_id=1, source_target_pairs={{0,8},{1,9},{2,10},{3,11},{4,12},{5,13},{6,14},{7,15},{8,0},{9,1},... | collective-permute-start | bytes 112904 | tf_op jit(solution)/shard_map/ppermute | solution.py:72
  164.9 5.5 %collective-permute-start.16 = (f32[9408]{0:T(1024)S(1)}, f32[9408]{0:T(1024)S(1)}, u32[]{:S(2)}, u32[]{:S(2)}) collective-permute-start(f32[9408]{0:T(1024)S(1)} %add.164), channel_id=1, source_target_pairs={{0,16},{1,17},{2,18},{3,19},{4,20},{5,21},{6,22},{7,23},{8,24},{9,... | collective-permute-start | bytes 112904 | tf_op jit(solution)/shard_map/ppermute | solution.py:72
  170.4 4.0 %collective-permute-start.17 = (f32[9408]{0:T(1024)S(1)}, f32[9408]{0:T(1024)S(1)}, u32[]{:S(2)}, u32[]{:S(2)}) collective-permute-start(f32[9408]{0:T(1024)S(1)} %add.165), channel_id=1, source_target_pairs={{0,32},{32,0},{64,96},{96,64},{128,160},{160,128},{192,224},{224,1... | collective-permute-start | bytes 112904 | tf_op jit(solution)/shard_map/ppermute | solution.py:72
  174.4 5.5 %collective-permute-start.18 = (f32[9408]{0:T(1024)S(1)}, f32[9408]{0:T(1024)S(1)}, u32[]{:S(2)}, u32[]{:S(2)}) collective-permute-start(f32[9408]{0:T(1024)S(1)} %add.166), channel_id=1, source_target_pairs={{0,64},{32,96},{64,0},{96,32},{128,192},{160,224},{192,128},{224,1... | collective-permute-start | bytes 112904 | tf_op jit(solution)/shard_map/ppermute | solution.py:72
  179.9 4.0 %collective-permute-start.19 = (f32[9408]{0:T(1024)S(1)}, f32[9408]{0:T(1024)S(1)}, u32[]{:S(2)}, u32[]{:S(2)}) collective-permute-start(f32[9408]{0:T(1024)S(1)} %add.167), channel_id=1, source_target_pairs={{0,128},{32,160},{64,192},{96,224},{128,0},{160,32},{192,64},{224,... | collective-permute-start | bytes 112904 | tf_op jit(solution)/shard_map/ppermute | solution.py:72
  183.9 5.3 %collective-permute-start.20 = (f32[9408]{0:T(1024)S(1)}, f32[9408]{0:T(1024)S(1)}, u32[]{:S(2)}, u32[]{:S(2)}) collective-permute-start(f32[9408]{0:T(1024)S(1)} %add.168), channel_id=1, source_target_pairs={{0,4},{1,5},{2,6},{3,7},{4,0},{5,1},{6,2},{7,3},{8,12},{9,13},{10,... | collective-permute-start | bytes 112904 | tf_op jit(solution)/shard_map/ppermute | solution.py:76
  189.4 4.5 %collective-permute-start.21 = (f32[18816]{0:T(1024)S(1)}, f32[18816]{0:T(1024)S(1)}, u32[]{:S(2)}, u32[]{:S(2)}) collective-permute-start(f32[18816]{0:T(1024)S(1)} %maximum_select_fusion.2), channel_id=1, source_target_pairs={{0,2},{1,3},{2,0},{3,1},{4,6},{5,7},{6,4},{7,5},{8,10},{9,11},{10,... | collective-permute-start | bytes 225800 | tf_op jit(solution)/shard_map/ppermute | solution.py:76
  193.9 2.7 %collective-permute-start.22 = (f32[37632]{0:T(1024)S(1)}, f32[37632]{0:T(1024)S(1)}, u32[]{:S(2)}, u32[]{:S(2)}) collective-permute-start(f32[37632]{0:T(1024)S(1)} %maximum_select_fusion.1), channel_id=1, source_target_pairs={{0,1},{1,0},{2,3},{3,2},{4,5},{5,4},{6,7},{7,6},{8,9},{9,8},{10,11... | collective-permute-start | bytes 451592 | tf_op jit(solution)/shard_map/ppermute | solution.py:76

commit v11 on v6

--- a/solution.py
+++ b/solution.py
@@ -228,7 +228,7 @@
     kernel_part = kernel_terms(grad_own[0], padded_all[0], reach_rows)
     for image in range(1, batch_dev):
         kernel_part = kernel_part + kernel_terms(grad_own[image], padded_all[image], reach_rows)
-    kernel_sum, input_parts = halving_sum(kernel_part, ("space", "dp"), 3, input_parts)
+    kernel_sum, input_parts = halving_sum(kernel_part, ("space", "dp"), 2, input_parts)
     input_grad = jnp.stack(
         [jnp.concatenate([half[image] for half in input_parts], axis=-1) for image in range(batch_dev)]
     )

time: 198 us -> 198 us (level)
  starting transfers between devices: 39.7 us -> 35.5 us
  waiting for transfers between devices: 58.7 us -> 62.3 us
    ppermute x5 -> x6, waiting for transfers between devices: 20.4 us -> 28.1 us  [halving_sum(): chunk = chunk + lax.ppermute(chunk, axis, pairs)]
    ppermute x3 -> x2, waiting for transfers between devices: 3.63 us -> 0.01 us  [halving_sum(): received = lax.ppermute(give, axis, pairs)]
    ppermute x3 -> x2, starting transfers between devices: 2.36 us -> 0.19 us  [halving_sum(): other = lax.ppermute(chunk, axis, pairs)]
    ppermute x3 -> x2, starting transfers between devices: 4.62 us -> 2.91 us  [halving_sum(): received = lax.ppermute(give, axis, pairs)]
    ppermute x5 -> x6, starting transfers between devices: 6.59 us -> 6.26 us  [halving_sum(): chunk = chunk + lax.ppermute(chunk, axis, pairs)]
  transfers between devices with their start and end apart: 23 -> 22, of which waited for: 17 -> 16; matrix products, arithmetic and copies ran while one was open for 10% -> 10% of each run, Pallas kernels for 15% -> 15%
where the time goes in v11:
time: 198 us; the launch traced here: 195 us
  waiting for transfers between devices  62.3 us (31%)
  starting transfers between devices  35.5 us (18%)
  Pallas kernels  29.8 us (15%)
  matrix products  27.7 us (14%)
  other arithmetic  25.2 us (13%)
  local copies, waits for them, and re-layouts  9.38 us (5%)
  between operations  4.75 us (2%)
    ppermute x6, waiting for transfers between devices, halving_sum(): chunk = chunk + lax.ppermute(chunk, axis, pairs)  28.1 us
    ppermute x8, waiting for transfers between devices, butterfly_sum(): received = lax.ppermute(values, axis, pairs)  24.5 us
    conv_general_dilated x1, matrix products, depthwise(): lax.conv_general_dilated(extended, kernel.reshape(kernel.shape[0], kernel...  21.5 us
    pallas_call x2, Pallas kernels, input_terms(): pl.pallas_call(body, grid=(block_count,), in_specs=[pl.BlockSpec(padded.s...  15.1 us
    pallas_call x1, Pallas kernels, kernel_terms(): pl.pallas_call(body, grid=(channels // lanes,), in_specs=[pl.BlockSpec((r...  14.7 us
    ppermute x8, starting transfers between devices, butterfly_sum(): received = lax.ppermute(values, axis, pairs)  11.6 us
    ppermute x2, starting transfers between devices, with_halo(): lax.ppermute(lax.slice_in_dim(block, 0, width, axis=dim), axis, backward)  10 us
    ppermute x6, starting transfers between devices, halving_sum(): chunk = chunk + lax.ppermute(chunk, axis, pairs)  6.26 us
  transfers between devices with their start and end apart: 22, of which 16 were waited for; matrix products, arithmetic and copies ran while one was open for 10% of the time, Pallas kernels for 15%

profile of v11, /device:TPU:28, one launch (start us, length us, event | category | flops | bytes accessed | tf_op | source)
XLA Modules:
  0.0 194.6 jit_solution(15331102070057561721)
XLA Ops:
  0.7 1.5 fusion.28
  2.1 2.1 %collective-permute-start = (bf16[1,3,64,1536]{3,2,1,0:T(8,128)(2,1)S(1)}, bf16[1,3,64,1536]{3,2,1,0:T(8,128)(2,1)S(1)}, u32[]{:S(2)}, u32[]{:S(2)}) collective-permute-start(bf16[1,3,64,1536]{3,2,1,0:T(8,128)(2,1)S(1)} %get-tuple-element.30), channel_id=1, source_target_pairs={{0,1},{1,2},{2,3},{3,4},{4,5},{5,6},{6,7},{7,8},{8,9},{9,10},{10,1... | collective-permute-start | bytes 1769480 | tf_op jit(solution)/shard_map/ppermute | solution.py:13
  4.2 7.9 %collective-permute-start.1 = (bf16[1,3,64,1536]{3,2,1,0:T(8,128)(2,1)S(1)}, bf16[1,3,64,1536]{3,2,1,0:T(8,128)(2,1)S(1)}, u32[]{:S(2)}, u32[]{:S(2)}) collective-permute-start(bf16[1,3,64,1536]{3,2,1,0:T(8,128)(2,1)S(1)} %get-tuple-element.29), channel_id=1, source_target_pairs={{1,0},{2,1},{3,2},{4,3},{5,4},{6,5},{7,6},{8,7},{9,8},{10,9},{11,1... | collective-permute-start | bytes 1769480 | tf_op jit(solution)/shard_map/ppermute | solution.py:16
  12.1 5.6 %collective-permute-done = bf16[1,3,64,1536]{3,2,1,0:T(8,128)(2,1)S(1)} collective-permute-done((bf16[1,3,64,1536]{3,2,1,0:T(8,128)(2,1)S(1)}, bf16[1,3,64,1536]{3,2,1,0:T(8,128)(2,1)S(1)}, u32[]{:S(2)}, u32[]{:S(2)}) %collective-permute-start) | collective-permute-done | bytes 589856 | tf_op jit(solution)/shard_map/ppermute | solution.py:13
  17.9 1.6 collective-permute-done.1
  19.5 21.5 %fusion.2 = f32[1,8,64,1536]{3,0,2,1:T(1,128)S(1)} fusion(bf16[1,14,64,1536]{3,2,1,0:T(8,128)(2,1)S(1)} %constant_dynamic-update-slice_fusion, bf16[7,7,1,1536]{3,1,0,2:T(8,128)(2,1)S(1)} %bitcast.23), kind=kOutput, calls=%fused_computation.6 | convolution fusion | flops 75005952 | bytes 6048768 | tf_op jit(solution)/shard_map/conv_general_dilated | solution.py:93
  41.3 0.5 multiply_reduce_fusion.1
  41.9 0.8 copy-done.1
  42.6 0.7 add_reduce_fusion
  43.5 3.5 %pad_convert_fusion = f32[1,14,70,1536]{3,2,1,0:T(8,128)} fusion(bf16[1,14,64,1536]{3,2,1,0:T(8,128)(2,1)S(1)} %constant_dynamic-update-slice_fusion), kind=kLoop, calls=%fused_computation.13 | loop fusion | flops 1505280 | bytes 8773632 | tf_op jit(solution)/shard_map/jit(_pad)/pad | solution.py:167
  47.1 3.6 %collective-permute-done.3 = f32[1,1536]{1,0:T(1,128)S(1)} collective-permute-done((f32[1,1536]{1,0:T(1,128)S(1)}, f32[1,1536]{1,0:T(1,128)S(1)}, u32[]{:S(2)}, u32[]{:S(2)}) %collective-permute-start.3) | collective-permute-done | bytes 6176 | tf_op jit(solution)/shard_map/ppermute | solution.py:31
  50.7 3.6 %collective-permute-start.4 = (f32[1,1536]{1,0:T(1,128)S(1)}, f32[1,1536]{1,0:T(1,128)S(1)}, u32[]{:S(2)}, u32[]{:S(2)}) collective-permute-start(f32[1,1536]{1,0:T(1,128)S(1)} %add.123), channel_id=1, source_target_pairs={{0,4},{1,5},{2,6},{3,7},{4,0},{5,1},{6,2},{7,3},{8,12},{9,13},{10,... | collective-permute-start | bytes 18440 | tf_op jit(solution)/shard_map/ppermute | solution.py:31
  54.3 1.6 collective-permute-done.4
  56.0 3.7 %collective-permute-start.5 = (f32[1,1536]{1,0:T(1,128)S(1)}, f32[1,1536]{1,0:T(1,128)S(1)}, u32[]{:S(2)}, u32[]{:S(2)}) collective-permute-start(f32[1,1536]{1,0:T(1,128)S(1)} %add.124), channel_id=1, source_target_pairs={{0,8},{1,9},{2,10},{3,11},{4,12},{5,13},{6,14},{7,15},{8,0},{9,1},... | collective-permute-start | bytes 18440 | tf_op jit(solution)/shard_map/ppermute | solution.py:31
  59.7 3.9 %collective-permute-done.5 = f32[1,1536]{1,0:T(1,128)S(1)} collective-permute-done((f32[1,1536]{1,0:T(1,128)S(1)}, f32[1,1536]{1,0:T(1,128)S(1)}, u32[]{:S(2)}, u32[]{:S(2)}) %collective-permute-start.5) | collective-permute-done | bytes 6176 | tf_op jit(solution)/shard_map/ppermute | solution.py:31
  63.6 1.3 collective-permute-start.6
  64.9 3.9 %collective-permute-done.6 = f32[1,1536]{1,0:T(1,128)S(1)} collective-permute-done((f32[1,1536]{1,0:T(1,128)S(1)}, f32[1,1536]{1,0:T(1,128)S(1)}, u32[]{:S(2)}, u32[]{:S(2)}) %collective-permute-start.6) | collective-permute-done | bytes 6176 | tf_op jit(solution)/shard_map/ppermute | solution.py:31
  69.1 1.3 collective-permute-start.7
  70.4 3.7 %collective-permute-done.7 = f32[8,2560]{1,0:T(8,128)S(1)} collective-permute-done((f32[8,2560]{1,0:T(8,128)S(1)}, f32[8,2560]{1,0:T(8,128)S(1)}, u32[]{:S(2)}, u32[]{:S(2)}) %collective-permute-start.7) | collective-permute-done | bytes 81952 | tf_op jit(solution)/shard_map/ppermute | solution.py:31
  74.4 0.5 collective-permute-start.8
  74.9 5.5 %collective-permute-done.8 = f32[8,2560]{1,0:T(8,128)S(1)} collective-permute-done((f32[8,2560]{1,0:T(8,128)S(1)}, f32[8,2560]{1,0:T(8,128)S(1)}, u32[]{:S(2)}, u32[]{:S(2)}) %collective-permute-start.8) | collective-permute-done | bytes 81952 | tf_op jit(solution)/shard_map/ppermute | solution.py:31
  80.4 1.0 collective-permute-start.9
  81.4 0.8 convert_element_type.20.k_ref
  82.8 2.3 %collective-permute-done.9 = f32[8,2560]{1,0:T(8,128)S(1)} collective-permute-done((f32[8,2560]{1,0:T(8,128)S(1)}, f32[8,2560]{1,0:T(8,128)S(1)}, u32[]{:S(2)}, u32[]{:S(2)}) %collective-permute-start.9) | collective-permute-done | bytes 81952 | tf_op jit(solution)/shard_map/ppermute | solution.py:31
  85.3 1.4 multiply_reduce_fusion.5
  86.7 0.6 dynamic-slice.2
  87.9 0.6 subtract_reduce_fusion
  88.9 0.6 dynamic-slice.1
  89.5 3.7 %convolution_reduce_fusion = f32[1536]{0:T(1024)S(1)} fusion(bf16[1536,1024]{1,0:T(8,128)(2,1)S(1)} %copy-done, f32[8,1024]{1,0:T(8,128)S(1)} %get-tuple-element.35, s32[]{:T(128)S(6)} %select_n.67, f32[8,1024]{1,0:T(8,128)S(1)} %get-tuple-element.39, f32[1]{0:T(128)} %dynamic-slice.2, f32[1]{0:T(128)} %dynamic-slice.1), kind=kOutput, calls=%fused_computation.19 | convolution fusion | flops 18877440 | bytes 3160076 | tf_op jit(solution)/shard_map/dot_general | solution.py:215
  93.2 0.6 fusion.26
  93.8 0.7 multiply_reduce_fusion
  95.2 2.7 %subtract_multiply_fusion = f32[1,8,64,1536]{3,2,1,0:T(8,128)S(1)} fusion(f32[1,8,64,1536]{3,0,2,1:T(1,128)} %copy-done.1, f32[8,64]{1,0:T(8,128)S(1)} %broadcast_multiply_fusion, f32[1536]{0:T(1024)S(1)} %broadcast_subtract_fusion, f32[8,64]{1,0:T(8,128)S(1)} %add_rsqrt_fusion, f32[8,64]{1,0:T(8,128)S(1)} %broadcast_multiply_fusion.1, f32[1536]{0:T(1024)S(1)} %copy-done.8), kind=kLoop, calls=%fused_computation.9 | loop fusion | flops 4718592 | bytes 6309888 | tf_op jit(solution)/shard_map/mul | solution.py:219
  97.9 1.6 fusion.27
  99.5 2.2 %collective-permute-start.12 = (f32[1,3,64,1536]{3,2,1,0:T(8,128)}, f32[1,3,64,1536]{3,2,1,0:T(8,128)}, u32[]{:S(2)}, u32[]{:S(2)}) collective-permute-start(f32[1,3,64,1536]{3,2,1,0:T(8,128)} %get-tuple-element.28), channel_id=1, source_target_pairs={{1,0},{2,1},{3,2},{4,3},{5,4},{6,5},{7,6},{8,7},{9,8},{10,9},{11,1... | collective-permute-start | bytes 3538952 | tf_op jit(solution)/shard_map/ppermute | solution.py:16
  101.7 2.4 %collective-permute-start.11 = (f32[1,3,64,1536]{3,2,1,0:T(8,128)}, f32[1,3,64,1536]{3,2,1,0:T(8,128)}, u32[]{:S(2)}, u32[]{:S(2)}) collective-permute-start(f32[1,3,64,1536]{3,2,1,0:T(8,128)} %get-tuple-element.27), channel_id=1, source_target_pairs={{0,1},{1,2},{2,3},{3,4},{4,5},{5,6},{6,7},{7,8},{8,9},{9,10},{10,1... | collective-permute-start | bytes 3538952 | tf_op jit(solution)/shard_map/ppermute | solution.py:13
  104.1 2.5 %fusion.35.g_ref = f32[8,64,1536]{2,1,0:T(8,128)} fusion(f32[8,64]{1,0:T(8,128)S(1)} %broadcast_multiply_fusion, f32[8,64]{1,0:T(8,128)S(1)} %broadcast_multiply_fusion.1, f32[1536]{0:T(1024)S(1)} %copy-done.8, f32[1,8,64,1536]{3,0,2,1:T(1,128)S(1)} %copy-done.3, f32[1536]{0:T(1024)S(1)} %broadcast_subtract_fusion, f32[8,64]{1,0:T(8,128)S(1)} %add_rsqrt_fusion), kind=kLoop, calls=%fused_computation.79 | loop fusion | flops 4718592 | bytes 6309888 | tf_op jit(solution)/shard_map/squeeze | solution.py:228
  106.6 14.7 %shard_map.111 = f32[7,7,1536]{2,1,0:T(8,128)} custom-call(f32[8,64,1536]{2,1,0:T(8,128)} %fusion.35.g_ref, f32[14,70,1536]{2,1,0:T(8,128)} %bitcast.22), custom_call_target="tpu_custom_call" | custom-call | tf_op jit(solution)/shard_map/pallas_call | solution.py:118
  121.3 1.0 reshape.152
  122.3 0.7 slice_select_fusion
  123.0 1.4 collective-permute-start.10
  124.4 4.7 %fusion.x_ref = f32[14,70,1536]{2,1,0:T(8,128)} fusion(f32[1,3,64,1536]{3,2,1,0:T(8,128)} %collective-permute-done.12, f32[1,8,64,1536]{3,2,1,0:T(8,128)} %copy-done.4, f32[1,3,64,1536]{3,2,1,0:T(8,128)} %collective-permute-done.11), kind=kLoop, calls=%fused_computation.3 | loop fusion | flops 12042240 | bytes 11526144 | tf_op jit(solution)/shard_map/squeeze | solution.py:225
  129.0 7.5 %shard_map.112 = bf16[8,64,768]{2,1,0:T(8,128)(2,1)} custom-call(f32[14,70,1536]{2,1,0:T(8,128)} %fusion.x_ref, f32[7,7,1536]{2,1,0:T(8,128)} %convert_element_type.20.k_ref), custom_call_target="tpu_custom_call" | custom-call | tf_op jit(solution)/shard_map/pallas_call | solution.py:143
  136.6 0.9 select_add_fusion
  137.5 0.7 copy-done.6
  138.2 1.6 collective-permute-start.13
  139.8 7.5 %shard_map.113 = bf16[8,64,768]{2,1,0:T(8,128)(2,1)} custom-call(f32[14,70,1536]{2,1,0:T(8,128)} %fusion.x_ref, f32[7,7,1536]{2,1,0:T(8,128)} %convert_element_type.20.k_ref), custom_call_target="tpu_custom_call" | custom-call | tf_op jit(solution)/shard_map/pallas_call | solution.py:143
  147.3 0.9 select_add_fusion.1
  148.2 1.8 collective-permute-start.14
  150.0 4.8 %collective-permute-done.14 = f32[18816]{0:T(1024)S(1)} collective-permute-done((f32[18816]{0:T(1024)S(1)}, f32[18816]{0:T(1024)S(1)}, u32[]{:S(2)}, u32[]{:S(2)}) %collective-permute-start.14) | collective-permute-done | bytes 75296 | tf_op jit(solution)/shard_map/ppermute | solution.py:72
  154.9 2.1 %collective-permute-start.15 = (f32[18816]{0:T(1024)S(1)}, f32[18816]{0:T(1024)S(1)}, u32[]{:S(2)}, u32[]{:S(2)}) collective-permute-start(f32[18816]{0:T(1024)S(1)} %add.139), channel_id=1, source_target_pairs={{0,8},{1,9},{2,10},{3,11},{4,12},{5,13},{6,14},{7,15},{8,0},{9,1},... | collective-permute-start | bytes 225800 | tf_op jit(solution)/shard_map/ppermute | solution.py:72
  157.0 7.2 %collective-permute-done.15 = f32[18816]{0:T(1024)S(1)} collective-permute-done((f32[18816]{0:T(1024)S(1)}, f32[18816]{0:T(1024)S(1)}, u32[]{:S(2)}, u32[]{:S(2)}) %collective-permute-start.15) | collective-permute-done | bytes 75296 | tf_op jit(solution)/shard_map/ppermute | solution.py:72
  164.2 1.0 collective-permute-start.16
  165.2 5.2 %collective-permute-done.16 = f32[18816]{0:T(1024)S(1)} collective-permute-done((f32[18816]{0:T(1024)S(1)}, f32[18816]{0:T(1024)S(1)}, u32[]{:S(2)}, u32[]{:S(2)}) %collective-permute-start.16) | collective-permute-done | bytes 75296 | tf_op jit(solution)/shard_map/ppermute | solution.py:72
  170.4 0.5 collective-permute-start.17
  170.9 4.0 %collective-permute-done.17 = f32[18816]{0:T(1024)S(1)} collective-permute-done((f32[18816]{0:T(1024)S(1)}, f32[18816]{0:T(1024)S(1)}, u32[]{:S(2)}, u32[]{:S(2)}) %collective-permute-start.17) | collective-permute-done | bytes 75296 | tf_op jit(solution)/shard_map/ppermute | solution.py:72
  174.9 0.7 collective-permute-start.18
  175.6 5.3 %collective-permute-done.18 = f32[18816]{0:T(1024)S(1)} collective-permute-done((f32[18816]{0:T(1024)S(1)}, f32[18816]{0:T(1024)S(1)}, u32[]{:S(2)}, u32[]{:S(2)}) %collective-permute-start.18) | collective-permute-done | bytes 75296 | tf_op jit(solution)/shard_map/ppermute | solution.py:72
  181.4 0.6 dynamic-slice.4
  182.0 0.6 dynamic-slice.3
  183.8 1.6 collective-permute-done.19
  185.5 1.9 fusion.9
  187.4 2.5 %collective-permute-done.20 = f32[18816]{0:T(1024)S(1)} collective-permute-done((f32[18816]{0:T(1024)S(1)}, f32[18816]{0:T(1024)S(1)}, u32[]{:S(2)}, u32[]{:S(2)}) %collective-permute-start.20) | collective-permute-done | bytes 75296 | tf_op jit(solution)/shard_map/ppermute | solution.py:76
  190.0 2.6 %maximum_bitcast_fusion = bf16[1,8,64,1536]{3,2,1,0:T(8,128)(2,1)} fusion(bf16[8,64,768]{2,1,0:T(8,128)(2,1)} %shard_map.113, bf16[8,64,768]{2,1,0:T(8,128)(2,1)} %shard_map.112), kind=kLoop, calls=%fused_computation.16 | loop fusion | flops 3145728 | bytes 3145728 | tf_op jit(solution)/shard_map/stack | solution.py:232
  192.7 0.8 div.85
  (73 shorter events, 3.3 us)
Async XLA Ops:
  0.6 84.6 %copy-start = (bf16[1536,1024]{1,0:T(8,128)(2,1)S(1)}, bf16[1536,1024]{1,0:T(8,128)(2,1)}, u32[]{:S(2)}) copy-start(bf16[1536,1024]{1,0:T(8,128)(2,1)} %param.13) | copy-start | bytes 9437188
  0.6 17.1 %copy-start.5 = (bf16[1,8,64,1536]{3,2,1,0:T(8,128)(2,1)S(1)}, bf16[1,8,64,1536]{3,2,1,0:T(8,128)(2,1)}, u32[]{:S(2)}) copy-start(bf16[1,8,64,1536]{3,2,1,0:T(8,128)(2,1)} %param.8) | copy-start | bytes 4718596
  2.1 17.4 %copy-start.9 = (bf16[7,7,1536]{2,1,0:T(8,128)(2,1)S(1)}, bf16[7,7,1536]{2,1,0:T(8,128)(2,1)}, u32[]{:S(2)}) copy-start(bf16[7,7,1536]{2,1,0:T(8,128)(2,1)} %param.9) | copy-start | bytes 451588
  2.1 15.6 %collective-permute-start = (bf16[1,3,64,1536]{3,2,1,0:T(8,128)(2,1)S(1)}, bf16[1,3,64,1536]{3,2,1,0:T(8,128)(2,1)S(1)}, u32[]{:S(2)}, u32[]{:S(2)}) collective-permute-start(bf16[1,3,64,1536]{3,2,1,0:T(8,128)(2,1)S(1)} %get-tuple-element.30), channel_id=1, source_target_pairs={{0,1},{1,2},{2,3},{3,4},{4,5},{5,6},{6,7},{7,8},{8,9},{9,10},{10,1... | collective-permute-start | bytes 1769480 | tf_op jit(solution)/shard_map/ppermute | solution.py:13
  4.2 15.3 %collective-permute-start.1 = (bf16[1,3,64,1536]{3,2,1,0:T(8,128)(2,1)S(1)}, bf16[1,3,64,1536]{3,2,1,0:T(8,128)(2,1)S(1)}, u32[]{:S(2)}, u32[]{:S(2)}) collective-permute-start(bf16[1,3,64,1536]{3,2,1,0:T(8,128)(2,1)S(1)} %get-tuple-element.29), channel_id=1, source_target_pairs={{1,0},{2,1},{3,2},{4,3},{5,4},{6,5},{7,6},{8,7},{9,8},{10,9},{11,1... | collective-permute-start | bytes 1769480 | tf_op jit(solution)/shard_map/ppermute | solution.py:16
  19.5 21.5 %copy-start.8 = (f32[1536]{0:T(1024)S(1)}, f32[1536]{0:T(1024)}, u32[]{:S(2)}) copy-start(f32[1536]{0:T(1024)} %param.10) | copy-start | bytes 18436
  41.0 1.6 copy-start.1
  41.0 1.6 copy-start.10
  41.0 1.6 copy-start.12
  43.3 25.5 %copy-start.11 = (f32[1,1024]{1,0:T(1,128)S(1)}, f32[1,1024]{1,0:T(1,128)}, u32[]{:S(2)}) copy-start(f32[1,1024]{1,0:T(1,128)} %param.14) | copy-start | bytes 12292
  43.4 3.6 %collective-permute-start.2 = (f32[1,1536]{1,0:T(1,128)S(1)}, f32[1,1536]{1,0:T(1,128)S(1)}, u32[]{:S(2)}, u32[]{:S(2)}) collective-permute-start(f32[1,1536]{1,0:T(1,128)S(1)} %reduce_sum.131), channel_id=1, source_target_pairs={{0,1},{1,0},{2,3},{3,2},{4,5},{5,4},{6,7},{7,6},{8,9},{9,8},{10,11... | collective-permute-start | bytes 18440 | tf_op jit(solution)/shard_map/ppermute | solution.py:31
  47.0 3.7 %collective-permute-start.3 = (f32[1,1536]{1,0:T(1,128)S(1)}, f32[1,1536]{1,0:T(1,128)S(1)}, u32[]{:S(2)}, u32[]{:S(2)}) collective-permute-start(f32[1,1536]{1,0:T(1,128)S(1)} %reshape_add_fusion), channel_id=1, source_target_pairs={{0,2},{1,3},{2,0},{3,1},{4,6},{5,7},{6,4},{7,5},{8,10},{9,11},{10,... | collective-permute-start | bytes 18440 | tf_op jit(solution)/shard_map/ppermute | solution.py:31
  50.7 5.2 %collective-permute-start.4 = (f32[1,1536]{1,0:T(1,128)S(1)}, f32[1,1536]{1,0:T(1,128)S(1)}, u32[]{:S(2)}, u32[]{:S(2)}) collective-permute-start(f32[1,1536]{1,0:T(1,128)S(1)} %add.123), channel_id=1, source_target_pairs={{0,4},{1,5},{2,6},{3,7},{4,0},{5,1},{6,2},{7,3},{8,12},{9,13},{10,... | collective-permute-start | bytes 18440 | tf_op jit(solution)/shard_map/ppermute | solution.py:31
  56.0 7.6 %collective-permute-start.5 = (f32[1,1536]{1,0:T(1,128)S(1)}, f32[1,1536]{1,0:T(1,128)S(1)}, u32[]{:S(2)}, u32[]{:S(2)}) collective-permute-start(f32[1,1536]{1,0:T(1,128)S(1)} %add.124), channel_id=1, source_target_pairs={{0,8},{1,9},{2,10},{3,11},{4,12},{5,13},{6,14},{7,15},{8,0},{9,1},... | collective-permute-start | bytes 18440 | tf_op jit(solution)/shard_map/ppermute | solution.py:31
  63.6 5.2 %collective-permute-start.6 = (f32[1,1536]{1,0:T(1,128)S(1)}, f32[1,1536]{1,0:T(1,128)S(1)}, u32[]{:S(2)}, u32[]{:S(2)}) collective-permute-start(f32[1,1536]{1,0:T(1,128)S(1)} %add.125), channel_id=1, source_target_pairs={{0,16},{1,17},{2,18},{3,19},{4,20},{5,21},{6,22},{7,23},{8,24},{9,... | collective-permute-start | bytes 18440 | tf_op jit(solution)/shard_map/ppermute | solution.py:31
  69.1 4.9 %collective-permute-start.7 = (f32[8,2560]{1,0:T(8,128)S(1)}, f32[8,2560]{1,0:T(8,128)S(1)}, u32[]{:S(2)}, u32[]{:S(2)}) collective-permute-start(f32[8,2560]{1,0:T(8,128)S(1)} %dynamic_update_slice.5), channel_id=1, source_target_pairs={{0,32},{32,0},{64,96},{96,64},{128,160},{160,128},{192,224},{224,1... | collective-permute-start | bytes 245768 | tf_op jit(solution)/shard_map/ppermute | solution.py:31
  74.4 6.0 %collective-permute-start.8 = (f32[8,2560]{1,0:T(8,128)S(1)}, f32[8,2560]{1,0:T(8,128)S(1)}, u32[]{:S(2)}, u32[]{:S(2)}) collective-permute-start(f32[8,2560]{1,0:T(8,128)S(1)} %add.128), channel_id=1, source_target_pairs={{0,64},{32,96},{64,0},{96,32},{128,192},{160,224},{192,128},{224,1... | collective-permute-start | bytes 245768 | tf_op jit(solution)/shard_map/ppermute | solution.py:31
  80.4 4.7 %collective-permute-start.9 = (f32[8,2560]{1,0:T(8,128)S(1)}, f32[8,2560]{1,0:T(8,128)S(1)}, u32[]{:S(2)}, u32[]{:S(2)}) collective-permute-start(f32[8,2560]{1,0:T(8,128)S(1)} %add.129), channel_id=1, source_target_pairs={{0,128},{32,160},{64,192},{96,224},{128,0},{160,32},{192,64},{224,... | collective-permute-start | bytes 245768 | tf_op jit(solution)/shard_map/ppermute | solution.py:31
  85.3 8.6 %copy-start.2 = (f32[1,8,64,1536]{3,0,2,1:T(1,128)S(1)}, f32[1,8,64,1536]{3,0,2,1:T(1,128)}, u32[]{:S(2)}) copy-start(f32[1,8,64,1536]{3,0,2,1:T(1,128)} %copy-done.1) | copy-start | bytes 9437188
  97.9 8.7 %copy-start.4 = (f32[1,8,64,1536]{3,2,1,0:T(8,128)}, f32[1,8,64,1536]{3,2,1,0:T(8,128)S(1)}, u32[]{:S(2)}) copy-start(f32[1,8,64,1536]{3,2,1,0:T(8,128)S(1)} %subtract_multiply_fusion) | copy-start | bytes 9437188
  97.9 6.2 %copy-start.3 = (f32[1,8,64,1536]{3,0,2,1:T(1,128)S(1)}, f32[1,8,64,1536]{3,0,2,1:T(1,128)}, u32[]{:S(2)}) copy-start(f32[1,8,64,1536]{3,0,2,1:T(1,128)} %copy-done.1) | copy-start | bytes 9437188
  99.5 24.8 %collective-permute-start.12 = (f32[1,3,64,1536]{3,2,1,0:T(8,128)}, f32[1,3,64,1536]{3,2,1,0:T(8,128)}, u32[]{:S(2)}, u32[]{:S(2)}) collective-permute-start(f32[1,3,64,1536]{3,2,1,0:T(8,128)} %get-tuple-element.28), channel_id=1, source_target_pairs={{1,0},{2,1},{3,2},{4,3},{5,4},{6,5},{7,6},{8,7},{9,8},{10,9},{11,1... | collective-permute-start | bytes 3538952 | tf_op jit(solution)/shard_map/ppermute | solution.py:16
  101.7 22.7 %collective-permute-start.11 = (f32[1,3,64,1536]{3,2,1,0:T(8,128)}, f32[1,3,64,1536]{3,2,1,0:T(8,128)}, u32[]{:S(2)}, u32[]{:S(2)}) collective-permute-start(f32[1,3,64,1536]{3,2,1,0:T(8,128)} %get-tuple-element.27), channel_id=1, source_target_pairs={{0,1},{1,2},{2,3},{3,4},{4,5},{5,6},{6,7},{7,8},{8,9},{9,10},{10,1... | collective-permute-start | bytes 3538952 | tf_op jit(solution)/shard_map/ppermute | solution.py:13
  123.0 13.6 %collective-permute-start.10 = (f32[37632]{0:T(1024)}, f32[37632]{0:T(1024)}, u32[]{:S(2)}, u32[]{:S(2)}) collective-permute-start(f32[37632]{0:T(1024)} %slice_select_fusion), channel_id=1, source_target_pairs={{0,1},{1,0},{2,3},{3,2},{4,5},{5,4},{6,7},{7,6},{8,9},{9,8},{10,11... | collective-permute-start | bytes 451592 | tf_op jit(solution)/shard_map/ppermute | solution.py:65
  137.5 0.7 copy-start.6
  138.2 9.1 %copy-start.7 = (f32[37632]{0:T(1024)S(1)}, f32[37632]{0:T(1024)}, u32[]{:S(2)}) copy-start(f32[37632]{0:T(1024)} %copy-done.6) | copy-start | bytes 451588
  138.2 9.1 %collective-permute-start.13 = (f32[18816]{0:T(1024)S(1)}, f32[18816]{0:T(1024)}, u32[]{:S(2)}, u32[]{:S(2)}) collective-permute-start(f32[18816]{0:T(1024)S(1)} %slice_select_fusion.1), channel_id=1, source_target_pairs={{0,2},{1,3},{2,0},{3,1},{4,6},{5,7},{6,4},{7,5},{8,10},{9,11},{10,... | collective-permute-start | bytes 225800 | tf_op jit(solution)/shard_map/ppermute | solution.py:65
  148.2 6.6 %collective-permute-start.14 = (f32[18816]{0:T(1024)S(1)}, f32[18816]{0:T(1024)S(1)}, u32[]{:S(2)}, u32[]{:S(2)}) collective-permute-start(f32[18816]{0:T(1024)S(1)} %select_add_fusion.1), channel_id=1, source_target_pairs={{0,4},{1,5},{2,6},{3,7},{4,0},{5,1},{6,2},{7,3},{8,12},{9,13},{10,... | collective-permute-start | bytes 225800 | tf_op jit(solution)/shard_map/ppermute | solution.py:72
  154.9 9.3 %collective-permute-start.15 = (f32[18816]{0:T(1024)S(1)}, f32[18816]{0:T(1024)S(1)}, u32[]{:S(2)}, u32[]{:S(2)}) collective-permute-start(f32[18816]{0:T(1024)S(1)} %add.139), channel_id=1, source_target_pairs={{0,8},{1,9},{2,10},{3,11},{4,12},{5,13},{6,14},{7,15},{8,0},{9,1},... | collective-permute-start | bytes 225800 | tf_op jit(solution)/shard_map/ppermute | solution.py:72
  164.2 6.2 %collective-permute-start.16 = (f32[18816]{0:T(1024)S(1)}, f32[18816]{0:T(1024)S(1)}, u32[]{:S(2)}, u32[]{:S(2)}) collective-permute-start(f32[18816]{0:T(1024)S(1)} %add.140), channel_id=1, source_target_pairs={{0,16},{1,17},{2,18},{3,19},{4,20},{5,21},{6,22},{7,23},{8,24},{9,... | collective-permute-start | bytes 225800 | tf_op jit(solution)/shard_map/ppermute | solution.py:72
  170.4 4.5 %collective-permute-start.17 = (f32[18816]{0:T(1024)S(1)}, f32[18816]{0:T(1024)S(1)}, u32[]{:S(2)}, u32[]{:S(2)}) collective-permute-start(f32[18816]{0:T(1024)S(1)} %add.141), channel_id=1, source_target_pairs={{0,32},{32,0},{64,96},{96,64},{128,160},{160,128},{192,224},{224,1... | collective-permute-start | bytes 225800 | tf_op jit(solution)/shard_map/ppermute | solution.py:72
  174.9 6.0 %collective-permute-start.18 = (f32[18816]{0:T(1024)S(1)}, f32[18816]{0:T(1024)S(1)}, u32[]{:S(2)}, u32[]{:S(2)}) collective-permute-start(f32[18816]{0:T(1024)S(1)} %add.142), channel_id=1, source_target_pairs={{0,64},{32,96},{64,0},{96,32},{128,192},{160,224},{192,128},{224,1... | collective-permute-start | bytes 225800 | tf_op jit(solution)/shard_map/ppermute | solution.py:72
  180.9 4.5 %collective-permute-start.19 = (f32[18816]{0:T(1024)S(1)}, f32[18816]{0:T(1024)S(1)}, u32[]{:S(2)}, u32[]{:S(2)}) collective-permute-start(f32[18816]{0:T(1024)S(1)} %add.143), channel_id=1, source_target_pairs={{0,128},{32,160},{64,192},{96,224},{128,0},{160,32},{192,64},{224,... | collective-permute-start | bytes 225800 | tf_op jit(solution)/shard_map/ppermute | solution.py:72
  185.4 4.5 %collective-permute-start.20 = (f32[18816]{0:T(1024)S(1)}, f32[18816]{0:T(1024)S(1)}, u32[]{:S(2)}, u32[]{:S(2)}) collective-permute-start(f32[18816]{0:T(1024)S(1)} %add.144), channel_id=1, source_target_pairs={{0,2},{1,3},{2,0},{3,1},{4,6},{5,7},{6,4},{7,5},{8,10},{9,11},{10,... | collective-permute-start | bytes 225800 | tf_op jit(solution)/shard_map/ppermute | solution.py:76
  189.9 2.7 %collective-permute-start.21 = (f32[37632]{0:T(1024)S(1)}, f32[37632]{0:T(1024)S(1)}, u32[]{:S(2)}, u32[]{:S(2)}) collective-permute-start(f32[37632]{0:T(1024)S(1)} %maximum_select_fusion.1), channel_id=1, source_target_pairs={{0,1},{1,0},{2,3},{3,2},{4,5},{5,4},{6,7},{7,6},{8,9},{9,8},{10,11... | collective-permute-start | bytes 451592 | tf_op jit(solution)/shard_map/ppermute | solution.py:76

commit v12 on v6

--- a/solution.py
+++ b/solution.py
@@ -48,6 +48,8 @@
         while step < count:
             steps.append((axis, count, step))
             step *= 2
+    nearest = [s for s in steps if s[2] == 1][1:]
+    steps = steps[:2] + nearest + [s for s in steps[2:] if s not in nearest]
     split_steps = min(split_steps, len(steps))
     riders_done = []
     parts = 1 << split_steps

time: 198 us -> 197 us (level)
  no operation moved by 1% of the time
where the time goes in v12:
time: 197 us; the launch traced here: 194 us
  waiting for transfers between devices  59.3 us (30%)
  starting transfers between devices  38.1 us (19%)
  Pallas kernels  29.8 us (15%)
  matrix products  27.7 us (14%)
  other arithmetic  25.2 us (13%)
  local copies, waits for them, and re-layouts  9.38 us (5%)
  between operations  4.73 us (2%)
    ppermute x8, waiting for transfers between devices, butterfly_sum(): received = lax.ppermute(values, axis, pairs)  24.5 us
    ppermute x5, waiting for transfers between devices, halving_sum(): chunk = chunk + lax.ppermute(chunk, axis, pairs)  22 us
    conv_general_dilated x1, matrix products, depthwise(): lax.conv_general_dilated(extended, kernel.reshape(kernel.shape[0], kernel...  21.5 us
    pallas_call x2, Pallas kernels, input_terms(): pl.pallas_call(body, grid=(block_count,), in_specs=[pl.BlockSpec(padded.s...  15.1 us
    pallas_call x1, Pallas kernels, kernel_terms(): pl.pallas_call(body, grid=(channels // lanes,), in_specs=[pl.BlockSpec((r...  14.7 us
    ppermute x8, starting transfers between devices, butterfly_sum(): received = lax.ppermute(values, axis, pairs)  11.6 us
    ppermute x2, starting transfers between devices, with_halo(): lax.ppermute(lax.slice_in_dim(block, 0, width, axis=dim), axis, backward)  10 us
    ppermute x5, starting transfers between devices, halving_sum(): chunk = chunk + lax.ppermute(chunk, axis, pairs)  6.77 us
  transfers between devices with their start and end apart: 23, of which 17 were waited for; matrix products, arithmetic and copies ran while one was open for 10% of the time, Pallas kernels for 15%

profile of v12, /device:TPU:28, one launch (start us, length us, event | category | flops | bytes accessed | tf_op | source)
XLA Modules:
  0.0 194.3 jit_solution(14497992646021760912)
XLA Ops:
  0.7 1.5 fusion.28
  2.1 2.1 %collective-permute-start = (bf16[1,3,64,1536]{3,2,1,0:T(8,128)(2,1)S(1)}, bf16[1,3,64,1536]{3,2,1,0:T(8,128)(2,1)S(1)}, u32[]{:S(2)}, u32[]{:S(2)}) collective-permute-start(bf16[1,3,64,1536]{3,2,1,0:T(8,128)(2,1)S(1)} %get-tuple-element.30), channel_id=1, source_target_pairs={{0,1},{1,2},{2,3},{3,4},{4,5},{5,6},{6,7},{7,8},{8,9},{9,10},{10,1... | collective-permute-start | bytes 1769480 | tf_op jit(solution)/shard_map/ppermute | solution.py:13
  4.2 7.9 %collective-permute-start.1 = (bf16[1,3,64,1536]{3,2,1,0:T(8,128)(2,1)S(1)}, bf16[1,3,64,1536]{3,2,1,0:T(8,128)(2,1)S(1)}, u32[]{:S(2)}, u32[]{:S(2)}) collective-permute-start(bf16[1,3,64,1536]{3,2,1,0:T(8,128)(2,1)S(1)} %get-tuple-element.29), channel_id=1, source_target_pairs={{1,0},{2,1},{3,2},{4,3},{5,4},{6,5},{7,6},{8,7},{9,8},{10,9},{11,1... | collective-permute-start | bytes 1769480 | tf_op jit(solution)/shard_map/ppermute | solution.py:16
  12.1 5.6 %collective-permute-done = bf16[1,3,64,1536]{3,2,1,0:T(8,128)(2,1)S(1)} collective-permute-done((bf16[1,3,64,1536]{3,2,1,0:T(8,128)(2,1)S(1)}, bf16[1,3,64,1536]{3,2,1,0:T(8,128)(2,1)S(1)}, u32[]{:S(2)}, u32[]{:S(2)}) %collective-permute-start) | collective-permute-done | bytes 589856 | tf_op jit(solution)/shard_map/ppermute | solution.py:13
  17.9 1.6 collective-permute-done.1
  19.5 21.5 %fusion.2 = f32[1,8,64,1536]{3,0,2,1:T(1,128)S(1)} fusion(bf16[1,14,64,1536]{3,2,1,0:T(8,128)(2,1)S(1)} %constant_dynamic-update-slice_fusion, bf16[7,7,1,1536]{3,1,0,2:T(8,128)(2,1)S(1)} %bitcast.23), kind=kOutput, calls=%fused_computation.6 | convolution fusion | flops 75005952 | bytes 6048768 | tf_op jit(solution)/shard_map/conv_general_dilated | solution.py:95
  41.9 0.8 copy-done.1
  42.6 0.7 add_reduce_fusion
  43.5 3.5 %pad_convert_fusion = f32[1,14,70,1536]{3,2,1,0:T(8,128)} fusion(bf16[1,14,64,1536]{3,2,1,0:T(8,128)(2,1)S(1)} %constant_dynamic-update-slice_fusion), kind=kLoop, calls=%fused_computation.13 | loop fusion | flops 1505280 | bytes 8773632 | tf_op jit(solution)/shard_map/jit(_pad)/pad | solution.py:169
  47.1 3.6 %collective-permute-done.3 = f32[1,1536]{1,0:T(1,128)S(1)} collective-permute-done((f32[1,1536]{1,0:T(1,128)S(1)}, f32[1,1536]{1,0:T(1,128)S(1)}, u32[]{:S(2)}, u32[]{:S(2)}) %collective-permute-start.3) | collective-permute-done | bytes 6176 | tf_op jit(solution)/shard_map/ppermute | solution.py:31
  50.7 3.6 %collective-permute-start.4 = (f32[1,1536]{1,0:T(1,128)S(1)}, f32[1,1536]{1,0:T(1,128)S(1)}, u32[]{:S(2)}, u32[]{:S(2)}) collective-permute-start(f32[1,1536]{1,0:T(1,128)S(1)} %add.128), channel_id=1, source_target_pairs={{0,4},{1,5},{2,6},{3,7},{4,0},{5,1},{6,2},{7,3},{8,12},{9,13},{10,... | collective-permute-start | bytes 18440 | tf_op jit(solution)/shard_map/ppermute | solution.py:31
  54.3 1.6 collective-permute-done.4
  56.0 3.7 %collective-permute-start.5 = (f32[1,1536]{1,0:T(1,128)S(1)}, f32[1,1536]{1,0:T(1,128)S(1)}, u32[]{:S(2)}, u32[]{:S(2)}) collective-permute-start(f32[1,1536]{1,0:T(1,128)S(1)} %add.129), channel_id=1, source_target_pairs={{0,8},{1,9},{2,10},{3,11},{4,12},{5,13},{6,14},{7,15},{8,0},{9,1},... | collective-permute-start | bytes 18440 | tf_op jit(solution)/shard_map/ppermute | solution.py:31
  59.7 3.9 %collective-permute-done.5 = f32[1,1536]{1,0:T(1,128)S(1)} collective-permute-done((f32[1,1536]{1,0:T(1,128)S(1)}, f32[1,1536]{1,0:T(1,128)S(1)}, u32[]{:S(2)}, u32[]{:S(2)}) %collective-permute-start.5) | collective-permute-done | bytes 6176 | tf_op jit(solution)/shard_map/ppermute | solution.py:31
  63.6 1.3 collective-permute-start.6
  64.9 3.9 %collective-permute-done.6 = f32[1,1536]{1,0:T(1,128)S(1)} collective-permute-done((f32[1,1536]{1,0:T(1,128)S(1)}, f32[1,1536]{1,0:T(1,128)S(1)}, u32[]{:S(2)}, u32[]{:S(2)}) %collective-permute-start.6) | collective-permute-done | bytes 6176 | tf_op jit(solution)/shard_map/ppermute | solution.py:31
  69.1 1.3 collective-permute-start.7
  70.4 3.7 %collective-permute-done.7 = f32[8,2560]{1,0:T(8,128)S(1)} collective-permute-done((f32[8,2560]{1,0:T(8,128)S(1)}, f32[8,2560]{1,0:T(8,128)S(1)}, u32[]{:S(2)}, u32[]{:S(2)}) %collective-permute-start.7) | collective-permute-done | bytes 81952 | tf_op jit(solution)/shard_map/ppermute | solution.py:31
  74.9 5.5 %collective-permute-done.8 = f32[8,2560]{1,0:T(8,128)S(1)} collective-permute-done((f32[8,2560]{1,0:T(8,128)S(1)}, f32[8,2560]{1,0:T(8,128)S(1)}, u32[]{:S(2)}, u32[]{:S(2)}) %collective-permute-start.8) | collective-permute-done | bytes 81952 | tf_op jit(solution)/shard_map/ppermute | solution.py:31
  80.4 1.0 collective-permute-start.9
  81.4 0.8 convert_element_type.20.k_ref
  82.8 2.3 %collective-permute-done.9 = f32[8,2560]{1,0:T(8,128)S(1)} collective-permute-done((f32[8,2560]{1,0:T(8,128)S(1)}, f32[8,2560]{1,0:T(8,128)S(1)}, u32[]{:S(2)}, u32[]{:S(2)}) %collective-permute-start.9) | collective-permute-done | bytes 81952 | tf_op jit(solution)/shard_map/ppermute | solution.py:31
  85.3 1.4 multiply_reduce_fusion.5
  86.7 0.6 dynamic-slice.2
  87.9 0.6 subtract_reduce_fusion
  88.9 0.6 dynamic-slice.1
  89.5 3.7 %convolution_reduce_fusion = f32[1536]{0:T(1024)S(1)} fusion(bf16[1536,1024]{1,0:T(8,128)(2,1)S(1)} %copy-done, f32[8,1024]{1,0:T(8,128)S(1)} %get-tuple-element.35, s32[]{:T(128)S(6)} %select_n.93, f32[8,1024]{1,0:T(8,128)S(1)} %get-tuple-element.39, f32[1]{0:T(128)} %dynamic-slice.2, f32[1]{0:T(128)} %dynamic-slice.1), kind=kOutput, calls=%fused_computation.19 | convolution fusion | flops 18877440 | bytes 3160076 | tf_op jit(solution)/shard_map/dot_general | solution.py:217
  93.2 0.6 fusion.26
  93.8 0.7 multiply_reduce_fusion
  95.2 2.7 %subtract_multiply_fusion = f32[1,8,64,1536]{3,2,1,0:T(8,128)S(1)} fusion(f32[1,8,64,1536]{3,0,2,1:T(1,128)} %copy-done.1, f32[8,64]{1,0:T(8,128)S(1)} %broadcast_multiply_fusion, f32[1536]{0:T(1024)S(1)} %broadcast_subtract_fusion, f32[8,64]{1,0:T(8,128)S(1)} %add_rsqrt_fusion, f32[8,64]{1,0:T(8,128)S(1)} %broadcast_multiply_fusion.1, f32[1536]{0:T(1024)S(1)} %copy-done.8), kind=kLoop, calls=%fused_computation.9 | loop fusion | flops 4718592 | bytes 6309888 | tf_op jit(solution)/shard_map/mul | solution.py:221
  97.9 1.6 fusion.27
  99.5 2.2 %collective-permute-start.12 = (f32[1,3,64,1536]{3,2,1,0:T(8,128)}, f32[1,3,64,1536]{3,2,1,0:T(8,128)}, u32[]{:S(2)}, u32[]{:S(2)}) collective-permute-start(f32[1,3,64,1536]{3,2,1,0:T(8,128)} %get-tuple-element.28), channel_id=1, source_target_pairs={{1,0},{2,1},{3,2},{4,3},{5,4},{6,5},{7,6},{8,7},{9,8},{10,9},{11,1... | collective-permute-start | bytes 3538952 | tf_op jit(solution)/shard_map/ppermute | solution.py:16
  101.7 2.4 %collective-permute-start.11 = (f32[1,3,64,1536]{3,2,1,0:T(8,128)}, f32[1,3,64,1536]{3,2,1,0:T(8,128)}, u32[]{:S(2)}, u32[]{:S(2)}) collective-permute-start(f32[1,3,64,1536]{3,2,1,0:T(8,128)} %get-tuple-element.27), channel_id=1, source_target_pairs={{0,1},{1,2},{2,3},{3,4},{4,5},{5,6},{6,7},{7,8},{8,9},{9,10},{10,1... | collective-permute-start | bytes 3538952 | tf_op jit(solution)/shard_map/ppermute | solution.py:13
  104.1 2.5 %fusion.35.g_ref = f32[8,64,1536]{2,1,0:T(8,128)} fusion(f32[8,64]{1,0:T(8,128)S(1)} %broadcast_multiply_fusion, f32[8,64]{1,0:T(8,128)S(1)} %broadcast_multiply_fusion.1, f32[1536]{0:T(1024)S(1)} %copy-done.8, f32[1,8,64,1536]{3,0,2,1:T(1,128)S(1)} %copy-done.3, f32[1536]{0:T(1024)S(1)} %broadcast_subtract_fusion, f32[8,64]{1,0:T(8,128)S(1)} %add_rsqrt_fusion), kind=kLoop, calls=%fused_computation.82 | loop fusion | flops 4718592 | bytes 6309888 | tf_op jit(solution)/shard_map/squeeze | solution.py:230
  106.6 14.7 %shard_map.111 = f32[7,7,1536]{2,1,0:T(8,128)} custom-call(f32[8,64,1536]{2,1,0:T(8,128)} %fusion.35.g_ref, f32[14,70,1536]{2,1,0:T(8,128)} %bitcast.22), custom_call_target="tpu_custom_call" | custom-call | tf_op jit(solution)/shard_map/pallas_call | solution.py:120
  121.3 1.0 reshape.152
  122.3 0.7 slice_select_fusion
  123.0 1.4 collective-permute-start.10
  124.4 4.7 %fusion.x_ref = f32[14,70,1536]{2,1,0:T(8,128)} fusion(f32[1,3,64,1536]{3,2,1,0:T(8,128)} %collective-permute-done.12, f32[1,8,64,1536]{3,2,1,0:T(8,128)} %copy-done.4, f32[1,3,64,1536]{3,2,1,0:T(8,128)} %collective-permute-done.11), kind=kLoop, calls=%fused_computation.3 | loop fusion | flops 12042240 | bytes 11526144 | tf_op jit(solution)/shard_map/squeeze | solution.py:227
  129.0 7.5 %shard_map.112 = bf16[8,64,768]{2,1,0:T(8,128)(2,1)} custom-call(f32[14,70,1536]{2,1,0:T(8,128)} %fusion.x_ref, f32[7,7,1536]{2,1,0:T(8,128)} %convert_element_type.20.k_ref), custom_call_target="tpu_custom_call" | custom-call | tf_op jit(solution)/shard_map/pallas_call | solution.py:145
  136.6 0.9 select_add_fusion
  137.5 0.7 copy-done.6
  138.2 0.6 slice_select_fusion.1
  138.8 1.5 collective-permute-start.13
  140.3 7.6 %shard_map.113 = bf16[8,64,768]{2,1,0:T(8,128)(2,1)} custom-call(f32[14,70,1536]{2,1,0:T(8,128)} %fusion.x_ref, f32[7,7,1536]{2,1,0:T(8,128)} %convert_element_type.20.k_ref), custom_call_target="tpu_custom_call" | custom-call | tf_op jit(solution)/shard_map/pallas_call | solution.py:145
  148.0 1.1 collective-permute-start.14
  149.1 2.9 %collective-permute-done.14 = f32[9408]{0:T(1024)S(1)} collective-permute-done((f32[9408]{0:T(1024)S(1)}, f32[9408]{0:T(1024)S(1)}, u32[]{:S(2)}, u32[]{:S(2)}) %collective-permute-start.14) | collective-permute-done | bytes 37664 | tf_op jit(solution)/shard_map/ppermute | solution.py:67
  152.1 1.8 collective-permute-start.15
  153.9 3.6 %collective-permute-done.15 = f32[9408]{0:T(1024)S(1)} collective-permute-done((f32[9408]{0:T(1024)S(1)}, f32[9408]{0:T(1024)S(1)}, u32[]{:S(2)}, u32[]{:S(2)}) %collective-permute-start.15) | collective-permute-done | bytes 37664 | tf_op jit(solution)/shard_map/ppermute | solution.py:74
  157.6 1.6 collective-permute-start.16
  159.2 6.3 %collective-permute-done.16 = f32[9408]{0:T(1024)S(1)} collective-permute-done((f32[9408]{0:T(1024)S(1)}, f32[9408]{0:T(1024)S(1)}, u32[]{:S(2)}, u32[]{:S(2)}) %collective-permute-start.16) | collective-permute-done | bytes 37664 | tf_op jit(solution)/shard_map/ppermute | solution.py:74
  165.5 1.2 collective-permute-start.17
  166.7 4.3 %collective-permute-done.17 = f32[9408]{0:T(1024)S(1)} collective-permute-done((f32[9408]{0:T(1024)S(1)}, f32[9408]{0:T(1024)S(1)}, u32[]{:S(2)}, u32[]{:S(2)}) %collective-permute-start.17) | collective-permute-done | bytes 37664 | tf_op jit(solution)/shard_map/ppermute | solution.py:74
  171.0 1.0 collective-permute-start.18
  172.0 4.9 %collective-permute-done.18 = f32[9408]{0:T(1024)S(1)} collective-permute-done((f32[9408]{0:T(1024)S(1)}, f32[9408]{0:T(1024)S(1)}, u32[]{:S(2)}, u32[]{:S(2)}) %collective-permute-start.18) | collective-permute-done | bytes 37664 | tf_op jit(solution)/shard_map/ppermute | solution.py:74
  176.9 1.1 collective-permute-start.19
  178.1 2.9 %collective-permute-done.19 = f32[9408]{0:T(1024)S(1)} collective-permute-done((f32[9408]{0:T(1024)S(1)}, f32[9408]{0:T(1024)S(1)}, u32[]{:S(2)}, u32[]{:S(2)}) %collective-permute-start.19) | collective-permute-done | bytes 37664 | tf_op jit(solution)/shard_map/ppermute | solution.py:74
  181.0 1.1 collective-permute-start.20
  182.4 0.6 dynamic-slice.4
  183.0 0.6 dynamic-slice.3
  185.2 1.9 fusion.9
  187.1 2.5 %collective-permute-done.21 = f32[18816]{0:T(1024)S(1)} collective-permute-done((f32[18816]{0:T(1024)S(1)}, f32[18816]{0:T(1024)S(1)}, u32[]{:S(2)}, u32[]{:S(2)}) %collective-permute-start.21) | collective-permute-done | bytes 75296 | tf_op jit(solution)/shard_map/ppermute | solution.py:78
  189.7 2.6 %maximum_bitcast_fusion = bf16[1,8,64,1536]{3,2,1,0:T(8,128)(2,1)} fusion(bf16[8,64,768]{2,1,0:T(8,128)(2,1)} %shard_map.113, bf16[8,64,768]{2,1,0:T(8,128)(2,1)} %shard_map.112), kind=kLoop, calls=%fused_computation.16 | loop fusion | flops 3145728 | bytes 3145728 | tf_op jit(solution)/shard_map/stack | solution.py:234
  192.4 0.8 div.87
  (77 shorter events, 4.6 us)
Async XLA Ops:
  0.6 84.6 %copy-start = (bf16[1536,1024]{1,0:T(8,128)(2,1)S(1)}, bf16[1536,1024]{1,0:T(8,128)(2,1)}, u32[]{:S(2)}) copy-start(bf16[1536,1024]{1,0:T(8,128)(2,1)} %param.13) | copy-start | bytes 9437188
  0.6 17.1 %copy-start.5 = (bf16[1,8,64,1536]{3,2,1,0:T(8,128)(2,1)S(1)}, bf16[1,8,64,1536]{3,2,1,0:T(8,128)(2,1)}, u32[]{:S(2)}) copy-start(bf16[1,8,64,1536]{3,2,1,0:T(8,128)(2,1)} %param.8) | copy-start | bytes 4718596
  2.1 17.4 %copy-start.9 = (bf16[7,7,1536]{2,1,0:T(8,128)(2,1)S(1)}, bf16[7,7,1536]{2,1,0:T(8,128)(2,1)}, u32[]{:S(2)}) copy-start(bf16[7,7,1536]{2,1,0:T(8,128)(2,1)} %param.9) | copy-start | bytes 451588
  2.1 15.6 %collective-permute-start = (bf16[1,3,64,1536]{3,2,1,0:T(8,128)(2,1)S(1)}, bf16[1,3,64,1536]{3,2,1,0:T(8,128)(2,1)S(1)}, u32[]{:S(2)}, u32[]{:S(2)}) collective-permute-start(bf16[1,3,64,1536]{3,2,1,0:T(8,128)(2,1)S(1)} %get-tuple-element.30), channel_id=1, source_target_pairs={{0,1},{1,2},{2,3},{3,4},{4,5},{5,6},{6,7},{7,8},{8,9},{9,10},{10,1... | collective-permute-start | bytes 1769480 | tf_op jit(solution)/shard_map/ppermute | solution.py:13
  4.2 15.3 %collective-permute-start.1 = (bf16[1,3,64,1536]{3,2,1,0:T(8,128)(2,1)S(1)}, bf16[1,3,64,1536]{3,2,1,0:T(8,128)(2,1)S(1)}, u32[]{:S(2)}, u32[]{:S(2)}) collective-permute-start(bf16[1,3,64,1536]{3,2,1,0:T(8,128)(2,1)S(1)} %get-tuple-element.29), channel_id=1, source_target_pairs={{1,0},{2,1},{3,2},{4,3},{5,4},{6,5},{7,6},{8,7},{9,8},{10,9},{11,1... | collective-permute-start | bytes 1769480 | tf_op jit(solution)/shard_map/ppermute | solution.py:16
  19.5 21.5 %copy-start.8 = (f32[1536]{0:T(1024)S(1)}, f32[1536]{0:T(1024)}, u32[]{:S(2)}) copy-start(f32[1536]{0:T(1024)} %param.10) | copy-start | bytes 18436
  41.0 1.6 copy-start.1
  41.0 1.6 copy-start.10
  41.0 1.6 copy-start.12
  43.3 25.5 %copy-start.11 = (f32[1,1024]{1,0:T(1,128)S(1)}, f32[1,1024]{1,0:T(1,128)}, u32[]{:S(2)}) copy-start(f32[1,1024]{1,0:T(1,128)} %param.14) | copy-start | bytes 12292
  43.4 3.6 %collective-permute-start.2 = (f32[1,1536]{1,0:T(1,128)S(1)}, f32[1,1536]{1,0:T(1,128)S(1)}, u32[]{:S(2)}, u32[]{:S(2)}) collective-permute-start(f32[1,1536]{1,0:T(1,128)S(1)} %reduce_sum.131), channel_id=1, source_target_pairs={{0,1},{1,0},{2,3},{3,2},{4,5},{5,4},{6,7},{7,6},{8,9},{9,8},{10,11... | collective-permute-start | bytes 18440 | tf_op jit(solution)/shard_map/ppermute | solution.py:31
  47.0 3.7 %collective-permute-start.3 = (f32[1,1536]{1,0:T(1,128)S(1)}, f32[1,1536]{1,0:T(1,128)S(1)}, u32[]{:S(2)}, u32[]{:S(2)}) collective-permute-start(f32[1,1536]{1,0:T(1,128)S(1)} %reshape_add_fusion), channel_id=1, source_target_pairs={{0,2},{1,3},{2,0},{3,1},{4,6},{5,7},{6,4},{7,5},{8,10},{9,11},{10,... | collective-permute-start | bytes 18440 | tf_op jit(solution)/shard_map/ppermute | solution.py:31
  50.7 5.2 %collective-permute-start.4 = (f32[1,1536]{1,0:T(1,128)S(1)}, f32[1,1536]{1,0:T(1,128)S(1)}, u32[]{:S(2)}, u32[]{:S(2)}) collective-permute-start(f32[1,1536]{1,0:T(1,128)S(1)} %add.128), channel_id=1, source_target_pairs={{0,4},{1,5},{2,6},{3,7},{4,0},{5,1},{6,2},{7,3},{8,12},{9,13},{10,... | collective-permute-start | bytes 18440 | tf_op jit(solution)/shard_map/ppermute | solution.py:31
  56.0 7.6 %collective-permute-start.5 = (f32[1,1536]{1,0:T(1,128)S(1)}, f32[1,1536]{1,0:T(1,128)S(1)}, u32[]{:S(2)}, u32[]{:S(2)}) collective-permute-start(f32[1,1536]{1,0:T(1,128)S(1)} %add.129), channel_id=1, source_target_pairs={{0,8},{1,9},{2,10},{3,11},{4,12},{5,13},{6,14},{7,15},{8,0},{9,1},... | collective-permute-start | bytes 18440 | tf_op jit(solution)/shard_map/ppermute | solution.py:31
  63.6 5.2 %collective-permute-start.6 = (f32[1,1536]{1,0:T(1,128)S(1)}, f32[1,1536]{1,0:T(1,128)S(1)}, u32[]{:S(2)}, u32[]{:S(2)}) collective-permute-start(f32[1,1536]{1,0:T(1,128)S(1)} %add.130), channel_id=1, source_target_pairs={{0,16},{1,17},{2,18},{3,19},{4,20},{5,21},{6,22},{7,23},{8,24},{9,... | collective-permute-start | bytes 18440 | tf_op jit(solution)/shard_map/ppermute | solution.py:31
  69.1 4.9 %collective-permute-start.7 = (f32[8,2560]{1,0:T(8,128)S(1)}, f32[8,2560]{1,0:T(8,128)S(1)}, u32[]{:S(2)}, u32[]{:S(2)}) collective-permute-start(f32[8,2560]{1,0:T(8,128)S(1)} %dynamic_update_slice.5), channel_id=1, source_target_pairs={{0,32},{32,0},{64,96},{96,64},{128,160},{160,128},{192,224},{224,1... | collective-permute-start | bytes 245768 | tf_op jit(solution)/shard_map/ppermute | solution.py:31
  74.4 6.0 %collective-permute-start.8 = (f32[8,2560]{1,0:T(8,128)S(1)}, f32[8,2560]{1,0:T(8,128)S(1)}, u32[]{:S(2)}, u32[]{:S(2)}) collective-permute-start(f32[8,2560]{1,0:T(8,128)S(1)} %add.133), channel_id=1, source_target_pairs={{0,64},{32,96},{64,0},{96,32},{128,192},{160,224},{192,128},{224,1... | collective-permute-start | bytes 245768 | tf_op jit(solution)/shard_map/ppermute | solution.py:31
  80.4 4.7 %collective-permute-start.9 = (f32[8,2560]{1,0:T(8,128)S(1)}, f32[8,2560]{1,0:T(8,128)S(1)}, u32[]{:S(2)}, u32[]{:S(2)}) collective-permute-start(f32[8,2560]{1,0:T(8,128)S(1)} %add.134), channel_id=1, source_target_pairs={{0,128},{32,160},{64,192},{96,224},{128,0},{160,32},{192,64},{224,... | collective-permute-start | bytes 245768 | tf_op jit(solution)/shard_map/ppermute | solution.py:31
  85.3 8.6 %copy-start.2 = (f32[1,8,64,1536]{3,0,2,1:T(1,128)S(1)}, f32[1,8,64,1536]{3,0,2,1:T(1,128)}, u32[]{:S(2)}) copy-start(f32[1,8,64,1536]{3,0,2,1:T(1,128)} %copy-done.1) | copy-start | bytes 9437188
  97.9 8.7 %copy-start.4 = (f32[1,8,64,1536]{3,2,1,0:T(8,128)}, f32[1,8,64,1536]{3,2,1,0:T(8,128)S(1)}, u32[]{:S(2)}) copy-start(f32[1,8,64,1536]{3,2,1,0:T(8,128)S(1)} %subtract_multiply_fusion) | copy-start | bytes 9437188
  97.9 6.2 %copy-start.3 = (f32[1,8,64,1536]{3,0,2,1:T(1,128)S(1)}, f32[1,8,64,1536]{3,0,2,1:T(1,128)}, u32[]{:S(2)}) copy-start(f32[1,8,64,1536]{3,0,2,1:T(1,128)} %copy-done.1) | copy-start | bytes 9437188
  99.5 24.8 %collective-permute-start.12 = (f32[1,3,64,1536]{3,2,1,0:T(8,128)}, f32[1,3,64,1536]{3,2,1,0:T(8,128)}, u32[]{:S(2)}, u32[]{:S(2)}) collective-permute-start(f32[1,3,64,1536]{3,2,1,0:T(8,128)} %get-tuple-element.28), channel_id=1, source_target_pairs={{1,0},{2,1},{3,2},{4,3},{5,4},{6,5},{7,6},{8,7},{9,8},{10,9},{11,1... | collective-permute-start | bytes 3538952 | tf_op jit(solution)/shard_map/ppermute | solution.py:16
  101.7 22.7 %collective-permute-start.11 = (f32[1,3,64,1536]{3,2,1,0:T(8,128)}, f32[1,3,64,1536]{3,2,1,0:T(8,128)}, u32[]{:S(2)}, u32[]{:S(2)}) collective-permute-start(f32[1,3,64,1536]{3,2,1,0:T(8,128)} %get-tuple-element.27), channel_id=1, source_target_pairs={{0,1},{1,2},{2,3},{3,4},{4,5},{5,6},{6,7},{7,8},{8,9},{9,10},{10,1... | collective-permute-start | bytes 3538952 | tf_op jit(solution)/shard_map/ppermute | solution.py:13
  123.0 13.6 %collective-permute-start.10 = (f32[37632]{0:T(1024)}, f32[37632]{0:T(1024)}, u32[]{:S(2)}, u32[]{:S(2)}) collective-permute-start(f32[37632]{0:T(1024)} %slice_select_fusion), channel_id=1, source_target_pairs={{0,1},{1,0},{2,3},{3,2},{4,5},{5,4},{6,7},{7,6},{8,9},{9,8},{10,11... | collective-permute-start | bytes 451592 | tf_op jit(solution)/shard_map/ppermute | solution.py:67
  137.5 0.7 copy-start.6
  138.8 9.0 %collective-permute-start.13 = (f32[18816]{0:T(1024)}, f32[18816]{0:T(1024)S(1)}, u32[]{:S(2)}, u32[]{:S(2)}) collective-permute-start(f32[18816]{0:T(1024)} %slice_select_fusion.1), channel_id=1, source_target_pairs={{0,2},{1,3},{2,0},{3,1},{4,6},{5,7},{6,4},{7,5},{8,10},{9,11},{10,... | collective-permute-start | bytes 225800 | tf_op jit(solution)/shard_map/ppermute | solution.py:67
  140.3 7.6 %copy-start.7 = (f32[37632]{0:T(1024)S(1)}, f32[37632]{0:T(1024)}, u32[]{:S(2)}) copy-start(f32[37632]{0:T(1024)} %copy-done.6) | copy-start | bytes 451588
  148.0 4.1 %collective-permute-start.14 = (f32[9408]{0:T(1024)S(1)}, f32[9408]{0:T(1024)S(1)}, u32[]{:S(2)}, u32[]{:S(2)}) collective-permute-start(f32[9408]{0:T(1024)S(1)} %slice_select_fusion.2), channel_id=1, source_target_pairs={{0,32},{32,0},{64,96},{96,64},{128,160},{160,128},{192,224},{224,1... | collective-permute-start | bytes 112904 | tf_op jit(solution)/shard_map/ppermute | solution.py:67
  152.1 5.4 %collective-permute-start.15 = (f32[9408]{0:T(1024)S(1)}, f32[9408]{0:T(1024)S(1)}, u32[]{:S(2)}, u32[]{:S(2)}) collective-permute-start(f32[9408]{0:T(1024)S(1)} %select_add_fusion.2), channel_id=1, source_target_pairs={{0,4},{1,5},{2,6},{3,7},{4,0},{5,1},{6,2},{7,3},{8,12},{9,13},{10,... | collective-permute-start | bytes 112904 | tf_op jit(solution)/shard_map/ppermute | solution.py:74
  157.6 7.9 %collective-permute-start.16 = (f32[9408]{0:T(1024)S(1)}, f32[9408]{0:T(1024)S(1)}, u32[]{:S(2)}, u32[]{:S(2)}) collective-permute-start(f32[9408]{0:T(1024)S(1)} %add.146), channel_id=1, source_target_pairs={{0,8},{1,9},{2,10},{3,11},{4,12},{5,13},{6,14},{7,15},{8,0},{9,1},... | collective-permute-start | bytes 112904 | tf_op jit(solution)/shard_map/ppermute | solution.py:74
  165.5 5.5 %collective-permute-start.17 = (f32[9408]{0:T(1024)S(1)}, f32[9408]{0:T(1024)S(1)}, u32[]{:S(2)}, u32[]{:S(2)}) collective-permute-start(f32[9408]{0:T(1024)S(1)} %add.147), channel_id=1, source_target_pairs={{0,16},{1,17},{2,18},{3,19},{4,20},{5,21},{6,22},{7,23},{8,24},{9,... | collective-permute-start | bytes 112904 | tf_op jit(solution)/shard_map/ppermute | solution.py:74
  171.0 5.9 %collective-permute-start.18 = (f32[9408]{0:T(1024)S(1)}, f32[9408]{0:T(1024)S(1)}, u32[]{:S(2)}, u32[]{:S(2)}) collective-permute-start(f32[9408]{0:T(1024)S(1)} %add.148), channel_id=1, source_target_pairs={{0,64},{32,96},{64,0},{96,32},{128,192},{160,224},{192,128},{224,1... | collective-permute-start | bytes 112904 | tf_op jit(solution)/shard_map/ppermute | solution.py:74
  176.9 4.0 %collective-permute-start.19 = (f32[9408]{0:T(1024)S(1)}, f32[9408]{0:T(1024)S(1)}, u32[]{:S(2)}, u32[]{:S(2)}) collective-permute-start(f32[9408]{0:T(1024)S(1)} %add.149), channel_id=1, source_target_pairs={{0,128},{32,160},{64,192},{96,224},{128,0},{160,32},{192,64},{224,... | collective-permute-start | bytes 112904 | tf_op jit(solution)/shard_map/ppermute | solution.py:74
  181.0 4.0 %collective-permute-start.20 = (f32[9408]{0:T(1024)S(1)}, f32[9408]{0:T(1024)S(1)}, u32[]{:S(2)}, u32[]{:S(2)}) collective-permute-start(f32[9408]{0:T(1024)S(1)} %add.150), channel_id=1, source_target_pairs={{0,32},{32,0},{64,96},{96,64},{128,160},{160,128},{192,224},{224,1... | collective-permute-start | bytes 112904 | tf_op jit(solution)/shard_map/ppermute | solution.py:78
  185.1 4.5 %collective-permute-start.21 = (f32[18816]{0:T(1024)S(1)}, f32[18816]{0:T(1024)S(1)}, u32[]{:S(2)}, u32[]{:S(2)}) collective-permute-start(f32[18816]{0:T(1024)S(1)} %maximum_select_fusion.2), channel_id=1, source_target_pairs={{0,2},{1,3},{2,0},{3,1},{4,6},{5,7},{6,4},{7,5},{8,10},{9,11},{10,... | collective-permute-start | bytes 225800 | tf_op jit(solution)/shard_map/ppermute | solution.py:78
  189.6 2.7 %collective-permute-start.22 = (f32[37632]{0:T(1024)S(1)}, f32[37632]{0:T(1024)S(1)}, u32[]{:S(2)}, u32[]{:S(2)}) collective-permute-start(f32[37632]{0:T(1024)S(1)} %maximum_select_fusion.1), channel_id=1, source_target_pairs={{0,1},{1,0},{2,3},{3,2},{4,5},{5,4},{6,7},{7,6},{8,9},{9,8},{10,11... | collective-permute-start | bytes 451592 | tf_op jit(solution)/shard_map/ppermute | solution.py:78
